TPU v7x, 32 devices: a whole 2x2x4 slice. The times are simulated.
32 devices in a mesh: gx: 4 (over x, core), gy: 8 (over z, y).
Axes of the slice: x: 2, y: 2, z: 4, core: 2. Of those that a mesh axis runs over, the one named last changes fastest.
Arguments:
- fine_wave: float32 [9, 12, 24, 3072], P(None, None, 'gx', 'gy'), may hold values from -6 to 6
- fine_memory: float32 [6, 12, 24, 3072], P(None, None, 'gx', 'gy'), may hold values from -6 to 6
- fine_material: int32 [12, 24, 3072], P(None, 'gx', 'gy'), may hold values from 0 to 7
- fine_mechanism: int32 [12, 24, 3072], P(None, 'gx', 'gy'), may hold values from 0 to 3
- fine_metric: float32 [12, 24, 3072], P(None, 'gx', 'gy'), may hold values from 0.7 to 1.4
- coarse_wave: float32 [9, 8, 8, 1024], P(None, None, 'gx', 'gy'), may hold values from -6 to 6
- coarse_memory: float32 [6, 8, 8, 1024], P(None, None, 'gx', 'gy'), may hold values from -6 to 6
- coarse_material: int32 [8, 8, 1024], P(None, 'gx', 'gy'), may hold values from 0 to 7
- coarse_mechanism: int32 [8, 8, 1024], P(None, 'gx', 'gy'), may hold values from 0 to 3
- material_table: float32 [3, 8], replicated, may hold values from 0.4 to 1.5
- attenuation_table: float32 [2, 4], replicated, may hold values from 0.2 to 0.9
Outputs:
- fine_wavefield_output: float32 [9, 12, 24, 3072], P(None, None, 'gx', 'gy')
- fine_memory_out: float32 [6, 12, 24, 3072], P(None, None, 'gx', 'gy')
- coarse_wave_out: float32 [9, 8, 8, 1024], P(None, None, 'gx', 'gy')
- coarse_memory_out: float32 [6, 8, 8, 1024], P(None, None, 'gx', 'gy')
All inputs are finite; a program needn't handle non-finite values.
Results may differ from a plain program's by a relative error of at most 0.000062.
Values sent between devices are 32-bit elements; how exact they have to be, the bound alone decides.
No kernel may reach another device: no remote copies, remote signals or barrier semaphores. Data moves between devices by JAX's collectives and lax.ppermute only.
A program may use at most 64 MiB of HBM per device.

v0:
```python
import jax
import jax.numpy as jnp
import numpy as np
from jax import lax
from jax.sharding import PartitionSpec as P

step_size = 0.1
penalty = 0.1 * 48.0 / 17.0
closure = [
    [-24.0 / 17.0, 59.0 / 34.0, -4.0 / 17.0, -3.0 / 34.0, 0.0, 0.0],
    [-0.5, 0.0, 0.5, 0.0, 0.0, 0.0],
    [4.0 / 43.0, -59.0 / 86.0, 0.0, 59.0 / 86.0, -4.0 / 43.0, 0.0],
    [3.0 / 98.0, 0.0, -59.0 / 98.0, 0.0, 32.0 / 49.0, -4.0 / 49.0],
]
face_rows = np.array([0, 1, 2, 7, 8, 5])


def padded_2(block, sides, width):
    for axis, dim in sides:
        count = lax.axis_size(axis)
        forward = [(i, i + 1) for i in range(count - 1)]
        backward = [(target, source) for source, target in forward]
        low = lax.ppermute(
            lax.slice_in_dim(block, block.shape[dim] - width, None, axis=dim), axis, forward
        )
        high = lax.ppermute(lax.slice_in_dim(block, 0, width, axis=dim), axis, backward)
        block = jnp.concatenate([low, block, high], axis=dim)
    return block


def sbp_table(layers, spacing):
    table = np.zeros((layers, layers))
    for line_at in range(4):
        for column in range(6):
            table[line_at, column] = closure[line_at][column]
            table[layers - 1 - line_at, layers - 1 - column] = -closure[line_at][column]
    for line_at in range(4, layers - 4):
        table[line_at, line_at - 2 : line_at + 3] = [
            1.0 / 12.0,
            -2.0 / 3.0,
            0.0,
            2.0 / 3.0,
            -1.0 / 12.0,
        ]
    return jnp.asarray(table / spacing, dtype=jnp.float32)


def shifted(padded, offset, length, along):
    return lax.slice_in_dim(padded, offset, offset + length, axis=along)


def central_diff(padded, along, spacing):
    length = padded.shape[along] - 4
    return (
        shifted(padded, 0, length, along)
        - 8.0 * shifted(padded, 1, length, along)
        + 8.0 * shifted(padded, 3, length, along)
        - shifted(padded, 4, length, along)
    ) / (12.0 * spacing)


def vertical_diff(fields, matrix):
    return jnp.einsum("kz,czxy->ckxy", matrix, fields, precision=lax.Precision.HIGHEST)


def lookup_table(grid_cell_index, values):
    result = jnp.zeros(grid_cell_index.shape, jnp.float32)
    for kind_at in range(values.shape[0]):
        result = result + jnp.where(grid_cell_index == kind_at, values[kind_at], jnp.float32(0.0))
    return result


def velocity_rate(stress_pad, buoyancy, metric, matrix, spacing):
    slope_x = central_diff(stress_pad[:, :, :, 2:-2], 2, spacing)
    slope_y = central_diff(stress_pad[:, :, 2:-2, :], 3, spacing)
    slope_z = metric * vertical_diff(stress_pad[:, :, 2:-2, 2:-2], matrix)
    rate_x = slope_x[0] + slope_y[3] + slope_z[4]
    rate_y = slope_x[3] + slope_y[1] + slope_z[5]
    rate_z = slope_x[4] + slope_y[5] + slope_z[2]
    return buoyancy * jnp.stack([rate_x, rate_y, rate_z])


def stress_rate(velocity_pad, lame, shear, metric, matrix, spacing):
    slope_x = central_diff(velocity_pad[:, :, :, 2:-2], 2, spacing)
    slope_y = central_diff(velocity_pad[:, :, 2:-2, :], 3, spacing)
    slope_z = metric * vertical_diff(velocity_pad[:, :, 2:-2, 2:-2], matrix)
    cell_volume = lame * (slope_x[0] + slope_y[1] + slope_z[2])
    return jnp.stack(
        [
            cell_volume + 2.0 * shear * slope_x[0],
            cell_volume + 2.0 * shear * slope_y[1],
            cell_volume + 2.0 * shear * slope_z[2],
            shear * (slope_y[0] + slope_x[1]),
            shear * (slope_z[0] + slope_x[2]),
            shear * (slope_z[1] + slope_y[2]),
        ]
    )


def finish_stress(
    wave, memory, velocity_pad, lame, shear, decay, strength, metric, matrix, spacing
):
    rate = stress_rate(velocity_pad, lame, shear, metric, matrix, spacing)
    memory_new = decay * memory + (1.0 - decay) * strength * rate
    stress = wave[3:] + step_size * (rate - memory_new)
    return (stress, memory_new)


def face_of(velocity, stress, depth):
    return jnp.stack(
        [
            velocity[0, depth],
            velocity[1, depth],
            velocity[2, depth],
            stress[4, depth],
            stress[5, depth],
            stress[2, depth],
        ]
    )


def prolong_axis(padded, along):
    length = padded.shape[along] - 2
    left = shifted(padded, 0, length, along)
    middle = shifted(padded, 1, length, along)
    right = shifted(padded, 2, length, along)
    parts = jnp.stack(
        [(left + 2.0 * middle) / 3.0, middle, (2.0 * middle + right) / 3.0], axis=along + 1
    )
    shape = list(middle.shape)
    shape[along] = shape[along] * 3
    return parts.reshape(tuple(shape))


def split_three(padded, offset, length, along):
    part = shifted(padded, offset, 3 * length, along)
    return part.reshape(part.shape[:along] + (length, 3) + part.shape[along + 1 :])


def pick_part(parts, number, along):
    return lax.index_in_dim(parts, number, along + 1, keepdims=False)


def restrict_axis(padded, along):
    length = (padded.shape[along] - 2) // 3
    first = split_three(padded, 0, length, along)
    middle = split_three(padded, 1, length, along)
    last = split_three(padded, 2, length, along)
    return (
        pick_part(first, 0, along)
        + 2.0 * pick_part(middle, 0, along)
        + 3.0 * pick_part(middle, 1, along)
        + 2.0 * pick_part(middle, 2, along)
        + pick_part(last, 2, along)
    ) / 9.0


def local(
    fine_wave,
    fine_memory,
    fine_material,
    fine_mechanism,
    fine_metric,
    coarse_wave,
    coarse_memory,
    coarse_material,
    coarse_mechanism,
    material_table,
    attenuation_table,
):
    fine_matrix = sbp_table(fine_wave.shape[1], 1.0)
    coarse_matrix = sbp_table(coarse_wave.shape[1], 3.0)
    fine_buoy = lookup_table(fine_material, material_table[0])
    fine_lame_moduli = lookup_table(fine_material, material_table[1])
    fine_shear = lookup_table(fine_material, material_table[2])
    fine_decay = lookup_table(fine_mechanism, attenuation_table[0])
    fine_strength = lookup_table(fine_mechanism, attenuation_table[1])
    coarse_buoy = lookup_table(coarse_material, material_table[0])
    coarse_lame = lookup_table(coarse_material, material_table[1])
    coarse_shear = lookup_table(coarse_material, material_table[2])
    coarse_decay = lookup_table(coarse_mechanism, attenuation_table[0])
    coarse_strength = lookup_table(coarse_mechanism, attenuation_table[1])
    stress_pad = padded_2(fine_wave[3:], (("gx", 2), ("gy", 3)), 2)
    fine_velocity = fine_wave[:3] + step_size * velocity_rate(
        stress_pad, fine_buoy, fine_metric, fine_matrix, 1.0
    )
    velocity_pad = padded_2(fine_velocity, (("gx", 2), ("gy", 3)), 2)
    fine_grid_stress, fine_mem = finish_stress(
        fine_wave,
        fine_memory,
        velocity_pad,
        fine_lame_moduli,
        fine_shear,
        fine_decay,
        fine_strength,
        fine_metric,
        fine_matrix,
        1.0,
    )
    coarse_pad = padded_2(coarse_wave[3:], (("gx", 2), ("gy", 3)), 2)
    coarse_grid_velocity = coarse_wave[:3] + step_size * velocity_rate(
        coarse_pad, coarse_buoy, 1.0, coarse_matrix, 3.0
    )
    coarse_velocity_padded = padded_2(coarse_grid_velocity, (("gx", 2), ("gy", 3)), 2)
    coarse_stress, coarse_mem = finish_stress(
        coarse_wave,
        coarse_memory,
        coarse_velocity_padded,
        coarse_lame,
        coarse_shear,
        coarse_decay,
        coarse_strength,
        1.0,
        coarse_matrix,
        3.0,
    )
    depth = fine_wave.shape[1] - 1
    fine_face = face_of(fine_velocity, fine_grid_stress, depth)
    coarse_face = face_of(coarse_grid_velocity, coarse_stress, 0)
    coarse_padded = padded_2(coarse_face, (("gx", 1), ("gy", 2)), 1)
    fine_padded = padded_2(fine_face, (("gx", 1), ("gy", 2)), 1)
    fine_new = fine_face - penalty * (fine_face - prolong_axis(prolong_axis(coarse_padded, 1), 2))
    coarse_updated_fields = coarse_face - penalty * (
        coarse_face - restrict_axis(restrict_axis(fine_padded, 1), 2)
    )
    fine_out = jnp.concatenate([fine_velocity, fine_grid_stress]).at[face_rows, depth].set(fine_new)
    coarse_out = (
        jnp.concatenate([coarse_grid_velocity, coarse_stress])
        .at[face_rows, 0]
        .set(coarse_updated_fields)
    )
    return (fine_out, fine_mem, coarse_out, coarse_mem)


def solution(mesh):
    in_specs = (
        P(None, None, "gx", "gy"),
        P(None, None, "gx", "gy"),
        P(None, "gx", "gy"),
        P(None, "gx", "gy"),
        P(None, "gx", "gy"),
        P(None, None, "gx", "gy"),
        P(None, None, "gx", "gy"),
        P(None, "gx", "gy"),
        P(None, "gx", "gy"),
        P(),
        P(),
    )
    out_specs = (
        P(None, None, "gx", "gy"),
        P(None, None, "gx", "gy"),
        P(None, None, "gx", "gy"),
        P(None, None, "gx", "gy"),
    )
    return jax.shard_map(local, mesh=mesh, in_specs=in_specs, out_specs=out_specs, check_vma=False)
```

profile of v0, /device:TPU:1, one launch (start us, length us, event | category | flops | bytes accessed | tf_op | source)
XLA Modules:
  0.0 197.1 jit_solution(13147142996353142430)
XLA Ops:
  3.5 4.5 %collective-permute-start.8 = (f32[6,8,2,128]{3,1,2,0:T(8,128)S(1)}, f32[6,8,2,128]{3,1,2,0:T(8,128)S(1)}, u32[]{:S(2)}, u32[]{:S(2)}) collective-permute-start(f32[6,8,2,128]{3,1,2,0:T(8,128)S(1)} %copy.151), channel_id=1, source_target_pairs={{0,8},{8,16},{16,24},{1,9},{9,17},{17,25},{2,10},{10,18},{18,26},{... | collective-permute-start | bytes 147464 | tf_op jit(solution)/shard_map/ppermute | solution.py:23
  13.6 2.7 %collective-permute-start.1 = (f32[6,12,2,384]{3,0,2,1:T(8,128)}, f32[6,12,2,384]{3,0,2,1:T(8,128)}, u32[]{:S(2)}, u32[]{:S(2)}) collective-permute-start(f32[6,12,2,384]{3,0,2,1:T(8,128)} %copy.144), channel_id=1, source_target_pairs={{8,0},{16,8},{24,16},{9,1},{17,9},{25,17},{10,2},{18,10},{26,18},{... | collective-permute-start | bytes 663560 | tf_op jit(solution)/shard_map/ppermute | solution.py:26
  18.5 6.0 %select_add_fusion.2 = (f32[12,6,384]{2,1,0:T(8,128)S(1)}, pred[12,6,384]{2,1,0:T(8,128)(4,1)}, pred[12,6,384]{2,1,0:T(8,128)(4,1)}, pred[12,6,384]{2,1,0:T(8,12...) fusion(f32[]{:T(128)} %bitcast.7, f32[]{:T(128)} %bitcast.6, ...), kind=kLoop, calls=%fused_computation.81 | loop fusion | flops 635904 | bytes 442400 | tf_op jit(solution)/shard_map/add | solution.py:69
  24.5 5.1 %select_add_fusion.5 = (f32[8,2,128]{2,0,1:T(8,128)S(1)}, pred[8,2,128]{2,0,1:T(8,128)(4,1)S(1)}, pred[8,2,128]{2,0,1:T(8,128)(4,1)S(1)}, pred[8,2,128]{2,0,1:T(...) fusion(f32[]{:T(128)} %bitcast.7, f32[]{:T(128)} %bitcast.6, ...), kind=kLoop, calls=%fused_computation.229 | loop fusion | flops 47104 | bytes 32800 | tf_op jit(solution)/shard_map/add | solution.py:69
  32.0 3.4 %select_add_fusion = (f32[12,6,384]{2,1,0:T(8,128)}, pred[12,6,384]{2,1,0:T(8,128)(4,1)S(1)}, pred[12,6,384]{2,1,0:T(8,128)(4,1)S(1)}, pred[12,6,384]{2,1,0:T(8,128)(4,1)S(1)}, pred[12,6,384]{2,1,0:T(8,128)(4,1)S(1)}) fusion(f32[]{:T(128)} %bitcast.43, f32[]{:T(128)} %bitcast.42, f32[]{:T(128)} %bitcast.41, f32[]{:T(128)} %bitcast.40, ...), kind=kLoop, calls=%fused_computation.79 | loop fusion | flops 304128 | bytes 331792 | tf_op jit(solution)/shard_map/add | solution.py:69
  35.5 6.2 %add_multiply_fusion = f32[12,6,384]{2,1,0:T(8,128)} fusion(pred[12,6,384]{2,1,0:T(8,128)(4,1)S(1)} %get-tuple-element.37, pred[12,6,384]{2,1,0:T(8,128)(4,1)S(1)} %get-tuple-element.36, pred[12,6,384]{2,1,0:T(8,128)(4,1)S(1)} %get-tuple-element.35, pred[12,6,384]{2,1,0:T(8,128)(4,1)S(1)} %get-tuple-element.34, f32[]{:T(128)} %bitcast.47, f32[]{:T(128)} %bitcast.46, ...), kind=kLoop, calls=%fused_computation.78 | loop fusion | flops 442368 | bytes 221216 | tf_op jit(solution)/shard_map/mul | solution.py:104
  41.6 2.7 %select_add_fusion.3 = (f32[8,2,128]{2,0,1:T(8,128)S(1)}, pred[8,2,128]{2,0,1:T(8,128)(4,1)S(1)}, pred[8,2,128]{2,0,1:T(8,128)(4,1)S(1)}, pred[8,2,128]{2,0,1:T(8,128)(4,1)S(1)}, pred[8,2,128]{2,0,1:T(8,128)(4,1)S(1)}) fusion(f32[]{:T(128)} %bitcast.43, f32[]{:T(128)} %bitcast.42, f32[]{:T(128)} %bitcast.41, f32[]{:T(128)} %bitcast.40, ...), kind=kLoop, calls=%fused_computation.226 | loop fusion | flops 22528 | bytes 24592 | tf_op jit(solution)/shard_map/add | solution.py:69
  44.5 3.2 %collective-permute-start.10 = (f32[6,8,6,2]{3,1,2,0:T(8,128)S(1)}, f32[6,8,6,2]{3,1,2,0:T(8,128)S(1)}, u32[]{:S(2)}, u32[]{:S(2)}) collective-permute-start(f32[6,8,6,2]{3,1,2,0:T(8,128)S(1)} %get-tuple-element.81), channel_id=1, source_target_pairs={{0,1},{1,2},{2,3},{3,4},{4,5},{5,6},{6,7},{8,9},{9,10},{10,11},{11... | collective-permute-start | bytes 6920 | tf_op jit(solution)/shard_map/ppermute | solution.py:23
  49.0 5.4 %add_multiply_fusion.1 = f32[8,2,128]{2,0,1:T(8,128)S(1)} fusion(pred[8,2,128]{2,0,1:T(8,128)(4,1)S(1)} %get-tuple-element.18, pred[8,2,128]{2,0,1:T(8,128)(4,1)S(1)} %get-tuple-element.17, pred[8,2,128]{2,0,1:T(8,128)(4,1)S(1)} %get-tuple-element.16, pred[8,2,128]{2,0,1:T(8,128)(4,1)S(1)} %get-tuple-element.15, f32[]{:T(128)} %bitcast.47, f32[]{:T(128)} %bitcast.46, ...), kind=kLoop, calls=%fused_computation.225 | loop fusion | flops 32768 | bytes 16416 | tf_op jit(solution)/shard_map/mul | solution.py:104
  60.3 3.0 %collective-permute-done.13 = f32[3,8,2,128]{3,1,2,0:T(8,128)S(1)} collective-permute-done((f32[3,8,2,128]{3,1,2,0:T(8,128)S(1)}, f32[3,8,2,128]{3,1,2,0:T(8,128)S(1)}, u32[]{:S(2)}, u32[]{:S(2)}) %collective-permute-start.13) | collective-permute-done | bytes 24608 | tf_op jit(solution)/shard_map/ppermute | solution.py:26
  63.4 4.0 %collective-permute-start.14 = (f32[3,8,6,2]{3,1,2,0:T(8,128)S(1)}, f32[3,8,6,2]{3,1,2,0:T(8,128)S(1)}, u32[]{:S(2)}, u32[]{:S(2)}) collective-permute-start(f32[3,8,6,2]{3,1,2,0:T(8,128)S(1)} %get-tuple-element.93), channel_id=1, source_target_pairs={{0,1},{1,2},{2,3},{3,4},{4,5},{5,6},{6,7},{8,9},{9,10},{10,11},{11... | collective-permute-start | bytes 3464 | tf_op jit(solution)/shard_map/ppermute | solution.py:23
  68.8 4.3 %collective-permute-done.15 = f32[3,8,6,2]{3,1,2,0:T(8,128)S(1)} collective-permute-done((f32[3,8,6,2]{3,1,2,0:T(8,128)S(1)}, f32[3,8,6,2]{3,1,2,0:T(8,128)S(1)}, u32[]{:S(2)}, u32[]{:S(2)}) %collective-permute-start.15) | collective-permute-done | bytes 1184 | tf_op jit(solution)/shard_map/ppermute | solution.py:26
  73.2 9.8 %constant_dynamic-update-slice_fusion.12 = (f32[6,8,2,128]{3,1,2,0:T(8,128)S(1)}, f32[8,2,128]{2,0,1:T(8,128)S(1)}, f32[8,2,128]{2,0,1:T(8,128)S(1)}) fusion(f32[3,8,2,128]{3,1,2,0:T(8,128)S(1)} %fusion.64, pred[8,2,128]{2,0,1:T(8,128)(4,1)S(1)} %get-tuple-element.30, f32[]{:T(128)} %bitcast.31, pred[8,2,128]{2,0,1:T(8,128)(4,1)S(1)} %get-tuple-element.29, ...), kind=kLoop, calls=%fused_computation.118 | loop fusion | flops 73727 | bytes 65600
  83.2 3.1 %collective-permute-start.16 = (f32[6,1,128]{2,1,0:T(1,128)S(1)}, f32[6,1,128]{2,1,0:T(1,128)S(1)}, u32[]{:S(2)}, u32[]{:S(2)}) collective-permute-start(f32[6,1,128]{2,1,0:T(1,128)S(1)} %get-tuple-element.114), channel_id=1, source_target_pairs={{0,8},{8,16},{16,24},{1,9},{9,17},{17,25},{2,10},{10,18},{18,26},{... | collective-permute-start | bytes 9224 | tf_op jit(solution)/shard_map/ppermute | solution.py:23
  91.3 4.5 %collective-permute-start.18 = (f32[6,4,1]{2,1,0:T(4,128)S(1)}, f32[6,4,1]{2,1,0:T(4,128)S(1)}, u32[]{:S(2)}, u32[]{:S(2)}) collective-permute-start(f32[6,4,1]{2,1,0:T(4,128)S(1)} %get-tuple-element.112), channel_id=1, source_target_pairs={{0,1},{1,2},{2,3},{3,4},{4,5},{5,6},{6,7},{8,9},{9,10},{10,11},{11... | collective-permute-start | bytes 296 | tf_op jit(solution)/shard_map/ppermute | solution.py:23
  97.1 3.1 %collective-permute-done.19 = f32[6,4,1]{2,1,0:T(4,128)S(1)} collective-permute-done((f32[6,4,1]{2,1,0:T(4,128)S(1)}, f32[6,4,1]{2,1,0:T(4,128)S(1)}, u32[]{:S(2)}, u32[]{:S(2)}) %collective-permute-start.19) | collective-permute-done | bytes 128 | tf_op jit(solution)/shard_map/ppermute | solution.py:26
  107.2 3.0 %collective-permute-start.2 = (f32[6,12,10,2]{3,0,2,1:T(8,128)S(1)}, f32[6,12,10,2]{3,0,2,1:T(8,128)S(1)}, u32[]{:S(2)}, u32[]{:S(2)}) collective-permute-start(f32[6,12,10,2]{3,0,2,1:T(8,128)S(1)} %get-tuple-element.53), channel_id=1, source_target_pairs={{0,1},{1,2},{2,3},{3,4},{4,5},{5,6},{6,7},{8,9},{9,10},{10,11},{11... | collective-permute-start | bytes 17288 | tf_op jit(solution)/shard_map/ppermute | solution.py:23
  111.7 19.8 %collective-permute-done.2 = f32[6,12,10,2]{3,0,2,1:T(8,128)S(1)} collective-permute-done((f32[6,12,10,2]{3,0,2,1:T(8,128)S(1)}, f32[6,12,10,2]{3,0,2,1:T(8,128)S(1)}, u32[]{:S(2)}, u32[]{:S(2)}) %collective-permute-start.2) | collective-permute-done | bytes 5792 | tf_op jit(solution)/shard_map/ppermute | solution.py:23
  141.3 3.4 %collective-permute-done.5 = f32[3,12,2,384]{3,2,1,0:T(2,128)S(1)} collective-permute-done((f32[3,12,2,384]{3,2,1,0:T(2,128)S(1)}, f32[3,12,2,384]{3,2,1,0:T(2,128)S(1)}, u32[]{:S(2)}, u32[]{:S(2)}) %collective-permute-start.5) | collective-permute-done | bytes 110624 | tf_op jit(solution)/shard_map/ppermute | solution.py:26
  146.5 4.7 %collective-permute-start.6 = (f32[3,12,10,2]{3,2,1,0:T(8,128)S(1)}, f32[3,12,10,2]{3,2,1,0:T(8,128)S(1)}, u32[]{:S(2)}, u32[]{:S(2)}) collective-permute-start(f32[3,12,10,2]{3,2,1,0:T(8,128)S(1)} %slice.806), channel_id=1, source_target_pairs={{0,1},{1,2},{2,3},{3,4},{4,5},{5,6},{6,7},{8,9},{9,10},{10,11},{11... | collective-permute-start | bytes 8648 | tf_op jit(solution)/shard_map/ppermute | solution.py:23
  153.3 6.9 %collective-permute-done.6 = f32[3,12,10,2]{3,2,1,0:T(8,128)S(1)} collective-permute-done((f32[3,12,10,2]{3,2,1,0:T(8,128)S(1)}, f32[3,12,10,2]{3,2,1,0:T(8,128)S(1)}, u32[]{:S(2)}, u32[]{:S(2)}) %collective-permute-start.6) | collective-permute-done | bytes 2912 | tf_op jit(solution)/shard_map/ppermute | solution.py:23
  161.9 10.0 %bitcast_dynamic-update-slice_fusion.1 = (f32[6,12,6,384]{3,2,1,0:T(8,128)S(1)}, f32[12,6,384]{2,1,0:T(8,128)S(1)}, f32[12,6,384]{2,1,0:T(8,128)S(1)}) fusion(f32[3,12,6,384]{3,2,1,0:T(8,128)S(1)} %fusion.17, pred[12,6,384]{2,1,0:T(8,128)(4,1)S(1)} %copy-done.16, f32[]{:T(128)} %bitcast.31, pred[12,6,384]{2,1,0:T(8,128)(4,1)S(1)} %copy-done.15, f32[]{:T(128)} %bitcast.30, ...), kind=kLoop, calls=%fused_computation.77 | loop fusion | flops 995327 | bytes 995392
  181.7 3.9 %collective-permute-start.22 = (f32[6,8,1]{2,0,1:T(8,128)S(1)}, f32[6,8,1]{2,0,1:T(8,128)S(1)}, u32[]{:S(2)}, u32[]{:S(2)}) collective-permute-start(f32[6,8,1]{2,0,1:T(8,128)S(1)} %get-tuple-element.89), channel_id=1, source_target_pairs={{0,1},{1,2},{2,3},{3,4},{4,5},{5,6},{6,7},{8,9},{9,10},{10,11},{11... | collective-permute-start | bytes 584 | tf_op jit(solution)/shard_map/ppermute | solution.py:23
  187.7 3.0 %collective-permute-done.23 = f32[6,8,1]{2,0,1:T(8,128)S(1)} collective-permute-done((f32[6,8,1]{2,0,1:T(8,128)S(1)}, f32[6,8,1]{2,0,1:T(8,128)S(1)}, u32[]{:S(2)}, u32[]{:S(2)}) %collective-permute-start.23) | collective-permute-done | bytes 224 | tf_op jit(solution)/shard_map/ppermute | solution.py:26
  (206 shorter events, 69.5 us)
Async XLA Ops:
  1.6 42.8 %collective-permute-start.9 = (f32[6,8,2,128]{3,1,2,0:T(8,128)S(1)}, f32[6,8,2,128]{3,1,2,0:T(8,128)S(1)}, u32[]{:S(2)}, u32[]{:S(2)}) collective-permute-start(f32[6,8,2,128]{3,1,2,0:T(8,128)S(1)} %copy.151), channel_id=1, source_target_pairs={{8,0},{16,8},{24,16},{9,1},{17,9},{25,17},{10,2},{18,10},{26,18},{... | collective-permute-start | bytes 147464 | tf_op jit(solution)/shard_map/ppermute | solution.py:26
  3.5 40.9 %collective-permute-start.8 = (f32[6,8,2,128]{3,1,2,0:T(8,128)S(1)}, f32[6,8,2,128]{3,1,2,0:T(8,128)S(1)}, u32[]{:S(2)}, u32[]{:S(2)}) collective-permute-start(f32[6,8,2,128]{3,1,2,0:T(8,128)S(1)} %copy.151), channel_id=1, source_target_pairs={{0,8},{8,16},{16,24},{1,9},{9,17},{17,25},{2,10},{10,18},{18,26},{... | collective-permute-start | bytes 147464 | tf_op jit(solution)/shard_map/ppermute | solution.py:23
  10.4 94.1 %collective-permute-start = (f32[6,12,2,384]{3,0,2,1:T(8,128)}, f32[6,12,2,384]{3,0,2,1:T(8,128)}, u32[]{:S(2)}, u32[]{:S(2)}) collective-permute-start(f32[6,12,2,384]{3,0,2,1:T(8,128)} %copy.142), channel_id=1, source_target_pairs={{0,8},{8,16},{16,24},{1,9},{9,17},{17,25},{2,10},{10,18},{18,26},{... | collective-permute-start | bytes 663560 | tf_op jit(solution)/shard_map/ppermute | solution.py:23
  13.6 92.4 %collective-permute-start.1 = (f32[6,12,2,384]{3,0,2,1:T(8,128)}, f32[6,12,2,384]{3,0,2,1:T(8,128)}, u32[]{:S(2)}, u32[]{:S(2)}) collective-permute-start(f32[6,12,2,384]{3,0,2,1:T(8,128)} %copy.144), channel_id=1, source_target_pairs={{8,0},{16,8},{24,16},{9,1},{17,9},{25,17},{10,2},{18,10},{26,18},{... | collective-permute-start | bytes 663560 | tf_op jit(solution)/shard_map/ppermute | solution.py:26
  44.5 9.9 %collective-permute-start.10 = (f32[6,8,6,2]{3,1,2,0:T(8,128)S(1)}, f32[6,8,6,2]{3,1,2,0:T(8,128)S(1)}, u32[]{:S(2)}, u32[]{:S(2)}) collective-permute-start(f32[6,8,6,2]{3,1,2,0:T(8,128)S(1)} %get-tuple-element.81), channel_id=1, source_target_pairs={{0,1},{1,2},{2,3},{3,4},{4,5},{5,6},{6,7},{8,9},{9,10},{10,11},{11... | collective-permute-start | bytes 6920 | tf_op jit(solution)/shard_map/ppermute | solution.py:23
  47.7 7.6 %collective-permute-start.11 = (f32[6,8,6,2]{3,1,2,0:T(8,128)S(1)}, f32[6,8,6,2]{3,1,2,0:T(8,128)S(1)}, u32[]{:S(2)}, u32[]{:S(2)}) collective-permute-start(f32[6,8,6,2]{3,1,2,0:T(8,128)S(1)} %get-tuple-element.82), channel_id=1, source_target_pairs={{1,0},{2,1},{3,2},{4,3},{5,4},{6,5},{7,6},{9,8},{10,9},{11,10},{12... | collective-permute-start | bytes 6920 | tf_op jit(solution)/shard_map/ppermute | solution.py:26
  55.5 4.8 %collective-permute-start.12 = (f32[3,8,2,128]{3,1,2,0:T(8,128)S(1)}, f32[3,8,2,128]{3,1,2,0:T(8,128)S(1)}, u32[]{:S(2)}, u32[]{:S(2)}) collective-permute-start(f32[3,8,2,128]{3,1,2,0:T(8,128)S(1)} %fusion.68), channel_id=1, source_target_pairs={{0,8},{8,16},{16,24},{1,9},{9,17},{17,25},{2,10},{10,18},{18,26},{... | collective-permute-start | bytes 73736 | tf_op jit(solution)/shard_map/ppermute | solution.py:23
  58.1 5.1 %collective-permute-start.13 = (f32[3,8,2,128]{3,1,2,0:T(8,128)S(1)}, f32[3,8,2,128]{3,1,2,0:T(8,128)S(1)}, u32[]{:S(2)}, u32[]{:S(2)}) collective-permute-start(f32[3,8,2,128]{3,1,2,0:T(8,128)S(1)} %fusion.68), channel_id=1, source_target_pairs={{8,0},{16,8},{24,16},{9,1},{17,9},{25,17},{10,2},{18,10},{26,18},{... | collective-permute-start | bytes 73736 | tf_op jit(solution)/shard_map/ppermute | solution.py:26
  63.4 5.4 %collective-permute-start.14 = (f32[3,8,6,2]{3,1,2,0:T(8,128)S(1)}, f32[3,8,6,2]{3,1,2,0:T(8,128)S(1)}, u32[]{:S(2)}, u32[]{:S(2)}) collective-permute-start(f32[3,8,6,2]{3,1,2,0:T(8,128)S(1)} %get-tuple-element.93), channel_id=1, source_target_pairs={{0,1},{1,2},{2,3},{3,4},{4,5},{5,6},{6,7},{8,9},{9,10},{10,11},{11... | collective-permute-start | bytes 3464 | tf_op jit(solution)/shard_map/ppermute | solution.py:23
  67.4 5.7 %collective-permute-start.15 = (f32[3,8,6,2]{3,1,2,0:T(8,128)S(1)}, f32[3,8,6,2]{3,1,2,0:T(8,128)S(1)}, u32[]{:S(2)}, u32[]{:S(2)}) collective-permute-start(f32[3,8,6,2]{3,1,2,0:T(8,128)S(1)} %get-tuple-element.94), channel_id=1, source_target_pairs={{1,0},{2,1},{3,2},{4,3},{5,4},{6,5},{7,6},{9,8},{10,9},{11,10},{12... | collective-permute-start | bytes 3464 | tf_op jit(solution)/shard_map/ppermute | solution.py:26
  83.2 6.3 %collective-permute-start.16 = (f32[6,1,128]{2,1,0:T(1,128)S(1)}, f32[6,1,128]{2,1,0:T(1,128)S(1)}, u32[]{:S(2)}, u32[]{:S(2)}) collective-permute-start(f32[6,1,128]{2,1,0:T(1,128)S(1)} %get-tuple-element.114), channel_id=1, source_target_pairs={{0,8},{8,16},{16,24},{1,9},{9,17},{17,25},{2,10},{10,18},{18,26},{... | collective-permute-start | bytes 9224 | tf_op jit(solution)/shard_map/ppermute | solution.py:23
  86.3 4.9 %collective-permute-start.17 = (f32[6,1,128]{2,1,0:T(1,128)S(1)}, f32[6,1,128]{2,1,0:T(1,128)S(1)}, u32[]{:S(2)}, u32[]{:S(2)}) collective-permute-start(f32[6,1,128]{2,1,0:T(1,128)S(1)} %get-tuple-element.115), channel_id=1, source_target_pairs={{8,0},{16,8},{24,16},{9,1},{17,9},{25,17},{10,2},{18,10},{26,18},{... | collective-permute-start | bytes 9224 | tf_op jit(solution)/shard_map/ppermute | solution.py:26
  91.3 5.8 %collective-permute-start.18 = (f32[6,4,1]{2,1,0:T(4,128)S(1)}, f32[6,4,1]{2,1,0:T(4,128)S(1)}, u32[]{:S(2)}, u32[]{:S(2)}) collective-permute-start(f32[6,4,1]{2,1,0:T(4,128)S(1)} %get-tuple-element.112), channel_id=1, source_target_pairs={{0,1},{1,2},{2,3},{3,4},{4,5},{5,6},{6,7},{8,9},{9,10},{10,11},{11... | collective-permute-start | bytes 296 | tf_op jit(solution)/shard_map/ppermute | solution.py:23
  95.8 4.4 %collective-permute-start.19 = (f32[6,4,1]{2,1,0:T(4,128)S(1)}, f32[6,4,1]{2,1,0:T(4,128)S(1)}, u32[]{:S(2)}, u32[]{:S(2)}) collective-permute-start(f32[6,4,1]{2,1,0:T(4,128)S(1)} %get-tuple-element.113), channel_id=1, source_target_pairs={{1,0},{2,1},{3,2},{4,3},{5,4},{6,5},{7,6},{9,8},{10,9},{11,10},{12... | collective-permute-start | bytes 296 | tf_op jit(solution)/shard_map/ppermute | solution.py:26
  107.2 24.3 %collective-permute-start.2 = (f32[6,12,10,2]{3,0,2,1:T(8,128)S(1)}, f32[6,12,10,2]{3,0,2,1:T(8,128)S(1)}, u32[]{:S(2)}, u32[]{:S(2)}) collective-permute-start(f32[6,12,10,2]{3,0,2,1:T(8,128)S(1)} %get-tuple-element.53), channel_id=1, source_target_pairs={{0,1},{1,2},{2,3},{3,4},{4,5},{5,6},{6,7},{8,9},{9,10},{10,11},{11... | collective-permute-start | bytes 17288 | tf_op jit(solution)/shard_map/ppermute | solution.py:23
  110.2 21.3 %collective-permute-start.3 = (f32[6,12,10,2]{3,0,2,1:T(8,128)S(1)}, f32[6,12,10,2]{3,0,2,1:T(8,128)S(1)}, u32[]{:S(2)}, u32[]{:S(2)}) collective-permute-start(f32[6,12,10,2]{3,0,2,1:T(8,128)S(1)} %get-tuple-element.54), channel_id=1, source_target_pairs={{1,0},{2,1},{3,2},{4,3},{5,4},{6,5},{7,6},{9,8},{10,9},{11,10},{12... | collective-permute-start | bytes 17288 | tf_op jit(solution)/shard_map/ppermute | solution.py:26
  136.7 4.6 %collective-permute-start.4 = (f32[3,12,2,384]{3,2,1,0:T(2,128)S(1)}, f32[3,12,2,384]{3,2,1,0:T(2,128)S(1)}, u32[]{:S(2)}, u32[]{:S(2)}) collective-permute-start(f32[3,12,2,384]{3,2,1,0:T(2,128)S(1)} %get-tuple-element.72), channel_id=1, source_target_pairs={{0,8},{8,16},{16,24},{1,9},{9,17},{17,25},{2,10},{10,18},{18,26},{... | collective-permute-start | bytes 331784 | tf_op jit(solution)/shard_map/ppermute | solution.py:23
  138.6 6.1 %collective-permute-start.5 = (f32[3,12,2,384]{3,2,1,0:T(2,128)S(1)}, f32[3,12,2,384]{3,2,1,0:T(2,128)S(1)}, u32[]{:S(2)}, u32[]{:S(2)}) collective-permute-start(f32[3,12,2,384]{3,2,1,0:T(2,128)S(1)} %get-tuple-element.73), channel_id=1, source_target_pairs={{8,0},{16,8},{24,16},{9,1},{17,9},{25,17},{10,2},{18,10},{26,18},{... | collective-permute-start | bytes 331784 | tf_op jit(solution)/shard_map/ppermute | solution.py:26
  145.0 7.9 %collective-permute-start.7 = (f32[3,12,10,2]{3,0,2,1:T(4,128)S(1)}, f32[3,12,10,2]{3,0,2,1:T(4,128)S(1)}, u32[]{:S(2)}, u32[]{:S(2)}) collective-permute-start(f32[3,12,10,2]{3,0,2,1:T(4,128)S(1)} %slice.807), channel_id=1, source_target_pairs={{1,0},{2,1},{3,2},{4,3},{5,4},{6,5},{7,6},{9,8},{10,9},{11,10},{12... | collective-permute-start | bytes 8648 | tf_op jit(solution)/shard_map/ppermute | solution.py:26
  146.5 13.8 %collective-permute-start.6 = (f32[3,12,10,2]{3,2,1,0:T(8,128)S(1)}, f32[3,12,10,2]{3,2,1,0:T(8,128)S(1)}, u32[]{:S(2)}, u32[]{:S(2)}) collective-permute-start(f32[3,12,10,2]{3,2,1,0:T(8,128)S(1)} %slice.806), channel_id=1, source_target_pairs={{0,1},{1,2},{2,3},{3,4},{4,5},{5,6},{6,7},{8,9},{9,10},{10,11},{11... | collective-permute-start | bytes 8648 | tf_op jit(solution)/shard_map/ppermute | solution.py:23
  174.7 4.8 %collective-permute-start.20 = (f32[6,1,384]{2,0,1:T(8,128)S(1)}, f32[6,1,384]{2,0,1:T(8,128)S(1)}, u32[]{:S(2)}, u32[]{:S(2)}) collective-permute-start(f32[6,1,384]{2,0,1:T(8,128)S(1)} %get-tuple-element.91), channel_id=1, source_target_pairs={{0,8},{8,16},{16,24},{1,9},{9,17},{17,25},{2,10},{10,18},{18,26},{... | collective-permute-start | bytes 27656 | tf_op jit(solution)/shard_map/ppermute | solution.py:23
  176.6 5.0 %collective-permute-start.21 = (f32[6,1,384]{2,0,1:T(8,128)S(1)}, f32[6,1,384]{2,0,1:T(8,128)S(1)}, u32[]{:S(2)}, u32[]{:S(2)}) collective-permute-start(f32[6,1,384]{2,0,1:T(8,128)S(1)} %get-tuple-element.92), channel_id=1, source_target_pairs={{8,0},{16,8},{24,16},{9,1},{17,9},{25,17},{10,2},{18,10},{26,18},{... | collective-permute-start | bytes 27656 | tf_op jit(solution)/shard_map/ppermute | solution.py:26
  181.7 6.0 %collective-permute-start.22 = (f32[6,8,1]{2,0,1:T(8,128)S(1)}, f32[6,8,1]{2,0,1:T(8,128)S(1)}, u32[]{:S(2)}, u32[]{:S(2)}) collective-permute-start(f32[6,8,1]{2,0,1:T(8,128)S(1)} %get-tuple-element.89), channel_id=1, source_target_pairs={{0,1},{1,2},{2,3},{3,4},{4,5},{5,6},{6,7},{8,9},{9,10},{10,11},{11... | collective-permute-start | bytes 584 | tf_op jit(solution)/shard_map/ppermute | solution.py:23
  185.6 5.1 %collective-permute-start.23 = (f32[6,8,1]{2,0,1:T(8,128)S(1)}, f32[6,8,1]{2,0,1:T(8,128)S(1)}, u32[]{:S(2)}, u32[]{:S(2)}) collective-permute-start(f32[6,8,1]{2,0,1:T(8,128)S(1)} %get-tuple-element.90), channel_id=1, source_target_pairs={{1,0},{2,1},{3,2},{4,3},{5,4},{6,5},{7,6},{9,8},{10,9},{11,10},{12... | collective-permute-start | bytes 584 | tf_op jit(solution)/shard_map/ppermute | solution.py:26
  (31 other events, 199.4 us)
where the time goes:
time: 199 us; the launch traced here: 197 us
  starting transfers between devices  60.8 us (31%)
  other arithmetic  59.8 us (30%)
  waiting for transfers between devices  49.7 us (25%)
  local copies, waits for them, and re-layouts  23.2 us (12%)
    ppermute x12, starting transfers between devices, padded_2(): lax.ppermute(lax.slice_in_dim(block, block.shape[dim] - width, None, axis...  39.7 us
    ppermute x12, waiting for transfers between devices, padded_2(): lax.ppermute(lax.slice_in_dim(block, block.shape[dim] - width, None, axis...  26.8 us
    ppermute x12, waiting for transfers between devices, padded_2(): lax.ppermute(lax.slice_in_dim(block, 0, width, axis=dim), axis, backward)  22.8 us
    ppermute x12, starting transfers between devices, padded_2(): lax.ppermute(lax.slice_in_dim(block, 0, width, axis=dim), axis, backward)  21.1 us
    unnamed x10, other arithmetic  20 us
    add x4, other arithmetic, lookup_table(): result + jnp.where(grid_cell_index == kind_at, values[kind_at], jnp.float...  17.2 us
    mul x2, other arithmetic, finish_stress(): memory_new = decay * memory + (1.0 - decay) * strength * rate  11.5 us
    unnamed x72, local copies, waits for them, and re-layouts  5.7 us
  transfers between devices with their start and end apart: 24, of which 12 were waited for; matrix products, arithmetic and copies ran while one was open for 29% of the time, Pallas kernels for 0%

commit v1 on v0

v1 whole, which is shorter than its diff:
```python
import math

import jax
import jax.numpy as jnp
import numpy as np
from jax import lax
from jax.sharding import PartitionSpec as P

step_size = 0.1
penalty = 0.1 * 48.0 / 17.0
closure = [
    [-24.0 / 17.0, 59.0 / 34.0, -4.0 / 17.0, -3.0 / 34.0, 0.0, 0.0],
    [-0.5, 0.0, 0.5, 0.0, 0.0, 0.0],
    [4.0 / 43.0, -59.0 / 86.0, 0.0, 59.0 / 86.0, -4.0 / 43.0, 0.0],
    [3.0 / 98.0, 0.0, -59.0 / 98.0, 0.0, 32.0 / 49.0, -4.0 / 49.0],
]


def sbp_table(layers, spacing):
    table = np.zeros((layers, layers))
    for line_at in range(4):
        for column in range(6):
            table[line_at, column] = closure[line_at][column]
            table[layers - 1 - line_at, layers - 1 - column] = -closure[line_at][column]
    for line_at in range(4, layers - 4):
        table[line_at, line_at - 2 : line_at + 3] = [
            1.0 / 12.0,
            -2.0 / 3.0,
            0.0,
            2.0 / 3.0,
            -1.0 / 12.0,
        ]
    return jnp.asarray(table / spacing, dtype=jnp.float32)


def shift_from(block, axis, offset):
    count = lax.axis_size(axis)
    pairs = [(i, i + offset) for i in range(count) if 0 <= i + offset < count]
    return lax.ppermute(block, axis, pairs)


def packed_shift(blocks, axis, offset):
    sizes = [math.prod(b.shape) for b in blocks]
    joined = jnp.concatenate([b.reshape(-1) for b in blocks])
    moved = shift_from(joined, axis, offset)
    out, start = [], 0
    for b, size in zip(blocks, sizes):
        out.append(moved[start : start + size].reshape(b.shape))
        start += size
    return out


def exchange(blocks, width):
    x_lo = packed_shift([b[..., -width:, :] for b in blocks], "gx", 1)
    x_hi = packed_shift([b[..., :width, :] for b in blocks], "gx", -1)
    y_lo = packed_shift([b[..., -width:] for b in blocks], "gy", 1)
    y_hi = packed_shift([b[..., :width] for b in blocks], "gy", -1)
    return [(x_lo[i], x_hi[i], y_lo[i], y_hi[i]) for i in range(len(blocks))]


def central_diff(padded, along, spacing):
    length = padded.shape[along] - 4
    s = lambda o: lax.slice_in_dim(padded, o, o + length, axis=along)
    return (s(0) - 8.0 * s(1) + 8.0 * s(3) - s(4)) / (12.0 * spacing)


def diff_x(block, halo, spacing):
    x_lo, x_hi, _, _ = halo
    return central_diff(jnp.concatenate([x_lo, block, x_hi], axis=-2), block.ndim - 2, spacing)


def diff_y(block, halo, spacing):
    _, _, y_lo, y_hi = halo
    return central_diff(jnp.concatenate([y_lo, block, y_hi], axis=-1), block.ndim - 1, spacing)


def vertical_diff(fields, matrix):
    return jnp.einsum("kz,czxy->ckxy", matrix, fields, precision=lax.Precision.HIGHEST)


def lookup_table(grid_cell_index, values):
    result = jnp.zeros(grid_cell_index.shape, jnp.float32)
    for kind_at in range(values.shape[0]):
        result = jnp.where(grid_cell_index == kind_at, values[kind_at], result)
    return result


def velocity_step(wave, halo_x3, halo_y3, buoyancy, metric, matrix, spacing):
    sx = jnp.stack([wave[3], wave[6], wave[7]])
    sy = jnp.stack([wave[6], wave[4], wave[8]])
    slope_x = diff_x(sx, halo_x3, spacing)
    slope_y = diff_y(sy, halo_y3, spacing)
    slope_z = metric * vertical_diff(jnp.stack([wave[7], wave[8], wave[5]]), matrix)
    rate_x = slope_x[0] + slope_y[0] + slope_z[0]
    rate_y = slope_x[1] + slope_y[1] + slope_z[1]
    rate_z = slope_x[2] + slope_y[2] + slope_z[2]
    return wave[:3] + step_size * (buoyancy * jnp.stack([rate_x, rate_y, rate_z]))


def stress_step(wave, memory, velocity, halo, lame, shear, decay, strength, metric, matrix, spacing):
    slope_x = diff_x(velocity, halo, spacing)
    slope_y = diff_y(velocity, halo, spacing)
    slope_z = metric * vertical_diff(velocity, matrix)
    cell_volume = lame * (slope_x[0] + slope_y[1] + slope_z[2])
    rate = jnp.stack(
        [
            cell_volume + 2.0 * shear * slope_x[0],
            cell_volume + 2.0 * shear * slope_y[1],
            cell_volume + 2.0 * shear * slope_z[2],
            shear * (slope_y[0] + slope_x[1]),
            shear * (slope_z[0] + slope_x[2]),
            shear * (slope_z[1] + slope_y[2]),
        ]
    )
    memory_new = decay * memory + (1.0 - decay) * strength * rate
    stress = wave[3:] + step_size * (rate - memory_new)
    return stress, memory_new


def face_of(velocity, stress, depth):
    return jnp.stack(
        [
            velocity[0, depth],
            velocity[1, depth],
            velocity[2, depth],
            stress[4, depth],
            stress[5, depth],
            stress[2, depth],
        ]
    )


def pad_faces(faces):
    x_lo = packed_shift([f[:, -1:, :] for f in faces], "gx", 1)
    x_hi = packed_shift([f[:, :1, :] for f in faces], "gx", -1)
    faces = [jnp.concatenate([lo, f, hi], axis=1) for lo, f, hi in zip(x_lo, faces, x_hi)]
    y_lo = packed_shift([f[:, :, -1:] for f in faces], "gy", 1)
    y_hi = packed_shift([f[:, :, :1] for f in faces], "gy", -1)
    return [jnp.concatenate([lo, f, hi], axis=2) for lo, f, hi in zip(y_lo, faces, y_hi)]


def shifted(padded, offset, length, along):
    return lax.slice_in_dim(padded, offset, offset + length, axis=along)


def prolong_axis(padded, along):
    length = padded.shape[along] - 2
    left = shifted(padded, 0, length, along)
    middle = shifted(padded, 1, length, along)
    right = shifted(padded, 2, length, along)
    parts = jnp.stack(
        [(left + 2.0 * middle) / 3.0, middle, (2.0 * middle + right) / 3.0], axis=along + 1
    )
    shape = list(middle.shape)
    shape[along] = shape[along] * 3
    return parts.reshape(tuple(shape))


def split_three(padded, offset, length, along):
    part = shifted(padded, offset, 3 * length, along)
    return part.reshape(part.shape[:along] + (length, 3) + part.shape[along + 1 :])


def pick_part(parts, number, along):
    return lax.index_in_dim(parts, number, along + 1, keepdims=False)


def restrict_axis(padded, along):
    length = (padded.shape[along] - 2) // 3
    first = split_three(padded, 0, length, along)
    middle = split_three(padded, 1, length, along)
    last = split_three(padded, 2, length, along)
    return (
        pick_part(first, 0, along)
        + 2.0 * pick_part(middle, 0, along)
        + 3.0 * pick_part(middle, 1, along)
        + 2.0 * pick_part(middle, 2, along)
        + pick_part(last, 2, along)
    ) / 9.0


def assemble(velocity, stress, face, depth):
    replace = {0: face[0], 1: face[1], 2: face[2], 7: face[3], 8: face[4], 5: face[5]}
    fields = [velocity[0], velocity[1], velocity[2]] + [stress[k] for k in range(6)]
    rows = []
    for k, field in enumerate(fields):
        if k in replace:
            field = lax.dynamic_update_slice_in_dim(field, replace[k][None], depth, axis=0)
        rows.append(field)
    return jnp.stack(rows)


def local(
    fine_wave,
    fine_memory,
    fine_material,
    fine_mechanism,
    fine_metric,
    coarse_wave,
    coarse_memory,
    coarse_material,
    coarse_mechanism,
    material_table,
    attenuation_table,
):
    fine_matrix = sbp_table(fine_wave.shape[1], 1.0)
    coarse_matrix = sbp_table(coarse_wave.shape[1], 3.0)
    fine_buoy = lookup_table(fine_material, material_table[0])
    fine_lame = lookup_table(fine_material, material_table[1])
    fine_shear = lookup_table(fine_material, material_table[2])
    fine_decay = lookup_table(fine_mechanism, attenuation_table[0])
    fine_strength = lookup_table(fine_mechanism, attenuation_table[1])
    coarse_buoy = lookup_table(coarse_material, material_table[0])
    coarse_lame = lookup_table(coarse_material, material_table[1])
    coarse_shear = lookup_table(coarse_material, material_table[2])
    coarse_decay = lookup_table(coarse_mechanism, attenuation_table[0])
    coarse_strength = lookup_table(coarse_mechanism, attenuation_table[1])

    def x_parts(w):
        return jnp.stack([w[3], w[6], w[7]])

    def y_parts(w):
        return jnp.stack([w[6], w[4], w[8]])

    fx, fy, cx, cy = x_parts(fine_wave), y_parts(fine_wave), x_parts(coarse_wave), y_parts(coarse_wave)
    x_lo = packed_shift([fx[..., -2:, :], cx[..., -2:, :]], "gx", 1)
    x_hi = packed_shift([fx[..., :2, :], cx[..., :2, :]], "gx", -1)
    y_lo = packed_shift([fy[..., -2:], cy[..., -2:]], "gy", 1)
    y_hi = packed_shift([fy[..., :2], cy[..., :2]], "gy", -1)
    fine_hx = (x_lo[0], x_hi[0], None, None)
    fine_hy = (None, None, y_lo[0], y_hi[0])
    coarse_hx = (x_lo[1], x_hi[1], None, None)
    coarse_hy = (None, None, y_lo[1], y_hi[1])

    fine_velocity = velocity_step(fine_wave, fine_hx, fine_hy, fine_buoy, fine_metric, fine_matrix, 1.0)
    coarse_velocity = velocity_step(coarse_wave, coarse_hx, coarse_hy, coarse_buoy, 1.0, coarse_matrix, 3.0)

    fine_vh, coarse_vh = exchange([fine_velocity, coarse_velocity], 2)
    fine_stress, fine_mem = stress_step(
        fine_wave, fine_memory, fine_velocity, fine_vh, fine_lame, fine_shear, fine_decay, fine_strength,
        fine_metric, fine_matrix, 1.0,
    )
    coarse_stress, coarse_mem = stress_step(
        coarse_wave, coarse_memory, coarse_velocity, coarse_vh, coarse_lame, coarse_shear, coarse_decay,
        coarse_strength, 1.0, coarse_matrix, 3.0,
    )

    depth = fine_wave.shape[1] - 1
    fine_face = face_of(fine_velocity, fine_stress, depth)
    coarse_face = face_of(coarse_velocity, coarse_stress, 0)
    fine_padded, coarse_padded = pad_faces([fine_face, coarse_face])
    fine_new = fine_face - penalty * (fine_face - prolong_axis(prolong_axis(coarse_padded, 1), 2))
    coarse_new = coarse_face - penalty * (coarse_face - restrict_axis(restrict_axis(fine_padded, 1), 2))
    fine_out = assemble(fine_velocity, fine_stress, fine_new, depth)
    coarse_out = assemble(coarse_velocity, coarse_stress, coarse_new, 0)
    return (fine_out, fine_mem, coarse_out, coarse_mem)


def solution(mesh):
    in_specs = (
        P(None, None, "gx", "gy"),
        P(None, None, "gx", "gy"),
        P(None, "gx", "gy"),
        P(None, "gx", "gy"),
        P(None, "gx", "gy"),
        P(None, None, "gx", "gy"),
        P(None, None, "gx", "gy"),
        P(None, "gx", "gy"),
        P(None, "gx", "gy"),
        P(),
        P(),
    )
    out_specs = (
        P(None, None, "gx", "gy"),
        P(None, None, "gx", "gy"),
        P(None, None, "gx", "gy"),
        P(None, None, "gx", "gy"),
    )
    return jax.shard_map(local, mesh=mesh, in_specs=in_specs, out_specs=out_specs, check_vma=False)
```

time: 199 us -> 157 us (0.79)
  waiting for transfers between devices: 49.7 us -> 1.67 us
  starting transfers between devices: 60.8 us -> 36.2 us
  other arithmetic: 59.8 us -> 77.1 us
  local copies, waits for them, and re-layouts: 23.2 us -> 35.3 us
    ppermute x24 -> x12, waiting for transfers between devices: 49.7 us -> 1.67 us  [shift_from(): return lax.ppermute(block, axis, pairs)]
    ppermute x24 -> x12, starting transfers between devices: 60.8 us -> 36.2 us  [shift_from(): return lax.ppermute(block, axis, pairs)]
    select_n x0 -> x4, other arithmetic: none -> 19.2 us  [lookup_table(): result = jnp.where(grid_cell_index == kind_at, values[kind_at], result)]
    add x12 -> x8, other arithmetic: 21.3 us -> 3.11 us  [the longest x2 2.82 us: stress_step(): stress = wave[3:] + step_size * (rate - memory_new)]
    another operation x2 -> x4, other arithmetic: 0.04 us -> 10.2 us  [the longest x3 10.1 us: stress_step(): jnp.stack([cell_volume + 2.0 * shear * slope_x[0], cell_volume + 2.0 * sh...]
    unnamed x10 -> x5, other arithmetic: 20 us -> 29.8 us
    slice x23 -> x63, local copies, waits for them, and re-layouts: 5.77 us -> 12.7 us  [the longest x3 3.15 us: x_parts(): return jnp.stack([w[3], w[6], w[7]])]
    another operation x0 -> x10, local copies, waits for them, and re-layouts: none -> 4.04 us  [the longest x3 2.21 us: assemble(): return jnp.stack(rows)]
  transfers between devices with their start and end apart: 24 -> 12, of which waited for: 12 -> 1; matrix products, arithmetic and copies ran while one was open for 29% -> 25% of each run, Pallas kernels for 0% -> 0%
where the time goes in v1:
time: 157 us; the launch traced here: 154 us
  other arithmetic  77.1 us (49%)
  starting transfers between devices  36.2 us (23%)
  local copies, waits for them, and re-layouts  35.3 us (22%)
  between operations  2.36 us (2%)
  waiting for transfers between devices  1.67 us (1%)
    ppermute x12, starting transfers between devices, shift_from(): return lax.ppermute(block, axis, pairs)  36.2 us
    unnamed x5, other arithmetic  29.8 us
    select_n x4, other arithmetic, lookup_table(): result = jnp.where(grid_cell_index == kind_at, values[kind_at], result)  19.2 us
    another operation x3, other arithmetic, stress_step(): jnp.stack([cell_volume + 2.0 * shear * slope_x[0], cell_volume + 2.0 * sh...  10.1 us
    unnamed x103, local copies, waits for them, and re-layouts  7.54 us
    mul x1, other arithmetic, stress_step(): memory_new = decay * memory + (1.0 - decay) * strength * rate  5.78 us
    mul x1, other arithmetic, stress_step(): shear * (slope_z[1] + slope_y[2])  5.08 us
    slice x3, local copies, waits for them, and re-layouts, x_parts(): return jnp.stack([w[3], w[6], w[7]])  3.15 us
  transfers between devices with their start and end apart: 12, of which 1 were waited for; matrix products, arithmetic and copies ran while one was open for 25% of the time, Pallas kernels for 0%

profile of v1, /device:TPU:1, one launch (start us, length us, event | category | flops | bytes accessed | tf_op | source)
XLA Modules:
  0.0 154.0 jit_solution(1961274184404643006)
XLA Ops:
  5.0 4.5 %collective-permute-start = (f32[33792]{0:T(1024)S(1)}, f32[33792]{0:T(1024)S(1)}, u32[]{:S(2)}, u32[]{:S(2)}) collective-permute-start(f32[33792]{0:T(1024)S(1)} %get-tuple-element.139), channel_id=1, source_target_pairs={{0,8},{8,16},{16,24},{1,9},{9,17},{17,25},{2,10},{10,18},{18,26},{... | collective-permute-start | bytes 405512 | tf_op jit(solution)/shard_map/ppermute | solution.py:39
  9.5 1.9 %collective-permute-start.1 = (f32[33792]{0:T(1024)S(1)}, f32[33792]{0:T(1024)S(1)}, u32[]{:S(2)}, u32[]{:S(2)}) collective-permute-start(f32[33792]{0:T(1024)S(1)} %get-tuple-element.140), channel_id=1, source_target_pairs={{8,0},{16,8},{24,16},{9,1},{17,9},{25,17},{10,2},{18,10},{26,18},{... | collective-permute-start | bytes 405512 | tf_op jit(solution)/shard_map/ppermute | solution.py:39
  13.6 4.0 %collective-permute-start.2 = (f32[528]{0:T(1024)S(1)}, f32[528]{0:T(1024)S(1)}, u32[]{:S(2)}, u32[]{:S(2)}) collective-permute-start(f32[528]{0:T(1024)S(1)} %pad_maximum_fusion.34), channel_id=1, source_target_pairs={{0,1},{1,2},{2,3},{3,4},{4,5},{5,6},{6,7},{8,9},{9,10},{10,11},{11... | collective-permute-start | bytes 6344 | tf_op jit(solution)/shard_map/ppermute | solution.py:39
  21.4 3.3 %select_select_fusion = (f32[12,6,384]{2,1,0:T(8,128)}, pred[12,6,384]{2,1,0:T(8,128)(4,1)S(1)}, pred[12,6,384]{2,1,0:T(8,128)(4,1)S(1)}, pred[12,6,384]{2,1,0:T(8,128)(4,1)S(1)}, pred[12,6,384]{2,1,0:T(8,128)(4,1)S(1)}) fusion(f32[]{:T(128)} %bitcast.53, f32[]{:T(128)} %bitcast.52, f32[]{:T(128)} %bitcast.51, f32[]{:T(128)} %bitcast.50, ...), kind=kLoop, calls=%fused_computation.75 | loop fusion | flops 221184 | bytes 331792 | tf_op jit(solution)/shard_map/jit(_where)/select_n | solution.py:84
  24.7 5.6 %select_select_fusion.3 = (f32[8,2,128]{2,1,0:T(2,128)}, f32[8,2,128]{2,1,0:T(2,128)}) fusion(f32[]{:T(128)} %bitcast.53, f32[]{:T(128)} %bitcast.52, f32[]{:T(128)} %bitcast.51, f32[]{:T(128)} %bitcast.50, s32[8,2,128]{2,1,0:T(2,128)S(1)} %copy-done.36, f32[]{:T(128)} %bitcast.57, f32[]{:T(128)} %bitcast.56, f32[]{:T(128)} %bitcast.55, f32[]{:T(128)} %bitcast.54), kind=kLoop, calls=%fused_computation.244 | loop fusion | flops 28672 | bytes 24608 | tf_op jit(solution)/shard_map/jit(_where)/select_n | solution.py:84
  30.4 5.8 %select_multiply_fusion = f32[12,6,384]{2,1,0:T(8,128)} fusion(pred[12,6,384]{2,1,0:T(8,128)(4,1)S(1)} %get-tuple-element.26, pred[12,6,384]{2,1,0:T(8,128)(4,1)S(1)} %get-tuple-element.25, pred[12,6,384]{2,1,0:T(8,128)(4,1)S(1)} %get-tuple-element.24, pred[12,6,384]{2,1,0:T(8,128)(4,1)S(1)} %get-tuple-element.23, f32[]{:T(128)} %bitcast.57, f32[]{:T(128)} %bitcast.56, ...), kind=kLoop, calls=%fused_computation.74 | loop fusion | flops 276480 | bytes 221216 | tf_op jit(solution)/shard_map/mul | solution.py:115
  36.1 5.2 %select_select_fusion.2 = (f32[12,6,384]{2,1,0:T(8,128)S(1)}, pred[12,6,384]{2,1,0:T(8,128)(4,1)S(1)}, pred[12,6,384]{2,1,0:T(8,128)(4,1)S(1)}, pred[12,6,384]{2...) fusion(f32[]{:T(128)} %bitcast.7, f32[]{:T(128)} %bitcast.6, ...), kind=kLoop, calls=%fused_computation.81 | loop fusion | flops 442368 | bytes 442400 | tf_op jit(solution)/shard_map/jit(_where)/select_n | solution.py:84
  41.4 5.1 %select_select_fusion.5 = f32[8,2,128]{2,1,0:T(2,128)S(1)} fusion(f32[]{:T(128)} %bitcast.7, f32[]{:T(128)} %bitcast.6, f32[]{:T(128)} %bitcast.5, f32[]{:T(128)} %bitcast.4, f32[]{:T(128)} %bitcast.3, f32[]{:T(128)} %bitcast.2, f32[]{:T(128)} %bitcast.1, f32[]{:T(128)} %bitcast, s32[8,2,128]{2,1,0:T(2,128)S(1)} %copy-done.12), kind=kLoop, calls=%fused_computation.247 | loop fusion | flops 32768 | bytes 16416 | tf_op jit(solution)/shard_map/jit(_where)/select_n | solution.py:84
  55.6 4.7 %collective-permute-start.6 = (f32[528]{0:T(1024)S(1)}, f32[528]{0:T(1024)S(1)}, u32[]{:S(2)}, u32[]{:S(2)}) collective-permute-start(f32[528]{0:T(1024)S(1)} %pad_maximum_fusion.36), channel_id=1, source_target_pairs={{0,1},{1,2},{2,3},{3,4},{4,5},{5,6},{6,7},{8,9},{9,10},{10,11},{11... | collective-permute-start | bytes 6344 | tf_op jit(solution)/shard_map/ppermute | solution.py:39
  60.7 4.5 %collective-permute-start.4 = (f32[33792]{0:T(1024)S(1)}, f32[33792]{0:T(1024)S(1)}, u32[]{:S(2)}, u32[]{:S(2)}) collective-permute-start(f32[33792]{0:T(1024)S(1)} %get-tuple-element.131), channel_id=1, source_target_pairs={{0,8},{8,16},{16,24},{1,9},{9,17},{17,25},{2,10},{10,18},{18,26},{... | collective-permute-start | bytes 405512 | tf_op jit(solution)/shard_map/ppermute | solution.py:39
  65.2 2.1 %collective-permute-start.5 = (f32[33792]{0:T(1024)S(1)}, f32[33792]{0:T(1024)S(1)}, u32[]{:S(2)}, u32[]{:S(2)}) collective-permute-start(f32[33792]{0:T(1024)S(1)} %get-tuple-element.132), channel_id=1, source_target_pairs={{8,0},{16,8},{24,16},{9,1},{17,9},{25,17},{10,2},{18,10},{26,18},{... | collective-permute-start | bytes 405512 | tf_op jit(solution)/shard_map/ppermute | solution.py:39
  69.9 1.6 %collective-permute-done.5 = f32[33792]{0:T(1024)S(1)} collective-permute-done((f32[33792]{0:T(1024)S(1)}, f32[33792]{0:T(1024)S(1)}, u32[]{:S(2)}, u32[]{:S(2)}) %collective-permute-start.5) | collective-permute-done | bytes 135200 | tf_op jit(solution)/shard_map/ppermute | solution.py:39
  71.8 9.9 %constant_dynamic-update-slice_fusion.9 = (f32[6,8,2,128]{3,2,1,0:T(2,128)S(1)}, f32[8,2,128]{2,1,0:T(2,128)S(1)}) fusion(f32[3,8,2,128]{3,2,1,0:T(2,128)S(1)} %get-tuple-element.128, f32[]{:T(128)} %bitcast.41, s32[8,2,128]{2,1,0:T(2,128)S(1)} %copy-done.12, f32[]{:T(128)} %bitcast.40, f32[]{:T(128)} %bitcast.39, f32[]{:T(128)} %bitcast.38, f32[]{:T(128)} %bitcast.37, ...), kind=kLoop, calls=%fused_computation.108 | loop fusion | flops 61439 | bytes 49216
  81.7 5.0 %constant_dynamic-update-slice_fusion.8 = f32[6,8,2,128]{3,2,1,0:T(2,128)S(1)} fusion(f32[6,8,2,128]{3,2,1,0:T(2,128)S(1)} %get-tuple-element.18, f32[8,2,128]{2,1,0:T(2,128)S(1)} %get-tuple-element.19, f32[3,8,2,128]{3,2,1,0:T(2,128)S(1)} %get-tuple-element.127, f32[]{:T(128)} %bitcast.41, s32[8,2,128]{2,1,0:T(2,128)S(1)} %copy-done.12, f32[]{:T(128)} %bitcast.40, ...), kind=kLoop, calls=%fused_computation.107 | loop fusion | flops 38912 | bytes 32800
  86.7 5.0 %constant_dynamic-update-slice_fusion.7 = f32[6,8,2,128]{3,2,1,0:T(2,128)S(1)} fusion(f32[6,8,2,128]{3,2,1,0:T(2,128)S(1)} %constant_dynamic-update-slice_fusion.8, f32[8,2,128]{2,1,0:T(2,128)S(1)} %get-tuple-element.19, f32[3,8,2,128]{3,2,1,0:T(2,128)S(1)} %bitcast.306, f32[]{:T(128)} %bitcast.41, s32[8,2,128]{2,1,0:T(2,128)S(1)} %copy-done.12, ...), kind=kLoop, calls=%fused_computation.106 | loop fusion | flops 38912 | bytes 32800
  91.7 5.0 %constant_dynamic-update-slice_fusion.6 = f32[6,8,2,128]{3,2,1,0:T(2,128)S(1)} fusion(f32[6,8,2,128]{3,2,1,0:T(2,128)S(1)} %constant_dynamic-update-slice_fusion.7, f32[3,8,2,128]{3,2,1,0:T(2,128)S(1)} %get-tuple-element.128, f32[3,8,2,128]{3,2,1,0:T(2,128)S(1)} %get-tuple-element.127, f32[]{:T(128)} %bitcast.41, s32[8,2,128]{2,1,0:T(2,128)S(1)} %copy-done.12, ...), kind=kLoop, calls=%fused_computation.105 | loop fusion | flops 36864 | bytes 32800
  96.7 5.0 %constant_dynamic-update-slice_fusion.5 = f32[6,8,2,128]{3,2,1,0:T(2,128)S(1)} fusion(f32[6,8,2,128]{3,2,1,0:T(2,128)S(1)} %constant_dynamic-update-slice_fusion.6, f32[3,8,2,128]{3,2,1,0:T(2,128)S(1)} %get-tuple-element.128, f32[3,8,2,128]{3,2,1,0:T(2,128)S(1)} %bitcast.307, f32[]{:T(128)} %bitcast.41, s32[8,2,128]{2,1,0:T(2,128)S(1)} %copy-done.12, ...), kind=kLoop, calls=%fused_computation.104 | loop fusion | flops 36864 | bytes 32800
  101.7 5.0 %constant_dynamic-update-slice_fusion.4 = f32[6,8,2,128]{3,2,1,0:T(2,128)S(1)} fusion(f32[6,8,2,128]{3,2,1,0:T(2,128)S(1)} %constant_dynamic-update-slice_fusion.5, f32[3,8,2,128]{3,2,1,0:T(2,128)S(1)} %get-tuple-element.127, f32[3,8,2,128]{3,2,1,0:T(2,128)S(1)} %bitcast.308, f32[]{:T(128)} %bitcast.41, s32[8,2,128]{2,1,0:T(2,128)S(1)} %copy-done.12, ...), kind=kLoop, calls=%fused_computation.103 | loop fusion | flops 36864 | bytes 32800 | tf_op jit(solution)/shard_map/stack | solution.py:105
  108.3 5.1 %fusion.25 = (f32[12,6,384]{2,1,0:T(8,128)S(1)}, f32[12,6,384]{2,1,0:T(8,128)S(1)}) fusion(f32[3,12,6,384]{3,2,1,0:T(8,128)S(1)} %get-tuple-element.68, f32[3,12,6,384]{3,2,1,0:T(8,128)S(1)} %bitcast_multiply_fusion, pred[12,6,384]{2,1,0:T(8,128)(4,1)S(1)} %get-tuple-element.39, pred[12,6,384]{2,1,0:T(8,128)(4,1)S(1)} %get-tuple-element.38, ...), kind=kLoop, calls=%fused_computation.53 | loop fusion | flops 276480 | bytes 663584 | tf_op jit(solution)/shard_map/mul | solution.py:112
  113.5 5.1 %add_bitcast_fusion = (f32[1,12,6,384]{3,2,1,0:T(8,128)S(1)}, f32[12,6,384]{2,1,0:T(8,128)S(1)}) fusion(f32[3,12,6,384]{3,2,1,0:T(8,128)S(1)} %bitcast_multiply_fusion, f32[12,6,384]{2,1,0:T(8,128)S(1)} %get-tuple-element.28, f32[3,12,6,384]{3,2,1,0:T(8,128)S(1)} %get-tuple-element.68, f32[3,12,6,384]{3,2,1,0:T(8,128)S(1)} %get-tuple-element.67, ...), kind=kLoop, calls=%fused_computation.76 | loop fusion | flops 387072 | bytes 884768 | tf_op jit(solution)/shard_map/stack | solution.py:105
  120.5 2.1 %copy_add_fusion = (f32[6,12,6,384]{3,0,2,1:T(8,128)S(1)}, f32[6,12,6,384]{3,0,2,1:T(8,128)S(1)}) fusion(f32[6,12,6,384]{3,2,1,0:T(8,128)S(1)} %slice-done.1, f32[6,12,6,384]{3,0,2,1:T(8,128)S(1)} %stack.168, f32[12,6,384]{2,1,0:T(8,128)} %select_multiply_fusion, f32[6,12,6,384]{3,2,1,0:T(8,128)} %param.14, f32[12,6,384]{2,1,0:T(8,128)} %get-tuple-element.22), kind=kLoop, calls=%fused_computation.3 | loop fusion | flops 995328 | bytes 3538944 | tf_op jit(solution)/shard_map/add | solution.py:116
  123.6 1.9 %collective-permute-start.9 = (f32[3072]{0:T(1024)S(1)}, f32[3072]{0:T(1024)S(1)}, u32[]{:S(2)}, u32[]{:S(2)}) collective-permute-start(f32[3072]{0:T(1024)S(1)} %pad_maximum_fusion.32), channel_id=1, source_target_pairs={{8,0},{16,8},{24,16},{9,1},{17,9},{25,17},{10,2},{18,10},{26,18},{... | collective-permute-start | bytes 36872 | tf_op jit(solution)/shard_map/ppermute | solution.py:39
  125.5 3.6 %collective-permute-start.8 = (f32[3072]{0:T(1024)S(1)}, f32[3072]{0:T(1024)S(1)}, u32[]{:S(2)}, u32[]{:S(2)}) collective-permute-start(f32[3072]{0:T(1024)S(1)} %pad_maximum_fusion.31), channel_id=1, source_target_pairs={{0,8},{8,16},{16,24},{1,9},{9,17},{17,25},{2,10},{10,18},{18,26},{... | collective-permute-start | bytes 36872 | tf_op jit(solution)/shard_map/ppermute | solution.py:39
  134.1 5.2 %collective-permute-start.10 = (f32[72]{0:T(128)S(1)}, f32[72]{0:T(128)S(1)}, u32[]{:S(2)}, u32[]{:S(2)}) collective-permute-start(f32[72]{0:T(128)S(1)} %pad_maximum_fusion.38), channel_id=1, source_target_pairs={{0,1},{1,2},{2,3},{3,4},{4,5},{5,6},{6,7},{8,9},{9,10},{10,11},{11... | collective-permute-start | bytes 872 | tf_op jit(solution)/shard_map/ppermute | solution.py:39
  (304 shorter events, 45.5 us)
Async XLA Ops:
  4.6 13.1 %copy-start.18 = (f32[3,8]{1,0:T(4,128)S(1)}, f32[3,8]{1,0:T(4,128)}, u32[]{:S(2)}) copy-start(f32[3,8]{1,0:T(4,128)} %param.22) | copy-start | bytes 292
  4.6 14.4 %copy-start.33 = (f32[2,4]{1,0:T(2,128)S(1)}, f32[2,4]{1,0:T(2,128)}, u32[]{:S(2)}) copy-start(f32[2,4]{1,0:T(2,128)} %param.23) | copy-start | bytes 100
  4.7 15.0 %copy-start.34 = (f32[8,8,1,1]{1,0,3,2:T(8,128)S(1)}, f32[8,8,1,1]{1,0,3,2:T(8,128)}, u32[]{:S(2)}) copy-start(f32[8,8,1,1]{1,0,3,2:T(8,128)} %constant.106) | copy-start | bytes 772
  4.7 15.8 %copy-start.5 = (f32[12,6,384]{2,1,0:T(8,128)S(1)}, f32[12,6,384]{2,1,0:T(8,128)}, u32[]{:S(2)}) copy-start(f32[12,6,384]{2,1,0:T(8,128)} %param.17) | copy-start | bytes 331780
  5.0 15.6 %copy-start.24 = (f32[12,12,1,1]{1,0,3,2:T(8,128)S(1)}, f32[12,12,1,1]{1,0,3,2:T(8,128)}, u32[]{:S(2)}) copy-start(f32[12,12,1,1]{1,0,3,2:T(8,128)} %constant.105) | copy-start | bytes 1732
  5.0 43.3 %collective-permute-start = (f32[33792]{0:T(1024)S(1)}, f32[33792]{0:T(1024)S(1)}, u32[]{:S(2)}, u32[]{:S(2)}) collective-permute-start(f32[33792]{0:T(1024)S(1)} %get-tuple-element.139), channel_id=1, source_target_pairs={{0,8},{8,16},{16,24},{1,9},{9,17},{17,25},{2,10},{10,18},{18,26},{... | collective-permute-start | bytes 405512 | tf_op jit(solution)/shard_map/ppermute | solution.py:39
  9.5 38.8 %collective-permute-start.1 = (f32[33792]{0:T(1024)S(1)}, f32[33792]{0:T(1024)S(1)}, u32[]{:S(2)}, u32[]{:S(2)}) collective-permute-start(f32[33792]{0:T(1024)S(1)} %get-tuple-element.140), channel_id=1, source_target_pairs={{8,0},{16,8},{24,16},{9,1},{17,9},{25,17},{10,2},{18,10},{26,18},{... | collective-permute-start | bytes 405512 | tf_op jit(solution)/shard_map/ppermute | solution.py:39
  12.0 34.8 %collective-permute-start.3 = (f32[528]{0:T(1024)S(1)}, f32[528]{0:T(1024)S(1)}, u32[]{:S(2)}, u32[]{:S(2)}) collective-permute-start(f32[528]{0:T(1024)S(1)} %pad_maximum_fusion.35), channel_id=1, source_target_pairs={{1,0},{2,1},{3,2},{4,3},{5,4},{6,5},{7,6},{9,8},{10,9},{11,10},{12... | collective-permute-start | bytes 6344 | tf_op jit(solution)/shard_map/ppermute | solution.py:39
  13.6 32.9 %collective-permute-start.2 = (f32[528]{0:T(1024)S(1)}, f32[528]{0:T(1024)S(1)}, u32[]{:S(2)}, u32[]{:S(2)}) collective-permute-start(f32[528]{0:T(1024)S(1)} %pad_maximum_fusion.34), channel_id=1, source_target_pairs={{0,1},{1,2},{2,3},{3,4},{4,5},{5,6},{6,7},{8,9},{9,10},{10,11},{11... | collective-permute-start | bytes 6344 | tf_op jit(solution)/shard_map/ppermute | solution.py:39
  20.6 15.6 %copy-start.17 = (s32[12,6,384]{2,1,0:T(8,128)S(1)}, s32[12,6,384]{2,1,0:T(8,128)}, u32[]{:S(2)}) copy-start(s32[12,6,384]{2,1,0:T(8,128)} %param.15) | copy-start | bytes 331780
  20.6 20.7 %copy-start.12 = (s32[8,2,128]{2,1,0:T(2,128)S(1)}, s32[8,2,128]{2,1,0:T(2,128)}, u32[]{:S(2)}) copy-start(s32[8,2,128]{2,1,0:T(2,128)} %param.20) | copy-start | bytes 24580
  54.1 14.9 %collective-permute-start.7 = (f32[528]{0:T(1024)S(1)}, f32[528]{0:T(1024)S(1)}, u32[]{:S(2)}, u32[]{:S(2)}) collective-permute-start(f32[528]{0:T(1024)S(1)} %pad_maximum_fusion.37), channel_id=1, source_target_pairs={{1,0},{2,1},{3,2},{4,3},{5,4},{6,5},{7,6},{9,8},{10,9},{11,10},{12... | collective-permute-start | bytes 6344 | tf_op jit(solution)/shard_map/ppermute | solution.py:39
  55.6 13.7 %collective-permute-start.6 = (f32[528]{0:T(1024)S(1)}, f32[528]{0:T(1024)S(1)}, u32[]{:S(2)}, u32[]{:S(2)}) collective-permute-start(f32[528]{0:T(1024)S(1)} %pad_maximum_fusion.36), channel_id=1, source_target_pairs={{0,1},{1,2},{2,3},{3,4},{4,5},{5,6},{6,7},{8,9},{9,10},{10,11},{11... | collective-permute-start | bytes 6344 | tf_op jit(solution)/shard_map/ppermute | solution.py:39
  60.7 9.1 %collective-permute-start.4 = (f32[33792]{0:T(1024)S(1)}, f32[33792]{0:T(1024)S(1)}, u32[]{:S(2)}, u32[]{:S(2)}) collective-permute-start(f32[33792]{0:T(1024)S(1)} %get-tuple-element.131), channel_id=1, source_target_pairs={{0,8},{8,16},{16,24},{1,9},{9,17},{17,25},{2,10},{10,18},{18,26},{... | collective-permute-start | bytes 405512 | tf_op jit(solution)/shard_map/ppermute | solution.py:39
  65.2 6.3 %collective-permute-start.5 = (f32[33792]{0:T(1024)S(1)}, f32[33792]{0:T(1024)S(1)}, u32[]{:S(2)}, u32[]{:S(2)}) collective-permute-start(f32[33792]{0:T(1024)S(1)} %get-tuple-element.132), channel_id=1, source_target_pairs={{8,0},{16,8},{24,16},{9,1},{17,9},{25,17},{10,2},{18,10},{26,18},{... | collective-permute-start | bytes 405512 | tf_op jit(solution)/shard_map/ppermute | solution.py:39
  67.4 39.2 %copy-start.13 = (f32[9,8,2,128]{3,2,1,0:T(2,128)S(1)}, f32[9,8,2,128]{3,2,1,0:T(2,128)}, u32[]{:S(2)}) copy-start(f32[9,8,2,128]{3,2,1,0:T(2,128)} %param.18) | copy-start | bytes 221188
  67.4 39.2 %copy-start.23 = (f32[6,8,2,128]{3,2,1,0:T(2,128)S(1)}, f32[6,8,2,128]{3,2,1,0:T(2,128)}, u32[]{:S(2)}) copy-start(f32[6,8,2,128]{3,2,1,0:T(2,128)} %param.19) | copy-start | bytes 147460
  67.4 39.2 %copy-start.26 = (f32[8,2,128]{2,1,0:T(2,128)S(1)}, f32[8,2,128]{2,1,0:T(2,128)}, u32[]{:S(2)}) copy-start(f32[8,2,128]{2,1,0:T(2,128)} %get-tuple-element.143) | copy-start | bytes 24580
  67.4 39.2 %copy-start.27 = (f32[8,2,128]{2,1,0:T(2,128)S(1)}, f32[8,2,128]{2,1,0:T(2,128)}, u32[]{:S(2)}) copy-start(f32[8,2,128]{2,1,0:T(2,128)} %get-tuple-element.144) | copy-start | bytes 24580
  123.5 17.9 %copy-start = (f32[6,6,384]{2,0,1:T(8,128)}, f32[6,6,384]{2,0,1:T(8,128)S(1)}, u32[]{:S(2)}) copy-start(f32[6,6,384]{2,0,1:T(8,128)S(1)} %stack.169) | copy-start | bytes 165892
  123.6 8.2 %collective-permute-start.9 = (f32[3072]{0:T(1024)S(1)}, f32[3072]{0:T(1024)S(1)}, u32[]{:S(2)}, u32[]{:S(2)}) collective-permute-start(f32[3072]{0:T(1024)S(1)} %pad_maximum_fusion.32), channel_id=1, source_target_pairs={{8,0},{16,8},{24,16},{9,1},{17,9},{25,17},{10,2},{18,10},{26,18},{... | collective-permute-start | bytes 36872 | tf_op jit(solution)/shard_map/ppermute | solution.py:39
  125.5 6.3 %collective-permute-start.8 = (f32[3072]{0:T(1024)S(1)}, f32[3072]{0:T(1024)S(1)}, u32[]{:S(2)}, u32[]{:S(2)}) collective-permute-start(f32[3072]{0:T(1024)S(1)} %pad_maximum_fusion.31), channel_id=1, source_target_pairs={{0,8},{8,16},{16,24},{1,9},{9,17},{17,25},{2,10},{10,18},{18,26},{... | collective-permute-start | bytes 36872 | tf_op jit(solution)/shard_map/ppermute | solution.py:39
  132.7 7.6 %collective-permute-start.11 = (f32[72]{0:T(128)S(1)}, f32[72]{0:T(128)S(1)}, u32[]{:S(2)}, u32[]{:S(2)}) collective-permute-start(f32[72]{0:T(128)S(1)} %pad_maximum_fusion.39), channel_id=1, source_target_pairs={{1,0},{2,1},{3,2},{4,3},{5,4},{6,5},{7,6},{9,8},{10,9},{11,10},{12... | collective-permute-start | bytes 872 | tf_op jit(solution)/shard_map/ppermute | solution.py:39
  134.1 6.3 %collective-permute-start.10 = (f32[72]{0:T(128)S(1)}, f32[72]{0:T(128)S(1)}, u32[]{:S(2)}, u32[]{:S(2)}) collective-permute-start(f32[72]{0:T(128)S(1)} %pad_maximum_fusion.38), channel_id=1, source_target_pairs={{0,1},{1,2},{2,3},{3,4},{4,5},{5,6},{6,7},{8,9},{9,10},{10,11},{11... | collective-permute-start | bytes 872 | tf_op jit(solution)/shard_map/ppermute | solution.py:39
  (30 other events, 43.7 us)

commit v2 on v1

--- a/solution.py
+++ b/solution.py
@@ -1,3 +1,4 @@
+import functools
 import math
 
 import jax
@@ -17,6 +18,10 @@
 
 
 def sbp_table(layers, spacing):
+    return jnp.asarray(sbp_numpy(layers, spacing))
+
+
+def sbp_numpy(layers, spacing):
     table = np.zeros((layers, layers))
     for line_at in range(4):
         for column in range(6):
@@ -30,7 +35,7 @@
             2.0 / 3.0,
             -1.0 / 12.0,
         ]
-    return jnp.asarray(table / spacing, dtype=jnp.float32)
+    return (table / spacing).astype(np.float32)
 
 
 def shift_from(block, axis, offset):
@@ -190,6 +195,165 @@
     return jnp.stack(rows)
 
 
+from jax.experimental import pallas as pl
+from jax.experimental.pallas import tpu as pltpu
+
+
+def sbp_rows(layers, spacing):
+    table = sbp_numpy(layers, spacing)
+    return [[(j, float(table[k, j])) for j in range(layers) if table[k, j] != 0.0] for k in range(layers)]
+
+
+def pick(values_ref, row, index):
+    result = jnp.zeros(index.shape, jnp.float32)
+    for kind_at in range(values_ref.shape[1]):
+        result = jnp.where(index == kind_at, values_ref[row, kind_at], result)
+    return result
+
+
+def fill_x(scratch, slot, lo, block, hi):
+    width = lo.shape[-2]
+    size = block.shape[-2]
+    scratch[slot, :, 0:width, :] = lo
+    scratch[slot, :, width : width + size, :] = block
+    scratch[slot, :, width + size :, :] = hi
+
+
+def slope_x(scratch, slot, z, size, spacing):
+    s = lambda o: scratch[slot, z, o : o + size, :]
+    return (s(0) - 8.0 * s(1) + 8.0 * s(3) - s(4)) / (12.0 * spacing)
+
+
+def slope_y(f, lo, hi, spacing):
+    n = f.shape[-1]
+    lane = lax.broadcasted_iota(jnp.int32, f.shape, f.ndim - 1)
+    m1 = jnp.where(lane == 0, lo[:, 1:2], pltpu.roll(f, 1, f.ndim - 1))
+    m2 = jnp.where(lane == 0, lo[:, 0:1], jnp.where(lane == 1, lo[:, 1:2], pltpu.roll(f, 2, f.ndim - 1)))
+    p1 = jnp.where(lane == n - 1, hi[:, 0:1], pltpu.roll(f, n - 1, f.ndim - 1))
+    p2 = jnp.where(lane == n - 2, hi[:, 0:1], jnp.where(lane == n - 1, hi[:, 1:2], pltpu.roll(f, n - 2, f.ndim - 1)))
+    return (m2 - 8.0 * m1 + 8.0 * p1 - p2) / (12.0 * spacing)
+
+
+def slope_z(field_ref, index, row):
+    total = None
+    for j, weight in row:
+        term = jnp.float32(weight) * field_ref[index, j]
+        total = term if total is None else total + term
+    return total
+
+
+def velocity_kernel(rows, spacing, has_metric, *refs):
+    if has_metric:
+        w, xlo, xhi, ylo, yhi, mat, metric, table, out, sx = refs
+    else:
+        w, xlo, xhi, ylo, yhi, mat, table, out, sx = refs
+        metric = None
+    layers, size = w.shape[1], w.shape[2]
+    for slot, field in enumerate((3, 6, 7)):
+        fill_x(sx, slot, xlo[slot], w[field], xhi[slot])
+    for z in range(layers):
+        dx = [slope_x(sx, slot, z, size, spacing) for slot in range(3)]
+        dy = [slope_y(w[field, z], ylo[slot, z], yhi[slot, z], spacing) for slot, field in enumerate((6, 4, 8))]
+        dz = [slope_z(w, field, rows[z]) for field in (7, 8, 5)]
+        if metric is not None:
+            m = metric[z]
+            dz = [m * d for d in dz]
+        buoy = pick(table, 0, mat[z])
+        for k in range(3):
+            out[k, z] = w[k, z] + step_size * (buoy * (dx[k] + dy[k] + dz[k]))
+
+
+def stress_kernel(rows, spacing, has_metric, depth, *refs):
+    if has_metric:
+        w, mem, vel, xlo, xhi, ylo, yhi, mat, mech, metric, mtab, atab, out, mem_out, face, sx = refs
+    else:
+        w, mem, vel, xlo, xhi, ylo, yhi, mat, mech, mtab, atab, out, mem_out, face, sx = refs
+        metric = None
+    layers, size = w.shape[1], w.shape[2]
+    for slot in range(3):
+        fill_x(sx, slot, xlo[slot], vel[slot], xhi[slot])
+    for z in range(layers):
+        dx = [slope_x(sx, slot, z, size, spacing) for slot in range(3)]
+        dy = [slope_y(vel[slot, z], ylo[slot, z], yhi[slot, z], spacing) for slot in range(3)]
+        dz = [slope_z(vel, slot, rows[z]) for slot in range(3)]
+        if metric is not None:
+            m = metric[z]
+            dz = [m * d for d in dz]
+        kind, mechanism = mat[z], mech[z]
+        lame, shear = pick(mtab, 1, kind), pick(mtab, 2, kind)
+        decay, strength = pick(atab, 0, mechanism), pick(atab, 1, mechanism)
+        cell_volume = lame * (dx[0] + dy[1] + dz[2])
+        rate = [
+            cell_volume + 2.0 * shear * dx[0],
+            cell_volume + 2.0 * shear * dy[1],
+            cell_volume + 2.0 * shear * dz[2],
+            shear * (dy[0] + dx[1]),
+            shear * (dz[0] + dx[2]),
+            shear * (dz[1] + dy[2]),
+        ]
+        values = []
+        for k in range(3):
+            v = vel[k, z]
+            out[k, z] = v
+            values.append(v)
+        for k in range(6):
+            memory_new = decay * mem[k, z] + (1.0 - decay) * strength * rate[k]
+            mem_out[k, z] = memory_new
+            stress = w[3 + k, z] + step_size * (rate[k] - memory_new)
+            out[3 + k, z] = stress
+            values.append(stress)
+        if z == depth:
+            for i, k in enumerate((0, 1, 2, 7, 8, 5)):
+                face[i] = values[k]
+
+
+def vmem_specs(count):
+    return [pl.BlockSpec(memory_space=pltpu.VMEM)] * count
+
+
+def velocity_call(wave, halo_x, halo_y, material, metric, table, spacing):
+    layers, size, lanes = wave.shape[1:]
+    rows = sbp_rows(layers, spacing)
+    args = [wave, halo_x[0], halo_x[1], halo_y[0], halo_y[1], material]
+    if metric is not None:
+        args.append(metric)
+    kernel = functools.partial(velocity_kernel, rows, spacing, metric is not None)
+    return pl.pallas_call(
+        kernel,
+        out_shape=jax.ShapeDtypeStruct((3, layers, size, lanes), jnp.float32),
+        in_specs=vmem_specs(len(args)) + [pl.BlockSpec(memory_space=pltpu.SMEM)],
+        out_specs=pl.BlockSpec(memory_space=pltpu.VMEM),
+        scratch_shapes=[pltpu.VMEM((3, layers, size + 4, lanes), jnp.float32)],
+    )(*args, table)
+
+
+def stress_call(wave, memory, velocity, halo, material, mechanism, metric, mtab, atab, spacing, depth):
+    layers, size, lanes = wave.shape[1:]
+    rows = sbp_rows(layers, spacing)
+    args = [wave, memory, velocity, halo[0], halo[1], halo[2], halo[3], material, mechanism]
+    if metric is not None:
+        args.append(metric)
+    kernel = functools.partial(stress_kernel, rows, spacing, metric is not None, depth)
+    return pl.pallas_call(
+        kernel,
+        out_shape=(
+            jax.ShapeDtypeStruct(wave.shape, jnp.float32),
+            jax.ShapeDtypeStruct(memory.shape, jnp.float32),
+            jax.ShapeDtypeStruct((6, size, lanes), jnp.float32),
+        ),
+        in_specs=vmem_specs(len(args)) + [pl.BlockSpec(memory_space=pltpu.SMEM)] * 2,
+        out_specs=tuple(vmem_specs(3)),
+        scratch_shapes=[pltpu.VMEM((3, layers, size + 4, lanes), jnp.float32)],
+    )(*args, mtab, atab)
+
+
+def put_face(out, face, depth):
+    out = lax.dynamic_update_slice(out, face[0:3][:, None], (0, depth, 0, 0))
+    out = lax.dynamic_update_slice(out, face[5:6][:, None], (5, depth, 0, 0))
+    out = lax.dynamic_update_slice(out, face[3:5][:, None], (7, depth, 0, 0))
+    return out
+
+
 def local(
     fine_wave,
     fine_memory,
@@ -203,19 +367,6 @@
     material_table,
     attenuation_table,
 ):
-    fine_matrix = sbp_table(fine_wave.shape[1], 1.0)
-    coarse_matrix = sbp_table(coarse_wave.shape[1], 3.0)
-    fine_buoy = lookup_table(fine_material, material_table[0])
-    fine_lame = lookup_table(fine_material, material_table[1])
-    fine_shear = lookup_table(fine_material, material_table[2])
-    fine_decay = lookup_table(fine_mechanism, attenuation_table[0])
-    fine_strength = lookup_table(fine_mechanism, attenuation_table[1])
-    coarse_buoy = lookup_table(coarse_material, material_table[0])
-    coarse_lame = lookup_table(coarse_material, material_table[1])
-    coarse_shear = lookup_table(coarse_material, material_table[2])
-    coarse_decay = lookup_table(coarse_mechanism, attenuation_table[0])
-    coarse_strength = lookup_table(coarse_mechanism, attenuation_table[1])
-
     def x_parts(w):
         return jnp.stack([w[3], w[6], w[7]])
 
@@ -227,33 +378,29 @@
     x_hi = packed_shift([fx[..., :2, :], cx[..., :2, :]], "gx", -1)
     y_lo = packed_shift([fy[..., -2:], cy[..., -2:]], "gy", 1)
     y_hi = packed_shift([fy[..., :2], cy[..., :2]], "gy", -1)
-    fine_hx = (x_lo[0], x_hi[0], None, None)
-    fine_hy = (None, None, y_lo[0], y_hi[0])
-    coarse_hx = (x_lo[1], x_hi[1], None, None)
-    coarse_hy = (None, None, y_lo[1], y_hi[1])
-
-    fine_velocity = velocity_step(fine_wave, fine_hx, fine_hy, fine_buoy, fine_metric, fine_matrix, 1.0)
-    coarse_velocity = velocity_step(coarse_wave, coarse_hx, coarse_hy, coarse_buoy, 1.0, coarse_matrix, 3.0)
+
+    fine_velocity = velocity_call(
+        fine_wave, (x_lo[0], x_hi[0]), (y_lo[0], y_hi[0]), fine_material, fine_metric, material_table, 1.0
+    )
+    coarse_velocity = velocity_call(
+        coarse_wave, (x_lo[1], x_hi[1]), (y_lo[1], y_hi[1]), coarse_material, None, material_table, 3.0
+    )
 
     fine_vh, coarse_vh = exchange([fine_velocity, coarse_velocity], 2)
-    fine_stress, fine_mem = stress_step(
-        fine_wave, fine_memory, fine_velocity, fine_vh, fine_lame, fine_shear, fine_decay, fine_strength,
-        fine_metric, fine_matrix, 1.0,
-    )
-    coarse_stress, coarse_mem = stress_step(
-        coarse_wave, coarse_memory, coarse_velocity, coarse_vh, coarse_lame, coarse_shear, coarse_decay,
-        coarse_strength, 1.0, coarse_matrix, 3.0,
-    )
-
     depth = fine_wave.shape[1] - 1
-    fine_face = face_of(fine_velocity, fine_stress, depth)
-    coarse_face = face_of(coarse_velocity, coarse_stress, 0)
+    fine_out, fine_mem, fine_face = stress_call(
+        fine_wave, fine_memory, fine_velocity, fine_vh, fine_material, fine_mechanism, fine_metric,
+        material_table, attenuation_table, 1.0, depth,
+    )
+    coarse_out, coarse_mem, coarse_face = stress_call(
+        coarse_wave, coarse_memory, coarse_velocity, coarse_vh, coarse_material, coarse_mechanism, None,
+        material_table, attenuation_table, 3.0, 0,
+    )
+
     fine_padded, coarse_padded = pad_faces([fine_face, coarse_face])
     fine_new = fine_face - penalty * (fine_face - prolong_axis(prolong_axis(coarse_padded, 1), 2))
     coarse_new = coarse_face - penalty * (coarse_face - restrict_axis(restrict_axis(fine_padded, 1), 2))
-    fine_out = assemble(fine_velocity, fine_stress, fine_new, depth)
-    coarse_out = assemble(coarse_velocity, coarse_stress, coarse_new, 0)
-    return (fine_out, fine_mem, coarse_out, coarse_mem)
+    return (put_face(fine_out, fine_new, depth), fine_mem, put_face(coarse_out, coarse_new, 0), coarse_mem)
 
 
 def solution(mesh):

time: 157 us -> 92.4 us (0.59)
  the two profiles are of different devices: /device:TPU:1 before, /device:TPU:10 now
where the time goes in v2:
time: 92.4 us; the launch traced here: 91.5 us
  starting transfers between devices  34.9 us (38%)
  local copies, waits for them, and re-layouts  31 us (34%)
  Pallas kernels  11.8 us (13%)
  waiting for transfers between devices  9.67 us (10%)
  other arithmetic  2.9 us (3%)
  between operations  1.2 us (1%)
    ppermute x12, starting transfers between devices, shift_from(): return lax.ppermute(block, axis, pairs)  34.9 us
    ppermute x12, waiting for transfers between devices, shift_from(): return lax.ppermute(block, axis, pairs)  9.67 us
    reshape x16, local copies, waits for them, and re-layouts, packed_shift(): out.append(moved[start:start + size].reshape(b.shape))  9.45 us
    pallas_call x2, Pallas kernels, stress_call(): pl.pallas_call(kernel, out_shape=(jax.ShapeDtypeStruct(wave.shape, jnp.fl...  6.62 us
    pallas_call x2, Pallas kernels, velocity_call(): pl.pallas_call(kernel, out_shape=jax.ShapeDtypeStruct((3, layers, size, l...  5.13 us
    slice x24, local copies, waits for them, and re-layouts, packed_shift(): out.append(moved[start:start + size].reshape(b.shape))  2.96 us
    slice x6, local copies, waits for them, and re-layouts, x_parts(): return jnp.stack([w[3], w[6], w[7]])  1.98 us
    slice x2, local copies, waits for them, and re-layouts, exchange(): y_hi = packed_shift([b[..., :width] for b in blocks], 'gy', -1)  1.97 us
  transfers between devices with their start and end apart: 12, of which 4 were waited for; matrix products, arithmetic and copies ran while one was open for 11% of the time, Pallas kernels for 0%

profile of v2, /device:TPU:10, one launch (start us, length us, event | category | flops | bytes accessed | tf_op | source)
XLA Modules:
  0.0 91.5 jit_solution(14144595981897459296)
XLA Ops:
  1.4 1.2 %fusion.21 = (f32[1,12,6,384]{3,2,1,0:T(8,128)S(1)}, f32[1,12,6,384]{3,2,1,0:T(8,128)S(1)}, f32[1,12,6,384]{3,2,1,0:T(8,128)S(1)}, f32[1,12,6,384]{3,2,1,0:T(8,128)S(1)}) fusion(f32[9,12,6,384]{3,2,1,0:T(8,128)} %refs_0_.6), kind=kLoop, calls=%fused_computation.75 | loop fusion | bytes 884736 | tf_op jit(solution)/shard_map/slice | solution.py:371
  3.0 1.9 %collective-permute-start = (f32[33792]{0:T(1024)S(1)}, f32[33792]{0:T(1024)S(1)}, u32[]{:S(2)}, u32[]{:S(2)}) collective-permute-start(f32[33792]{0:T(1024)S(1)} %get-tuple-element.62), channel_id=1, source_target_pairs={{0,8},{8,16},{16,24},{1,9},{9,17},{17,25},{2,10},{10,18},{18,26},{... | collective-permute-start | bytes 405512 | tf_op jit(solution)/shard_map/ppermute | solution.py:44
  4.9 3.6 %collective-permute-start.1 = (f32[33792]{0:T(1024)S(1)}, f32[33792]{0:T(1024)S(1)}, u32[]{:S(2)}, u32[]{:S(2)}) collective-permute-start(f32[33792]{0:T(1024)S(1)} %get-tuple-element.61), channel_id=1, source_target_pairs={{8,0},{16,8},{24,16},{9,1},{17,9},{25,17},{10,2},{18,10},{26,18},{... | collective-permute-start | bytes 405512 | tf_op jit(solution)/shard_map/ppermute | solution.py:44
  9.1 3.4 %collective-permute-start.2 = (f32[528]{0:T(1024)S(1)}, f32[528]{0:T(1024)S(1)}, u32[]{:S(2)}, u32[]{:S(2)}) collective-permute-start(f32[528]{0:T(1024)S(1)} %pad_maximum_fusion.20), channel_id=1, source_target_pairs={{0,1},{1,2},{2,3},{3,4},{4,5},{5,6},{6,7},{8,9},{9,10},{10,11},{11... | collective-permute-start | bytes 6344 | tf_op jit(solution)/shard_map/ppermute | solution.py:44
  12.9 3.3 %collective-permute-start.3 = (f32[528]{0:T(1024)S(1)}, f32[528]{0:T(1024)S(1)}, u32[]{:S(2)}, u32[]{:S(2)}) collective-permute-start(f32[528]{0:T(1024)S(1)} %pad_maximum_fusion.21), channel_id=1, source_target_pairs={{1,0},{2,1},{3,2},{4,3},{5,4},{6,5},{7,6},{9,8},{10,9},{11,10},{12... | collective-permute-start | bytes 6344 | tf_op jit(solution)/shard_map/ppermute | solution.py:44
  17.0 1.4 %collective-permute-done.3 = f32[528]{0:T(1024)S(1)} collective-permute-done((f32[528]{0:T(1024)S(1)}, f32[528]{0:T(1024)S(1)}, u32[]{:S(2)}, u32[]{:S(2)}) %collective-permute-start.3) | collective-permute-done | bytes 2144 | tf_op jit(solution)/shard_map/ppermute | solution.py:44
  22.3 3.3 %shard_map.138.refs_2_ = f32[3,12,6,384]{3,2,1,0:T(8,128)} custom-call(f32[9,12,6,384]{3,2,1,0:T(8,128)} %refs_0_.6, f32[3,12,2,384]{3,2,1,0:T(2,128)} %reshape.248.refs_1_, f32[3,12,2,384]{3,2,1,0:T(2,128)} %reshape.250.refs_2_, f32[3,12,6,2]{3,2,1,0:T(8,128)} %reshape.253.refs_3_, f32[3,12,6,2]{3,2,1,0:T(8,128)} %reshape.256.refs_4_, ...), custom_call_target="tpu_custom_call" | custom-call | tf_op jit(solution)/shard_map/pallas_call | solution.py:321
  25.6 1.2 %fusion.24 = (f32[3,12,2,384]{3,2,1,0:T(2,128)S(1)}, f32[3,12,2,384]{3,2,1,0:T(2,128)S(1)}) fusion(f32[3,12,6,384]{3,2,1,0:T(8,128)} %shard_map.138.refs_2_), kind=kLoop, calls=%fused_computation.78 | loop fusion | bytes 442368 | tf_op jit(solution)/shard_map/slice | solution.py:60
  26.8 1.1 %fusion.23 = (f32[3,12,6,2]{3,2,1,0:T(8,128)S(1)}, f32[3,12,6,2]{3,2,1,0:T(8,128)S(1)}) fusion(f32[3,12,6,384]{3,2,1,0:T(8,128)} %shard_map.138.refs_2_), kind=kLoop, calls=%fused_computation.77 | loop fusion | bytes 6912 | tf_op jit(solution)/shard_map/slice | solution.py:62
  29.3 1.9 %shard_map.139.refs_2_ = f32[3,8,2,128]{3,2,1,0:T(2,128)} custom-call(f32[9,8,2,128]{3,2,1,0:T(2,128)} %refs_0_.7, f32[3,8,2,128]{3,2,1,0:T(2,128)} %bitcast.86, f32[3,8,2,128]{3,2,1,0:T(2,128)} %bitcast.87, f32[3,8,2,2]{3,2,1,0:T(2,128)} %reshape.260.refs_3_, f32[3,8,2,2]{3,2,1,0:T(2,128)} %reshape.261.refs_4_, s32[8,2,128]{2,1,0:T(2,128)} %refs_7_.5, ...), custom_call_target="tpu_custom_call" | custom-call | tf_op jit(solution)/shard_map/pallas_call | solution.py:321
  32.8 1.9 %collective-permute-start.4 = (f32[33792]{0:T(1024)S(1)}, f32[33792]{0:T(1024)S(1)}, u32[]{:S(2)}, u32[]{:S(2)}) collective-permute-start(f32[33792]{0:T(1024)S(1)} %get-tuple-element.58), channel_id=1, source_target_pairs={{0,8},{8,16},{16,24},{1,9},{9,17},{17,25},{2,10},{10,18},{18,26},{... | collective-permute-start | bytes 405512 | tf_op jit(solution)/shard_map/ppermute | solution.py:44
  34.8 3.6 %collective-permute-start.5 = (f32[33792]{0:T(1024)S(1)}, f32[33792]{0:T(1024)S(1)}, u32[]{:S(2)}, u32[]{:S(2)}) collective-permute-start(f32[33792]{0:T(1024)S(1)} %get-tuple-element.57), channel_id=1, source_target_pairs={{8,0},{16,8},{24,16},{9,1},{17,9},{25,17},{10,2},{18,10},{26,18},{... | collective-permute-start | bytes 405512 | tf_op jit(solution)/shard_map/ppermute | solution.py:44
  38.8 4.3 %collective-permute-start.6 = (f32[528]{0:T(1024)S(1)}, f32[528]{0:T(1024)S(1)}, u32[]{:S(2)}, u32[]{:S(2)}) collective-permute-start(f32[528]{0:T(1024)S(1)} %pad_maximum_fusion.22), channel_id=1, source_target_pairs={{0,1},{1,2},{2,3},{3,4},{4,5},{5,6},{6,7},{8,9},{9,10},{10,11},{11... | collective-permute-start | bytes 6344 | tf_op jit(solution)/shard_map/ppermute | solution.py:44
  43.4 2.4 %collective-permute-start.7 = (f32[528]{0:T(1024)S(1)}, f32[528]{0:T(1024)S(1)}, u32[]{:S(2)}, u32[]{:S(2)}) collective-permute-start(f32[528]{0:T(1024)S(1)} %pad_maximum_fusion.23), channel_id=1, source_target_pairs={{1,0},{2,1},{3,2},{4,3},{5,4},{6,5},{7,6},{9,8},{10,9},{11,10},{12... | collective-permute-start | bytes 6344 | tf_op jit(solution)/shard_map/ppermute | solution.py:44
  46.7 2.3 %collective-permute-done.7 = f32[528]{0:T(1024)S(1)} collective-permute-done((f32[528]{0:T(1024)S(1)}, f32[528]{0:T(1024)S(1)}, u32[]{:S(2)}, u32[]{:S(2)}) %collective-permute-start.7) | collective-permute-done | bytes 2144 | tf_op jit(solution)/shard_map/ppermute | solution.py:44
  54.1 2.0 %shard_map.141 = (f32[9,8,2,128]{3,2,1,0:T(2,128)}, f32[6,8,2,128]{3,2,1,0:T(2,128)}, f32[6,2,128]{2,1,0:T(2,128)}) custom-call(f32[9,8,2,128]{3,2,1,0:T(2,128)} %refs_0_.7, f32[6,8,2,128]{3,2,1,0:T(2,128)} %refs_1_.3, f32[3,8,2,128]{3,2,1,0:T(2,128)} %shard_map.139.refs_2_, f32[3,8,2,128]{3,2,1,0:T(2,128)} %bitcast.84, f32[3,8,2,128]{3,2,1,0:T(2,128)} %bitcast.85, ...), custom_call_target="tpu_custom_call" | custom-call | tf_op jit(solution)/shard_map/pallas_call | solution.py:337
  56.8 4.7 %shard_map.140 = (f32[9,12,6,384]{3,2,1,0:T(8,128)}, f32[6,12,6,384]{3,2,1,0:T(8,128)}, f32[6,6,384]{2,1,0:T(8,128)}) custom-call(f32[9,12,6,384]{3,2,1,0:T(8,128)} %refs_0_.6, f32[6,12,6,384]{3,2,1,0:T(8,128)} %refs_1_.2, f32[3,12,6,384]{3,2,1,0:T(8,128)} %shard_map.138.refs_2_, f32[3,12,2,384]{3,2,1,0:T(2,128)} %reshape.263.refs_3_, ...), custom_call_target="tpu_custom_call" | custom-call | tf_op jit(solution)/shard_map/pallas_call | solution.py:337
  62.5 1.9 %collective-permute-start.9 = (f32[3072]{0:T(1024)S(1)}, f32[3072]{0:T(1024)S(1)}, u32[]{:S(2)}, u32[]{:S(2)}) collective-permute-start(f32[3072]{0:T(1024)S(1)} %pad_maximum_fusion.18), channel_id=1, source_target_pairs={{8,0},{16,8},{24,16},{9,1},{17,9},{25,17},{10,2},{18,10},{26,18},{... | collective-permute-start | bytes 36872 | tf_op jit(solution)/shard_map/ppermute | solution.py:44
  64.5 2.4 %collective-permute-start.8 = (f32[3072]{0:T(1024)S(1)}, f32[3072]{0:T(1024)S(1)}, u32[]{:S(2)}, u32[]{:S(2)}) collective-permute-start(f32[3072]{0:T(1024)S(1)} %pad_maximum_fusion.17), channel_id=1, source_target_pairs={{0,8},{8,16},{16,24},{1,9},{9,17},{17,25},{2,10},{10,18},{18,26},{... | collective-permute-start | bytes 36872 | tf_op jit(solution)/shard_map/ppermute | solution.py:44
  66.9 2.6 %collective-permute-done.8 = f32[3072]{0:T(1024)S(1)} collective-permute-done((f32[3072]{0:T(1024)S(1)}, f32[3072]{0:T(1024)S(1)}, u32[]{:S(2)}, u32[]{:S(2)}) %collective-permute-start.8) | collective-permute-done | bytes 12320 | tf_op jit(solution)/shard_map/ppermute | solution.py:44
  70.9 3.3 %collective-permute-start.11 = (f32[72]{0:T(128)S(1)}, f32[72]{0:T(128)S(1)}, u32[]{:S(2)}, u32[]{:S(2)}) collective-permute-start(f32[72]{0:T(128)S(1)} %pad_maximum_fusion.25), channel_id=1, source_target_pairs={{1,0},{2,1},{3,2},{4,3},{5,4},{6,5},{7,6},{9,8},{10,9},{11,10},{12... | collective-permute-start | bytes 872 | tf_op jit(solution)/shard_map/ppermute | solution.py:44
  74.4 2.7 %collective-permute-start.10 = (f32[72]{0:T(128)S(1)}, f32[72]{0:T(128)S(1)}, u32[]{:S(2)}, u32[]{:S(2)}) collective-permute-start(f32[72]{0:T(128)S(1)} %pad_maximum_fusion.24), channel_id=1, source_target_pairs={{0,1},{1,2},{2,3},{3,4},{4,5},{5,6},{6,7},{8,9},{9,10},{10,11},{11... | collective-permute-start | bytes 872 | tf_op jit(solution)/shard_map/ppermute | solution.py:44
  77.3 3.5 %collective-permute-done.10 = f32[72]{0:T(128)S(1)} collective-permute-done((f32[72]{0:T(128)S(1)}, f32[72]{0:T(128)S(1)}, u32[]{:S(2)}, u32[]{:S(2)}) %collective-permute-start.10) | collective-permute-done | bytes 320 | tf_op jit(solution)/shard_map/ppermute | solution.py:44
  82.0 1.2 %reshape.287 = f32[6,6,384]{2,1,0:T(8,128)S(1)} reshape(f32[6,6,128,3]{3,2,1,0:T(8,128)S(1)} %copy.30) | data formatting | bytes 110592 | tf_op jit(solution)/shard_map/reshape | solution.py:161
  (127 shorter events, 29.3 us)
Async XLA Ops:
  0.6 2.0 %slice-start = ((f32[9,12,6,384]{3,2,1,0:T(8,128)}), f32[2,12,6,384]{3,2,1,0:T(8,128)S(1)}, s32[]{:S(2)}) async-start(f32[9,12,6,384]{3,2,1,0:T(8,128)} %refs_0_.6), calls=%async_computation | async-start | bytes 589824 | tf_op jit(solution)/shard_map/slice | solution.py:371
  1.4 1.5 %slice-start.1 = ((f32[9,8,2,128]{3,2,1,0:T(2,128)}), f32[2,8,2,128]{3,2,1,0:T(2,128)S(1)}, s32[]{:S(2)}) async-start(f32[9,8,2,128]{3,2,1,0:T(2,128)} %refs_0_.7), calls=%async_computation.1 | async-start | bytes 32768 | tf_op jit(solution)/shard_map/slice | solution.py:371
  3.0 17.9 %collective-permute-start = (f32[33792]{0:T(1024)S(1)}, f32[33792]{0:T(1024)S(1)}, u32[]{:S(2)}, u32[]{:S(2)}) collective-permute-start(f32[33792]{0:T(1024)S(1)} %get-tuple-element.62), channel_id=1, source_target_pairs={{0,8},{8,16},{16,24},{1,9},{9,17},{17,25},{2,10},{10,18},{18,26},{... | collective-permute-start | bytes 405512 | tf_op jit(solution)/shard_map/ppermute | solution.py:44
  4.9 16.6 %collective-permute-start.1 = (f32[33792]{0:T(1024)S(1)}, f32[33792]{0:T(1024)S(1)}, u32[]{:S(2)}, u32[]{:S(2)}) collective-permute-start(f32[33792]{0:T(1024)S(1)} %get-tuple-element.61), channel_id=1, source_target_pairs={{8,0},{16,8},{24,16},{9,1},{17,9},{25,17},{10,2},{18,10},{26,18},{... | collective-permute-start | bytes 405512 | tf_op jit(solution)/shard_map/ppermute | solution.py:44
  9.1 7.1 %collective-permute-start.2 = (f32[528]{0:T(1024)S(1)}, f32[528]{0:T(1024)S(1)}, u32[]{:S(2)}, u32[]{:S(2)}) collective-permute-start(f32[528]{0:T(1024)S(1)} %pad_maximum_fusion.20), channel_id=1, source_target_pairs={{0,1},{1,2},{2,3},{3,4},{4,5},{5,6},{6,7},{8,9},{9,10},{10,11},{11... | collective-permute-start | bytes 6344 | tf_op jit(solution)/shard_map/ppermute | solution.py:44
  12.9 5.5 %collective-permute-start.3 = (f32[528]{0:T(1024)S(1)}, f32[528]{0:T(1024)S(1)}, u32[]{:S(2)}, u32[]{:S(2)}) collective-permute-start(f32[528]{0:T(1024)S(1)} %pad_maximum_fusion.21), channel_id=1, source_target_pairs={{1,0},{2,1},{3,2},{4,3},{5,4},{6,5},{7,6},{9,8},{10,9},{11,10},{12... | collective-permute-start | bytes 6344 | tf_op jit(solution)/shard_map/ppermute | solution.py:44
  32.8 18.5 %collective-permute-start.4 = (f32[33792]{0:T(1024)S(1)}, f32[33792]{0:T(1024)S(1)}, u32[]{:S(2)}, u32[]{:S(2)}) collective-permute-start(f32[33792]{0:T(1024)S(1)} %get-tuple-element.58), channel_id=1, source_target_pairs={{0,8},{8,16},{16,24},{1,9},{9,17},{17,25},{2,10},{10,18},{18,26},{... | collective-permute-start | bytes 405512 | tf_op jit(solution)/shard_map/ppermute | solution.py:44
  34.8 17.4 %collective-permute-start.5 = (f32[33792]{0:T(1024)S(1)}, f32[33792]{0:T(1024)S(1)}, u32[]{:S(2)}, u32[]{:S(2)}) collective-permute-start(f32[33792]{0:T(1024)S(1)} %get-tuple-element.57), channel_id=1, source_target_pairs={{8,0},{16,8},{24,16},{9,1},{17,9},{25,17},{10,2},{18,10},{26,18},{... | collective-permute-start | bytes 405512 | tf_op jit(solution)/shard_map/ppermute | solution.py:44
  38.8 7.1 %collective-permute-start.6 = (f32[528]{0:T(1024)S(1)}, f32[528]{0:T(1024)S(1)}, u32[]{:S(2)}, u32[]{:S(2)}) collective-permute-start(f32[528]{0:T(1024)S(1)} %pad_maximum_fusion.22), channel_id=1, source_target_pairs={{0,1},{1,2},{2,3},{3,4},{4,5},{5,6},{6,7},{8,9},{9,10},{10,11},{11... | collective-permute-start | bytes 6344 | tf_op jit(solution)/shard_map/ppermute | solution.py:44
  43.4 5.5 %collective-permute-start.7 = (f32[528]{0:T(1024)S(1)}, f32[528]{0:T(1024)S(1)}, u32[]{:S(2)}, u32[]{:S(2)}) collective-permute-start(f32[528]{0:T(1024)S(1)} %pad_maximum_fusion.23), channel_id=1, source_target_pairs={{1,0},{2,1},{3,2},{4,3},{5,4},{6,5},{7,6},{9,8},{10,9},{11,10},{12... | collective-permute-start | bytes 6344 | tf_op jit(solution)/shard_map/ppermute | solution.py:44
  56.8 12.7 %copy-start.1 = (f32[6,2,128]{2,1,0:T(2,128)S(1)}, f32[6,2,128]{2,1,0:T(2,128)}, u32[]{:S(2)}) copy-start(f32[6,2,128]{2,1,0:T(2,128)} %get-tuple-element.12) | copy-start | bytes 18436
  62.5 4.4 %collective-permute-start.9 = (f32[3072]{0:T(1024)S(1)}, f32[3072]{0:T(1024)S(1)}, u32[]{:S(2)}, u32[]{:S(2)}) collective-permute-start(f32[3072]{0:T(1024)S(1)} %pad_maximum_fusion.18), channel_id=1, source_target_pairs={{8,0},{16,8},{24,16},{9,1},{17,9},{25,17},{10,2},{18,10},{26,18},{... | collective-permute-start | bytes 36872 | tf_op jit(solution)/shard_map/ppermute | solution.py:44
  64.5 5.0 %collective-permute-start.8 = (f32[3072]{0:T(1024)S(1)}, f32[3072]{0:T(1024)S(1)}, u32[]{:S(2)}, u32[]{:S(2)}) collective-permute-start(f32[3072]{0:T(1024)S(1)} %pad_maximum_fusion.17), channel_id=1, source_target_pairs={{0,8},{8,16},{16,24},{1,9},{9,17},{17,25},{2,10},{10,18},{18,26},{... | collective-permute-start | bytes 36872 | tf_op jit(solution)/shard_map/ppermute | solution.py:44
  70.9 6.3 %collective-permute-start.11 = (f32[72]{0:T(128)S(1)}, f32[72]{0:T(128)S(1)}, u32[]{:S(2)}, u32[]{:S(2)}) collective-permute-start(f32[72]{0:T(128)S(1)} %pad_maximum_fusion.25), channel_id=1, source_target_pairs={{1,0},{2,1},{3,2},{4,3},{5,4},{6,5},{7,6},{9,8},{10,9},{11,10},{12... | collective-permute-start | bytes 872 | tf_op jit(solution)/shard_map/ppermute | solution.py:44
  74.4 6.4 %collective-permute-start.10 = (f32[72]{0:T(128)S(1)}, f32[72]{0:T(128)S(1)}, u32[]{:S(2)}, u32[]{:S(2)}) collective-permute-start(f32[72]{0:T(128)S(1)} %pad_maximum_fusion.24), channel_id=1, source_target_pairs={{0,1},{1,2},{2,3},{3,4},{4,5},{5,6},{6,7},{8,9},{9,10},{10,11},{11... | collective-permute-start | bytes 872 | tf_op jit(solution)/shard_map/ppermute | solution.py:44
  82.0 1.2 %copy-start = (f32[6,6,384]{2,1,0:T(8,128)S(1)}, f32[6,6,384]{2,1,0:T(8,128)}, u32[]{:S(2)}) copy-start(f32[6,6,384]{2,1,0:T(8,128)} %get-tuple-element.11) | copy-start | bytes 165892

commit v3 on v2

--- a/solution.py
+++ b/solution.py
@@ -242,19 +242,130 @@
     return total
 
 
-def velocity_kernel(rows, spacing, has_metric, *refs):
-    if has_metric:
-        w, xlo, xhi, ylo, yhi, mat, metric, table, out, sx = refs
-    else:
-        w, xlo, xhi, ylo, yhi, mat, table, out, sx = refs
-        metric = None
-    layers, size = w.shape[1], w.shape[2]
-    for slot, field in enumerate((3, 6, 7)):
-        fill_x(sx, slot, xlo[slot], w[field], xhi[slot])
-    for z in range(layers):
-        dx = [slope_x(sx, slot, z, size, spacing) for slot in range(3)]
-        dy = [slope_y(w[field, z], ylo[slot, z], yhi[slot, z], spacing) for slot, field in enumerate((6, 4, 8))]
-        dz = [slope_z(w, field, rows[z]) for field in (7, 8, 5)]
+class Block:
+    def __init__(self, shape, spacing, has_metric, x_base, y_base):
+        self.layers, self.size, self.lanes = shape
+        self.chunks = self.lanes // 128
+        self.spacing = spacing
+        self.has_metric = has_metric
+        self.rows = sbp_rows(self.layers, spacing)
+        self.x_base, self.y_base = x_base, y_base
+
+    @property
+    def x_rows(self):
+        return 3 * self.layers * self.chunks * 2
+
+    @property
+    def y_rows(self):
+        return self.layers * self.size
+
+
+def plan_blocks(fine_shape, coarse_shape):
+    fine = Block(fine_shape, 1.0, True, 0, 0)
+    coarse = Block(coarse_shape, 3.0, False, fine.x_rows, fine.y_rows)
+    return fine, coarse, fine.x_rows + coarse.x_rows, fine.y_rows + coarse.y_rows
+
+
+def write_rims(b, src, fields, x_prev, x_next, y_prev, y_next):
+    size, lanes = b.size, b.lanes
+    for c, field in enumerate(fields):
+        for z in range(b.layers):
+            lo = src[field, z, 0:2, :]
+            hi = src[field, z, size - 2 : size, :]
+            for j in range(b.chunks):
+                row = b.x_base + ((c * b.layers + z) * b.chunks + j) * 2
+                x_prev[row : row + 2, :] = lo[:, j * 128 : (j + 1) * 128]
+                x_next[row : row + 2, :] = hi[:, j * 128 : (j + 1) * 128]
+    lane = lax.broadcasted_iota(jnp.int32, (size, 128), 1)
+    for z in range(b.layers):
+        acc_lo = jnp.zeros((size, 128), jnp.float32)
+        acc_hi = jnp.zeros((size, 128), jnp.float32)
+        for c, field in enumerate(fields):
+            v = src[field, z]
+            rl = v if c == 0 else pltpu.roll(v, 2 * c, 1)
+            rh = pltpu.roll(v, (2 * c + 2) % lanes, 1)
+            keep = (lane >= 2 * c) & (lane < 2 * c + 2)
+            acc_lo = jnp.where(keep, rl[:, 0:128], acc_lo)
+            acc_hi = jnp.where(keep, rh[:, 0:128], acc_hi)
+        row = b.y_base + z * size
+        y_prev[row : row + size, :] = acc_lo
+        y_next[row : row + size, :] = acc_hi
+
+
+def read_x_halo(b, buf, c, z):
+    parts = [buf[pl.ds(b.x_base + ((c * b.layers + z) * b.chunks + j) * 2, 2), :] for j in range(b.chunks)]
+    return parts[0] if len(parts) == 1 else jnp.concatenate(parts, axis=1)
+
+
+def read_y_halo(b, buf, c, z):
+    row = b.y_base + z * b.size
+    return buf[pl.ds(row, b.size), pl.ds(2 * c, 1)], buf[pl.ds(row, b.size), pl.ds(2 * c + 1, 1)]
+
+
+def fill_x2(b, scratch, slot, src, field, lo_buf, hi_buf):
+    size = b.size
+    scratch[slot, :, 2 : 2 + size, :] = src[field]
+    for z in range(b.layers):
+        scratch[slot, z, 0:2, :] = read_x_halo(b, lo_buf, slot, z)
+        scratch[slot, z, 2 + size :, :] = read_x_halo(b, hi_buf, slot, z)
+
+
+def slope_y2(f, lo, hi, spacing):
+    n = f.shape[-1]
+    lane = lax.broadcasted_iota(jnp.int32, f.shape, 1)
+    m1 = jnp.where(lane == 0, lo[1], pltpu.roll(f, 1, 1))
+    m2 = jnp.where(lane == 0, lo[0], jnp.where(lane == 1, lo[1], pltpu.roll(f, 2, 1)))
+    p1 = jnp.where(lane == n - 1, hi[0], pltpu.roll(f, n - 1, 1))
+    p2 = jnp.where(lane == n - 2, hi[0], jnp.where(lane == n - 1, hi[1], pltpu.roll(f, n - 2, 1)))
+    return (m2 - 8.0 * m1 + 8.0 * p1 - p2) / (12.0 * spacing)
+
+
+STRESS_X = (3, 6, 7)
+STRESS_Y = (6, 4, 8)
+VELOCITY = (0, 1, 2)
+
+
+def pack_kernel(blocks, fw, cw, x_prev, x_next, y_prev, y_next):
+    for b, w in zip(blocks, (fw, cw)):
+        write_rims_split(b, w, x_prev, x_next, y_prev, y_next)
+
+
+def write_rims_split(b, w, x_prev, x_next, y_prev, y_next):
+    size, lanes = b.size, b.lanes
+    for c, field in enumerate(STRESS_X):
+        for z in range(b.layers):
+            lo = w[field, z, 0:2, :]
+            hi = w[field, z, size - 2 : size, :]
+            for j in range(b.chunks):
+                row = b.x_base + ((c * b.layers + z) * b.chunks + j) * 2
+                x_prev[row : row + 2, :] = lo[:, j * 128 : (j + 1) * 128]
+                x_next[row : row + 2, :] = hi[:, j * 128 : (j + 1) * 128]
+    lane = lax.broadcasted_iota(jnp.int32, (size, 128), 1)
+    for z in range(b.layers):
+        acc_lo = jnp.zeros((size, 128), jnp.float32)
+        acc_hi = jnp.zeros((size, 128), jnp.float32)
+        for c, field in enumerate(STRESS_Y):
+            v = w[field, z]
+            rl = v if c == 0 else pltpu.roll(v, 2 * c, 1)
+            rh = pltpu.roll(v, (2 * c + 2) % lanes, 1)
+            keep = (lane >= 2 * c) & (lane < 2 * c + 2)
+            acc_lo = jnp.where(keep, rl[:, 0:128], acc_lo)
+            acc_hi = jnp.where(keep, rh[:, 0:128], acc_hi)
+        row = b.y_base + z * size
+        y_prev[row : row + size, :] = acc_lo
+        y_next[row : row + size, :] = acc_hi
+
+
+def velocity_block(b, w, mat, metric, table, out, sx, hx_lo, hx_hi, hy_lo, hy_hi):
+    for slot, field in enumerate(STRESS_X):
+        fill_x2(b, sx, slot, w, field, hx_lo, hx_hi)
+    for z in range(b.layers):
+        dx = [slope_x(sx, slot, z, b.size, b.spacing) for slot in range(3)]
+        dy = [
+            slope_y2(w[field, z], read_y_halo(b, hy_lo, slot, z), read_y_halo(b, hy_hi, slot, z), b.spacing)
+            for slot, field in enumerate(STRESS_Y)
+        ]
+        dz = [slope_z(w, field, b.rows[z]) for field in (7, 8, 5)]
         if metric is not None:
             m = metric[z]
             dz = [m * d for d in dz]
@@ -263,19 +374,26 @@
             out[k, z] = w[k, z] + step_size * (buoy * (dx[k] + dy[k] + dz[k]))
 
 
-def stress_kernel(rows, spacing, has_metric, depth, *refs):
-    if has_metric:
-        w, mem, vel, xlo, xhi, ylo, yhi, mat, mech, metric, mtab, atab, out, mem_out, face, sx = refs
-    else:
-        w, mem, vel, xlo, xhi, ylo, yhi, mat, mech, mtab, atab, out, mem_out, face, sx = refs
-        metric = None
-    layers, size = w.shape[1], w.shape[2]
+def velocity_kernel(blocks, fw, cw, hx_lo, hx_hi, hy_lo, hy_hi, fmat, fmetric, cmat, table,
+                    fvel, cvel, vx_prev, vx_next, vy_prev, vy_next, sx_f, sx_c):
+    fine, coarse = blocks
+    velocity_block(fine, fw, fmat, fmetric, table, fvel, sx_f, hx_lo, hx_hi, hy_lo, hy_hi)
+    velocity_block(coarse, cw, cmat, None, table, cvel, sx_c, hx_lo, hx_hi, hy_lo, hy_hi)
+    write_rims(fine, fvel, VELOCITY, vx_prev, vx_next, vy_prev, vy_next)
+    write_rims(coarse, cvel, VELOCITY, vx_prev, vx_next, vy_prev, vy_next)
+
+
+def stress_block(b, depth, w, mem, vel, mat, mech, metric, mtab, atab, out, mem_out, face, sx,
+                 hx_lo, hx_hi, hy_lo, hy_hi):
     for slot in range(3):
-        fill_x(sx, slot, xlo[slot], vel[slot], xhi[slot])
-    for z in range(layers):
-        dx = [slope_x(sx, slot, z, size, spacing) for slot in range(3)]
-        dy = [slope_y(vel[slot, z], ylo[slot, z], yhi[slot, z], spacing) for slot in range(3)]
-        dz = [slope_z(vel, slot, rows[z]) for slot in range(3)]
+        fill_x2(b, sx, slot, vel, slot, hx_lo, hx_hi)
+    for z in range(b.layers):
+        dx = [slope_x(sx, slot, z, b.size, b.spacing) for slot in range(3)]
+        dy = [
+            slope_y2(vel[slot, z], read_y_halo(b, hy_lo, slot, z), read_y_halo(b, hy_hi, slot, z), b.spacing)
+            for slot in range(3)
+        ]
+        dz = [slope_z(vel, slot, b.rows[z]) for slot in range(3)]
         if metric is not None:
             m = metric[z]
             dz = [m * d for d in dz]
@@ -307,44 +425,40 @@
                 face[i] = values[k]
 
 
+def stress_kernel(blocks, fw, fmem, fvel, cw, cmem, cvel, hx_lo, hx_hi, hy_lo, hy_hi,
+                  fmat, fmech, fmetric, cmat, cmech, mtab, atab,
+                  fout, fmem_out, fface, cout, cmem_out, cface, sx_f, sx_c):
+    fine, coarse = blocks
+    stress_block(fine, fine.layers - 1, fw, fmem, fvel, fmat, fmech, fmetric, mtab, atab, fout, fmem_out,
+                 fface, sx_f, hx_lo, hx_hi, hy_lo, hy_hi)
+    stress_block(coarse, 0, cw, cmem, cvel, cmat, cmech, None, mtab, atab, cout, cmem_out,
+                 cface, sx_c, hx_lo, hx_hi, hy_lo, hy_hi)
+
+
 def vmem_specs(count):
     return [pl.BlockSpec(memory_space=pltpu.VMEM)] * count
 
 
-def velocity_call(wave, halo_x, halo_y, material, metric, table, spacing):
-    layers, size, lanes = wave.shape[1:]
-    rows = sbp_rows(layers, spacing)
-    args = [wave, halo_x[0], halo_x[1], halo_y[0], halo_y[1], material]
-    if metric is not None:
-        args.append(metric)
-    kernel = functools.partial(velocity_kernel, rows, spacing, metric is not None)
-    return pl.pallas_call(
-        kernel,
-        out_shape=jax.ShapeDtypeStruct((3, layers, size, lanes), jnp.float32),
-        in_specs=vmem_specs(len(args)) + [pl.BlockSpec(memory_space=pltpu.SMEM)],
-        out_specs=pl.BlockSpec(memory_space=pltpu.VMEM),
-        scratch_shapes=[pltpu.VMEM((3, layers, size + 4, lanes), jnp.float32)],
-    )(*args, table)
-
-
-def stress_call(wave, memory, velocity, halo, material, mechanism, metric, mtab, atab, spacing, depth):
-    layers, size, lanes = wave.shape[1:]
-    rows = sbp_rows(layers, spacing)
-    args = [wave, memory, velocity, halo[0], halo[1], halo[2], halo[3], material, mechanism]
-    if metric is not None:
-        args.append(metric)
-    kernel = functools.partial(stress_kernel, rows, spacing, metric is not None, depth)
-    return pl.pallas_call(
-        kernel,
-        out_shape=(
-            jax.ShapeDtypeStruct(wave.shape, jnp.float32),
-            jax.ShapeDtypeStruct(memory.shape, jnp.float32),
-            jax.ShapeDtypeStruct((6, size, lanes), jnp.float32),
-        ),
-        in_specs=vmem_specs(len(args)) + [pl.BlockSpec(memory_space=pltpu.SMEM)] * 2,
-        out_specs=tuple(vmem_specs(3)),
-        scratch_shapes=[pltpu.VMEM((3, layers, size + 4, lanes), jnp.float32)],
-    )(*args, mtab, atab)
+def f32(shape):
+    return jax.ShapeDtypeStruct(shape, jnp.float32)
+
+
+def halo_shapes(x_rows, y_rows):
+    return (f32((x_rows, 128)), f32((x_rows, 128)), f32((y_rows, 128)), f32((y_rows, 128)))
+
+
+def scratch_for(b):
+    return pltpu.VMEM((3, b.layers, b.size + 4, b.lanes), jnp.float32)
+
+
+def receive(buffers):
+    x_prev, x_next, y_prev, y_next = buffers
+    return (
+        shift_from(x_next, "gx", 1),
+        shift_from(x_prev, "gx", -1),
+        shift_from(y_next, "gy", 1),
+        shift_from(y_prev, "gy", -1),
+    )
 
 
 def put_face(out, face, depth):
@@ -367,36 +481,41 @@
     material_table,
     attenuation_table,
 ):
-    def x_parts(w):
-        return jnp.stack([w[3], w[6], w[7]])
-
-    def y_parts(w):
-        return jnp.stack([w[6], w[4], w[8]])
-
-    fx, fy, cx, cy = x_parts(fine_wave), y_parts(fine_wave), x_parts(coarse_wave), y_parts(coarse_wave)
-    x_lo = packed_shift([fx[..., -2:, :], cx[..., -2:, :]], "gx", 1)
-    x_hi = packed_shift([fx[..., :2, :], cx[..., :2, :]], "gx", -1)
-    y_lo = packed_shift([fy[..., -2:], cy[..., -2:]], "gy", 1)
-    y_hi = packed_shift([fy[..., :2], cy[..., :2]], "gy", -1)
-
-    fine_velocity = velocity_call(
-        fine_wave, (x_lo[0], x_hi[0]), (y_lo[0], y_hi[0]), fine_material, fine_metric, material_table, 1.0
-    )
-    coarse_velocity = velocity_call(
-        coarse_wave, (x_lo[1], x_hi[1]), (y_lo[1], y_hi[1]), coarse_material, None, material_table, 3.0
-    )
-
-    fine_vh, coarse_vh = exchange([fine_velocity, coarse_velocity], 2)
+    fine, coarse, x_rows, y_rows = plan_blocks(fine_wave.shape[1:], coarse_wave.shape[1:])
+    blocks = (fine, coarse)
+    smem = pl.BlockSpec(memory_space=pltpu.SMEM)
+
+    rims = pl.pallas_call(
+        functools.partial(pack_kernel, blocks),
+        out_shape=halo_shapes(x_rows, y_rows),
+        in_specs=vmem_specs(2),
+        out_specs=tuple(vmem_specs(4)),
+    )(fine_wave, coarse_wave)
+    halos = receive(rims)
+
+    fine_velocity, coarse_velocity, *vrims = pl.pallas_call(
+        functools.partial(velocity_kernel, blocks),
+        out_shape=(f32((3,) + fine_wave.shape[1:]), f32((3,) + coarse_wave.shape[1:])) + halo_shapes(x_rows, y_rows),
+        in_specs=vmem_specs(9) + [smem],
+        out_specs=tuple(vmem_specs(6)),
+        scratch_shapes=[scratch_for(fine), scratch_for(coarse)],
+    )(fine_wave, coarse_wave, *halos, fine_material, fine_metric, coarse_material, material_table)
+
+    vhalos = receive(vrims)
+    fine_out, fine_mem, fine_face, coarse_out, coarse_mem, coarse_face = pl.pallas_call(
+        functools.partial(stress_kernel, blocks),
+        out_shape=(
+            f32(fine_wave.shape), f32(fine_memory.shape), f32((6,) + fine_wave.shape[2:]),
+            f32(coarse_wave.shape), f32(coarse_memory.shape), f32((6,) + coarse_wave.shape[2:]),
+        ),
+        in_specs=vmem_specs(15) + [smem, smem],
+        out_specs=tuple(vmem_specs(6)),
+        scratch_shapes=[scratch_for(fine), scratch_for(coarse)],
+    )(fine_wave, fine_memory, fine_velocity, coarse_wave, coarse_memory, coarse_velocity, *vhalos,
+      fine_material, fine_mechanism, fine_metric, coarse_material, coarse_mechanism, material_table,
+      attenuation_table)
+
     depth = fine_wave.shape[1] - 1
-    fine_out, fine_mem, fine_face = stress_call(
-        fine_wave, fine_memory, fine_velocity, fine_vh, fine_material, fine_mechanism, fine_metric,
-        material_table, attenuation_table, 1.0, depth,
-    )
-    coarse_out, coarse_mem, coarse_face = stress_call(
-        coarse_wave, coarse_memory, coarse_velocity, coarse_vh, coarse_material, coarse_mechanism, None,
-        material_table, attenuation_table, 3.0, 0,
-    )
-
     fine_padded, coarse_padded = pad_faces([fine_face, coarse_face])
     fine_new = fine_face - penalty * (fine_face - prolong_axis(prolong_axis(coarse_padded, 1), 2))
     coarse_new = coarse_face - penalty * (coarse_face - restrict_axis(restrict_axis(fine_padded, 1), 2))

time: 92.4 us -> 77.5 us (0.84)
  local copies, waits for them, and re-layouts: 31 us -> 14.5 us
  waiting for transfers between devices: 9.67 us -> 12.8 us
  Pallas kernels: 11.8 us -> 10.8 us
    reshape x16 -> x4, local copies, waits for them, and re-layouts: 9.45 us -> 0.42 us  [packed_shift(): out.append(moved[start:start + size].reshape(b.shape))]
    slice x10 -> x0, local copies, waits for them, and re-layouts: 5.29 us -> none  [the longest x6 1.98 us: x_parts(): return jnp.stack([w[3], w[6], w[7]])]
    ppermute x12, waiting for transfers between devices: 9.67 us -> 12.8 us  [shift_from(): return lax.ppermute(block, axis, pairs)]
    slice x24 -> x8, local copies, waits for them, and re-layouts: 2.96 us -> 0.2 us  [packed_shift(): out.append(moved[start:start + size].reshape(b.shape))]
    unnamed x9 -> x25, local copies, waits for them, and re-layouts: 1.35 us -> 3.36 us
    reshape x18 -> x6, local copies, waits for them, and re-layouts: 1.76 us -> 0.34 us  [packed_shift(): joined = jnp.concatenate([b.reshape(-1) for b in blocks])]
    concatenate x10 -> x4, other arithmetic: 1.27 us -> 0.17 us  [packed_shift(): joined = jnp.concatenate([b.reshape(-1) for b in blocks])]
    pallas_call x4 -> x3, Pallas kernels: 11.8 us -> 10.8 us  [the longest x1 4.82 us: local(): pl.pallas_call(functools.partial(stress_kernel, blocks), out_shape=(f32(f...]
  transfers between devices with their start and end apart: 12 -> 12, of which waited for: 4 -> 6; matrix products, arithmetic and copies ran while one was open for 11% -> 1% of each run, Pallas kernels for 0% -> 0%
where the time goes in v3:
time: 77.5 us; the launch traced here: 76.8 us
  starting transfers between devices  34.7 us (45%)
  local copies, waits for them, and re-layouts  14.5 us (19%)
  waiting for transfers between devices  12.8 us (17%)
  Pallas kernels  10.8 us (14%)
  other arithmetic  2.96 us (4%)
  between operations  1.03 us (1%)
    ppermute x12, starting transfers between devices, shift_from(): return lax.ppermute(block, axis, pairs)  34.7 us
    ppermute x12, waiting for transfers between devices, shift_from(): return lax.ppermute(block, axis, pairs)  12.8 us
    pallas_call x1, Pallas kernels, local(): pl.pallas_call(functools.partial(stress_kernel, blocks), out_shape=(f32(f...  4.82 us
    pallas_call x1, Pallas kernels, local(): pl.pallas_call(functools.partial(velocity_kernel, blocks), out_shape=(f32...  3.72 us
    unnamed x25, local copies, waits for them, and re-layouts  3.36 us
    pallas_call x1, Pallas kernels, local(): pl.pallas_call(functools.partial(pack_kernel, blocks), out_shape=halo_sha...  2.25 us
    reshape x3, local copies, waits for them, and re-layouts, split_three(): part.reshape(part.shape[:along] + (length, 3) + part.shape[along + 1:])  1.87 us
    slice x2, local copies, waits for them, and re-layouts, pad_faces(): x_lo = packed_shift([f[:, -1:, :] for f in faces], 'gx', 1)  1.8 us
  transfers between devices with their start and end apart: 12, of which 6 were waited for; matrix products, arithmetic and copies ran while one was open for 1% of the time, Pallas kernels for 0%

profile of v3, /device:TPU:10, one launch (start us, length us, event | category | flops | bytes accessed | tf_op | source)
XLA Modules:
  0.0 76.8 jit_solution(13897717438498475357)
XLA Ops:
  0.6 2.2 %shard_map.138 = (f32[264,128]{1,0:T(8,128)}, f32[264,128]{1,0:T(8,128)}, f32[88,128]{1,0:T(8,128)}, f32[88,128]{1,0:T(8,128)}) custom-call(f32[9,12,6,384]{3,2,1,0:T(8,128)} %fw.5, f32[9,8,2,128]{3,2,1,0:T(2,128)} %cw.5), custom_call_target="tpu_custom_call" | custom-call | tf_op jit(solution)/shard_map/pallas_call | solution.py:488
  2.9 1.9 %collective-permute-start = (f32[264,128]{1,0:T(8,128)}, f32[264,128]{1,0:T(8,128)S(1)}, u32[]{:S(2)}, u32[]{:S(2)}) collective-permute-start(f32[264,128]{1,0:T(8,128)} %get-tuple-element.20), channel_id=1, source_target_pairs={{0,8},{8,16},{16,24},{1,9},{9,17},{17,25},{2,10},{10,18},{18,26},{... | collective-permute-start | bytes 405512 | tf_op jit(solution)/shard_map/ppermute | solution.py:44
  4.8 3.6 %collective-permute-start.1 = (f32[264,128]{1,0:T(8,128)}, f32[264,128]{1,0:T(8,128)S(1)}, u32[]{:S(2)}, u32[]{:S(2)}) collective-permute-start(f32[264,128]{1,0:T(8,128)} %get-tuple-element.21), channel_id=1, source_target_pairs={{8,0},{16,8},{24,16},{9,1},{17,9},{25,17},{10,2},{18,10},{26,18},{... | collective-permute-start | bytes 405512 | tf_op jit(solution)/shard_map/ppermute | solution.py:44
  8.4 3.4 %collective-permute-start.2 = (f32[88,128]{1,0:T(8,128)}, f32[88,128]{1,0:T(8,128)S(1)}, u32[]{:S(2)}, u32[]{:S(2)}) collective-permute-start(f32[88,128]{1,0:T(8,128)} %get-tuple-element.22), channel_id=1, source_target_pairs={{0,1},{1,2},{2,3},{3,4},{4,5},{5,6},{6,7},{8,9},{9,10},{10,11},{11... | collective-permute-start | bytes 135176 | tf_op jit(solution)/shard_map/ppermute | solution.py:44
  11.9 3.3 %collective-permute-start.3 = (f32[88,128]{1,0:T(8,128)}, f32[88,128]{1,0:T(8,128)S(1)}, u32[]{:S(2)}, u32[]{:S(2)}) collective-permute-start(f32[88,128]{1,0:T(8,128)} %get-tuple-element.23), channel_id=1, source_target_pairs={{1,0},{2,1},{3,2},{4,3},{5,4},{6,5},{7,6},{9,8},{10,9},{11,10},{12... | collective-permute-start | bytes 135176 | tf_op jit(solution)/shard_map/ppermute | solution.py:44
  15.5 2.5 %collective-permute-done.3.hy_hi = f32[88,128]{1,0:T(8,128)S(1)} collective-permute-done((f32[88,128]{1,0:T(8,128)}, f32[88,128]{1,0:T(8,128)S(1)}, u32[]{:S(2)}, u32[]{:S(2)}) %collective-permute-start.3) | collective-permute-done | bytes 45088 | tf_op jit(solution)/shard_map/ppermute | solution.py:44
  19.4 3.7 %shard_map.139 = (f32[3,12,6,384]{3,2,1,0:T(8,128)}, f32[3,8,2,128]{3,2,1,0:T(2,128)}, f32[264,128]{1,0:T(8,128)}, f32[264,128]{1,0:T(8,128)}, f32[88,128]{1,0:T(8,128)}, /*index=5*/f32[88,128]{1,0:T(8,128)}) custom-call(f32[9,12,6,384]{3,2,1,0:T(8,128)} %fw.5, f32[9,8,2,128]{3,2,1,0:T(2,128)} %cw.5, f32[264,128]{1,0:T(8,128)} %copy-done.1, ...), custom_call_target="tpu_custom_call" | custom-call | tf_op jit(solution)/shard_map/pallas_call | solution.py:496
  23.1 1.9 %collective-permute-start.4 = (f32[264,128]{1,0:T(8,128)}, f32[264,128]{1,0:T(8,128)S(1)}, u32[]{:S(2)}, u32[]{:S(2)}) collective-permute-start(f32[264,128]{1,0:T(8,128)} %get-tuple-element.26), channel_id=1, source_target_pairs={{0,8},{8,16},{16,24},{1,9},{9,17},{17,25},{2,10},{10,18},{18,26},{... | collective-permute-start | bytes 405512 | tf_op jit(solution)/shard_map/ppermute | solution.py:44
  25.0 3.6 %collective-permute-start.5 = (f32[264,128]{1,0:T(8,128)}, f32[264,128]{1,0:T(8,128)S(1)}, u32[]{:S(2)}, u32[]{:S(2)}) collective-permute-start(f32[264,128]{1,0:T(8,128)} %get-tuple-element.27), channel_id=1, source_target_pairs={{8,0},{16,8},{24,16},{9,1},{17,9},{25,17},{10,2},{18,10},{26,18},{... | collective-permute-start | bytes 405512 | tf_op jit(solution)/shard_map/ppermute | solution.py:44
  28.6 4.3 %collective-permute-start.6 = (f32[88,128]{1,0:T(8,128)}, f32[88,128]{1,0:T(8,128)S(1)}, u32[]{:S(2)}, u32[]{:S(2)}) collective-permute-start(f32[88,128]{1,0:T(8,128)} %get-tuple-element.28), channel_id=1, source_target_pairs={{0,1},{1,2},{2,3},{3,4},{4,5},{5,6},{6,7},{8,9},{9,10},{10,11},{11... | collective-permute-start | bytes 135176 | tf_op jit(solution)/shard_map/ppermute | solution.py:44
  33.0 2.4 %collective-permute-start.7 = (f32[88,128]{1,0:T(8,128)}, f32[88,128]{1,0:T(8,128)S(1)}, u32[]{:S(2)}, u32[]{:S(2)}) collective-permute-start(f32[88,128]{1,0:T(8,128)} %get-tuple-element.29), channel_id=1, source_target_pairs={{1,0},{2,1},{3,2},{4,3},{5,4},{6,5},{7,6},{9,8},{10,9},{11,10},{12... | collective-permute-start | bytes 135176 | tf_op jit(solution)/shard_map/ppermute | solution.py:44
  35.7 3.4 %collective-permute-done.7.hy_hi = f32[88,128]{1,0:T(8,128)S(1)} collective-permute-done((f32[88,128]{1,0:T(8,128)}, f32[88,128]{1,0:T(8,128)S(1)}, u32[]{:S(2)}, u32[]{:S(2)}) %collective-permute-start.7) | collective-permute-done | bytes 45088 | tf_op jit(solution)/shard_map/ppermute | solution.py:44
  39.9 4.8 %shard_map.140 = (f32[9,12,6,384]{3,2,1,0:T(8,128)}, f32[6,12,6,384]{3,2,1,0:T(8,128)}, f32[6,6,384]{2,1,0:T(8,128)}, f32[9,8,2,128]{3,2,1,0:T(2,128)}, f32[6,8,2,128]{3,2,1,0:T(2,128)}, /*index=5*/f32[6,2,128]{2,1,0:T(2,128)}) custom-call(f32[9,12,6,384]{3,2,1,0:T(8,128)} %fw.5, f32[6,12,6,384]{3,2,1,0:T(8,128)} %fmem.1, ...), custom_call_target="tpu_custom_call" | custom-call | tf_op jit(solution)/shard_map/pallas_call | solution.py:505
  44.7 0.8 %slice_reduce_fusion.5 = (f32[6,128]{1,0:T(8,128)S(1)}, f32[6,128]{1,0:T(8,128)S(1)}) fusion(f32[6,2,128]{2,1,0:T(2,128)} %get-tuple-element.32), kind=kLoop, calls=%fused_computation.53 | loop fusion | bytes 12288 | tf_op jit(solution)/shard_map/slice | solution.py:139
  45.5 1.0 %slice_reduce_fusion.3 = (f32[6,384]{1,0:T(8,128)S(1)}, f32[6,384]{1,0:T(8,128)S(1)}) fusion(f32[6,6,384]{2,1,0:T(8,128)} %get-tuple-element.31), kind=kLoop, calls=%fused_computation.46 | loop fusion | bytes 36864 | tf_op jit(solution)/shard_map/slice | solution.py:139
  46.5 1.9 %collective-permute-start.9 = (f32[3072]{0:T(1024)S(1)}, f32[3072]{0:T(1024)S(1)}, u32[]{:S(2)}, u32[]{:S(2)}) collective-permute-start(f32[3072]{0:T(1024)S(1)} %pad_maximum_fusion.7), channel_id=1, source_target_pairs={{8,0},{16,8},{24,16},{9,1},{17,9},{25,17},{10,2},{18,10},{26,18},{... | collective-permute-start | bytes 36872 | tf_op jit(solution)/shard_map/ppermute | solution.py:44
  48.5 2.4 %collective-permute-start.8 = (f32[3072]{0:T(1024)S(1)}, f32[3072]{0:T(1024)S(1)}, u32[]{:S(2)}, u32[]{:S(2)}) collective-permute-start(f32[3072]{0:T(1024)S(1)} %pad_maximum_fusion.6), channel_id=1, source_target_pairs={{0,8},{8,16},{16,24},{1,9},{9,17},{17,25},{2,10},{10,18},{18,26},{... | collective-permute-start | bytes 36872 | tf_op jit(solution)/shard_map/ppermute | solution.py:44
  50.9 2.6 %collective-permute-done.8 = f32[3072]{0:T(1024)S(1)} collective-permute-done((f32[3072]{0:T(1024)S(1)}, f32[3072]{0:T(1024)S(1)}, u32[]{:S(2)}, u32[]{:S(2)}) %collective-permute-start.8) | collective-permute-done | bytes 12320 | tf_op jit(solution)/shard_map/ppermute | solution.py:44
  54.5 0.9 %maximum_reduce_fusion = (f32[6,8]{1,0:T(8,128)S(1)}, f32[6,8]{1,0:T(8,128)S(1)}) fusion(f32[6,1,384]{2,1,0:T(1,128)S(1)} %slice.211, f32[6,6,384]{2,1,0:T(8,128)} %get-tuple-element.31, f32[6,1,384]{2,1,0:T(1,128)S(1)} %slice.207), kind=kLoop, calls=%fused_computation.26 | loop fusion | flops 192 | bytes 74112 | tf_op jit(solution)/shard_map/slice | solution.py:142
  55.5 3.3 %collective-permute-start.11 = (f32[72]{0:T(128)S(1)}, f32[72]{0:T(128)S(1)}, u32[]{:S(2)}, u32[]{:S(2)}) collective-permute-start(f32[72]{0:T(128)S(1)} %pad_maximum_fusion.10), channel_id=1, source_target_pairs={{1,0},{2,1},{3,2},{4,3},{5,4},{6,5},{7,6},{9,8},{10,9},{11,10},{12... | collective-permute-start | bytes 872 | tf_op jit(solution)/shard_map/ppermute | solution.py:44
  59.1 2.5 %collective-permute-start.10 = (f32[72]{0:T(128)S(1)}, f32[72]{0:T(128)S(1)}, u32[]{:S(2)}, u32[]{:S(2)}) collective-permute-start(f32[72]{0:T(128)S(1)} %pad_maximum_fusion.9), channel_id=1, source_target_pairs={{0,1},{1,2},{2,3},{3,4},{4,5},{5,6},{6,7},{8,9},{9,10},{10,11},{11... | collective-permute-start | bytes 872 | tf_op jit(solution)/shard_map/ppermute | solution.py:44
  61.8 3.6 %collective-permute-done.10 = f32[72]{0:T(128)S(1)} collective-permute-done((f32[72]{0:T(128)S(1)}, f32[72]{0:T(128)S(1)}, u32[]{:S(2)}, u32[]{:S(2)}) %collective-permute-start.10) | collective-permute-done | bytes 320 | tf_op jit(solution)/shard_map/ppermute | solution.py:44
  65.6 0.8 %pad_maximum_fusion.5 = f32[6,4,130]{2,1,0:T(4,128)S(1)} fusion(f32[6,4,1]{2,1,0:T(4,128)S(1)} %reshape.181, f32[6,1,128]{2,1,0:T(1,128)S(1)} %slice.216, f32[6,2,128]{2,1,0:T(2,128)} %get-tuple-element.32, f32[6,1,128]{2,1,0:T(1,128)S(1)} %slice.214, f32[6,4,1]{2,1,0:T(4,128)S(1)} %reshape.180), kind=kLoop, calls=%fused_computation.27 | loop fusion | flops 12480 | bytes 24960 | tf_op jit(solution)/shard_map/concatenate | solution.py:144
  67.3 1.2 %reshape.165 = f32[6,6,384]{2,1,0:T(8,128)S(1)} reshape(f32[6,6,128,3]{3,2,1,0:T(8,128)S(1)} %copy.30) | data formatting | bytes 110592 | tf_op jit(solution)/shard_map/reshape | solution.py:161
  (83 shorter events, 13.5 us)
Async XLA Ops:
  2.9 15.2 %collective-permute-start = (f32[264,128]{1,0:T(8,128)}, f32[264,128]{1,0:T(8,128)S(1)}, u32[]{:S(2)}, u32[]{:S(2)}) collective-permute-start(f32[264,128]{1,0:T(8,128)} %get-tuple-element.20), channel_id=1, source_target_pairs={{0,8},{8,16},{16,24},{1,9},{9,17},{17,25},{2,10},{10,18},{18,26},{... | collective-permute-start | bytes 405512 | tf_op jit(solution)/shard_map/ppermute | solution.py:44
  4.8 13.2 %collective-permute-start.1 = (f32[264,128]{1,0:T(8,128)}, f32[264,128]{1,0:T(8,128)S(1)}, u32[]{:S(2)}, u32[]{:S(2)}) collective-permute-start(f32[264,128]{1,0:T(8,128)} %get-tuple-element.21), channel_id=1, source_target_pairs={{8,0},{16,8},{24,16},{9,1},{17,9},{25,17},{10,2},{18,10},{26,18},{... | collective-permute-start | bytes 405512 | tf_op jit(solution)/shard_map/ppermute | solution.py:44
  8.4 7.1 %collective-permute-start.2 = (f32[88,128]{1,0:T(8,128)}, f32[88,128]{1,0:T(8,128)S(1)}, u32[]{:S(2)}, u32[]{:S(2)}) collective-permute-start(f32[88,128]{1,0:T(8,128)} %get-tuple-element.22), channel_id=1, source_target_pairs={{0,1},{1,2},{2,3},{3,4},{4,5},{5,6},{6,7},{8,9},{9,10},{10,11},{11... | collective-permute-start | bytes 135176 | tf_op jit(solution)/shard_map/ppermute | solution.py:44
  11.9 6.2 %collective-permute-start.3 = (f32[88,128]{1,0:T(8,128)}, f32[88,128]{1,0:T(8,128)S(1)}, u32[]{:S(2)}, u32[]{:S(2)}) collective-permute-start(f32[88,128]{1,0:T(8,128)} %get-tuple-element.23), channel_id=1, source_target_pairs={{1,0},{2,1},{3,2},{4,3},{5,4},{6,5},{7,6},{9,8},{10,9},{11,10},{12... | collective-permute-start | bytes 135176 | tf_op jit(solution)/shard_map/ppermute | solution.py:44
  15.5 2.5 %copy-start.6 = (f32[88,128]{1,0:T(8,128)}, f32[88,128]{1,0:T(8,128)S(1)}, u32[]{:S(2)}) copy-start(f32[88,128]{1,0:T(8,128)S(1)} %collective-permute-done.2.hy_lo) | copy-start | bytes 135172
  18.0 0.6 copy-start.7
  18.0 0.7 copy-start.1
  18.7 0.7 copy-start.2
  23.1 16.1 %collective-permute-start.4 = (f32[264,128]{1,0:T(8,128)}, f32[264,128]{1,0:T(8,128)S(1)}, u32[]{:S(2)}, u32[]{:S(2)}) collective-permute-start(f32[264,128]{1,0:T(8,128)} %get-tuple-element.26), channel_id=1, source_target_pairs={{0,8},{8,16},{16,24},{1,9},{9,17},{17,25},{2,10},{10,18},{18,26},{... | collective-permute-start | bytes 405512 | tf_op jit(solution)/shard_map/ppermute | solution.py:44
  25.0 14.1 %collective-permute-start.5 = (f32[264,128]{1,0:T(8,128)}, f32[264,128]{1,0:T(8,128)S(1)}, u32[]{:S(2)}, u32[]{:S(2)}) collective-permute-start(f32[264,128]{1,0:T(8,128)} %get-tuple-element.27), channel_id=1, source_target_pairs={{8,0},{16,8},{24,16},{9,1},{17,9},{25,17},{10,2},{18,10},{26,18},{... | collective-permute-start | bytes 405512 | tf_op jit(solution)/shard_map/ppermute | solution.py:44
  28.6 7.0 %collective-permute-start.6 = (f32[88,128]{1,0:T(8,128)}, f32[88,128]{1,0:T(8,128)S(1)}, u32[]{:S(2)}, u32[]{:S(2)}) collective-permute-start(f32[88,128]{1,0:T(8,128)} %get-tuple-element.28), channel_id=1, source_target_pairs={{0,1},{1,2},{2,3},{3,4},{4,5},{5,6},{6,7},{8,9},{9,10},{10,11},{11... | collective-permute-start | bytes 135176 | tf_op jit(solution)/shard_map/ppermute | solution.py:44
  33.0 6.2 %collective-permute-start.7 = (f32[88,128]{1,0:T(8,128)}, f32[88,128]{1,0:T(8,128)S(1)}, u32[]{:S(2)}, u32[]{:S(2)}) collective-permute-start(f32[88,128]{1,0:T(8,128)} %get-tuple-element.29), channel_id=1, source_target_pairs={{1,0},{2,1},{3,2},{4,3},{5,4},{6,5},{7,6},{9,8},{10,9},{11,10},{12... | collective-permute-start | bytes 135176 | tf_op jit(solution)/shard_map/ppermute | solution.py:44
  35.7 3.5 %copy-start.8 = (f32[88,128]{1,0:T(8,128)}, f32[88,128]{1,0:T(8,128)S(1)}, u32[]{:S(2)}) copy-start(f32[88,128]{1,0:T(8,128)S(1)} %collective-permute-done.6.hy_lo) | copy-start | bytes 135172
  39.1 0.6 copy-start.9
  39.1 0.7 copy-start.3
  39.1 0.7 copy-start.4
  46.5 4.4 %collective-permute-start.9 = (f32[3072]{0:T(1024)S(1)}, f32[3072]{0:T(1024)S(1)}, u32[]{:S(2)}, u32[]{:S(2)}) collective-permute-start(f32[3072]{0:T(1024)S(1)} %pad_maximum_fusion.7), channel_id=1, source_target_pairs={{8,0},{16,8},{24,16},{9,1},{17,9},{25,17},{10,2},{18,10},{26,18},{... | collective-permute-start | bytes 36872 | tf_op jit(solution)/shard_map/ppermute | solution.py:44
  48.5 5.0 %collective-permute-start.8 = (f32[3072]{0:T(1024)S(1)}, f32[3072]{0:T(1024)S(1)}, u32[]{:S(2)}, u32[]{:S(2)}) collective-permute-start(f32[3072]{0:T(1024)S(1)} %pad_maximum_fusion.6), channel_id=1, source_target_pairs={{0,8},{8,16},{16,24},{1,9},{9,17},{17,25},{2,10},{10,18},{18,26},{... | collective-permute-start | bytes 36872 | tf_op jit(solution)/shard_map/ppermute | solution.py:44
  55.5 6.1 %collective-permute-start.11 = (f32[72]{0:T(128)S(1)}, f32[72]{0:T(128)S(1)}, u32[]{:S(2)}, u32[]{:S(2)}) collective-permute-start(f32[72]{0:T(128)S(1)} %pad_maximum_fusion.10), channel_id=1, source_target_pairs={{1,0},{2,1},{3,2},{4,3},{5,4},{6,5},{7,6},{9,8},{10,9},{11,10},{12... | collective-permute-start | bytes 872 | tf_op jit(solution)/shard_map/ppermute | solution.py:44
  59.1 6.4 %collective-permute-start.10 = (f32[72]{0:T(128)S(1)}, f32[72]{0:T(128)S(1)}, u32[]{:S(2)}, u32[]{:S(2)}) collective-permute-start(f32[72]{0:T(128)S(1)} %pad_maximum_fusion.9), channel_id=1, source_target_pairs={{0,1},{1,2},{2,3},{3,4},{4,5},{5,6},{6,7},{8,9},{9,10},{10,11},{11... | collective-permute-start | bytes 872 | tf_op jit(solution)/shard_map/ppermute | solution.py:44
  67.3 1.2 %copy-start = (f32[6,6,384]{2,1,0:T(8,128)S(1)}, f32[6,6,384]{2,1,0:T(8,128)}, u32[]{:S(2)}) copy-start(f32[6,6,384]{2,1,0:T(8,128)} %get-tuple-element.31) | copy-start | bytes 165892
  73.9 1.2 %copy-start.5 = (f32[6,2,128]{2,1,0:T(2,128)S(1)}, f32[6,2,128]{2,1,0:T(2,128)}, u32[]{:S(2)}) copy-start(f32[6,2,128]{2,1,0:T(2,128)} %get-tuple-element.32) | copy-start | bytes 18436

commit v4 on v3

--- a/solution.py
+++ b/solution.py
@@ -263,7 +263,13 @@
 def plan_blocks(fine_shape, coarse_shape):
     fine = Block(fine_shape, 1.0, True, 0, 0)
     coarse = Block(coarse_shape, 3.0, False, fine.x_rows, fine.y_rows)
+    fine.fx_base, fine.fy_base = 0, 0
+    coarse.fx_base, coarse.fy_base = 6 * fine.chunks, fine.size
     return fine, coarse, fine.x_rows + coarse.x_rows, fine.y_rows + coarse.y_rows
+
+
+def round8(n):
+    return -(-n // 8) * 8
 
 
 def write_rims(b, src, fields, x_prev, x_next, y_prev, y_next):
@@ -384,7 +390,7 @@
 
 
 def stress_block(b, depth, w, mem, vel, mat, mech, metric, mtab, atab, out, mem_out, face, sx,
-                 hx_lo, hx_hi, hy_lo, hy_hi):
+                 hx_lo, hx_hi, hy_lo, hy_hi, face_rims):
     for slot in range(3):
         fill_x2(b, sx, slot, vel, slot, hx_lo, hx_hi)
     for z in range(b.layers):
@@ -423,16 +429,37 @@
         if z == depth:
             for i, k in enumerate((0, 1, 2, 7, 8, 5)):
                 face[i] = values[k]
+            write_face_rims(b, [values[k] for k in (0, 1, 2, 7, 8, 5)], *face_rims)
+
+
+def write_face_rims(b, planes, x_prev, x_next, y_prev, y_next):
+    size, lanes = b.size, b.lanes
+    for i, v in enumerate(planes):
+        for j in range(b.chunks):
+            row = b.fx_base + i * b.chunks + j
+            x_prev[row : row + 1, :] = v[0:1, j * 128 : (j + 1) * 128]
+            x_next[row : row + 1, :] = v[size - 1 : size, j * 128 : (j + 1) * 128]
+    lane = lax.broadcasted_iota(jnp.int32, (size, 128), 1)
+    acc_lo = jnp.zeros((size, 128), jnp.float32)
+    acc_hi = jnp.zeros((size, 128), jnp.float32)
+    for i, v in enumerate(planes):
+        rl = v if i == 0 else pltpu.roll(v, i, 1)
+        rh = pltpu.roll(v, (i + 1) % lanes, 1)
+        acc_lo = jnp.where(lane == i, rl[:, 0:128], acc_lo)
+        acc_hi = jnp.where(lane == i, rh[:, 0:128], acc_hi)
+    y_prev[b.fy_base : b.fy_base + size, :] = acc_lo
+    y_next[b.fy_base : b.fy_base + size, :] = acc_hi
 
 
 def stress_kernel(blocks, fw, fmem, fvel, cw, cmem, cvel, hx_lo, hx_hi, hy_lo, hy_hi,
                   fmat, fmech, fmetric, cmat, cmech, mtab, atab,
-                  fout, fmem_out, fface, cout, cmem_out, cface, sx_f, sx_c):
+                  fout, fmem_out, fface, cout, cmem_out, cface, rx_prev, rx_next, ry_prev, ry_next, sx_f, sx_c):
     fine, coarse = blocks
+    rims = (rx_prev, rx_next, ry_prev, ry_next)
     stress_block(fine, fine.layers - 1, fw, fmem, fvel, fmat, fmech, fmetric, mtab, atab, fout, fmem_out,
-                 fface, sx_f, hx_lo, hx_hi, hy_lo, hy_hi)
+                 fface, sx_f, hx_lo, hx_hi, hy_lo, hy_hi, rims)
     stress_block(coarse, 0, cw, cmem, cvel, cmat, cmech, None, mtab, atab, cout, cmem_out,
-                 cface, sx_c, hx_lo, hx_hi, hy_lo, hy_hi)
+                 cface, sx_c, hx_lo, hx_hi, hy_lo, hy_hi, rims)
 
 
 def vmem_specs(count):
@@ -466,6 +493,162 @@
     out = lax.dynamic_update_slice(out, face[5:6][:, None], (5, depth, 0, 0))
     out = lax.dynamic_update_slice(out, face[3:5][:, None], (7, depth, 0, 0))
     return out
+
+
+def prolong_y_matrix(coarse_lanes):
+    m = np.zeros((coarse_lanes, 3 * coarse_lanes), np.float32)
+    for d in range(coarse_lanes):
+        m[d, 3 * d] = 2.0 / 3.0
+        m[d, 3 * d + 1] = 1.0
+        m[d, 3 * d + 2] = 2.0 / 3.0
+        if d >= 1:
+            m[d - 1, 3 * d] = 1.0 / 3.0
+        if d + 1 < coarse_lanes:
+            m[d + 1, 3 * d + 2] = 1.0 / 3.0
+    return m
+
+
+def restrict_y_matrix(coarse_lanes):
+    m = np.zeros((3 * coarse_lanes, coarse_lanes), np.float32)
+    for c in range(coarse_lanes):
+        for offset, weight in ((-1, 1.0), (0, 2.0), (1, 3.0), (2, 2.0), (3, 1.0)):
+            f = 3 * c + offset
+            if 0 <= f < 3 * coarse_lanes:
+                m[f, c] = weight / 9.0
+    return m
+
+
+def padded_rows(b, face, hx_lo, hx_hi, hy_lo, hy_hi, c_mm, c_pm, c_mp, c_pp, i):
+    size = b.size
+
+    def x_row(buf):
+        parts = [buf[pl.ds(b.fx_base + i * b.chunks + j, 1), :] for j in range(b.chunks)]
+        return parts[0] if len(parts) == 1 else jnp.concatenate(parts, axis=1)
+
+    def lane_of(buf, row):
+        return buf[pl.ds(b.fy_base + row, 1), pl.ds(i, 1)]
+
+    rows = [(x_row(hx_lo), lane_of(c_mm, size - 1), lane_of(c_mp, size - 1))]
+    for x in range(size):
+        rows.append((face[i, pl.ds(x, 1), :], lane_of(hy_lo, x), lane_of(hy_hi, x)))
+    rows.append((x_row(hx_hi), lane_of(c_pm, 0), lane_of(c_pp, 0)))
+    return rows
+
+
+def combine(terms):
+    out = []
+    for part in range(3):
+        total = None
+        for weight, row in terms:
+            v = row[part] if weight == 1.0 else weight * row[part]
+            total = v if total is None else total + v
+        out.append(total)
+    return out
+
+
+def face_kernel(blocks, fine_depth, fout_in, cout_in, fface, cface, hx_lo, hx_hi, hy_lo, hy_hi,
+                c_mm, c_pm, c_mp, c_pp, py, ry, fout, cout, fnew, cnew, stage_p, stage_r, sems):
+    fine, coarse = blocks
+    halos = (hx_lo, hx_hi, hy_lo, hy_hi, c_mm, c_pm, c_mp, c_pp)
+    lane_f = lax.broadcasted_iota(jnp.int32, (1, fine.lanes), 1)
+    p_lo, p_hi = [], []
+    for i in range(6):
+        rows = padded_rows(coarse, cface, *halos, i)
+        for c in range(coarse.size):
+            left, middle, right = rows[c], rows[c + 1], rows[c + 2]
+            parts = [
+                [(1.0, left), (2.0, middle)],
+                [(1.0, middle)],
+                [(2.0, middle), (1.0, right)],
+            ]
+            for a, terms in enumerate(parts):
+                interior, lo, hi = combine(terms)
+                if a != 1:
+                    interior, lo, hi = interior / 3.0, lo / 3.0, hi / 3.0
+                r = i * fine.size + 3 * c + a
+                stage_p[pl.ds(r, 1), :] = interior
+                p_lo.append(lo)
+                p_hi.append(hi)
+    prolonged = jnp.dot(stage_p[...], py[...], precision=lax.Precision.HIGHEST, preferred_element_type=jnp.float32)
+    for i in range(6):
+        for x in range(fine.size):
+            r = i * fine.size + x
+            value = prolonged[r : r + 1, :]
+            value = value + jnp.where(lane_f == 0, p_lo[r] / 3.0, 0.0) + jnp.where(lane_f == fine.lanes - 1, p_hi[r] / 3.0, 0.0)
+            own = fface[i, pl.ds(x, 1), :]
+            fnew[i, 0, pl.ds(x, 1), :] = own - penalty * (own - value)
+    lane_c = lax.broadcasted_iota(jnp.int32, (1, coarse.lanes), 1)
+    r_lo, r_hi = [], []
+    for i in range(6):
+        rows = padded_rows(fine, fface, *halos, i)
+        for c in range(coarse.size):
+            terms = [(1.0, rows[3 * c]), (2.0, rows[3 * c + 1]), (3.0, rows[3 * c + 2]), (2.0, rows[3 * c + 3]),
+                     (1.0, rows[3 * c + 4])]
+            interior, lo, hi = combine(terms)
+            r = i * coarse.size + c
+            stage_r[pl.ds(r, 1), :] = interior / 9.0
+            r_lo.append(lo / 9.0)
+            r_hi.append(hi / 9.0)
+    restricted = jnp.dot(stage_r[...], ry[...], precision=lax.Precision.HIGHEST, preferred_element_type=jnp.float32)
+    for i in range(6):
+        for c in range(coarse.size):
+            r = i * coarse.size + c
+            value = restricted[r : r + 1, :]
+            value = value + jnp.where(lane_c == 0, r_lo[r] / 9.0, 0.0) + jnp.where(lane_c == coarse.lanes - 1, r_hi[r] / 9.0, 0.0)
+            own = cface[i, pl.ds(c, 1), :]
+            cnew[i, 0, pl.ds(c, 1), :] = own - penalty * (own - value)
+    copies = []
+    for n, (src, dst, depth) in enumerate(((fnew, fout, fine_depth), (cnew, cout, 0))):
+        for k, (first, count, field) in enumerate(((0, 3, 0), (5, 1, 5), (3, 2, 7))):
+            copy = pltpu.make_async_copy(
+                src.at[pl.ds(first, count)], dst.at[pl.ds(field, count), pl.ds(depth, 1)], sems.at[3 * n + k]
+            )
+            copy.start()
+            copies.append(copy)
+    for copy in copies:
+        copy.wait()
+
+
+def diag_from(block, dx, dy):
+    nx, ny = lax.axis_size("gx"), lax.axis_size("gy")
+    pairs = []
+    for i in range(nx):
+        for j in range(ny):
+            if 0 <= i + dx < nx and 0 <= j + dy < ny:
+                pairs.append((i * ny + j, (i + dx) * ny + (j + dy)))
+    return lax.ppermute(block, ("gx", "gy"), pairs)
+
+
+def face_call(blocks, fine_out, coarse_out, fine_face, coarse_face, rims):
+    fine, coarse = blocks
+    x_prev, x_next, y_prev, y_next = rims
+    received = (
+        shift_from(x_next, "gx", 1),
+        shift_from(x_prev, "gx", -1),
+        shift_from(y_next, "gy", 1),
+        shift_from(y_prev, "gy", -1),
+        diag_from(y_next, 1, 1),
+        diag_from(y_next, -1, 1),
+        diag_from(y_prev, 1, -1),
+        diag_from(y_prev, -1, -1),
+    )
+    py = jnp.asarray(prolong_y_matrix(coarse.lanes))
+    ry = jnp.asarray(restrict_y_matrix(coarse.lanes))
+    anyspace = pl.BlockSpec(memory_space=pl.ANY)
+    return pl.pallas_call(
+        functools.partial(face_kernel, blocks, fine.layers - 1),
+        out_shape=(f32(fine_out.shape), f32(coarse_out.shape)),
+        in_specs=[anyspace, anyspace] + vmem_specs(12),
+        out_specs=(anyspace, anyspace),
+        input_output_aliases={0: 0, 1: 1},
+        scratch_shapes=[
+            pltpu.VMEM((6, 1, fine.size, fine.lanes), jnp.float32),
+            pltpu.VMEM((6, 1, coarse.size, coarse.lanes), jnp.float32),
+            pltpu.VMEM((round8(6 * fine.size), coarse.lanes), jnp.float32),
+            pltpu.VMEM((round8(6 * coarse.size), fine.lanes), jnp.float32),
+            pltpu.SemaphoreType.DMA((6,)),
+        ],
+    )(fine_out, coarse_out, fine_face, coarse_face, *received, py, ry)
 
 
 def local(
@@ -502,24 +685,24 @@
     )(fine_wave, coarse_wave, *halos, fine_material, fine_metric, coarse_material, material_table)
 
     vhalos = receive(vrims)
-    fine_out, fine_mem, fine_face, coarse_out, coarse_mem, coarse_face = pl.pallas_call(
+    fx_rows = 6 * (fine.chunks + coarse.chunks)
+    fy_rows = round8(fine.size + coarse.size)
+    fine_out, fine_mem, fine_face, coarse_out, coarse_mem, coarse_face, *face_rims = pl.pallas_call(
         functools.partial(stress_kernel, blocks),
         out_shape=(
             f32(fine_wave.shape), f32(fine_memory.shape), f32((6,) + fine_wave.shape[2:]),
             f32(coarse_wave.shape), f32(coarse_memory.shape), f32((6,) + coarse_wave.shape[2:]),
+            f32((fx_rows, 128)), f32((fx_rows, 128)), f32((fy_rows, 128)), f32((fy_rows, 128)),
         ),
         in_specs=vmem_specs(15) + [smem, smem],
-        out_specs=tuple(vmem_specs(6)),
+        out_specs=tuple(vmem_specs(10)),
         scratch_shapes=[scratch_for(fine), scratch_for(coarse)],
     )(fine_wave, fine_memory, fine_velocity, coarse_wave, coarse_memory, coarse_velocity, *vhalos,
       fine_material, fine_mechanism, fine_metric, coarse_material, coarse_mechanism, material_table,
       attenuation_table)
 
-    depth = fine_wave.shape[1] - 1
-    fine_padded, coarse_padded = pad_faces([fine_face, coarse_face])
-    fine_new = fine_face - penalty * (fine_face - prolong_axis(prolong_axis(coarse_padded, 1), 2))
-    coarse_new = coarse_face - penalty * (coarse_face - restrict_axis(restrict_axis(fine_padded, 1), 2))
-    return (put_face(fine_out, fine_new, depth), fine_mem, put_face(coarse_out, coarse_new, 0), coarse_mem)
+    fine_out, coarse_out = face_call(blocks, fine_out, coarse_out, fine_face, coarse_face, face_rims)
+    return (fine_out, fine_mem, coarse_out, coarse_mem)
 
 
 def solution(mesh):

time: 77.5 us -> 76.4 us (0.986)
  the two profiles are of different devices: /device:TPU:10 before, /device:TPU:13 now
where the time goes in v4:
time: 76.4 us; the launch traced here: 75.8 us
  starting transfers between devices  49.2 us (64%)
  Pallas kernels  13.1 us (17%)
  waiting for transfers between devices  9.89 us (13%)
  local copies, waits for them, and re-layouts  2.59 us (3%)
  between operations  0.97 us (1%)
    ppermute x12, starting transfers between devices, shift_from(): return lax.ppermute(block, axis, pairs)  34.4 us
    ppermute x4, starting transfers between devices, diag_from(): return lax.ppermute(block, ('gx', 'gy'), pairs)  14.8 us
    ppermute x12, waiting for transfers between devices, shift_from(): return lax.ppermute(block, axis, pairs)  9.88 us
    pallas_call x1, Pallas kernels, local(): pl.pallas_call(functools.partial(stress_kernel, blocks), out_shape=(f32(f...  5.03 us
    pallas_call x1, Pallas kernels, local(): pl.pallas_call(functools.partial(velocity_kernel, blocks), out_shape=(f32...  3.7 us
    unnamed x32, local copies, waits for them, and re-layouts  2.59 us
    pallas_call x1, Pallas kernels, local(): pl.pallas_call(functools.partial(pack_kernel, blocks), out_shape=halo_sha...  2.25 us
    pallas_call x1, Pallas kernels, face_call(): pl.pallas_call(functools.partial(face_kernel, blocks, fine.layers - 1), o...  2.17 us
  transfers between devices with their start and end apart: 16, of which 3 were waited for; matrix products, arithmetic and copies ran while one was open for 0% of the time, Pallas kernels for 0%

profile of v4, /device:TPU:13, one launch (start us, length us, event | category | flops | bytes accessed | tf_op | source)
XLA Modules:
  0.0 75.8 jit_solution(1653512362456913323)
XLA Ops:
  0.6 2.2 %shard_map.156 = (f32[264,128]{1,0:T(8,128)}, f32[264,128]{1,0:T(8,128)}, f32[88,128]{1,0:T(8,128)}, f32[88,128]{1,0:T(8,128)}) custom-call(f32[9,12,6,384]{3,2,1,0:T(8,128)} %fw.5, f32[9,8,2,128]{3,2,1,0:T(2,128)} %cw.5), custom_call_target="tpu_custom_call" | custom-call | tf_op jit(solution)/shard_map/pallas_call | solution.py:671
  2.9 3.7 %collective-permute-start = (f32[264,128]{1,0:T(8,128)}, f32[264,128]{1,0:T(8,128)S(1)}, u32[]{:S(2)}, u32[]{:S(2)}) collective-permute-start(f32[264,128]{1,0:T(8,128)} %get-tuple-element.26), channel_id=1, source_target_pairs={{0,8},{8,16},{16,24},{1,9},{9,17},{17,25},{2,10},{10,18},{18,26},{... | collective-permute-start | bytes 405512 | tf_op jit(solution)/shard_map/ppermute | solution.py:44
  6.6 1.9 %collective-permute-start.1 = (f32[264,128]{1,0:T(8,128)}, f32[264,128]{1,0:T(8,128)S(1)}, u32[]{:S(2)}, u32[]{:S(2)}) collective-permute-start(f32[264,128]{1,0:T(8,128)} %get-tuple-element.27), channel_id=1, source_target_pairs={{8,0},{16,8},{24,16},{9,1},{17,9},{25,17},{10,2},{18,10},{26,18},{... | collective-permute-start | bytes 405512 | tf_op jit(solution)/shard_map/ppermute | solution.py:44
  8.5 3.1 %collective-permute-start.2 = (f32[88,128]{1,0:T(8,128)}, f32[88,128]{1,0:T(8,128)S(1)}, u32[]{:S(2)}, u32[]{:S(2)}) collective-permute-start(f32[88,128]{1,0:T(8,128)} %get-tuple-element.28), channel_id=1, source_target_pairs={{0,1},{1,2},{2,3},{3,4},{4,5},{5,6},{6,7},{8,9},{9,10},{10,11},{11... | collective-permute-start | bytes 135176 | tf_op jit(solution)/shard_map/ppermute | solution.py:44
  11.6 2.1 %collective-permute-start.3 = (f32[88,128]{1,0:T(8,128)}, f32[88,128]{1,0:T(8,128)S(1)}, u32[]{:S(2)}, u32[]{:S(2)}) collective-permute-start(f32[88,128]{1,0:T(8,128)} %get-tuple-element.29), channel_id=1, source_target_pairs={{1,0},{2,1},{3,2},{4,3},{5,4},{6,5},{7,6},{9,8},{10,9},{11,10},{12... | collective-permute-start | bytes 135176 | tf_op jit(solution)/shard_map/ppermute | solution.py:44
  13.8 3.7 %collective-permute-done.3.hy_hi = f32[88,128]{1,0:T(8,128)S(1)} collective-permute-done((f32[88,128]{1,0:T(8,128)}, f32[88,128]{1,0:T(8,128)S(1)}, u32[]{:S(2)}, u32[]{:S(2)}) %collective-permute-start.3) | collective-permute-done | bytes 45088 | tf_op jit(solution)/shard_map/ppermute | solution.py:44
  18.2 0.7 copy-done.1
  18.9 3.7 %shard_map.157 = (f32[3,12,6,384]{3,2,1,0:T(8,128)}, f32[3,8,2,128]{3,2,1,0:T(2,128)}, f32[264,128]{1,0:T(8,128)}, f32[264,128]{1,0:T(8,128)}, f32[88,128]{1,0:T(8,128)}, /*index=5*/f32[88,128]{1,0:T(8,128)}) custom-call(f32[9,12,6,384]{3,2,1,0:T(8,128)} %fw.5, f32[9,8,2,128]{3,2,1,0:T(2,128)} %cw.5, f32[264,128]{1,0:T(8,128)} %copy-done, ...), custom_call_target="tpu_custom_call" | custom-call | tf_op jit(solution)/shard_map/pallas_call | solution.py:679
  22.6 5.1 %collective-permute-start.4 = (f32[264,128]{1,0:T(8,128)}, f32[264,128]{1,0:T(8,128)S(1)}, u32[]{:S(2)}, u32[]{:S(2)}) collective-permute-start(f32[264,128]{1,0:T(8,128)} %get-tuple-element.32), channel_id=1, source_target_pairs={{0,8},{8,16},{16,24},{1,9},{9,17},{17,25},{2,10},{10,18},{18,26},{... | collective-permute-start | bytes 405512 | tf_op jit(solution)/shard_map/ppermute | solution.py:44
  27.6 1.9 %collective-permute-start.5 = (f32[264,128]{1,0:T(8,128)}, f32[264,128]{1,0:T(8,128)S(1)}, u32[]{:S(2)}, u32[]{:S(2)}) collective-permute-start(f32[264,128]{1,0:T(8,128)} %get-tuple-element.33), channel_id=1, source_target_pairs={{8,0},{16,8},{24,16},{9,1},{17,9},{25,17},{10,2},{18,10},{26,18},{... | collective-permute-start | bytes 405512 | tf_op jit(solution)/shard_map/ppermute | solution.py:44
  29.6 2.2 %collective-permute-start.6 = (f32[88,128]{1,0:T(8,128)}, f32[88,128]{1,0:T(8,128)S(1)}, u32[]{:S(2)}, u32[]{:S(2)}) collective-permute-start(f32[88,128]{1,0:T(8,128)} %get-tuple-element.34), channel_id=1, source_target_pairs={{0,1},{1,2},{2,3},{3,4},{4,5},{5,6},{6,7},{8,9},{9,10},{10,11},{11... | collective-permute-start | bytes 135176 | tf_op jit(solution)/shard_map/ppermute | solution.py:44
  31.8 3.0 %collective-permute-start.7 = (f32[88,128]{1,0:T(8,128)}, f32[88,128]{1,0:T(8,128)S(1)}, u32[]{:S(2)}, u32[]{:S(2)}) collective-permute-start(f32[88,128]{1,0:T(8,128)} %get-tuple-element.35), channel_id=1, source_target_pairs={{1,0},{2,1},{3,2},{4,3},{5,4},{6,5},{7,6},{9,8},{10,9},{11,10},{12... | collective-permute-start | bytes 135176 | tf_op jit(solution)/shard_map/ppermute | solution.py:44
  34.9 2.8 %collective-permute-done.7.hy_hi = f32[88,128]{1,0:T(8,128)S(1)} collective-permute-done((f32[88,128]{1,0:T(8,128)}, f32[88,128]{1,0:T(8,128)S(1)}, u32[]{:S(2)}, u32[]{:S(2)}) %collective-permute-start.7) | collective-permute-done | bytes 45088 | tf_op jit(solution)/shard_map/ppermute | solution.py:44
  38.5 5.0 %shard_map.158 = (f32[9,12,6,384]{3,2,1,0:T(8,128)}, f32[6,12,6,384]{3,2,1,0:T(8,128)}, f32[6,6,384]{2,1,0:T(8,128)}, f32[9,8,2,128]{3,2,1,0:T(2,128)}, f32[6,8,...) custom-call(f32[9,12,6,384]{3,2,1,0:T(8,128)} %fw.5, ...), custom_call_target="tpu_custom_call" | custom-call | tf_op jit(solution)/shard_map/pallas_call | solution.py:690
  43.5 5.1 %collective-permute-start.8 = (f32[24,128]{1,0:T(8,128)}, f32[24,128]{1,0:T(8,128)S(1)}, u32[]{:S(2)}, u32[]{:S(2)}) collective-permute-start(f32[24,128]{1,0:T(8,128)} %get-tuple-element.40), channel_id=1, source_target_pairs={{0,8},{8,16},{16,24},{1,9},{9,17},{17,25},{2,10},{10,18},{18,26},{... | collective-permute-start | bytes 36872 | tf_op jit(solution)/shard_map/ppermute | solution.py:44
  48.6 1.9 %collective-permute-start.9 = (f32[24,128]{1,0:T(8,128)}, f32[24,128]{1,0:T(8,128)S(1)}, u32[]{:S(2)}, u32[]{:S(2)}) collective-permute-start(f32[24,128]{1,0:T(8,128)} %get-tuple-element.41), channel_id=1, source_target_pairs={{8,0},{16,8},{24,16},{9,1},{17,9},{25,17},{10,2},{18,10},{26,18},{... | collective-permute-start | bytes 36872 | tf_op jit(solution)/shard_map/ppermute | solution.py:44
  50.5 1.9 %collective-permute-start.13 = (f32[8,128]{1,0:T(8,128)}, f32[8,128]{1,0:T(8,128)S(1)}, u32[]{:S(2)}, u32[]{:S(2)}) collective-permute-start(f32[8,128]{1,0:T(8,128)} %get-tuple-element.42), channel_id=1, source_target_pairs={{8,1},{9,2},{10,3},{11,4},{12,5},{13,6},{14,7},{16,9},{17,10},{18,... | collective-permute-start | bytes 12296 | tf_op jit(solution)/shard_map/ppermute | solution.py:619
  52.4 5.6 %collective-permute-start.12 = (f32[8,128]{1,0:T(8,128)}, f32[8,128]{1,0:T(8,128)S(1)}, u32[]{:S(2)}, u32[]{:S(2)}) collective-permute-start(f32[8,128]{1,0:T(8,128)} %get-tuple-element.42), channel_id=1, source_target_pairs={{0,9},{1,10},{2,11},{3,12},{4,13},{5,14},{6,15},{8,17},{9,18},{10,... | collective-permute-start | bytes 12296 | tf_op jit(solution)/shard_map/ppermute | solution.py:619
  58.0 2.2 %collective-permute-start.10 = (f32[8,128]{1,0:T(8,128)}, f32[8,128]{1,0:T(8,128)S(1)}, u32[]{:S(2)}, u32[]{:S(2)}) collective-permute-start(f32[8,128]{1,0:T(8,128)} %get-tuple-element.42), channel_id=1, source_target_pairs={{0,1},{1,2},{2,3},{3,4},{4,5},{5,6},{6,7},{8,9},{9,10},{10,11},{11... | collective-permute-start | bytes 12296 | tf_op jit(solution)/shard_map/ppermute | solution.py:44
  60.2 1.9 %collective-permute-start.15 = (f32[8,128]{1,0:T(8,128)}, f32[8,128]{1,0:T(8,128)S(1)}, u32[]{:S(2)}, u32[]{:S(2)}) collective-permute-start(f32[8,128]{1,0:T(8,128)} %get-tuple-element.43), channel_id=1, source_target_pairs={{9,0},{10,1},{11,2},{12,3},{13,4},{14,5},{15,6},{17,8},{18,9},{19,... | collective-permute-start | bytes 12296 | tf_op jit(solution)/shard_map/ppermute | solution.py:619
  62.2 5.4 %collective-permute-start.14 = (f32[8,128]{1,0:T(8,128)}, f32[8,128]{1,0:T(8,128)S(1)}, u32[]{:S(2)}, u32[]{:S(2)}) collective-permute-start(f32[8,128]{1,0:T(8,128)} %get-tuple-element.43), channel_id=1, source_target_pairs={{1,8},{2,9},{3,10},{4,11},{5,12},{6,13},{7,14},{9,16},{10,17},{11,... | collective-permute-start | bytes 12296 | tf_op jit(solution)/shard_map/ppermute | solution.py:619
  67.6 2.1 %collective-permute-start.11 = (f32[8,128]{1,0:T(8,128)}, f32[8,128]{1,0:T(8,128)S(1)}, u32[]{:S(2)}, u32[]{:S(2)}) collective-permute-start(f32[8,128]{1,0:T(8,128)} %get-tuple-element.43), channel_id=1, source_target_pairs={{1,0},{2,1},{3,2},{4,3},{5,4},{6,5},{7,6},{9,8},{10,9},{11,10},{12... | collective-permute-start | bytes 12296 | tf_op jit(solution)/shard_map/ppermute | solution.py:44
  69.8 3.3 %collective-permute-done.11.hy_hi = f32[8,128]{1,0:T(8,128)S(1)} collective-permute-done((f32[8,128]{1,0:T(8,128)}, f32[8,128]{1,0:T(8,128)S(1)}, u32[]{:S(2)}, u32[]{:S(2)}) %collective-permute-start.11) | collective-permute-done | bytes 4128 | tf_op jit(solution)/shard_map/ppermute | solution.py:44
  73.6 2.2 %shard_map.159 = (f32[9,12,6,384]{3,2,1,0:T(8,128)}, f32[9,8,2,128]{3,2,1,0:T(2,128)}) custom-call(f32[9,12,6,384]{3,2,1,0:T(8,128)} %get-tuple-element.36.fout_in, f32[9,8,2,128]{3,2,1,0:T(2,128)} %get-tuple-element.37.cout_in, f32[6,6,384]{2,1,0:T(8,128)} %get-tuple-element.38.fface, ...), custom_call_target="tpu_custom_call", output_to_operand_aliasing={{0}: (0, {}), {1}: (1, {})} | custom-call | tf_op jit(solution)/shard_map/pallas_call | solution.py:638
  (44 shorter events, 2.0 us)
Async XLA Ops:
  2.9 14.7 %collective-permute-start = (f32[264,128]{1,0:T(8,128)}, f32[264,128]{1,0:T(8,128)S(1)}, u32[]{:S(2)}, u32[]{:S(2)}) collective-permute-start(f32[264,128]{1,0:T(8,128)} %get-tuple-element.26), channel_id=1, source_target_pairs={{0,8},{8,16},{16,24},{1,9},{9,17},{17,25},{2,10},{10,18},{18,26},{... | collective-permute-start | bytes 405512 | tf_op jit(solution)/shard_map/ppermute | solution.py:44
  6.6 11.0 %collective-permute-start.1 = (f32[264,128]{1,0:T(8,128)}, f32[264,128]{1,0:T(8,128)S(1)}, u32[]{:S(2)}, u32[]{:S(2)}) collective-permute-start(f32[264,128]{1,0:T(8,128)} %get-tuple-element.27), channel_id=1, source_target_pairs={{8,0},{16,8},{24,16},{9,1},{17,9},{25,17},{10,2},{18,10},{26,18},{... | collective-permute-start | bytes 405512 | tf_op jit(solution)/shard_map/ppermute | solution.py:44
  8.5 5.3 %collective-permute-start.2 = (f32[88,128]{1,0:T(8,128)}, f32[88,128]{1,0:T(8,128)S(1)}, u32[]{:S(2)}, u32[]{:S(2)}) collective-permute-start(f32[88,128]{1,0:T(8,128)} %get-tuple-element.28), channel_id=1, source_target_pairs={{0,1},{1,2},{2,3},{3,4},{4,5},{5,6},{6,7},{8,9},{9,10},{10,11},{11... | collective-permute-start | bytes 135176 | tf_op jit(solution)/shard_map/ppermute | solution.py:44
  11.6 5.9 %collective-permute-start.3 = (f32[88,128]{1,0:T(8,128)}, f32[88,128]{1,0:T(8,128)S(1)}, u32[]{:S(2)}, u32[]{:S(2)}) collective-permute-start(f32[88,128]{1,0:T(8,128)} %get-tuple-element.29), channel_id=1, source_target_pairs={{1,0},{2,1},{3,2},{4,3},{5,4},{6,5},{7,6},{9,8},{10,9},{11,10},{12... | collective-permute-start | bytes 135176 | tf_op jit(solution)/shard_map/ppermute | solution.py:44
  13.8 3.8 %copy-start.4 = (f32[88,128]{1,0:T(8,128)}, f32[88,128]{1,0:T(8,128)S(1)}, u32[]{:S(2)}) copy-start(f32[88,128]{1,0:T(8,128)S(1)} %collective-permute-done.2.hy_lo) | copy-start | bytes 135172
  22.6 15.2 %collective-permute-start.4 = (f32[264,128]{1,0:T(8,128)}, f32[264,128]{1,0:T(8,128)S(1)}, u32[]{:S(2)}, u32[]{:S(2)}) collective-permute-start(f32[264,128]{1,0:T(8,128)} %get-tuple-element.32), channel_id=1, source_target_pairs={{0,8},{8,16},{16,24},{1,9},{9,17},{17,25},{2,10},{10,18},{18,26},{... | collective-permute-start | bytes 405512 | tf_op jit(solution)/shard_map/ppermute | solution.py:44
  27.6 10.1 %collective-permute-start.5 = (f32[264,128]{1,0:T(8,128)}, f32[264,128]{1,0:T(8,128)S(1)}, u32[]{:S(2)}, u32[]{:S(2)}) collective-permute-start(f32[264,128]{1,0:T(8,128)} %get-tuple-element.33), channel_id=1, source_target_pairs={{8,0},{16,8},{24,16},{9,1},{17,9},{25,17},{10,2},{18,10},{26,18},{... | collective-permute-start | bytes 405512 | tf_op jit(solution)/shard_map/ppermute | solution.py:44
  29.6 5.3 %collective-permute-start.6 = (f32[88,128]{1,0:T(8,128)}, f32[88,128]{1,0:T(8,128)S(1)}, u32[]{:S(2)}, u32[]{:S(2)}) collective-permute-start(f32[88,128]{1,0:T(8,128)} %get-tuple-element.34), channel_id=1, source_target_pairs={{0,1},{1,2},{2,3},{3,4},{4,5},{5,6},{6,7},{8,9},{9,10},{10,11},{11... | collective-permute-start | bytes 135176 | tf_op jit(solution)/shard_map/ppermute | solution.py:44
  31.8 5.9 %collective-permute-start.7 = (f32[88,128]{1,0:T(8,128)}, f32[88,128]{1,0:T(8,128)S(1)}, u32[]{:S(2)}, u32[]{:S(2)}) collective-permute-start(f32[88,128]{1,0:T(8,128)} %get-tuple-element.35), channel_id=1, source_target_pairs={{1,0},{2,1},{3,2},{4,3},{5,4},{6,5},{7,6},{9,8},{10,9},{11,10},{12... | collective-permute-start | bytes 135176 | tf_op jit(solution)/shard_map/ppermute | solution.py:44
  34.9 2.9 %copy-start.6 = (f32[88,128]{1,0:T(8,128)}, f32[88,128]{1,0:T(8,128)S(1)}, u32[]{:S(2)}) copy-start(f32[88,128]{1,0:T(8,128)S(1)} %collective-permute-done.6.hy_lo) | copy-start | bytes 135172
  37.7 0.7 copy-start.3
  43.5 29.5 %collective-permute-start.8 = (f32[24,128]{1,0:T(8,128)}, f32[24,128]{1,0:T(8,128)S(1)}, u32[]{:S(2)}, u32[]{:S(2)}) collective-permute-start(f32[24,128]{1,0:T(8,128)} %get-tuple-element.40), channel_id=1, source_target_pairs={{0,8},{8,16},{16,24},{1,9},{9,17},{17,25},{2,10},{10,18},{18,26},{... | collective-permute-start | bytes 36872 | tf_op jit(solution)/shard_map/ppermute | solution.py:44
  48.6 24.5 %collective-permute-start.9 = (f32[24,128]{1,0:T(8,128)}, f32[24,128]{1,0:T(8,128)S(1)}, u32[]{:S(2)}, u32[]{:S(2)}) collective-permute-start(f32[24,128]{1,0:T(8,128)} %get-tuple-element.41), channel_id=1, source_target_pairs={{8,0},{16,8},{24,16},{9,1},{17,9},{25,17},{10,2},{18,10},{26,18},{... | collective-permute-start | bytes 36872 | tf_op jit(solution)/shard_map/ppermute | solution.py:44
  50.5 9.7 %collective-permute-start.13 = (f32[8,128]{1,0:T(8,128)}, f32[8,128]{1,0:T(8,128)S(1)}, u32[]{:S(2)}, u32[]{:S(2)}) collective-permute-start(f32[8,128]{1,0:T(8,128)} %get-tuple-element.42), channel_id=1, source_target_pairs={{8,1},{9,2},{10,3},{11,4},{12,5},{13,6},{14,7},{16,9},{17,10},{18,... | collective-permute-start | bytes 12296 | tf_op jit(solution)/shard_map/ppermute | solution.py:619
  52.4 9.7 %collective-permute-start.12 = (f32[8,128]{1,0:T(8,128)}, f32[8,128]{1,0:T(8,128)S(1)}, u32[]{:S(2)}, u32[]{:S(2)}) collective-permute-start(f32[8,128]{1,0:T(8,128)} %get-tuple-element.42), channel_id=1, source_target_pairs={{0,9},{1,10},{2,11},{3,12},{4,13},{5,14},{6,15},{8,17},{9,18},{10,... | collective-permute-start | bytes 12296 | tf_op jit(solution)/shard_map/ppermute | solution.py:619
  58.0 9.6 %collective-permute-start.10 = (f32[8,128]{1,0:T(8,128)}, f32[8,128]{1,0:T(8,128)S(1)}, u32[]{:S(2)}, u32[]{:S(2)}) collective-permute-start(f32[8,128]{1,0:T(8,128)} %get-tuple-element.42), channel_id=1, source_target_pairs={{0,1},{1,2},{2,3},{3,4},{4,5},{5,6},{6,7},{8,9},{9,10},{10,11},{11... | collective-permute-start | bytes 12296 | tf_op jit(solution)/shard_map/ppermute | solution.py:44
  60.2 12.9 %copy-start.10 = (f32[8,128]{1,0:T(8,128)}, f32[8,128]{1,0:T(8,128)S(1)}, u32[]{:S(2)}) copy-start(f32[8,128]{1,0:T(8,128)S(1)} %collective-permute-done.13.c_pm) | copy-start | bytes 12292
  60.2 9.5 %collective-permute-start.15 = (f32[8,128]{1,0:T(8,128)}, f32[8,128]{1,0:T(8,128)S(1)}, u32[]{:S(2)}, u32[]{:S(2)}) collective-permute-start(f32[8,128]{1,0:T(8,128)} %get-tuple-element.43), channel_id=1, source_target_pairs={{9,0},{10,1},{11,2},{12,3},{13,4},{14,5},{15,6},{17,8},{18,9},{19,... | collective-permute-start | bytes 12296 | tf_op jit(solution)/shard_map/ppermute | solution.py:619
  62.2 10.9 %copy-start.11 = (f32[8,128]{1,0:T(8,128)}, f32[8,128]{1,0:T(8,128)S(1)}, u32[]{:S(2)}) copy-start(f32[8,128]{1,0:T(8,128)S(1)} %collective-permute-done.12.c_mm) | copy-start | bytes 12292
  62.2 7.6 %collective-permute-start.14 = (f32[8,128]{1,0:T(8,128)}, f32[8,128]{1,0:T(8,128)S(1)}, u32[]{:S(2)}, u32[]{:S(2)}) collective-permute-start(f32[8,128]{1,0:T(8,128)} %get-tuple-element.43), channel_id=1, source_target_pairs={{1,8},{2,9},{3,10},{4,11},{5,12},{6,13},{7,14},{9,16},{10,17},{11,... | collective-permute-start | bytes 12296 | tf_op jit(solution)/shard_map/ppermute | solution.py:619
  67.6 5.5 %copy-start.12 = (f32[8,128]{1,0:T(8,128)}, f32[8,128]{1,0:T(8,128)S(1)}, u32[]{:S(2)}) copy-start(f32[8,128]{1,0:T(8,128)S(1)} %collective-permute-done.10.hy_lo) | copy-start | bytes 12292
  67.6 5.5 %collective-permute-start.11 = (f32[8,128]{1,0:T(8,128)}, f32[8,128]{1,0:T(8,128)S(1)}, u32[]{:S(2)}, u32[]{:S(2)}) collective-permute-start(f32[8,128]{1,0:T(8,128)} %get-tuple-element.43), channel_id=1, source_target_pairs={{1,0},{2,1},{3,2},{4,3},{5,4},{6,5},{7,6},{9,8},{10,9},{11,10},{12... | collective-permute-start | bytes 12296 | tf_op jit(solution)/shard_map/ppermute | solution.py:44
  69.7 3.4 %copy-start.13 = (f32[8,128]{1,0:T(8,128)}, f32[8,128]{1,0:T(8,128)S(1)}, u32[]{:S(2)}) copy-start(f32[8,128]{1,0:T(8,128)S(1)} %collective-permute-done.15.c_pp) | copy-start | bytes 12292
  69.7 3.4 %copy-start.14 = (f32[8,128]{1,0:T(8,128)}, f32[8,128]{1,0:T(8,128)S(1)}, u32[]{:S(2)}) copy-start(f32[8,128]{1,0:T(8,128)S(1)} %collective-permute-done.14.c_mp) | copy-start | bytes 12292
  (8 other events, 5.0 us)

commit v5 on v4

--- a/solution.py
+++ b/solution.py
@@ -265,6 +265,9 @@
     coarse = Block(coarse_shape, 3.0, False, fine.x_rows, fine.y_rows)
     fine.fx_base, fine.fy_base = 0, 0
     coarse.fx_base, coarse.fy_base = 6 * fine.chunks, fine.size
+    corner_base = fine.size + coarse.size
+    fine.corner_rows = (corner_base, corner_base + 1)
+    coarse.corner_rows = (corner_base + 2, corner_base + 3)
     return fine, coarse, fine.x_rows + coarse.x_rows, fine.y_rows + coarse.y_rows
 
 
@@ -518,7 +521,7 @@
     return m
 
 
-def padded_rows(b, face, hx_lo, hx_hi, hy_lo, hy_hi, c_mm, c_pm, c_mp, c_pp, i):
+def padded_rows(b, face, hx_lo, hx_hi, hy_lo, hy_hi, i):
     size = b.size
 
     def x_row(buf):
@@ -526,12 +529,13 @@
         return parts[0] if len(parts) == 1 else jnp.concatenate(parts, axis=1)
 
     def lane_of(buf, row):
-        return buf[pl.ds(b.fy_base + row, 1), pl.ds(i, 1)]
-
-    rows = [(x_row(hx_lo), lane_of(c_mm, size - 1), lane_of(c_mp, size - 1))]
+        return buf[pl.ds(row, 1), pl.ds(i, 1)]
+
+    lo_row, hi_row = b.corner_rows
+    rows = [(x_row(hx_lo), lane_of(hy_lo, lo_row), lane_of(hy_hi, lo_row))]
     for x in range(size):
-        rows.append((face[i, pl.ds(x, 1), :], lane_of(hy_lo, x), lane_of(hy_hi, x)))
-    rows.append((x_row(hx_hi), lane_of(c_pm, 0), lane_of(c_pp, 0)))
+        rows.append((face[i, pl.ds(x, 1), :], lane_of(hy_lo, b.fy_base + x), lane_of(hy_hi, b.fy_base + x)))
+    rows.append((x_row(hx_hi), lane_of(hy_lo, hi_row), lane_of(hy_hi, hi_row)))
     return rows
 
 
@@ -547,9 +551,9 @@
 
 
 def face_kernel(blocks, fine_depth, fout_in, cout_in, fface, cface, hx_lo, hx_hi, hy_lo, hy_hi,
-                c_mm, c_pm, c_mp, c_pp, py, ry, fout, cout, fnew, cnew, stage_p, stage_r, sems):
+                py, ry, fout, cout, fnew, cnew, stage_p, stage_r, sems):
     fine, coarse = blocks
-    halos = (hx_lo, hx_hi, hy_lo, hy_hi, c_mm, c_pm, c_mp, c_pp)
+    halos = (hx_lo, hx_hi, hy_lo, hy_hi)
     lane_f = lax.broadcasted_iota(jnp.int32, (1, fine.lanes), 1)
     p_lo, p_hi = [], []
     for i in range(6):
@@ -619,26 +623,38 @@
     return lax.ppermute(block, ("gx", "gy"), pairs)
 
 
+def row_ends(buf, blocks, at_end):
+    out = []
+    for b in blocks:
+        chunk = b.chunks - 1 if at_end else 0
+        rows = [b.fx_base + i * b.chunks + chunk for i in range(6)]
+        out.append(buf[jnp.asarray(rows), 127 if at_end else 0])
+    return jnp.stack(out)
+
+
+def with_corners(y_rim, x_lo, x_hi, blocks, at_end):
+    lo, hi = row_ends(x_lo, blocks, at_end), row_ends(x_hi, blocks, at_end)
+    extra = jnp.stack([lo, hi], axis=1).reshape(2 * len(blocks), 6)
+    extra = jnp.pad(extra, ((0, 0), (0, 128 - 6)))
+    joined = jnp.concatenate([y_rim, extra])
+    return jnp.pad(joined, ((0, round8(joined.shape[0]) - joined.shape[0]), (0, 0)))
+
+
 def face_call(blocks, fine_out, coarse_out, fine_face, coarse_face, rims):
     fine, coarse = blocks
     x_prev, x_next, y_prev, y_next = rims
-    received = (
-        shift_from(x_next, "gx", 1),
-        shift_from(x_prev, "gx", -1),
-        shift_from(y_next, "gy", 1),
-        shift_from(y_prev, "gy", -1),
-        diag_from(y_next, 1, 1),
-        diag_from(y_next, -1, 1),
-        diag_from(y_prev, 1, -1),
-        diag_from(y_prev, -1, -1),
-    )
+    x_lo = shift_from(x_next, "gx", 1)
+    x_hi = shift_from(x_prev, "gx", -1)
+    y_lo = shift_from(with_corners(y_next, x_lo, x_hi, blocks, True), "gy", 1)
+    y_hi = shift_from(with_corners(y_prev, x_lo, x_hi, blocks, False), "gy", -1)
+    received = (x_lo, x_hi, y_lo, y_hi)
     py = jnp.asarray(prolong_y_matrix(coarse.lanes))
     ry = jnp.asarray(restrict_y_matrix(coarse.lanes))
     anyspace = pl.BlockSpec(memory_space=pl.ANY)
     return pl.pallas_call(
         functools.partial(face_kernel, blocks, fine.layers - 1),
         out_shape=(f32(fine_out.shape), f32(coarse_out.shape)),
-        in_specs=[anyspace, anyspace] + vmem_specs(12),
+        in_specs=[anyspace, anyspace] + vmem_specs(8),
         out_specs=(anyspace, anyspace),
         input_output_aliases={0: 0, 1: 1},
         scratch_shapes=[

time: 76.4 us -> 69.6 us (0.911)
  the two profiles are of different devices: /device:TPU:13 before, /device:TPU:9 now
where the time goes in v5:
time: 69.6 us; the launch traced here: 69.1 us
  starting transfers between devices  37.2 us (53%)
  Pallas kernels  13.2 us (19%)
  waiting for transfers between devices  9.75 us (14%)
  local copies, waits for them, and re-layouts  7.95 us (11%)
  between operations  0.97 us (1%)
    ppermute x12, starting transfers between devices, shift_from(): return lax.ppermute(block, axis, pairs)  37.2 us
    ppermute x12, waiting for transfers between devices, shift_from(): return lax.ppermute(block, axis, pairs)  9.75 us
    gather x8, local copies, waits for them, and re-layouts, row_ends(): out.append(buf[jnp.asarray(rows), 127 if at_end else 0])  5.27 us
    pallas_call x1, Pallas kernels, local(): pl.pallas_call(functools.partial(stress_kernel, blocks), out_shape=(f32(f...  5.03 us
    pallas_call x1, Pallas kernels, local(): pl.pallas_call(functools.partial(velocity_kernel, blocks), out_shape=(f32...  3.73 us
    unnamed x34, local copies, waits for them, and re-layouts  2.66 us
    pallas_call x1, Pallas kernels, local(): pl.pallas_call(functools.partial(pack_kernel, blocks), out_shape=halo_sha...  2.25 us
    pallas_call x1, Pallas kernels, face_call(): pl.pallas_call(functools.partial(face_kernel, blocks, fine.layers - 1), o...  2.17 us
  transfers between devices with their start and end apart: 12, of which 4 were waited for; matrix products, arithmetic and copies ran while one was open for 2% of the time, Pallas kernels for 0%

profile of v5, /device:TPU:9, one launch (start us, length us, event | category | flops | bytes accessed | tf_op | source)
XLA Modules:
  0.0 69.1 jit_solution(11739189092602589687)
XLA Ops:
  0.6 2.2 %shard_map.228 = (f32[264,128]{1,0:T(8,128)}, f32[264,128]{1,0:T(8,128)}, f32[88,128]{1,0:T(8,128)}, f32[88,128]{1,0:T(8,128)}) custom-call(f32[9,12,6,384]{3,2,1,0:T(8,128)} %fw.5, f32[9,8,2,128]{3,2,1,0:T(2,128)} %cw.5), custom_call_target="tpu_custom_call" | custom-call | tf_op jit(solution)/shard_map/pallas_call | solution.py:687
  2.9 3.7 %collective-permute-start = (f32[264,128]{1,0:T(8,128)}, f32[264,128]{1,0:T(8,128)S(1)}, u32[]{:S(2)}, u32[]{:S(2)}) collective-permute-start(f32[264,128]{1,0:T(8,128)} %get-tuple-element.26), channel_id=1, source_target_pairs={{0,8},{8,16},{16,24},{1,9},{9,17},{17,25},{2,10},{10,18},{18,26},{... | collective-permute-start | bytes 405512 | tf_op jit(solution)/shard_map/ppermute | solution.py:44
  6.6 1.9 %collective-permute-start.1 = (f32[264,128]{1,0:T(8,128)}, f32[264,128]{1,0:T(8,128)S(1)}, u32[]{:S(2)}, u32[]{:S(2)}) collective-permute-start(f32[264,128]{1,0:T(8,128)} %get-tuple-element.27), channel_id=1, source_target_pairs={{8,0},{16,8},{24,16},{9,1},{17,9},{25,17},{10,2},{18,10},{26,18},{... | collective-permute-start | bytes 405512 | tf_op jit(solution)/shard_map/ppermute | solution.py:44
  8.5 3.1 %collective-permute-start.2 = (f32[88,128]{1,0:T(8,128)}, f32[88,128]{1,0:T(8,128)S(1)}, u32[]{:S(2)}, u32[]{:S(2)}) collective-permute-start(f32[88,128]{1,0:T(8,128)} %get-tuple-element.28), channel_id=1, source_target_pairs={{0,1},{1,2},{2,3},{3,4},{4,5},{5,6},{6,7},{8,9},{9,10},{10,11},{11... | collective-permute-start | bytes 135176 | tf_op jit(solution)/shard_map/ppermute | solution.py:44
  11.6 3.0 %collective-permute-start.3 = (f32[88,128]{1,0:T(8,128)}, f32[88,128]{1,0:T(8,128)S(1)}, u32[]{:S(2)}, u32[]{:S(2)}) collective-permute-start(f32[88,128]{1,0:T(8,128)} %get-tuple-element.29), channel_id=1, source_target_pairs={{1,0},{2,1},{3,2},{4,3},{5,4},{6,5},{7,6},{9,8},{10,9},{11,10},{12... | collective-permute-start | bytes 135176 | tf_op jit(solution)/shard_map/ppermute | solution.py:44
  14.7 1.9 %collective-permute-done.3.hy_hi = f32[88,128]{1,0:T(8,128)S(1)} collective-permute-done((f32[88,128]{1,0:T(8,128)}, f32[88,128]{1,0:T(8,128)S(1)}, u32[]{:S(2)}, u32[]{:S(2)}) %collective-permute-start.3) | collective-permute-done | bytes 45088 | tf_op jit(solution)/shard_map/ppermute | solution.py:44
  18.0 3.7 %shard_map.229 = (f32[3,12,6,384]{3,2,1,0:T(8,128)}, f32[3,8,2,128]{3,2,1,0:T(2,128)}, f32[264,128]{1,0:T(8,128)}, f32[264,128]{1,0:T(8,128)}, f32[88,128]{1,0:T(8,128)}, /*index=5*/f32[88,128]{1,0:T(8,128)}) custom-call(f32[9,12,6,384]{3,2,1,0:T(8,128)} %fw.5, f32[9,8,2,128]{3,2,1,0:T(2,128)} %cw.5, f32[264,128]{1,0:T(8,128)} %copy-done.2, ...), custom_call_target="tpu_custom_call" | custom-call | tf_op jit(solution)/shard_map/pallas_call | solution.py:695
  21.7 5.1 %collective-permute-start.4 = (f32[264,128]{1,0:T(8,128)}, f32[264,128]{1,0:T(8,128)S(1)}, u32[]{:S(2)}, u32[]{:S(2)}) collective-permute-start(f32[264,128]{1,0:T(8,128)} %get-tuple-element.32), channel_id=1, source_target_pairs={{0,8},{8,16},{16,24},{1,9},{9,17},{17,25},{2,10},{10,18},{18,26},{... | collective-permute-start | bytes 405512 | tf_op jit(solution)/shard_map/ppermute | solution.py:44
  26.8 1.9 %collective-permute-start.5 = (f32[264,128]{1,0:T(8,128)}, f32[264,128]{1,0:T(8,128)S(1)}, u32[]{:S(2)}, u32[]{:S(2)}) collective-permute-start(f32[264,128]{1,0:T(8,128)} %get-tuple-element.33), channel_id=1, source_target_pairs={{8,0},{16,8},{24,16},{9,1},{17,9},{25,17},{10,2},{18,10},{26,18},{... | collective-permute-start | bytes 405512 | tf_op jit(solution)/shard_map/ppermute | solution.py:44
  28.7 4.0 %collective-permute-start.6 = (f32[88,128]{1,0:T(8,128)}, f32[88,128]{1,0:T(8,128)S(1)}, u32[]{:S(2)}, u32[]{:S(2)}) collective-permute-start(f32[88,128]{1,0:T(8,128)} %get-tuple-element.34), channel_id=1, source_target_pairs={{0,1},{1,2},{2,3},{3,4},{4,5},{5,6},{6,7},{8,9},{9,10},{10,11},{11... | collective-permute-start | bytes 135176 | tf_op jit(solution)/shard_map/ppermute | solution.py:44
  32.7 2.1 %collective-permute-start.7 = (f32[88,128]{1,0:T(8,128)}, f32[88,128]{1,0:T(8,128)S(1)}, u32[]{:S(2)}, u32[]{:S(2)}) collective-permute-start(f32[88,128]{1,0:T(8,128)} %get-tuple-element.35), channel_id=1, source_target_pairs={{1,0},{2,1},{3,2},{4,3},{5,4},{6,5},{7,6},{9,8},{10,9},{11,10},{12... | collective-permute-start | bytes 135176 | tf_op jit(solution)/shard_map/ppermute | solution.py:44
  34.9 2.8 %collective-permute-done.7.hy_hi = f32[88,128]{1,0:T(8,128)S(1)} collective-permute-done((f32[88,128]{1,0:T(8,128)}, f32[88,128]{1,0:T(8,128)S(1)}, u32[]{:S(2)}, u32[]{:S(2)}) %collective-permute-start.7) | collective-permute-done | bytes 45088 | tf_op jit(solution)/shard_map/ppermute | solution.py:44
  38.5 5.0 %shard_map.230 = (f32[9,12,6,384]{3,2,1,0:T(8,128)}, f32[6,12,6,384]{3,2,1,0:T(8,128)}, f32[6,6,384]{2,1,0:T(8,128)}, f32[9,8,2,128]{3,2,1,0:T(2,128)}, f32[6,8,...) custom-call(f32[9,12,6,384]{3,2,1,0:T(8,128)} %fw.5, ...), custom_call_target="tpu_custom_call" | custom-call | tf_op jit(solution)/shard_map/pallas_call | solution.py:706
  43.5 5.1 %collective-permute-start.8 = (f32[24,128]{1,0:T(8,128)}, f32[24,128]{1,0:T(8,128)S(1)}, u32[]{:S(2)}, u32[]{:S(2)}) collective-permute-start(f32[24,128]{1,0:T(8,128)} %get-tuple-element.40), channel_id=1, source_target_pairs={{0,8},{8,16},{16,24},{1,9},{9,17},{17,25},{2,10},{10,18},{18,26},{... | collective-permute-start | bytes 36872 | tf_op jit(solution)/shard_map/ppermute | solution.py:44
  48.6 1.9 %collective-permute-start.9 = (f32[24,128]{1,0:T(8,128)}, f32[24,128]{1,0:T(8,128)S(1)}, u32[]{:S(2)}, u32[]{:S(2)}) collective-permute-start(f32[24,128]{1,0:T(8,128)} %get-tuple-element.41), channel_id=1, source_target_pairs={{8,0},{16,8},{24,16},{9,1},{17,9},{25,17},{10,2},{18,10},{26,18},{... | collective-permute-start | bytes 36872 | tf_op jit(solution)/shard_map/ppermute | solution.py:44
  51.3 0.7 gather_fusion.4
  51.9 1.9 %collective-permute-done.9.hx_hi = f32[24,128]{1,0:T(8,128)S(1)} collective-permute-done((f32[24,128]{1,0:T(8,128)}, f32[24,128]{1,0:T(8,128)S(1)}, u32[]{:S(2)}, u32[]{:S(2)}) %collective-permute-start.9) | collective-permute-done | bytes 12320 | tf_op jit(solution)/shard_map/ppermute | solution.py:44
  54.5 0.7 gather_fusion.7
  55.9 0.7 gather_fusion.3
  57.2 0.7 gather_fusion.2
  58.0 3.0 %collective-permute-start.11 = (f32[16,128]{1,0:T(8,128)S(1)}, f32[16,128]{1,0:T(8,128)S(1)}, u32[]{:S(2)}, u32[]{:S(2)}) collective-permute-start(f32[16,128]{1,0:T(8,128)S(1)} %pad.25), channel_id=1, source_target_pairs={{1,0},{2,1},{3,2},{4,3},{5,4},{6,5},{7,6},{9,8},{10,9},{11,10},{12... | collective-permute-start | bytes 24584 | tf_op jit(solution)/shard_map/ppermute | solution.py:44
  61.0 2.2 %collective-permute-start.10 = (f32[16,128]{1,0:T(8,128)S(1)}, f32[16,128]{1,0:T(8,128)S(1)}, u32[]{:S(2)}, u32[]{:S(2)}) collective-permute-start(f32[16,128]{1,0:T(8,128)S(1)} %pad.23), channel_id=1, source_target_pairs={{0,1},{1,2},{2,3},{3,4},{4,5},{5,6},{6,7},{8,9},{9,10},{10,11},{11... | collective-permute-start | bytes 24584 | tf_op jit(solution)/shard_map/ppermute | solution.py:44
  63.3 3.0 %collective-permute-done.10.hy_lo = f32[16,128]{1,0:T(8,128)S(1)} collective-permute-done((f32[16,128]{1,0:T(8,128)S(1)}, f32[16,128]{1,0:T(8,128)S(1)}, u32[]{:S(2)}, u32[]{:S(2)}) %collective-permute-start.10) | collective-permute-done | bytes 8224 | tf_op jit(solution)/shard_map/ppermute | solution.py:44
  66.9 2.2 %shard_map.231 = (f32[9,12,6,384]{3,2,1,0:T(8,128)}, f32[9,8,2,128]{3,2,1,0:T(2,128)}) custom-call(f32[9,12,6,384]{3,2,1,0:T(8,128)} %get-tuple-element.36.fout_in, f32[9,8,2,128]{3,2,1,0:T(2,128)} %get-tuple-element.37.cout_in, f32[6,6,384]{2,1,0:T(8,128)} %get-tuple-element.38.fface, ...), custom_call_target="tpu_custom_call", output_to_operand_aliasing={{0}: (0, {}), {1}: (1, {})} | custom-call | tf_op jit(solution)/shard_map/pallas_call | solution.py:654
  (57 shorter events, 5.4 us)
Async XLA Ops:
  2.9 13.8 %collective-permute-start = (f32[264,128]{1,0:T(8,128)}, f32[264,128]{1,0:T(8,128)S(1)}, u32[]{:S(2)}, u32[]{:S(2)}) collective-permute-start(f32[264,128]{1,0:T(8,128)} %get-tuple-element.26), channel_id=1, source_target_pairs={{0,8},{8,16},{16,24},{1,9},{9,17},{17,25},{2,10},{10,18},{18,26},{... | collective-permute-start | bytes 405512 | tf_op jit(solution)/shard_map/ppermute | solution.py:44
  6.6 10.1 %collective-permute-start.1 = (f32[264,128]{1,0:T(8,128)}, f32[264,128]{1,0:T(8,128)S(1)}, u32[]{:S(2)}, u32[]{:S(2)}) collective-permute-start(f32[264,128]{1,0:T(8,128)} %get-tuple-element.27), channel_id=1, source_target_pairs={{8,0},{16,8},{24,16},{9,1},{17,9},{25,17},{10,2},{18,10},{26,18},{... | collective-permute-start | bytes 405512 | tf_op jit(solution)/shard_map/ppermute | solution.py:44
  8.5 6.2 %collective-permute-start.2 = (f32[88,128]{1,0:T(8,128)}, f32[88,128]{1,0:T(8,128)S(1)}, u32[]{:S(2)}, u32[]{:S(2)}) collective-permute-start(f32[88,128]{1,0:T(8,128)} %get-tuple-element.28), channel_id=1, source_target_pairs={{0,1},{1,2},{2,3},{3,4},{4,5},{5,6},{6,7},{8,9},{9,10},{10,11},{11... | collective-permute-start | bytes 135176 | tf_op jit(solution)/shard_map/ppermute | solution.py:44
  11.6 5.0 %collective-permute-start.3 = (f32[88,128]{1,0:T(8,128)}, f32[88,128]{1,0:T(8,128)S(1)}, u32[]{:S(2)}, u32[]{:S(2)}) collective-permute-start(f32[88,128]{1,0:T(8,128)} %get-tuple-element.29), channel_id=1, source_target_pairs={{1,0},{2,1},{3,2},{4,3},{5,4},{6,5},{7,6},{9,8},{10,9},{11,10},{12... | collective-permute-start | bytes 135176 | tf_op jit(solution)/shard_map/ppermute | solution.py:44
  14.7 2.0 %copy-start.9 = (f32[88,128]{1,0:T(8,128)}, f32[88,128]{1,0:T(8,128)S(1)}, u32[]{:S(2)}) copy-start(f32[88,128]{1,0:T(8,128)S(1)} %collective-permute-done.2.hy_lo) | copy-start | bytes 135172
  21.7 16.1 %collective-permute-start.4 = (f32[264,128]{1,0:T(8,128)}, f32[264,128]{1,0:T(8,128)S(1)}, u32[]{:S(2)}, u32[]{:S(2)}) collective-permute-start(f32[264,128]{1,0:T(8,128)} %get-tuple-element.32), channel_id=1, source_target_pairs={{0,8},{8,16},{16,24},{1,9},{9,17},{17,25},{2,10},{10,18},{18,26},{... | collective-permute-start | bytes 405512 | tf_op jit(solution)/shard_map/ppermute | solution.py:44
  26.8 11.0 %collective-permute-start.5 = (f32[264,128]{1,0:T(8,128)}, f32[264,128]{1,0:T(8,128)S(1)}, u32[]{:S(2)}, u32[]{:S(2)}) collective-permute-start(f32[264,128]{1,0:T(8,128)} %get-tuple-element.33), channel_id=1, source_target_pairs={{8,0},{16,8},{24,16},{9,1},{17,9},{25,17},{10,2},{18,10},{26,18},{... | collective-permute-start | bytes 405512 | tf_op jit(solution)/shard_map/ppermute | solution.py:44
  28.7 6.2 %collective-permute-start.6 = (f32[88,128]{1,0:T(8,128)}, f32[88,128]{1,0:T(8,128)S(1)}, u32[]{:S(2)}, u32[]{:S(2)}) collective-permute-start(f32[88,128]{1,0:T(8,128)} %get-tuple-element.34), channel_id=1, source_target_pairs={{0,1},{1,2},{2,3},{3,4},{4,5},{5,6},{6,7},{8,9},{9,10},{10,11},{11... | collective-permute-start | bytes 135176 | tf_op jit(solution)/shard_map/ppermute | solution.py:44
  32.7 5.0 %collective-permute-start.7 = (f32[88,128]{1,0:T(8,128)}, f32[88,128]{1,0:T(8,128)S(1)}, u32[]{:S(2)}, u32[]{:S(2)}) collective-permute-start(f32[88,128]{1,0:T(8,128)} %get-tuple-element.35), channel_id=1, source_target_pairs={{1,0},{2,1},{3,2},{4,3},{5,4},{6,5},{7,6},{9,8},{10,9},{11,10},{12... | collective-permute-start | bytes 135176 | tf_op jit(solution)/shard_map/ppermute | solution.py:44
  34.9 2.9 %copy-start.11 = (f32[88,128]{1,0:T(8,128)}, f32[88,128]{1,0:T(8,128)S(1)}, u32[]{:S(2)}) copy-start(f32[88,128]{1,0:T(8,128)S(1)} %collective-permute-done.6.hy_lo) | copy-start | bytes 135172
  37.7 0.7 copy-start.4
  37.8 0.7 %copy-start.5 = (f32[264,128]{1,0:T(8,128)}, f32[264,128]{1,0:T(8,128)S(1)}, u32[]{:S(2)}) copy-start(f32[264,128]{1,0:T(8,128)S(1)} %collective-permute-done.5.hx_hi) | copy-start | bytes 405508
  38.5 12.1 %copy-start.8 = (s32[6]{0:T(128)S(1)}, s32[6]{0:T(128)}, u32[]{:S(2)}) copy-start(s32[6]{0:T(128)} %constant.215) | copy-start | bytes 76
  43.5 11.7 %copy-start.7 = (s32[6]{0:T(128)S(1)}, s32[6]{0:T(128)}, u32[]{:S(2)}) copy-start(s32[6]{0:T(128)} %constant.189) | copy-start | bytes 76
  43.5 7.0 %collective-permute-start.8 = (f32[24,128]{1,0:T(8,128)}, f32[24,128]{1,0:T(8,128)S(1)}, u32[]{:S(2)}, u32[]{:S(2)}) collective-permute-start(f32[24,128]{1,0:T(8,128)} %get-tuple-element.40), channel_id=1, source_target_pairs={{0,8},{8,16},{16,24},{1,9},{9,17},{17,25},{2,10},{10,18},{18,26},{... | collective-permute-start | bytes 36872 | tf_op jit(solution)/shard_map/ppermute | solution.py:44
  48.6 5.2 %collective-permute-start.9 = (f32[24,128]{1,0:T(8,128)}, f32[24,128]{1,0:T(8,128)S(1)}, u32[]{:S(2)}, u32[]{:S(2)}) collective-permute-start(f32[24,128]{1,0:T(8,128)} %get-tuple-element.41), channel_id=1, source_target_pairs={{8,0},{16,8},{24,16},{9,1},{17,9},{25,17},{10,2},{18,10},{26,18},{... | collective-permute-start | bytes 36872 | tf_op jit(solution)/shard_map/ppermute | solution.py:44
  50.6 6.0 %copy-start = (f32[24,128]{1,0:T(8,128)}, f32[24,128]{1,0:T(8,128)S(1)}, u32[]{:S(2)}) copy-start(f32[24,128]{1,0:T(8,128)S(1)} %collective-permute-done.8.hx_lo) | copy-start | bytes 36868
  51.2 5.3 %copy-start.6 = (s32[6]{0:T(128)S(1)}, s32[6]{0:T(128)}, u32[]{:S(2)}) copy-start(s32[6]{0:T(128)} %constant.181) | copy-start | bytes 76
  53.8 3.4 %copy-start.1 = (f32[24,128]{1,0:T(8,128)}, f32[24,128]{1,0:T(8,128)S(1)}, u32[]{:S(2)}) copy-start(f32[24,128]{1,0:T(8,128)S(1)} %collective-permute-done.9.hx_hi) | copy-start | bytes 36868
  54.5 3.4 %copy-start.16 = (f32[8,128]{1,0:T(8,128)S(1)}, f32[8,128]{1,0:T(8,128)}, u32[]{:S(2)}) copy-start(f32[8,128]{1,0:T(8,128)} %get-tuple-element.42) | copy-start | bytes 12292
  54.5 3.5 %copy-start.15 = (f32[8,128]{1,0:T(8,128)S(1)}, f32[8,128]{1,0:T(8,128)}, u32[]{:S(2)}) copy-start(f32[8,128]{1,0:T(8,128)} %get-tuple-element.43) | copy-start | bytes 12292
  58.0 5.3 %collective-permute-start.11 = (f32[16,128]{1,0:T(8,128)S(1)}, f32[16,128]{1,0:T(8,128)S(1)}, u32[]{:S(2)}, u32[]{:S(2)}) collective-permute-start(f32[16,128]{1,0:T(8,128)S(1)} %pad.25), channel_id=1, source_target_pairs={{1,0},{2,1},{3,2},{4,3},{5,4},{6,5},{7,6},{9,8},{10,9},{11,10},{12... | collective-permute-start | bytes 24584 | tf_op jit(solution)/shard_map/ppermute | solution.py:44
  61.0 5.3 %collective-permute-start.10 = (f32[16,128]{1,0:T(8,128)S(1)}, f32[16,128]{1,0:T(8,128)S(1)}, u32[]{:S(2)}, u32[]{:S(2)}) collective-permute-start(f32[16,128]{1,0:T(8,128)S(1)} %pad.23), channel_id=1, source_target_pairs={{0,1},{1,2},{2,3},{3,4},{4,5},{5,6},{6,7},{8,9},{9,10},{10,11},{11... | collective-permute-start | bytes 24584 | tf_op jit(solution)/shard_map/ppermute | solution.py:44
  63.3 3.0 %copy-start.13 = (f32[16,128]{1,0:T(8,128)}, f32[16,128]{1,0:T(8,128)S(1)}, u32[]{:S(2)}) copy-start(f32[16,128]{1,0:T(8,128)S(1)} %collective-permute-done.11.hy_hi) | copy-start | bytes 24580
  (5 other events, 3.2 us)

commit v6 on v5

--- a/solution.py
+++ b/solution.py
@@ -483,12 +483,11 @@
 
 def receive(buffers):
     x_prev, x_next, y_prev, y_next = buffers
-    return (
-        shift_from(x_next, "gx", 1),
-        shift_from(x_prev, "gx", -1),
-        shift_from(y_next, "gy", 1),
-        shift_from(y_prev, "gy", -1),
-    )
+    y_lo = shift_from(y_next, "gy", 1)
+    y_hi = shift_from(y_prev, "gy", -1)
+    x_lo = shift_from(x_next, "gx", 1)
+    x_hi = shift_from(x_prev, "gx", -1)
+    return x_lo, x_hi, y_lo, y_hi
 
 
 def put_face(out, face, depth):
@@ -627,8 +626,9 @@
     out = []
     for b in blocks:
         chunk = b.chunks - 1 if at_end else 0
-        rows = [b.fx_base + i * b.chunks + chunk for i in range(6)]
-        out.append(buf[jnp.asarray(rows), 127 if at_end else 0])
+        first = b.fx_base + chunk
+        lane = 127 if at_end else 0
+        out.append(lax.slice(buf, (first, lane), (first + 5 * b.chunks + 1, lane + 1), (b.chunks, 1))[:, 0])
     return jnp.stack(out)
 
 

time: 69.6 us -> 67.7 us (0.973)
  the two profiles are of different devices: /device:TPU:9 before, /device:TPU:1 now
where the time goes in v6:
time: 67.7 us; the launch traced here: 67.1 us
  starting transfers between devices  34.6 us (51%)
  waiting for transfers between devices  13.4 us (20%)
  Pallas kernels  13.1 us (19%)
  local copies, waits for them, and re-layouts  3.18 us (5%)
  other arithmetic  1.89 us (3%)
  between operations  0.86 us (1%)
    ppermute x12, starting transfers between devices, shift_from(): return lax.ppermute(block, axis, pairs)  34.6 us
    ppermute x12, waiting for transfers between devices, shift_from(): return lax.ppermute(block, axis, pairs)  13.4 us
    pallas_call x1, Pallas kernels, local(): pl.pallas_call(functools.partial(stress_kernel, blocks), out_shape=(f32(f...  5.03 us
    pallas_call x1, Pallas kernels, local(): pl.pallas_call(functools.partial(velocity_kernel, blocks), out_shape=(f32...  3.7 us
    unnamed x24, local copies, waits for them, and re-layouts  2.61 us
    pallas_call x1, Pallas kernels, local(): pl.pallas_call(functools.partial(pack_kernel, blocks), out_shape=halo_sha...  2.25 us
    pallas_call x1, Pallas kernels, face_call(): pl.pallas_call(functools.partial(face_kernel, blocks, fine.layers - 1), o...  2.17 us
    concatenate x2, other arithmetic, with_corners(): joined = jnp.concatenate([y_rim, extra])  1.37 us
  transfers between devices with their start and end apart: 12, of which 6 were waited for; matrix products, arithmetic and copies ran while one was open for 1% of the time, Pallas kernels for 0%

profile of v6, /device:TPU:1, one launch (start us, length us, event | category | flops | bytes accessed | tf_op | source)
XLA Modules:
  0.0 67.1 jit_solution(17851483208330268625)
XLA Ops:
  0.6 2.2 %shard_map.156 = (f32[264,128]{1,0:T(8,128)}, f32[264,128]{1,0:T(8,128)}, f32[88,128]{1,0:T(8,128)}, f32[88,128]{1,0:T(8,128)}) custom-call(f32[9,12,6,384]{3,2,1,0:T(8,128)} %fw.5, f32[9,8,2,128]{3,2,1,0:T(2,128)} %cw.5), custom_call_target="tpu_custom_call" | custom-call | tf_op jit(solution)/shard_map/pallas_call | solution.py:687
  2.9 4.5 %collective-permute-start = (f32[264,128]{1,0:T(8,128)}, f32[264,128]{1,0:T(8,128)S(1)}, u32[]{:S(2)}, u32[]{:S(2)}) collective-permute-start(f32[264,128]{1,0:T(8,128)} %get-tuple-element.26), channel_id=1, source_target_pairs={{0,8},{8,16},{16,24},{1,9},{9,17},{17,25},{2,10},{10,18},{18,26},{... | collective-permute-start | bytes 405512 | tf_op jit(solution)/shard_map/ppermute | solution.py:44
  7.4 1.9 %collective-permute-start.1 = (f32[264,128]{1,0:T(8,128)}, f32[264,128]{1,0:T(8,128)S(1)}, u32[]{:S(2)}, u32[]{:S(2)}) collective-permute-start(f32[264,128]{1,0:T(8,128)} %get-tuple-element.27), channel_id=1, source_target_pairs={{8,0},{16,8},{24,16},{9,1},{17,9},{25,17},{10,2},{18,10},{26,18},{... | collective-permute-start | bytes 405512 | tf_op jit(solution)/shard_map/ppermute | solution.py:44
  9.3 3.1 %collective-permute-start.2 = (f32[88,128]{1,0:T(8,128)}, f32[88,128]{1,0:T(8,128)S(1)}, u32[]{:S(2)}, u32[]{:S(2)}) collective-permute-start(f32[88,128]{1,0:T(8,128)} %get-tuple-element.28), channel_id=1, source_target_pairs={{0,1},{1,2},{2,3},{3,4},{4,5},{5,6},{6,7},{8,9},{9,10},{10,11},{11... | collective-permute-start | bytes 135176 | tf_op jit(solution)/shard_map/ppermute | solution.py:44
  12.5 1.3 %collective-permute-start.3 = (f32[88,128]{1,0:T(8,128)}, f32[88,128]{1,0:T(8,128)S(1)}, u32[]{:S(2)}, u32[]{:S(2)}) collective-permute-start(f32[88,128]{1,0:T(8,128)} %get-tuple-element.29), channel_id=1, source_target_pairs={{1,0},{2,1},{3,2},{4,3},{5,4},{6,5},{7,6},{9,8},{10,9},{11,10},{12... | collective-permute-start | bytes 135176 | tf_op jit(solution)/shard_map/ppermute | solution.py:44
  13.9 3.6 %collective-permute-done.3.hy_hi = f32[88,128]{1,0:T(8,128)S(1)} collective-permute-done((f32[88,128]{1,0:T(8,128)}, f32[88,128]{1,0:T(8,128)S(1)}, u32[]{:S(2)}, u32[]{:S(2)}) %collective-permute-start.3) | collective-permute-done | bytes 45088 | tf_op jit(solution)/shard_map/ppermute | solution.py:44
  17.5 0.6 copy-done.7
  18.1 0.7 copy-done.1
  18.8 3.7 %shard_map.157 = (f32[3,12,6,384]{3,2,1,0:T(8,128)}, f32[3,8,2,128]{3,2,1,0:T(2,128)}, f32[264,128]{1,0:T(8,128)}, f32[264,128]{1,0:T(8,128)}, f32[88,128]{1,0:T(8,128)}, /*index=5*/f32[88,128]{1,0:T(8,128)}) custom-call(f32[9,12,6,384]{3,2,1,0:T(8,128)} %fw.5, f32[9,8,2,128]{3,2,1,0:T(2,128)} %cw.5, f32[264,128]{1,0:T(8,128)} %copy-done, ...), custom_call_target="tpu_custom_call" | custom-call | tf_op jit(solution)/shard_map/pallas_call | solution.py:695
  22.5 5.1 %collective-permute-start.4 = (f32[264,128]{1,0:T(8,128)}, f32[264,128]{1,0:T(8,128)S(1)}, u32[]{:S(2)}, u32[]{:S(2)}) collective-permute-start(f32[264,128]{1,0:T(8,128)} %get-tuple-element.32), channel_id=1, source_target_pairs={{0,8},{8,16},{16,24},{1,9},{9,17},{17,25},{2,10},{10,18},{18,26},{... | collective-permute-start | bytes 405512 | tf_op jit(solution)/shard_map/ppermute | solution.py:44
  27.6 1.9 %collective-permute-start.5 = (f32[264,128]{1,0:T(8,128)}, f32[264,128]{1,0:T(8,128)S(1)}, u32[]{:S(2)}, u32[]{:S(2)}) collective-permute-start(f32[264,128]{1,0:T(8,128)} %get-tuple-element.33), channel_id=1, source_target_pairs={{8,0},{16,8},{24,16},{9,1},{17,9},{25,17},{10,2},{18,10},{26,18},{... | collective-permute-start | bytes 405512 | tf_op jit(solution)/shard_map/ppermute | solution.py:44
  29.5 4.0 %collective-permute-start.6 = (f32[88,128]{1,0:T(8,128)}, f32[88,128]{1,0:T(8,128)S(1)}, u32[]{:S(2)}, u32[]{:S(2)}) collective-permute-start(f32[88,128]{1,0:T(8,128)} %get-tuple-element.34), channel_id=1, source_target_pairs={{0,1},{1,2},{2,3},{3,4},{4,5},{5,6},{6,7},{8,9},{9,10},{10,11},{11... | collective-permute-start | bytes 135176 | tf_op jit(solution)/shard_map/ppermute | solution.py:44
  33.5 1.3 %collective-permute-start.7 = (f32[88,128]{1,0:T(8,128)}, f32[88,128]{1,0:T(8,128)S(1)}, u32[]{:S(2)}, u32[]{:S(2)}) collective-permute-start(f32[88,128]{1,0:T(8,128)} %get-tuple-element.35), channel_id=1, source_target_pairs={{1,0},{2,1},{3,2},{4,3},{5,4},{6,5},{7,6},{9,8},{10,9},{11,10},{12... | collective-permute-start | bytes 135176 | tf_op jit(solution)/shard_map/ppermute | solution.py:44
  35.0 3.6 %collective-permute-done.7.hy_hi = f32[88,128]{1,0:T(8,128)S(1)} collective-permute-done((f32[88,128]{1,0:T(8,128)}, f32[88,128]{1,0:T(8,128)S(1)}, u32[]{:S(2)}, u32[]{:S(2)}) %collective-permute-start.7) | collective-permute-done | bytes 45088 | tf_op jit(solution)/shard_map/ppermute | solution.py:44
  39.3 5.0 %shard_map.158 = (f32[9,12,6,384]{3,2,1,0:T(8,128)}, f32[6,12,6,384]{3,2,1,0:T(8,128)}, f32[6,6,384]{2,1,0:T(8,128)}, f32[9,8,2,128]{3,2,1,0:T(2,128)}, f32[6,8,...) custom-call(f32[9,12,6,384]{3,2,1,0:T(8,128)} %fw.5, ...), custom_call_target="tpu_custom_call" | custom-call | tf_op jit(solution)/shard_map/pallas_call | solution.py:706
  44.3 5.1 %collective-permute-start.8 = (f32[24,128]{1,0:T(8,128)}, f32[24,128]{1,0:T(8,128)S(1)}, u32[]{:S(2)}, u32[]{:S(2)}) collective-permute-start(f32[24,128]{1,0:T(8,128)} %get-tuple-element.40), channel_id=1, source_target_pairs={{0,8},{8,16},{16,24},{1,9},{9,17},{17,25},{2,10},{10,18},{18,26},{... | collective-permute-start | bytes 36872 | tf_op jit(solution)/shard_map/ppermute | solution.py:44
  49.4 1.9 %collective-permute-start.9 = (f32[24,128]{1,0:T(8,128)}, f32[24,128]{1,0:T(8,128)S(1)}, u32[]{:S(2)}, u32[]{:S(2)}) collective-permute-start(f32[24,128]{1,0:T(8,128)} %get-tuple-element.41), channel_id=1, source_target_pairs={{8,0},{16,8},{24,16},{9,1},{17,9},{25,17},{10,2},{18,10},{26,18},{... | collective-permute-start | bytes 36872 | tf_op jit(solution)/shard_map/ppermute | solution.py:44
  51.7 2.9 %collective-permute-done.9.hx_hi = f32[24,128]{1,0:T(8,128)S(1)} collective-permute-done((f32[24,128]{1,0:T(8,128)}, f32[24,128]{1,0:T(8,128)S(1)}, u32[]{:S(2)}, u32[]{:S(2)}) %collective-permute-start.9) | collective-permute-done | bytes 12320 | tf_op jit(solution)/shard_map/ppermute | solution.py:44
  55.4 0.7 %select_maximum_fusion = f32[12,128]{1,0:T(8,128)S(1)} fusion(f32[4,6]{1,0:T(4,128)S(1)} %bitcast.18, f32[8,128]{1,0:T(8,128)} %get-tuple-element.43), kind=kLoop, calls=%fused_computation | loop fusion | flops 4608 | bytes 10336 | tf_op jit(solution)/shard_map/concatenate | solution.py:639
  56.1 0.7 %select_maximum_fusion.1 = f32[12,128]{1,0:T(8,128)S(1)} fusion(f32[4,6]{1,0:T(4,128)S(1)} %bitcast.19, f32[8,128]{1,0:T(8,128)} %get-tuple-element.42), kind=kLoop, calls=%fused_computation.1 | loop fusion | flops 4608 | bytes 10336 | tf_op jit(solution)/shard_map/concatenate | solution.py:639
  56.8 3.1 %collective-permute-start.10 = (f32[16,128]{1,0:T(8,128)S(1)}, f32[16,128]{1,0:T(8,128)S(1)}, u32[]{:S(2)}, u32[]{:S(2)}) collective-permute-start(f32[16,128]{1,0:T(8,128)S(1)} %pad.15), channel_id=1, source_target_pairs={{0,1},{1,2},{2,3},{3,4},{4,5},{5,6},{6,7},{8,9},{9,10},{10,11},{11... | collective-permute-start | bytes 24584 | tf_op jit(solution)/shard_map/ppermute | solution.py:44
  59.9 1.3 %collective-permute-start.11 = (f32[16,128]{1,0:T(8,128)S(1)}, f32[16,128]{1,0:T(8,128)S(1)}, u32[]{:S(2)}, u32[]{:S(2)}) collective-permute-start(f32[16,128]{1,0:T(8,128)S(1)} %pad.17), channel_id=1, source_target_pairs={{1,0},{2,1},{3,2},{4,3},{5,4},{6,5},{7,6},{9,8},{10,9},{11,10},{12... | collective-permute-start | bytes 24584 | tf_op jit(solution)/shard_map/ppermute | solution.py:44
  61.2 3.1 %collective-permute-done.11.hy_hi = f32[16,128]{1,0:T(8,128)S(1)} collective-permute-done((f32[16,128]{1,0:T(8,128)S(1)}, f32[16,128]{1,0:T(8,128)S(1)}, u32[]{:S(2)}, u32[]{:S(2)}) %collective-permute-start.11) | collective-permute-done | bytes 8224 | tf_op jit(solution)/shard_map/ppermute | solution.py:44
  64.9 2.2 %shard_map.159 = (f32[9,12,6,384]{3,2,1,0:T(8,128)}, f32[9,8,2,128]{3,2,1,0:T(2,128)}) custom-call(f32[9,12,6,384]{3,2,1,0:T(8,128)} %get-tuple-element.36.fout_in, f32[9,8,2,128]{3,2,1,0:T(2,128)} %get-tuple-element.37.cout_in, f32[6,6,384]{2,1,0:T(8,128)} %get-tuple-element.38.fface, ...), custom_call_target="tpu_custom_call", output_to_operand_aliasing={{0}: (0, {}), {1}: (1, {})} | custom-call | tf_op jit(solution)/shard_map/pallas_call | solution.py:654
  (48 shorter events, 2.7 us)
Async XLA Ops:
  2.9 14.6 %collective-permute-start = (f32[264,128]{1,0:T(8,128)}, f32[264,128]{1,0:T(8,128)S(1)}, u32[]{:S(2)}, u32[]{:S(2)}) collective-permute-start(f32[264,128]{1,0:T(8,128)} %get-tuple-element.26), channel_id=1, source_target_pairs={{0,8},{8,16},{16,24},{1,9},{9,17},{17,25},{2,10},{10,18},{18,26},{... | collective-permute-start | bytes 405512 | tf_op jit(solution)/shard_map/ppermute | solution.py:44
  7.4 10.1 %collective-permute-start.1 = (f32[264,128]{1,0:T(8,128)}, f32[264,128]{1,0:T(8,128)S(1)}, u32[]{:S(2)}, u32[]{:S(2)}) collective-permute-start(f32[264,128]{1,0:T(8,128)} %get-tuple-element.27), channel_id=1, source_target_pairs={{8,0},{16,8},{24,16},{9,1},{17,9},{25,17},{10,2},{18,10},{26,18},{... | collective-permute-start | bytes 405512 | tf_op jit(solution)/shard_map/ppermute | solution.py:44
  9.3 4.6 %collective-permute-start.2 = (f32[88,128]{1,0:T(8,128)}, f32[88,128]{1,0:T(8,128)S(1)}, u32[]{:S(2)}, u32[]{:S(2)}) collective-permute-start(f32[88,128]{1,0:T(8,128)} %get-tuple-element.28), channel_id=1, source_target_pairs={{0,1},{1,2},{2,3},{3,4},{4,5},{5,6},{6,7},{8,9},{9,10},{10,11},{11... | collective-permute-start | bytes 135176 | tf_op jit(solution)/shard_map/ppermute | solution.py:44
  12.5 5.0 %collective-permute-start.3 = (f32[88,128]{1,0:T(8,128)}, f32[88,128]{1,0:T(8,128)S(1)}, u32[]{:S(2)}, u32[]{:S(2)}) collective-permute-start(f32[88,128]{1,0:T(8,128)} %get-tuple-element.29), channel_id=1, source_target_pairs={{1,0},{2,1},{3,2},{4,3},{5,4},{6,5},{7,6},{9,8},{10,9},{11,10},{12... | collective-permute-start | bytes 135176 | tf_op jit(solution)/shard_map/ppermute | solution.py:44
  13.9 3.6 %copy-start.6 = (f32[88,128]{1,0:T(8,128)}, f32[88,128]{1,0:T(8,128)S(1)}, u32[]{:S(2)}) copy-start(f32[88,128]{1,0:T(8,128)S(1)} %collective-permute-done.2.hy_lo) | copy-start | bytes 135172
  17.5 0.6 copy-start.7
  17.5 0.7 copy-start
  18.1 0.7 copy-start.1
  22.5 16.1 %collective-permute-start.4 = (f32[264,128]{1,0:T(8,128)}, f32[264,128]{1,0:T(8,128)S(1)}, u32[]{:S(2)}, u32[]{:S(2)}) collective-permute-start(f32[264,128]{1,0:T(8,128)} %get-tuple-element.32), channel_id=1, source_target_pairs={{0,8},{8,16},{16,24},{1,9},{9,17},{17,25},{2,10},{10,18},{18,26},{... | collective-permute-start | bytes 405512 | tf_op jit(solution)/shard_map/ppermute | solution.py:44
  27.6 11.0 %collective-permute-start.5 = (f32[264,128]{1,0:T(8,128)}, f32[264,128]{1,0:T(8,128)S(1)}, u32[]{:S(2)}, u32[]{:S(2)}) collective-permute-start(f32[264,128]{1,0:T(8,128)} %get-tuple-element.33), channel_id=1, source_target_pairs={{8,0},{16,8},{24,16},{9,1},{17,9},{25,17},{10,2},{18,10},{26,18},{... | collective-permute-start | bytes 405512 | tf_op jit(solution)/shard_map/ppermute | solution.py:44
  29.5 5.5 %collective-permute-start.6 = (f32[88,128]{1,0:T(8,128)}, f32[88,128]{1,0:T(8,128)S(1)}, u32[]{:S(2)}, u32[]{:S(2)}) collective-permute-start(f32[88,128]{1,0:T(8,128)} %get-tuple-element.34), channel_id=1, source_target_pairs={{0,1},{1,2},{2,3},{3,4},{4,5},{5,6},{6,7},{8,9},{9,10},{10,11},{11... | collective-permute-start | bytes 135176 | tf_op jit(solution)/shard_map/ppermute | solution.py:44
  33.5 5.0 %collective-permute-start.7 = (f32[88,128]{1,0:T(8,128)}, f32[88,128]{1,0:T(8,128)S(1)}, u32[]{:S(2)}, u32[]{:S(2)}) collective-permute-start(f32[88,128]{1,0:T(8,128)} %get-tuple-element.35), channel_id=1, source_target_pairs={{1,0},{2,1},{3,2},{4,3},{5,4},{6,5},{7,6},{9,8},{10,9},{11,10},{12... | collective-permute-start | bytes 135176 | tf_op jit(solution)/shard_map/ppermute | solution.py:44
  35.0 3.6 %copy-start.8 = (f32[88,128]{1,0:T(8,128)}, f32[88,128]{1,0:T(8,128)S(1)}, u32[]{:S(2)}) copy-start(f32[88,128]{1,0:T(8,128)S(1)} %collective-permute-done.6.hy_lo) | copy-start | bytes 135172
  38.5 0.6 copy-start.9
  38.5 0.7 copy-start.2
  38.5 0.7 %copy-start.3 = (f32[264,128]{1,0:T(8,128)}, f32[264,128]{1,0:T(8,128)S(1)}, u32[]{:S(2)}) copy-start(f32[264,128]{1,0:T(8,128)S(1)} %collective-permute-done.5.hx_hi) | copy-start | bytes 405508
  44.3 7.0 %collective-permute-start.8 = (f32[24,128]{1,0:T(8,128)}, f32[24,128]{1,0:T(8,128)S(1)}, u32[]{:S(2)}, u32[]{:S(2)}) collective-permute-start(f32[24,128]{1,0:T(8,128)} %get-tuple-element.40), channel_id=1, source_target_pairs={{0,8},{8,16},{16,24},{1,9},{9,17},{17,25},{2,10},{10,18},{18,26},{... | collective-permute-start | bytes 36872 | tf_op jit(solution)/shard_map/ppermute | solution.py:44
  49.4 5.2 %collective-permute-start.9 = (f32[24,128]{1,0:T(8,128)}, f32[24,128]{1,0:T(8,128)S(1)}, u32[]{:S(2)}, u32[]{:S(2)}) collective-permute-start(f32[24,128]{1,0:T(8,128)} %get-tuple-element.41), channel_id=1, source_target_pairs={{8,0},{16,8},{24,16},{9,1},{17,9},{25,17},{10,2},{18,10},{26,18},{... | collective-permute-start | bytes 36872 | tf_op jit(solution)/shard_map/ppermute | solution.py:44
  51.3 13.0 %copy-start.4 = (f32[24,128]{1,0:T(8,128)}, f32[24,128]{1,0:T(8,128)S(1)}, u32[]{:S(2)}) copy-start(f32[24,128]{1,0:T(8,128)S(1)} %collective-permute-done.8.hx_lo) | copy-start | bytes 36868
  54.6 9.7 %copy-start.5 = (f32[24,128]{1,0:T(8,128)}, f32[24,128]{1,0:T(8,128)S(1)}, u32[]{:S(2)}) copy-start(f32[24,128]{1,0:T(8,128)S(1)} %collective-permute-done.9.hx_hi) | copy-start | bytes 36868
  56.8 4.5 %collective-permute-start.10 = (f32[16,128]{1,0:T(8,128)S(1)}, f32[16,128]{1,0:T(8,128)S(1)}, u32[]{:S(2)}, u32[]{:S(2)}) collective-permute-start(f32[16,128]{1,0:T(8,128)S(1)} %pad.15), channel_id=1, source_target_pairs={{0,1},{1,2},{2,3},{3,4},{4,5},{5,6},{6,7},{8,9},{9,10},{10,11},{11... | collective-permute-start | bytes 24584 | tf_op jit(solution)/shard_map/ppermute | solution.py:44
  59.9 4.4 %collective-permute-start.11 = (f32[16,128]{1,0:T(8,128)S(1)}, f32[16,128]{1,0:T(8,128)S(1)}, u32[]{:S(2)}, u32[]{:S(2)}) collective-permute-start(f32[16,128]{1,0:T(8,128)S(1)} %pad.17), channel_id=1, source_target_pairs={{1,0},{2,1},{3,2},{4,3},{5,4},{6,5},{7,6},{9,8},{10,9},{11,10},{12... | collective-permute-start | bytes 24584 | tf_op jit(solution)/shard_map/ppermute | solution.py:44
  61.2 3.1 %copy-start.10 = (f32[16,128]{1,0:T(8,128)}, f32[16,128]{1,0:T(8,128)S(1)}, u32[]{:S(2)}) copy-start(f32[16,128]{1,0:T(8,128)S(1)} %collective-permute-done.10.hy_lo) | copy-start | bytes 24580
  64.3 0.6 copy-start.11

commit v7 on v6

--- a/solution.py
+++ b/solution.py
@@ -40,8 +40,22 @@
 
 def shift_from(block, axis, offset):
     count = lax.axis_size(axis)
-    pairs = [(i, i + offset) for i in range(count) if 0 <= i + offset < count]
+    pairs = [(i, (i + offset) % count) for i in range(count)]
     return lax.ppermute(block, axis, pairs)
+
+
+def edge_flags():
+    gx, gy = lax.axis_index("gx"), lax.axis_index("gy")
+    nx, ny = lax.axis_size("gx"), lax.axis_size("gy")
+    return jnp.stack([gx > 0, gx < nx - 1, gy > 0, gy < ny - 1]).astype(jnp.int32)
+
+
+def valid_of(flags):
+    return tuple(flags[k] != 0 for k in range(4))
+
+
+def keep(ok, value):
+    return jnp.where(ok, value, 0.0)
 
 
 def packed_shift(blocks, axis, offset):
@@ -306,17 +320,17 @@
     return parts[0] if len(parts) == 1 else jnp.concatenate(parts, axis=1)
 
 
-def read_y_halo(b, buf, c, z):
+def read_y_halo(b, buf, c, z, ok):
     row = b.y_base + z * b.size
-    return buf[pl.ds(row, b.size), pl.ds(2 * c, 1)], buf[pl.ds(row, b.size), pl.ds(2 * c + 1, 1)]
-
-
-def fill_x2(b, scratch, slot, src, field, lo_buf, hi_buf):
+    return keep(ok, buf[pl.ds(row, b.size), pl.ds(2 * c, 1)]), keep(ok, buf[pl.ds(row, b.size), pl.ds(2 * c + 1, 1)])
+
+
+def fill_x2(b, scratch, slot, src, field, lo_buf, hi_buf, valid):
     size = b.size
     scratch[slot, :, 2 : 2 + size, :] = src[field]
     for z in range(b.layers):
-        scratch[slot, z, 0:2, :] = read_x_halo(b, lo_buf, slot, z)
-        scratch[slot, z, 2 + size :, :] = read_x_halo(b, hi_buf, slot, z)
+        scratch[slot, z, 0:2, :] = keep(valid[0], read_x_halo(b, lo_buf, slot, z))
+        scratch[slot, z, 2 + size :, :] = keep(valid[1], read_x_halo(b, hi_buf, slot, z))
 
 
 def slope_y2(f, lo, hi, spacing):
@@ -365,13 +379,14 @@
         y_next[row : row + size, :] = acc_hi
 
 
-def velocity_block(b, w, mat, metric, table, out, sx, hx_lo, hx_hi, hy_lo, hy_hi):
+def velocity_block(b, w, mat, metric, table, out, sx, hx_lo, hx_hi, hy_lo, hy_hi, valid):
     for slot, field in enumerate(STRESS_X):
-        fill_x2(b, sx, slot, w, field, hx_lo, hx_hi)
+        fill_x2(b, sx, slot, w, field, hx_lo, hx_hi, valid)
     for z in range(b.layers):
         dx = [slope_x(sx, slot, z, b.size, b.spacing) for slot in range(3)]
         dy = [
-            slope_y2(w[field, z], read_y_halo(b, hy_lo, slot, z), read_y_halo(b, hy_hi, slot, z), b.spacing)
+            slope_y2(w[field, z], read_y_halo(b, hy_lo, slot, z, valid[2]), read_y_halo(b, hy_hi, slot, z, valid[3]),
+                     b.spacing)
             for slot, field in enumerate(STRESS_Y)
         ]
         dz = [slope_z(w, field, b.rows[z]) for field in (7, 8, 5)]
@@ -383,23 +398,25 @@
             out[k, z] = w[k, z] + step_size * (buoy * (dx[k] + dy[k] + dz[k]))
 
 
-def velocity_kernel(blocks, fw, cw, hx_lo, hx_hi, hy_lo, hy_hi, fmat, fmetric, cmat, table,
+def velocity_kernel(blocks, fw, cw, hx_lo, hx_hi, hy_lo, hy_hi, fmat, fmetric, cmat, table, flags,
                     fvel, cvel, vx_prev, vx_next, vy_prev, vy_next, sx_f, sx_c):
     fine, coarse = blocks
-    velocity_block(fine, fw, fmat, fmetric, table, fvel, sx_f, hx_lo, hx_hi, hy_lo, hy_hi)
-    velocity_block(coarse, cw, cmat, None, table, cvel, sx_c, hx_lo, hx_hi, hy_lo, hy_hi)
+    valid = valid_of(flags)
+    velocity_block(fine, fw, fmat, fmetric, table, fvel, sx_f, hx_lo, hx_hi, hy_lo, hy_hi, valid)
+    velocity_block(coarse, cw, cmat, None, table, cvel, sx_c, hx_lo, hx_hi, hy_lo, hy_hi, valid)
     write_rims(fine, fvel, VELOCITY, vx_prev, vx_next, vy_prev, vy_next)
     write_rims(coarse, cvel, VELOCITY, vx_prev, vx_next, vy_prev, vy_next)
 
 
 def stress_block(b, depth, w, mem, vel, mat, mech, metric, mtab, atab, out, mem_out, face, sx,
-                 hx_lo, hx_hi, hy_lo, hy_hi, face_rims):
+                 hx_lo, hx_hi, hy_lo, hy_hi, face_rims, valid):
     for slot in range(3):
-        fill_x2(b, sx, slot, vel, slot, hx_lo, hx_hi)
+        fill_x2(b, sx, slot, vel, slot, hx_lo, hx_hi, valid)
     for z in range(b.layers):
         dx = [slope_x(sx, slot, z, b.size, b.spacing) for slot in range(3)]
         dy = [
-            slope_y2(vel[slot, z], read_y_halo(b, hy_lo, slot, z), read_y_halo(b, hy_hi, slot, z), b.spacing)
+            slope_y2(vel[slot, z], read_y_halo(b, hy_lo, slot, z, valid[2]), read_y_halo(b, hy_hi, slot, z, valid[3]),
+                     b.spacing)
             for slot in range(3)
         ]
         dz = [slope_z(vel, slot, b.rows[z]) for slot in range(3)]
@@ -455,14 +472,15 @@
 
 
 def stress_kernel(blocks, fw, fmem, fvel, cw, cmem, cvel, hx_lo, hx_hi, hy_lo, hy_hi,
-                  fmat, fmech, fmetric, cmat, cmech, mtab, atab,
+                  fmat, fmech, fmetric, cmat, cmech, mtab, atab, flags,
                   fout, fmem_out, fface, cout, cmem_out, cface, rx_prev, rx_next, ry_prev, ry_next, sx_f, sx_c):
     fine, coarse = blocks
+    valid = valid_of(flags)
     rims = (rx_prev, rx_next, ry_prev, ry_next)
     stress_block(fine, fine.layers - 1, fw, fmem, fvel, fmat, fmech, fmetric, mtab, atab, fout, fmem_out,
-                 fface, sx_f, hx_lo, hx_hi, hy_lo, hy_hi, rims)
+                 fface, sx_f, hx_lo, hx_hi, hy_lo, hy_hi, rims, valid)
     stress_block(coarse, 0, cw, cmem, cvel, cmat, cmech, None, mtab, atab, cout, cmem_out,
-                 cface, sx_c, hx_lo, hx_hi, hy_lo, hy_hi, rims)
+                 cface, sx_c, hx_lo, hx_hi, hy_lo, hy_hi, rims, valid)
 
 
 def vmem_specs(count):
@@ -520,21 +538,25 @@
     return m
 
 
-def padded_rows(b, face, hx_lo, hx_hi, hy_lo, hy_hi, i):
+def padded_rows(b, face, hx_lo, hx_hi, hy_lo, hy_hi, valid, i):
     size = b.size
 
     def x_row(buf):
         parts = [buf[pl.ds(b.fx_base + i * b.chunks + j, 1), :] for j in range(b.chunks)]
         return parts[0] if len(parts) == 1 else jnp.concatenate(parts, axis=1)
 
-    def lane_of(buf, row):
-        return buf[pl.ds(row, 1), pl.ds(i, 1)]
-
+    def lane_of(buf, row, ok):
+        return keep(ok, buf[pl.ds(row, 1), pl.ds(i, 1)])
+
+    x_lo_ok, x_hi_ok, y_lo_ok, y_hi_ok = valid
     lo_row, hi_row = b.corner_rows
-    rows = [(x_row(hx_lo), lane_of(hy_lo, lo_row), lane_of(hy_hi, lo_row))]
+    rows = [(keep(x_lo_ok, x_row(hx_lo)), lane_of(hy_lo, lo_row, x_lo_ok & y_lo_ok),
+             lane_of(hy_hi, lo_row, x_lo_ok & y_hi_ok))]
     for x in range(size):
-        rows.append((face[i, pl.ds(x, 1), :], lane_of(hy_lo, b.fy_base + x), lane_of(hy_hi, b.fy_base + x)))
-    rows.append((x_row(hx_hi), lane_of(hy_lo, hi_row), lane_of(hy_hi, hi_row)))
+        rows.append((face[i, pl.ds(x, 1), :], lane_of(hy_lo, b.fy_base + x, y_lo_ok),
+                     lane_of(hy_hi, b.fy_base + x, y_hi_ok)))
+    rows.append((keep(x_hi_ok, x_row(hx_hi)), lane_of(hy_lo, hi_row, x_hi_ok & y_lo_ok),
+                 lane_of(hy_hi, hi_row, x_hi_ok & y_hi_ok)))
     return rows
 
 
@@ -550,9 +572,9 @@
 
 
 def face_kernel(blocks, fine_depth, fout_in, cout_in, fface, cface, hx_lo, hx_hi, hy_lo, hy_hi,
-                py, ry, fout, cout, fnew, cnew, stage_p, stage_r, sems):
+                py, ry, flags, fout, cout, fnew, cnew, stage_p, stage_r, sems):
     fine, coarse = blocks
-    halos = (hx_lo, hx_hi, hy_lo, hy_hi)
+    halos = (hx_lo, hx_hi, hy_lo, hy_hi, valid_of(flags))
     lane_f = lax.broadcasted_iota(jnp.int32, (1, fine.lanes), 1)
     p_lo, p_hi = [], []
     for i in range(6):
@@ -654,7 +676,7 @@
     return pl.pallas_call(
         functools.partial(face_kernel, blocks, fine.layers - 1),
         out_shape=(f32(fine_out.shape), f32(coarse_out.shape)),
-        in_specs=[anyspace, anyspace] + vmem_specs(8),
+        in_specs=[anyspace, anyspace] + vmem_specs(8) + [pl.BlockSpec(memory_space=pltpu.SMEM)],
         out_specs=(anyspace, anyspace),
         input_output_aliases={0: 0, 1: 1},
         scratch_shapes=[
@@ -664,7 +686,7 @@
             pltpu.VMEM((round8(6 * coarse.size), fine.lanes), jnp.float32),
             pltpu.SemaphoreType.DMA((6,)),
         ],
-    )(fine_out, coarse_out, fine_face, coarse_face, *received, py, ry)
+    )(fine_out, coarse_out, fine_face, coarse_face, *received, py, ry, edge_flags())
 
 
 def local(
@@ -683,6 +705,7 @@
     fine, coarse, x_rows, y_rows = plan_blocks(fine_wave.shape[1:], coarse_wave.shape[1:])
     blocks = (fine, coarse)
     smem = pl.BlockSpec(memory_space=pltpu.SMEM)
+    flags = edge_flags()
 
     rims = pl.pallas_call(
         functools.partial(pack_kernel, blocks),
@@ -695,10 +718,10 @@
     fine_velocity, coarse_velocity, *vrims = pl.pallas_call(
         functools.partial(velocity_kernel, blocks),
         out_shape=(f32((3,) + fine_wave.shape[1:]), f32((3,) + coarse_wave.shape[1:])) + halo_shapes(x_rows, y_rows),
-        in_specs=vmem_specs(9) + [smem],
+        in_specs=vmem_specs(9) + [smem, smem],
         out_specs=tuple(vmem_specs(6)),
         scratch_shapes=[scratch_for(fine), scratch_for(coarse)],
-    )(fine_wave, coarse_wave, *halos, fine_material, fine_metric, coarse_material, material_table)
+    )(fine_wave, coarse_wave, *halos, fine_material, fine_metric, coarse_material, material_table, flags)
 
     vhalos = receive(vrims)
     fx_rows = 6 * (fine.chunks + coarse.chunks)
@@ -710,12 +733,12 @@
             f32(coarse_wave.shape), f32(coarse_memory.shape), f32((6,) + coarse_wave.shape[2:]),
             f32((fx_rows, 128)), f32((fx_rows, 128)), f32((fy_rows, 128)), f32((fy_rows, 128)),
         ),
-        in_specs=vmem_specs(15) + [smem, smem],
+        in_specs=vmem_specs(15) + [smem, smem, smem],
         out_specs=tuple(vmem_specs(10)),
         scratch_shapes=[scratch_for(fine), scratch_for(coarse)],
     )(fine_wave, fine_memory, fine_velocity, coarse_wave, coarse_memory, coarse_velocity, *vhalos,
       fine_material, fine_mechanism, fine_metric, coarse_material, coarse_mechanism, material_table,
-      attenuation_table)
+      attenuation_table, flags)
 
     fine_out, coarse_out = face_call(blocks, fine_out, coarse_out, fine_face, coarse_face, face_rims)
     return (fine_out, fine_mem, coarse_out, coarse_mem)

time: 67.7 us -> 48.1 us (0.71)
  starting transfers between devices: 34.6 us -> 21.2 us
  waiting for transfers between devices: 13.4 us -> 6.71 us
    ppermute x12, starting transfers between devices: 34.6 us -> 21.2 us  [shift_from(): return lax.ppermute(block, axis, pairs)]
    ppermute x12, waiting for transfers between devices: 13.4 us -> 6.71 us  [shift_from(): return lax.ppermute(block, axis, pairs)]
  transfers between devices with their start and end apart: 12 -> 12, of which waited for: 6 -> 5; matrix products, arithmetic and copies ran while one was open for 1% -> 2% of each run, Pallas kernels for 0% -> 0%
where the time goes in v7:
time: 48.1 us; the launch traced here: 47.8 us
  starting transfers between devices  21.2 us (44%)
  Pallas kernels  13.4 us (28%)
  waiting for transfers between devices  6.71 us (14%)
  local copies, waits for them, and re-layouts  3.17 us (7%)
  other arithmetic  2.54 us (5%)
  between operations  0.77 us (2%)
    ppermute x12, starting transfers between devices, shift_from(): return lax.ppermute(block, axis, pairs)  21.2 us
    ppermute x12, waiting for transfers between devices, shift_from(): return lax.ppermute(block, axis, pairs)  6.71 us
    pallas_call x1, Pallas kernels, local(): pl.pallas_call(functools.partial(stress_kernel, blocks), out_shape=(f32(f...  5.1 us
    pallas_call x1, Pallas kernels, local(): pl.pallas_call(functools.partial(velocity_kernel, blocks), out_shape=(f32...  3.84 us
    unnamed x24, local copies, waits for them, and re-layouts  2.61 us
    pallas_call x1, Pallas kernels, local(): pl.pallas_call(functools.partial(pack_kernel, blocks), out_shape=halo_sha...  2.25 us
    pallas_call x1, Pallas kernels, face_call(): pl.pallas_call(functools.partial(face_kernel, blocks, fine.layers - 1), o...  2.19 us
    concatenate x2, other arithmetic, with_corners(): joined = jnp.concatenate([y_rim, extra])  1.37 us
  transfers between devices with their start and end apart: 12, of which 5 were waited for; matrix products, arithmetic and copies ran while one was open for 2% of the time, Pallas kernels for 0%

profile of v7, /device:TPU:1, one launch (start us, length us, event | category | flops | bytes accessed | tf_op | source)
XLA Modules:
  0.0 47.8 jit_solution(7435459537857785375)
XLA Ops:
  0.6 2.2 %shard_map.156 = (f32[264,128]{1,0:T(8,128)}, f32[264,128]{1,0:T(8,128)}, f32[88,128]{1,0:T(8,128)}, f32[88,128]{1,0:T(8,128)}) custom-call(f32[9,12,6,384]{3,2,1,0:T(8,128)} %fw.5, f32[9,8,2,128]{3,2,1,0:T(2,128)} %cw.5), custom_call_target="tpu_custom_call" | custom-call | tf_op jit(solution)/shard_map/pallas_call | solution.py:710
  2.9 2.6 %collective-permute-start = (f32[264,128]{1,0:T(8,128)}, f32[264,128]{1,0:T(8,128)S(1)}, u32[]{:S(2)}, u32[]{:S(2)}) collective-permute-start(f32[264,128]{1,0:T(8,128)} %get-tuple-element.26), channel_id=1, source_target_pairs={{0,8},{8,16},{16,24},{24,0},{1,9},{9,17},{17,25},{25,1},{2,10},{10... | collective-permute-start | bytes 405512 | tf_op jit(solution)/shard_map/ppermute | solution.py:44
  5.5 1.2 %collective-permute-start.2 = (f32[88,128]{1,0:T(8,128)}, f32[88,128]{1,0:T(8,128)S(1)}, u32[]{:S(2)}, u32[]{:S(2)}) collective-permute-start(f32[88,128]{1,0:T(8,128)} %get-tuple-element.28), channel_id=1, source_target_pairs={{0,1},{1,2},{2,3},{3,4},{4,5},{5,6},{6,7},{7,0},{8,9},{9,10},{10,1... | collective-permute-start | bytes 135176 | tf_op jit(solution)/shard_map/ppermute | solution.py:44
  6.7 3.0 %collective-permute-start.3 = (f32[88,128]{1,0:T(8,128)}, f32[88,128]{1,0:T(8,128)S(1)}, u32[]{:S(2)}, u32[]{:S(2)}) collective-permute-start(f32[88,128]{1,0:T(8,128)} %get-tuple-element.29), channel_id=1, source_target_pairs={{0,7},{1,0},{2,1},{3,2},{4,3},{5,4},{6,5},{7,6},{8,15},{9,8},{10,9... | collective-permute-start | bytes 135176 | tf_op jit(solution)/shard_map/ppermute | solution.py:44
  9.8 0.6 %add_convert_fusion.flags = s32[4]{0:T(128)} fusion(pred[1]{0:T(512)(128)(4,1)} %bitcast.3, pred[1]{0:T(512)(128)(4,1)} %bitcast.2, pred[1]{0:T(512)(128)(4,1)} %bitcast.1, pred[1]{0:T(512)(128)(4,1)} %bitcast), kind=kLoop, calls=%fused_computation.9 | loop fusion | flops 16 | bytes 20 | tf_op jit(solution)/shard_map/convert_element_type | solution.py:50
  10.4 1.1 %collective-permute-done.2.hy_lo = f32[88,128]{1,0:T(8,128)S(1)} collective-permute-done((f32[88,128]{1,0:T(8,128)}, f32[88,128]{1,0:T(8,128)S(1)}, u32[]{:S(2)}, u32[]{:S(2)}) %collective-permute-start.2) | collective-permute-done | bytes 45088 | tf_op jit(solution)/shard_map/ppermute | solution.py:44
  11.5 0.6 %copy-done.6 = f32[88,128]{1,0:T(8,128)} copy-done((f32[88,128]{1,0:T(8,128)}, f32[88,128]{1,0:T(8,128)S(1)}, u32[]{:S(2)}) %copy-start.6) | copy-done | bytes 45080
  12.2 0.7 %copy-done.1 = f32[264,128]{1,0:T(8,128)} copy-done((f32[264,128]{1,0:T(8,128)}, f32[264,128]{1,0:T(8,128)S(1)}, u32[]{:S(2)}) %copy-start.1) | copy-done | bytes 135192
  12.8 3.8 %shard_map.157 = (f32[3,12,6,384]{3,2,1,0:T(8,128)}, f32[3,8,2,128]{3,2,1,0:T(2,128)}, f32[264,128]{1,0:T(8,128)}, f32[264,128]{1,0:T(8,128)}, f32[88,128]{1,0:T(8,128)}, /*index=5*/f32[88,128]{1,0:T(8,128)}) custom-call(f32[9,12,6,384]{3,2,1,0:T(8,128)} %fw.5, f32[9,8,2,128]{3,2,1,0:T(2,128)} %cw.5, f32[264,128]{1,0:T(8,128)} %copy-done, ...), custom_call_target="tpu_custom_call" | custom-call | tf_op jit(solution)/shard_map/pallas_call | solution.py:718
  16.7 2.7 %collective-permute-start.4 = (f32[264,128]{1,0:T(8,128)}, f32[264,128]{1,0:T(8,128)S(1)}, u32[]{:S(2)}, u32[]{:S(2)}) collective-permute-start(f32[264,128]{1,0:T(8,128)} %get-tuple-element.32), channel_id=1, source_target_pairs={{0,8},{8,16},{16,24},{24,0},{1,9},{9,17},{17,25},{25,1},{2,10},{10... | collective-permute-start | bytes 405512 | tf_op jit(solution)/shard_map/ppermute | solution.py:44
  19.4 0.9 %collective-permute-start.6 = (f32[88,128]{1,0:T(8,128)}, f32[88,128]{1,0:T(8,128)S(1)}, u32[]{:S(2)}, u32[]{:S(2)}) collective-permute-start(f32[88,128]{1,0:T(8,128)} %get-tuple-element.34), channel_id=1, source_target_pairs={{0,1},{1,2},{2,3},{3,4},{4,5},{5,6},{6,7},{7,0},{8,9},{9,10},{10,1... | collective-permute-start | bytes 135176 | tf_op jit(solution)/shard_map/ppermute | solution.py:44
  20.3 3.5 %collective-permute-start.7 = (f32[88,128]{1,0:T(8,128)}, f32[88,128]{1,0:T(8,128)S(1)}, u32[]{:S(2)}, u32[]{:S(2)}) collective-permute-start(f32[88,128]{1,0:T(8,128)} %get-tuple-element.35), channel_id=1, source_target_pairs={{0,7},{1,0},{2,1},{3,2},{4,3},{5,4},{6,5},{7,6},{8,15},{9,8},{10,9... | collective-permute-start | bytes 135176 | tf_op jit(solution)/shard_map/ppermute | solution.py:44
  23.8 1.6 %collective-permute-done.6.hy_lo = f32[88,128]{1,0:T(8,128)S(1)} collective-permute-done((f32[88,128]{1,0:T(8,128)}, f32[88,128]{1,0:T(8,128)S(1)}, u32[]{:S(2)}, u32[]{:S(2)}) %collective-permute-start.6) | collective-permute-done | bytes 45088 | tf_op jit(solution)/shard_map/ppermute | solution.py:44
  25.5 0.6 %copy-done.8 = f32[88,128]{1,0:T(8,128)} copy-done((f32[88,128]{1,0:T(8,128)}, f32[88,128]{1,0:T(8,128)S(1)}, u32[]{:S(2)}) %copy-start.8) | copy-done | bytes 45080
  26.2 5.1 %shard_map.158 = (f32[9,12,6,384]{3,2,1,0:T(8,128)}, f32[6,12,6,384]{3,2,1,0:T(8,128)}, f32[6,6,384]{2,1,0:T(8,128)}, f32[9,8,2,128]{3,2,1,0:T(2,128)}, f32[6,8,...) custom-call(f32[9,12,6,384]{3,2,1,0:T(8,128)} %fw.5, ...), custom_call_target="tpu_custom_call" | custom-call | tf_op jit(solution)/shard_map/pallas_call | solution.py:729
  31.3 2.7 %collective-permute-start.8 = (f32[24,128]{1,0:T(8,128)}, f32[24,128]{1,0:T(8,128)S(1)}, u32[]{:S(2)}, u32[]{:S(2)}) collective-permute-start(f32[24,128]{1,0:T(8,128)} %get-tuple-element.40), channel_id=1, source_target_pairs={{0,8},{8,16},{16,24},{24,0},{1,9},{9,17},{17,25},{25,1},{2,10},{10... | collective-permute-start | bytes 36872 | tf_op jit(solution)/shard_map/ppermute | solution.py:44
  34.0 1.0 %collective-permute-done.8.hx_lo = f32[24,128]{1,0:T(8,128)S(1)} collective-permute-done((f32[24,128]{1,0:T(8,128)}, f32[24,128]{1,0:T(8,128)S(1)}, u32[]{:S(2)}, u32[]{:S(2)}) %collective-permute-start.8) | collective-permute-done | bytes 12320 | tf_op jit(solution)/shard_map/ppermute | solution.py:44
  35.4 1.9 %collective-permute-done.9.hx_hi = f32[24,128]{1,0:T(8,128)S(1)} collective-permute-done((f32[24,128]{1,0:T(8,128)}, f32[24,128]{1,0:T(8,128)S(1)}, u32[]{:S(2)}, u32[]{:S(2)}) %collective-permute-start.9) | collective-permute-done | bytes 12320 | tf_op jit(solution)/shard_map/ppermute | solution.py:44
  38.1 0.7 %select_maximum_fusion = f32[12,128]{1,0:T(8,128)S(1)} fusion(f32[4,6]{1,0:T(4,128)S(1)} %bitcast.22, f32[8,128]{1,0:T(8,128)} %get-tuple-element.43), kind=kLoop, calls=%fused_computation | loop fusion | flops 4608 | bytes 10336 | tf_op jit(solution)/shard_map/concatenate | solution.py:661
  38.8 0.7 %select_maximum_fusion.1 = f32[12,128]{1,0:T(8,128)S(1)} fusion(f32[4,6]{1,0:T(4,128)S(1)} %bitcast.23, f32[8,128]{1,0:T(8,128)} %get-tuple-element.42), kind=kLoop, calls=%fused_computation.1 | loop fusion | flops 4608 | bytes 10336 | tf_op jit(solution)/shard_map/concatenate | solution.py:661
  39.5 4.5 %collective-permute-start.11 = (f32[16,128]{1,0:T(8,128)S(1)}, f32[16,128]{1,0:T(8,128)S(1)}, u32[]{:S(2)}, u32[]{:S(2)}) collective-permute-start(f32[16,128]{1,0:T(8,128)S(1)} %pad.17), channel_id=1, source_target_pairs={{0,7},{1,0},{2,1},{3,2},{4,3},{5,4},{6,5},{7,6},{8,15},{9,8},{10,9... | collective-permute-start | bytes 24584 | tf_op jit(solution)/shard_map/ppermute | solution.py:44
  44.0 1.0 %collective-permute-done.10.hy_lo = f32[16,128]{1,0:T(8,128)S(1)} collective-permute-done((f32[16,128]{1,0:T(8,128)S(1)}, f32[16,128]{1,0:T(8,128)S(1)}, u32[]{:S(2)}, u32[]{:S(2)}) %collective-permute-start.10) | collective-permute-done | bytes 8224 | tf_op jit(solution)/shard_map/ppermute | solution.py:44
  45.0 0.6 %copy-done.10 = f32[16,128]{1,0:T(8,128)} copy-done((f32[16,128]{1,0:T(8,128)}, f32[16,128]{1,0:T(8,128)S(1)}, u32[]{:S(2)}) %copy-start.10) | copy-done | bytes 8216
  45.6 2.2 %shard_map.159 = (f32[9,12,6,384]{3,2,1,0:T(8,128)}, f32[9,8,2,128]{3,2,1,0:T(2,128)}) custom-call(f32[9,12,6,384]{3,2,1,0:T(8,128)} %get-tuple-element.36.fout_in, f32[9,8,2,128]{3,2,1,0:T(2,128)} %get-tuple-element.37.cout_in, f32[6,6,384]{2,1,0:T(8,128)} %get-tuple-element.38.fface, ...), custom_call_target="tpu_custom_call", output_to_operand_aliasing={{0}: (0, {}), {1}: (1, {})} | custom-call | tf_op jit(solution)/shard_map/pallas_call | solution.py:676
  (49 shorter events, 1.4 us)
Async XLA Ops:
  2.9 8.6 %collective-permute-start = (f32[264,128]{1,0:T(8,128)}, f32[264,128]{1,0:T(8,128)S(1)}, u32[]{:S(2)}, u32[]{:S(2)}) collective-permute-start(f32[264,128]{1,0:T(8,128)} %get-tuple-element.26), channel_id=1, source_target_pairs={{0,8},{8,16},{16,24},{24,0},{1,9},{9,17},{17,25},{25,1},{2,10},{10... | collective-permute-start | bytes 405512 | tf_op jit(solution)/shard_map/ppermute | solution.py:44
  5.5 6.1 %collective-permute-start.1 = (f32[264,128]{1,0:T(8,128)}, f32[264,128]{1,0:T(8,128)S(1)}, u32[]{:S(2)}, u32[]{:S(2)}) collective-permute-start(f32[264,128]{1,0:T(8,128)} %get-tuple-element.27), channel_id=1, source_target_pairs={{0,24},{8,0},{16,8},{24,16},{1,25},{9,1},{17,9},{25,17},{2,26},{10... | collective-permute-start | bytes 405512 | tf_op jit(solution)/shard_map/ppermute | solution.py:44
  5.5 6.0 %collective-permute-start.2 = (f32[88,128]{1,0:T(8,128)}, f32[88,128]{1,0:T(8,128)S(1)}, u32[]{:S(2)}, u32[]{:S(2)}) collective-permute-start(f32[88,128]{1,0:T(8,128)} %get-tuple-element.28), channel_id=1, source_target_pairs={{0,1},{1,2},{2,3},{3,4},{4,5},{5,6},{6,7},{7,0},{8,9},{9,10},{10,1... | collective-permute-start | bytes 135176 | tf_op jit(solution)/shard_map/ppermute | solution.py:44
  6.7 4.8 %collective-permute-start.3 = (f32[88,128]{1,0:T(8,128)}, f32[88,128]{1,0:T(8,128)S(1)}, u32[]{:S(2)}, u32[]{:S(2)}) collective-permute-start(f32[88,128]{1,0:T(8,128)} %get-tuple-element.29), channel_id=1, source_target_pairs={{0,7},{1,0},{2,1},{3,2},{4,3},{5,4},{6,5},{7,6},{8,15},{9,8},{10,9... | collective-permute-start | bytes 135176 | tf_op jit(solution)/shard_map/ppermute | solution.py:44
  11.5 0.6 %copy-start.6 = (f32[88,128]{1,0:T(8,128)}, f32[88,128]{1,0:T(8,128)S(1)}, u32[]{:S(2)}) copy-start(f32[88,128]{1,0:T(8,128)S(1)} %collective-permute-done.2.hy_lo) | copy-start | bytes 135172
  11.5 0.6 %copy-start.7 = (f32[88,128]{1,0:T(8,128)}, f32[88,128]{1,0:T(8,128)S(1)}, u32[]{:S(2)}) copy-start(f32[88,128]{1,0:T(8,128)S(1)} %collective-permute-done.3.hy_hi) | copy-start | bytes 135172
  11.5 0.7 %copy-start = (f32[264,128]{1,0:T(8,128)}, f32[264,128]{1,0:T(8,128)S(1)}, u32[]{:S(2)}) copy-start(f32[264,128]{1,0:T(8,128)S(1)} %collective-permute-done.hx_lo) | copy-start | bytes 405508
  12.2 0.7 %copy-start.1 = (f32[264,128]{1,0:T(8,128)}, f32[264,128]{1,0:T(8,128)S(1)}, u32[]{:S(2)}) copy-start(f32[264,128]{1,0:T(8,128)S(1)} %collective-permute-done.1.hx_hi) | copy-start | bytes 405508
  16.7 8.8 %collective-permute-start.4 = (f32[264,128]{1,0:T(8,128)}, f32[264,128]{1,0:T(8,128)S(1)}, u32[]{:S(2)}, u32[]{:S(2)}) collective-permute-start(f32[264,128]{1,0:T(8,128)} %get-tuple-element.32), channel_id=1, source_target_pairs={{0,8},{8,16},{16,24},{24,0},{1,9},{9,17},{17,25},{25,1},{2,10},{10... | collective-permute-start | bytes 405512 | tf_op jit(solution)/shard_map/ppermute | solution.py:44
  19.4 6.1 %collective-permute-start.5 = (f32[264,128]{1,0:T(8,128)}, f32[264,128]{1,0:T(8,128)S(1)}, u32[]{:S(2)}, u32[]{:S(2)}) collective-permute-start(f32[264,128]{1,0:T(8,128)} %get-tuple-element.33), channel_id=1, source_target_pairs={{0,24},{8,0},{16,8},{24,16},{1,25},{9,1},{17,9},{25,17},{2,26},{10... | collective-permute-start | bytes 405512 | tf_op jit(solution)/shard_map/ppermute | solution.py:44
  19.4 6.1 %collective-permute-start.6 = (f32[88,128]{1,0:T(8,128)}, f32[88,128]{1,0:T(8,128)S(1)}, u32[]{:S(2)}, u32[]{:S(2)}) collective-permute-start(f32[88,128]{1,0:T(8,128)} %get-tuple-element.34), channel_id=1, source_target_pairs={{0,1},{1,2},{2,3},{3,4},{4,5},{5,6},{6,7},{7,0},{8,9},{9,10},{10,1... | collective-permute-start | bytes 135176 | tf_op jit(solution)/shard_map/ppermute | solution.py:44
  20.3 5.1 %collective-permute-start.7 = (f32[88,128]{1,0:T(8,128)}, f32[88,128]{1,0:T(8,128)S(1)}, u32[]{:S(2)}, u32[]{:S(2)}) collective-permute-start(f32[88,128]{1,0:T(8,128)} %get-tuple-element.35), channel_id=1, source_target_pairs={{0,7},{1,0},{2,1},{3,2},{4,3},{5,4},{6,5},{7,6},{8,15},{9,8},{10,9... | collective-permute-start | bytes 135176 | tf_op jit(solution)/shard_map/ppermute | solution.py:44
  25.4 0.6 %copy-start.8 = (f32[88,128]{1,0:T(8,128)}, f32[88,128]{1,0:T(8,128)S(1)}, u32[]{:S(2)}) copy-start(f32[88,128]{1,0:T(8,128)S(1)} %collective-permute-done.6.hy_lo) | copy-start | bytes 135172
  25.4 0.6 %copy-start.9 = (f32[88,128]{1,0:T(8,128)}, f32[88,128]{1,0:T(8,128)S(1)}, u32[]{:S(2)}) copy-start(f32[88,128]{1,0:T(8,128)S(1)} %collective-permute-done.7.hy_hi) | copy-start | bytes 135172
  25.5 0.7 %copy-start.2 = (f32[264,128]{1,0:T(8,128)}, f32[264,128]{1,0:T(8,128)S(1)}, u32[]{:S(2)}) copy-start(f32[264,128]{1,0:T(8,128)S(1)} %collective-permute-done.4.hx_lo) | copy-start | bytes 405508
  25.5 0.7 %copy-start.3 = (f32[264,128]{1,0:T(8,128)}, f32[264,128]{1,0:T(8,128)S(1)}, u32[]{:S(2)}) copy-start(f32[264,128]{1,0:T(8,128)S(1)} %collective-permute-done.5.hx_hi) | copy-start | bytes 405508
  31.3 3.7 %collective-permute-start.8 = (f32[24,128]{1,0:T(8,128)}, f32[24,128]{1,0:T(8,128)S(1)}, u32[]{:S(2)}, u32[]{:S(2)}) collective-permute-start(f32[24,128]{1,0:T(8,128)} %get-tuple-element.40), channel_id=1, source_target_pairs={{0,8},{8,16},{16,24},{24,0},{1,9},{9,17},{17,25},{25,1},{2,10},{10... | collective-permute-start | bytes 36872 | tf_op jit(solution)/shard_map/ppermute | solution.py:44
  34.0 3.3 %collective-permute-start.9 = (f32[24,128]{1,0:T(8,128)}, f32[24,128]{1,0:T(8,128)S(1)}, u32[]{:S(2)}, u32[]{:S(2)}) collective-permute-start(f32[24,128]{1,0:T(8,128)} %get-tuple-element.41), channel_id=1, source_target_pairs={{0,24},{8,0},{16,8},{24,16},{1,25},{9,1},{17,9},{25,17},{2,26},{10... | collective-permute-start | bytes 36872 | tf_op jit(solution)/shard_map/ppermute | solution.py:44
  35.0 10.0 %copy-start.4 = (f32[24,128]{1,0:T(8,128)}, f32[24,128]{1,0:T(8,128)S(1)}, u32[]{:S(2)}) copy-start(f32[24,128]{1,0:T(8,128)S(1)} %collective-permute-done.8.hx_lo) | copy-start | bytes 36868
  37.3 7.7 %copy-start.5 = (f32[24,128]{1,0:T(8,128)}, f32[24,128]{1,0:T(8,128)S(1)}, u32[]{:S(2)}) copy-start(f32[24,128]{1,0:T(8,128)S(1)} %collective-permute-done.9.hx_hi) | copy-start | bytes 36868
  39.5 5.5 %collective-permute-start.10 = (f32[16,128]{1,0:T(8,128)S(1)}, f32[16,128]{1,0:T(8,128)S(1)}, u32[]{:S(2)}, u32[]{:S(2)}) collective-permute-start(f32[16,128]{1,0:T(8,128)S(1)} %pad.15), channel_id=1, source_target_pairs={{0,1},{1,2},{2,3},{3,4},{4,5},{5,6},{6,7},{7,0},{8,9},{9,10},{10,1... | collective-permute-start | bytes 24584 | tf_op jit(solution)/shard_map/ppermute | solution.py:44
  39.5 5.5 %collective-permute-start.11 = (f32[16,128]{1,0:T(8,128)S(1)}, f32[16,128]{1,0:T(8,128)S(1)}, u32[]{:S(2)}, u32[]{:S(2)}) collective-permute-start(f32[16,128]{1,0:T(8,128)S(1)} %pad.17), channel_id=1, source_target_pairs={{0,7},{1,0},{2,1},{3,2},{4,3},{5,4},{6,5},{7,6},{8,15},{9,8},{10,9... | collective-permute-start | bytes 24584 | tf_op jit(solution)/shard_map/ppermute | solution.py:44
  45.0 0.6 %copy-start.10 = (f32[16,128]{1,0:T(8,128)}, f32[16,128]{1,0:T(8,128)S(1)}, u32[]{:S(2)}) copy-start(f32[16,128]{1,0:T(8,128)S(1)} %collective-permute-done.10.hy_lo) | copy-start | bytes 24580
  45.0 0.6 %copy-start.11 = (f32[16,128]{1,0:T(8,128)}, f32[16,128]{1,0:T(8,128)S(1)}, u32[]{:S(2)}) copy-start(f32[16,128]{1,0:T(8,128)S(1)} %collective-permute-done.11.hy_hi) | copy-start | bytes 24580

commit v8 on v7

--- a/solution.py
+++ b/solution.py
@@ -408,11 +408,11 @@
     write_rims(coarse, cvel, VELOCITY, vx_prev, vx_next, vy_prev, vy_next)
 
 
-def stress_block(b, depth, w, mem, vel, mat, mech, metric, mtab, atab, out, mem_out, face, sx,
-                 hx_lo, hx_hi, hy_lo, hy_hi, face_rims, valid):
+def stress_block(b, depth, face_only, w, mem, vel, mat, mech, metric, mtab, atab, outputs, sx,
+                 hx_lo, hx_hi, hy_lo, hy_hi, valid):
     for slot in range(3):
         fill_x2(b, sx, slot, vel, slot, hx_lo, hx_hi, valid)
-    for z in range(b.layers):
+    for z in ([depth] if face_only else range(b.layers)):
         dx = [slope_x(sx, slot, z, b.size, b.spacing) for slot in range(3)]
         dy = [
             slope_y2(vel[slot, z], read_y_halo(b, hy_lo, slot, z, valid[2]), read_y_halo(b, hy_hi, slot, z, valid[3]),
@@ -435,21 +435,21 @@
             shear * (dz[0] + dx[2]),
             shear * (dz[1] + dy[2]),
         ]
-        values = []
-        for k in range(3):
-            v = vel[k, z]
-            out[k, z] = v
-            values.append(v)
+        values = [vel[k, z] for k in range(3)]
         for k in range(6):
             memory_new = decay * mem[k, z] + (1.0 - decay) * strength * rate[k]
-            mem_out[k, z] = memory_new
             stress = w[3 + k, z] + step_size * (rate[k] - memory_new)
-            out[3 + k, z] = stress
             values.append(stress)
-        if z == depth:
-            for i, k in enumerate((0, 1, 2, 7, 8, 5)):
-                face[i] = values[k]
-            write_face_rims(b, [values[k] for k in (0, 1, 2, 7, 8, 5)], *face_rims)
+            if not face_only:
+                outputs[1][k, z] = memory_new
+        if face_only:
+            planes = [values[k] for k in (0, 1, 2, 7, 8, 5)]
+            for i, v in enumerate(planes):
+                outputs[0][i] = v
+            write_face_rims(b, planes, *outputs[1])
+        else:
+            for k in range(9):
+                outputs[0][k, z] = values[k]
 
 
 def write_face_rims(b, planes, x_prev, x_next, y_prev, y_next):
@@ -471,16 +471,21 @@
     y_next[b.fy_base : b.fy_base + size, :] = acc_hi
 
 
-def stress_kernel(blocks, fw, fmem, fvel, cw, cmem, cvel, hx_lo, hx_hi, hy_lo, hy_hi,
-                  fmat, fmech, fmetric, cmat, cmech, mtab, atab, flags,
-                  fout, fmem_out, fface, cout, cmem_out, cface, rx_prev, rx_next, ry_prev, ry_next, sx_f, sx_c):
+def stress_kernel(blocks, face_only, fw, fmem, fvel, cw, cmem, cvel, hx_lo, hx_hi, hy_lo, hy_hi,
+                  fmat, fmech, fmetric, cmat, cmech, mtab, atab, flags, *outs):
     fine, coarse = blocks
     valid = valid_of(flags)
-    rims = (rx_prev, rx_next, ry_prev, ry_next)
-    stress_block(fine, fine.layers - 1, fw, fmem, fvel, fmat, fmech, fmetric, mtab, atab, fout, fmem_out,
-                 fface, sx_f, hx_lo, hx_hi, hy_lo, hy_hi, rims, valid)
-    stress_block(coarse, 0, cw, cmem, cvel, cmat, cmech, None, mtab, atab, cout, cmem_out,
-                 cface, sx_c, hx_lo, hx_hi, hy_lo, hy_hi, rims, valid)
+    if face_only:
+        fface, cface, rx_prev, rx_next, ry_prev, ry_next, sx_f, sx_c = outs
+        rims = (rx_prev, rx_next, ry_prev, ry_next)
+        fine_outputs, coarse_outputs = (fface, rims), (cface, rims)
+    else:
+        fout, fmem_out, cout, cmem_out, sx_f, sx_c = outs
+        fine_outputs, coarse_outputs = (fout, fmem_out), (cout, cmem_out)
+    stress_block(fine, fine.layers - 1, face_only, fw, fmem, fvel, fmat, fmech, fmetric, mtab, atab, fine_outputs,
+                 sx_f, hx_lo, hx_hi, hy_lo, hy_hi, valid)
+    stress_block(coarse, 0, face_only, cw, cmem, cvel, cmat, cmech, None, mtab, atab, coarse_outputs,
+                 sx_c, hx_lo, hx_hi, hy_lo, hy_hi, valid)
 
 
 def vmem_specs(count):
@@ -726,19 +731,27 @@
     vhalos = receive(vrims)
     fx_rows = 6 * (fine.chunks + coarse.chunks)
     fy_rows = round8(fine.size + coarse.size)
-    fine_out, fine_mem, fine_face, coarse_out, coarse_mem, coarse_face, *face_rims = pl.pallas_call(
-        functools.partial(stress_kernel, blocks),
+    stress_args = (fine_wave, fine_memory, fine_velocity, coarse_wave, coarse_memory, coarse_velocity, *vhalos,
+                   fine_material, fine_mechanism, fine_metric, coarse_material, coarse_mechanism, material_table,
+                   attenuation_table, flags)
+    stress_specs = vmem_specs(15) + [smem, smem, smem]
+    fine_face, coarse_face, *face_rims = pl.pallas_call(
+        functools.partial(stress_kernel, blocks, True),
         out_shape=(
-            f32(fine_wave.shape), f32(fine_memory.shape), f32((6,) + fine_wave.shape[2:]),
-            f32(coarse_wave.shape), f32(coarse_memory.shape), f32((6,) + coarse_wave.shape[2:]),
+            f32((6,) + fine_wave.shape[2:]), f32((6,) + coarse_wave.shape[2:]),
             f32((fx_rows, 128)), f32((fx_rows, 128)), f32((fy_rows, 128)), f32((fy_rows, 128)),
         ),
-        in_specs=vmem_specs(15) + [smem, smem, smem],
-        out_specs=tuple(vmem_specs(10)),
+        in_specs=stress_specs,
+        out_specs=tuple(vmem_specs(6)),
         scratch_shapes=[scratch_for(fine), scratch_for(coarse)],
-    )(fine_wave, fine_memory, fine_velocity, coarse_wave, coarse_memory, coarse_velocity, *vhalos,
-      fine_material, fine_mechanism, fine_metric, coarse_material, coarse_mechanism, material_table,
-      attenuation_table, flags)
+    )(*stress_args)
+    fine_out, fine_mem, coarse_out, coarse_mem = pl.pallas_call(
+        functools.partial(stress_kernel, blocks, False),
+        out_shape=(f32(fine_wave.shape), f32(fine_memory.shape), f32(coarse_wave.shape), f32(coarse_memory.shape)),
+        in_specs=stress_specs,
+        out_specs=tuple(vmem_specs(4)),
+        scratch_shapes=[scratch_for(fine), scratch_for(coarse)],
+    )(*stress_args)
 
     fine_out, coarse_out = face_call(blocks, fine_out, coarse_out, fine_face, coarse_face, face_rims)
     return (fine_out, fine_mem, coarse_out, coarse_mem)

time: 48.1 us -> 49.8 us (1.035)
  Pallas kernels: 13.4 us -> 16.1 us
  waiting for transfers between devices: 6.71 us -> 5.78 us
    pallas_call x1 -> x2, Pallas kernels: 5.1 us -> 7.77 us  [the longest x1 4.92 us: local(): pl.pallas_call(functools.partial(stress_kernel, blocks, False), out_shape...]
    ppermute x12, waiting for transfers between devices: 6.71 us -> 5.78 us  [shift_from(): return lax.ppermute(block, axis, pairs)]
  transfers between devices with their start and end apart: 12 -> 12, of which waited for: 5 -> 4; matrix products, arithmetic and copies ran while one was open for 2% -> 2% of each run, Pallas kernels for 0% -> 10%
where the time goes in v8:
time: 49.8 us; the launch traced here: 49.5 us
  starting transfers between devices  21.2 us (43%)
  Pallas kernels  16.1 us (32%)
  waiting for transfers between devices  5.78 us (12%)
  local copies, waits for them, and re-layouts  3.18 us (6%)
  other arithmetic  2.52 us (5%)
  between operations  0.79 us (2%)
    ppermute x12, starting transfers between devices, shift_from(): return lax.ppermute(block, axis, pairs)  21.2 us
    ppermute x12, waiting for transfers between devices, shift_from(): return lax.ppermute(block, axis, pairs)  5.78 us
    pallas_call x1, Pallas kernels, local(): pl.pallas_call(functools.partial(stress_kernel, blocks, False), out_shape...  4.92 us
    pallas_call x1, Pallas kernels, local(): pl.pallas_call(functools.partial(velocity_kernel, blocks), out_shape=(f32...  3.84 us
    pallas_call x1, Pallas kernels, local(): pl.pallas_call(functools.partial(stress_kernel, blocks, True), out_shape=...  2.85 us
    unnamed x24, local copies, waits for them, and re-layouts  2.61 us
    pallas_call x1, Pallas kernels, local(): pl.pallas_call(functools.partial(pack_kernel, blocks), out_shape=halo_sha...  2.25 us
    pallas_call x1, Pallas kernels, face_call(): pl.pallas_call(functools.partial(face_kernel, blocks, fine.layers - 1), o...  2.19 us
  transfers between devices with their start and end apart: 12, of which 4 were waited for; matrix products, arithmetic and copies ran while one was open for 2% of the time, Pallas kernels for 10%

profile of v8, /device:TPU:1, one launch (start us, length us, event | category | flops | bytes accessed | tf_op | source)
XLA Modules:
  0.0 49.5 jit_solution(56042938281416779)
XLA Ops:
  0.6 2.2 %shard_map.156 = (f32[264,128]{1,0:T(8,128)}, f32[264,128]{1,0:T(8,128)}, f32[88,128]{1,0:T(8,128)}, f32[88,128]{1,0:T(8,128)}) custom-call(f32[9,12,6,384]{3,2,1,0:T(8,128)} %fw.7, f32[9,8,2,128]{3,2,1,0:T(2,128)} %cw.7), custom_call_target="tpu_custom_call" | custom-call | tf_op jit(solution)/shard_map/pallas_call | solution.py:715
  2.9 2.6 %collective-permute-start = (f32[264,128]{1,0:T(8,128)}, f32[264,128]{1,0:T(8,128)S(1)}, u32[]{:S(2)}, u32[]{:S(2)}) collective-permute-start(f32[264,128]{1,0:T(8,128)} %get-tuple-element.26), channel_id=1, source_target_pairs={{0,8},{8,16},{16,24},{24,0},{1,9},{9,17},{17,25},{25,1},{2,10},{10... | collective-permute-start | bytes 405512 | tf_op jit(solution)/shard_map/ppermute | solution.py:44
  5.5 1.2 %collective-permute-start.2 = (f32[88,128]{1,0:T(8,128)}, f32[88,128]{1,0:T(8,128)S(1)}, u32[]{:S(2)}, u32[]{:S(2)}) collective-permute-start(f32[88,128]{1,0:T(8,128)} %get-tuple-element.28), channel_id=1, source_target_pairs={{0,1},{1,2},{2,3},{3,4},{4,5},{5,6},{6,7},{7,0},{8,9},{9,10},{10,1... | collective-permute-start | bytes 135176 | tf_op jit(solution)/shard_map/ppermute | solution.py:44
  6.7 3.0 %collective-permute-start.3 = (f32[88,128]{1,0:T(8,128)}, f32[88,128]{1,0:T(8,128)S(1)}, u32[]{:S(2)}, u32[]{:S(2)}) collective-permute-start(f32[88,128]{1,0:T(8,128)} %get-tuple-element.29), channel_id=1, source_target_pairs={{0,7},{1,0},{2,1},{3,2},{4,3},{5,4},{6,5},{7,6},{8,15},{9,8},{10,9... | collective-permute-start | bytes 135176 | tf_op jit(solution)/shard_map/ppermute | solution.py:44
  9.8 0.6 %add_convert_fusion.flags = s32[4]{0:T(128)} fusion(pred[1]{0:T(512)(128)(4,1)} %bitcast.3, pred[1]{0:T(512)(128)(4,1)} %bitcast.2, pred[1]{0:T(512)(128)(4,1)} %bitcast.1, pred[1]{0:T(512)(128)(4,1)} %bitcast), kind=kLoop, calls=%fused_computation.9 | loop fusion | flops 16 | bytes 20 | tf_op jit(solution)/shard_map/convert_element_type | solution.py:50
  10.4 1.1 %collective-permute-done.2.hy_lo = f32[88,128]{1,0:T(8,128)S(1)} collective-permute-done((f32[88,128]{1,0:T(8,128)}, f32[88,128]{1,0:T(8,128)S(1)}, u32[]{:S(2)}, u32[]{:S(2)}) %collective-permute-start.2) | collective-permute-done | bytes 45088 | tf_op jit(solution)/shard_map/ppermute | solution.py:44
  11.5 0.6 %copy-done.8 = f32[88,128]{1,0:T(8,128)} copy-done((f32[88,128]{1,0:T(8,128)}, f32[88,128]{1,0:T(8,128)S(1)}, u32[]{:S(2)}) %copy-start.8) | copy-done | bytes 45080
  12.2 0.7 %copy-done.5 = f32[264,128]{1,0:T(8,128)} copy-done((f32[264,128]{1,0:T(8,128)}, f32[264,128]{1,0:T(8,128)S(1)}, u32[]{:S(2)}) %copy-start.5) | copy-done | bytes 135192
  12.8 3.8 %shard_map.157 = (f32[3,12,6,384]{3,2,1,0:T(8,128)}, f32[3,8,2,128]{3,2,1,0:T(2,128)}, f32[264,128]{1,0:T(8,128)}, f32[264,128]{1,0:T(8,128)}, f32[88,128]{1,0:T(8,128)}, /*index=5*/f32[88,128]{1,0:T(8,128)}) custom-call(f32[9,12,6,384]{3,2,1,0:T(8,128)} %fw.7, f32[9,8,2,128]{3,2,1,0:T(2,128)} %cw.7, f32[264,128]{1,0:T(8,128)} %copy-done.4, ...), custom_call_target="tpu_custom_call" | custom-call | tf_op jit(solution)/shard_map/pallas_call | solution.py:723
  16.7 2.7 %collective-permute-start.4 = (f32[264,128]{1,0:T(8,128)}, f32[264,128]{1,0:T(8,128)S(1)}, u32[]{:S(2)}, u32[]{:S(2)}) collective-permute-start(f32[264,128]{1,0:T(8,128)} %get-tuple-element.32), channel_id=1, source_target_pairs={{0,8},{8,16},{16,24},{24,0},{1,9},{9,17},{17,25},{25,1},{2,10},{10... | collective-permute-start | bytes 405512 | tf_op jit(solution)/shard_map/ppermute | solution.py:44
  19.4 0.9 %collective-permute-start.6 = (f32[88,128]{1,0:T(8,128)}, f32[88,128]{1,0:T(8,128)S(1)}, u32[]{:S(2)}, u32[]{:S(2)}) collective-permute-start(f32[88,128]{1,0:T(8,128)} %get-tuple-element.34), channel_id=1, source_target_pairs={{0,1},{1,2},{2,3},{3,4},{4,5},{5,6},{6,7},{7,0},{8,9},{9,10},{10,1... | collective-permute-start | bytes 135176 | tf_op jit(solution)/shard_map/ppermute | solution.py:44
  20.3 3.5 %collective-permute-start.7 = (f32[88,128]{1,0:T(8,128)}, f32[88,128]{1,0:T(8,128)S(1)}, u32[]{:S(2)}, u32[]{:S(2)}) collective-permute-start(f32[88,128]{1,0:T(8,128)} %get-tuple-element.35), channel_id=1, source_target_pairs={{0,7},{1,0},{2,1},{3,2},{4,3},{5,4},{6,5},{7,6},{8,15},{9,8},{10,9... | collective-permute-start | bytes 135176 | tf_op jit(solution)/shard_map/ppermute | solution.py:44
  23.8 1.6 %collective-permute-done.6.hy_lo = f32[88,128]{1,0:T(8,128)S(1)} collective-permute-done((f32[88,128]{1,0:T(8,128)}, f32[88,128]{1,0:T(8,128)S(1)}, u32[]{:S(2)}, u32[]{:S(2)}) %collective-permute-start.6) | collective-permute-done | bytes 45088 | tf_op jit(solution)/shard_map/ppermute | solution.py:44
  25.5 0.6 %copy-done.2 = f32[88,128]{1,0:T(8,128)} copy-done((f32[88,128]{1,0:T(8,128)}, f32[88,128]{1,0:T(8,128)S(1)}, u32[]{:S(2)}) %copy-start.2) | copy-done | bytes 45080
  26.2 2.9 %shard_map.159 = (f32[6,6,384]{2,1,0:T(8,128)}, f32[6,2,128]{2,1,0:T(2,128)}, f32[24,128]{1,0:T(8,128)}, f32[24,128]{1,0:T(8,128)}, f32[8,128]{1,0:T(8,128)}, /*index=5*/f32[8,128]{1,0:T(8,128)}) custom-call(f32[9,12,6,384]{3,2,1,0:T(8,128)} %fw.7, f32[6,12,6,384]{3,2,1,0:T(8,128)} %fmem.3, f32[3,12,6,384]{3,2,1,0:T(8,128)} %get-tuple-element.30.fvel, ...), custom_call_target="tpu_custom_call" | custom-call | tf_op jit(solution)/shard_map/pallas_call | solution.py:738
  29.0 2.7 %collective-permute-start.8 = (f32[24,128]{1,0:T(8,128)}, f32[24,128]{1,0:T(8,128)S(1)}, u32[]{:S(2)}, u32[]{:S(2)}) collective-permute-start(f32[24,128]{1,0:T(8,128)} %get-tuple-element.40), channel_id=1, source_target_pairs={{0,8},{8,16},{16,24},{24,0},{1,9},{9,17},{17,25},{25,1},{2,10},{10... | collective-permute-start | bytes 36872 | tf_op jit(solution)/shard_map/ppermute | solution.py:44
  31.7 1.0 %collective-permute-done.8.hx_lo = f32[24,128]{1,0:T(8,128)S(1)} collective-permute-done((f32[24,128]{1,0:T(8,128)}, f32[24,128]{1,0:T(8,128)S(1)}, u32[]{:S(2)}, u32[]{:S(2)}) %collective-permute-start.8) | collective-permute-done | bytes 12320 | tf_op jit(solution)/shard_map/ppermute | solution.py:44
  33.1 1.9 %collective-permute-done.9.hx_hi = f32[24,128]{1,0:T(8,128)S(1)} collective-permute-done((f32[24,128]{1,0:T(8,128)}, f32[24,128]{1,0:T(8,128)S(1)}, u32[]{:S(2)}, u32[]{:S(2)}) %collective-permute-start.9) | collective-permute-done | bytes 12320 | tf_op jit(solution)/shard_map/ppermute | solution.py:44
  35.8 0.7 %select_maximum_fusion = f32[12,128]{1,0:T(8,128)S(1)} fusion(f32[4,6]{1,0:T(4,128)S(1)} %bitcast.22, f32[8,128]{1,0:T(8,128)} %get-tuple-element.43), kind=kLoop, calls=%fused_computation | loop fusion | flops 4608 | bytes 10336 | tf_op jit(solution)/shard_map/concatenate | solution.py:666
  36.5 0.7 %select_maximum_fusion.1 = f32[12,128]{1,0:T(8,128)S(1)} fusion(f32[4,6]{1,0:T(4,128)S(1)} %bitcast.23, f32[8,128]{1,0:T(8,128)} %get-tuple-element.42), kind=kLoop, calls=%fused_computation.1 | loop fusion | flops 4608 | bytes 10336 | tf_op jit(solution)/shard_map/concatenate | solution.py:666
  37.3 4.5 %collective-permute-start.11 = (f32[16,128]{1,0:T(8,128)S(1)}, f32[16,128]{1,0:T(8,128)S(1)}, u32[]{:S(2)}, u32[]{:S(2)}) collective-permute-start(f32[16,128]{1,0:T(8,128)S(1)} %pad.17), channel_id=1, source_target_pairs={{0,7},{1,0},{2,1},{3,2},{4,3},{5,4},{6,5},{7,6},{8,15},{9,8},{10,9... | collective-permute-start | bytes 24584 | tf_op jit(solution)/shard_map/ppermute | solution.py:44
  41.8 4.9 %shard_map.158 = (f32[9,12,6,384]{3,2,1,0:T(8,128)}, f32[6,12,6,384]{3,2,1,0:T(8,128)}, f32[9,8,2,128]{3,2,1,0:T(2,128)}, f32[6,8,2,128]{3,2,1,0:T(2,128)}) custom-call(f32[9,12,6,384]{3,2,1,0:T(8,128)} %fw.7, f32[6,12,6,384]{3,2,1,0:T(8,128)} %fmem.3, f32[3,12,6,384]{3,2,1,0:T(8,128)} %get-tuple-element.30.fvel, f32[9,8,2,128]{3,2,1,0:T(2,128)} %cw.7, ...), custom_call_target="tpu_custom_call" | custom-call | tf_op jit(solution)/shard_map/pallas_call | solution.py:748
  46.7 0.6 %copy-done.10 = f32[16,128]{1,0:T(8,128)} copy-done((f32[16,128]{1,0:T(8,128)}, f32[16,128]{1,0:T(8,128)S(1)}, u32[]{:S(2)}) %copy-start.10) | copy-done | bytes 8216
  47.3 2.2 %shard_map.160 = (f32[9,12,6,384]{3,2,1,0:T(8,128)}, f32[9,8,2,128]{3,2,1,0:T(2,128)}) custom-call(f32[9,12,6,384]{3,2,1,0:T(8,128)} %get-tuple-element.36.fout_in, f32[9,8,2,128]{3,2,1,0:T(2,128)} %get-tuple-element.37.cout_in, f32[6,6,384]{2,1,0:T(8,128)} %get-tuple-element.38.fface, ...), custom_call_target="tpu_custom_call", output_to_operand_aliasing={{0}: (0, {}), {1}: (1, {})} | custom-call | tf_op jit(solution)/shard_map/pallas_call | solution.py:681
  (50 shorter events, 1.4 us)
Async XLA Ops:
  2.9 8.6 %collective-permute-start = (f32[264,128]{1,0:T(8,128)}, f32[264,128]{1,0:T(8,128)S(1)}, u32[]{:S(2)}, u32[]{:S(2)}) collective-permute-start(f32[264,128]{1,0:T(8,128)} %get-tuple-element.26), channel_id=1, source_target_pairs={{0,8},{8,16},{16,24},{24,0},{1,9},{9,17},{17,25},{25,1},{2,10},{10... | collective-permute-start | bytes 405512 | tf_op jit(solution)/shard_map/ppermute | solution.py:44
  5.5 6.1 %collective-permute-start.1 = (f32[264,128]{1,0:T(8,128)}, f32[264,128]{1,0:T(8,128)S(1)}, u32[]{:S(2)}, u32[]{:S(2)}) collective-permute-start(f32[264,128]{1,0:T(8,128)} %get-tuple-element.27), channel_id=1, source_target_pairs={{0,24},{8,0},{16,8},{24,16},{1,25},{9,1},{17,9},{25,17},{2,26},{10... | collective-permute-start | bytes 405512 | tf_op jit(solution)/shard_map/ppermute | solution.py:44
  5.5 6.0 %collective-permute-start.2 = (f32[88,128]{1,0:T(8,128)}, f32[88,128]{1,0:T(8,128)S(1)}, u32[]{:S(2)}, u32[]{:S(2)}) collective-permute-start(f32[88,128]{1,0:T(8,128)} %get-tuple-element.28), channel_id=1, source_target_pairs={{0,1},{1,2},{2,3},{3,4},{4,5},{5,6},{6,7},{7,0},{8,9},{9,10},{10,1... | collective-permute-start | bytes 135176 | tf_op jit(solution)/shard_map/ppermute | solution.py:44
  6.7 4.8 %collective-permute-start.3 = (f32[88,128]{1,0:T(8,128)}, f32[88,128]{1,0:T(8,128)S(1)}, u32[]{:S(2)}, u32[]{:S(2)}) collective-permute-start(f32[88,128]{1,0:T(8,128)} %get-tuple-element.29), channel_id=1, source_target_pairs={{0,7},{1,0},{2,1},{3,2},{4,3},{5,4},{6,5},{7,6},{8,15},{9,8},{10,9... | collective-permute-start | bytes 135176 | tf_op jit(solution)/shard_map/ppermute | solution.py:44
  11.5 0.6 %copy-start.8 = (f32[88,128]{1,0:T(8,128)}, f32[88,128]{1,0:T(8,128)S(1)}, u32[]{:S(2)}) copy-start(f32[88,128]{1,0:T(8,128)S(1)} %collective-permute-done.2.hy_lo) | copy-start | bytes 135172
  11.5 0.6 %copy-start.9 = (f32[88,128]{1,0:T(8,128)}, f32[88,128]{1,0:T(8,128)S(1)}, u32[]{:S(2)}) copy-start(f32[88,128]{1,0:T(8,128)S(1)} %collective-permute-done.3.hy_hi) | copy-start | bytes 135172
  11.5 0.7 %copy-start.4 = (f32[264,128]{1,0:T(8,128)}, f32[264,128]{1,0:T(8,128)S(1)}, u32[]{:S(2)}) copy-start(f32[264,128]{1,0:T(8,128)S(1)} %collective-permute-done.hx_lo) | copy-start | bytes 405508
  12.2 0.7 %copy-start.5 = (f32[264,128]{1,0:T(8,128)}, f32[264,128]{1,0:T(8,128)S(1)}, u32[]{:S(2)}) copy-start(f32[264,128]{1,0:T(8,128)S(1)} %collective-permute-done.1.hx_hi) | copy-start | bytes 405508
  16.7 8.8 %collective-permute-start.4 = (f32[264,128]{1,0:T(8,128)}, f32[264,128]{1,0:T(8,128)S(1)}, u32[]{:S(2)}, u32[]{:S(2)}) collective-permute-start(f32[264,128]{1,0:T(8,128)} %get-tuple-element.32), channel_id=1, source_target_pairs={{0,8},{8,16},{16,24},{24,0},{1,9},{9,17},{17,25},{25,1},{2,10},{10... | collective-permute-start | bytes 405512 | tf_op jit(solution)/shard_map/ppermute | solution.py:44
  19.4 6.1 %collective-permute-start.5 = (f32[264,128]{1,0:T(8,128)}, f32[264,128]{1,0:T(8,128)S(1)}, u32[]{:S(2)}, u32[]{:S(2)}) collective-permute-start(f32[264,128]{1,0:T(8,128)} %get-tuple-element.33), channel_id=1, source_target_pairs={{0,24},{8,0},{16,8},{24,16},{1,25},{9,1},{17,9},{25,17},{2,26},{10... | collective-permute-start | bytes 405512 | tf_op jit(solution)/shard_map/ppermute | solution.py:44
  19.4 6.1 %collective-permute-start.6 = (f32[88,128]{1,0:T(8,128)}, f32[88,128]{1,0:T(8,128)S(1)}, u32[]{:S(2)}, u32[]{:S(2)}) collective-permute-start(f32[88,128]{1,0:T(8,128)} %get-tuple-element.34), channel_id=1, source_target_pairs={{0,1},{1,2},{2,3},{3,4},{4,5},{5,6},{6,7},{7,0},{8,9},{9,10},{10,1... | collective-permute-start | bytes 135176 | tf_op jit(solution)/shard_map/ppermute | solution.py:44
  20.3 5.1 %collective-permute-start.7 = (f32[88,128]{1,0:T(8,128)}, f32[88,128]{1,0:T(8,128)S(1)}, u32[]{:S(2)}, u32[]{:S(2)}) collective-permute-start(f32[88,128]{1,0:T(8,128)} %get-tuple-element.35), channel_id=1, source_target_pairs={{0,7},{1,0},{2,1},{3,2},{4,3},{5,4},{6,5},{7,6},{8,15},{9,8},{10,9... | collective-permute-start | bytes 135176 | tf_op jit(solution)/shard_map/ppermute | solution.py:44
  25.4 0.6 %copy-start.2 = (f32[88,128]{1,0:T(8,128)}, f32[88,128]{1,0:T(8,128)S(1)}, u32[]{:S(2)}) copy-start(f32[88,128]{1,0:T(8,128)S(1)} %collective-permute-done.6.hy_lo) | copy-start | bytes 135172
  25.4 0.6 %copy-start.3 = (f32[88,128]{1,0:T(8,128)}, f32[88,128]{1,0:T(8,128)S(1)}, u32[]{:S(2)}) copy-start(f32[88,128]{1,0:T(8,128)S(1)} %collective-permute-done.7.hy_hi) | copy-start | bytes 135172
  25.5 0.7 %copy-start = (f32[264,128]{1,0:T(8,128)}, f32[264,128]{1,0:T(8,128)S(1)}, u32[]{:S(2)}) copy-start(f32[264,128]{1,0:T(8,128)S(1)} %collective-permute-done.4.hx_lo) | copy-start | bytes 405508
  25.5 0.7 %copy-start.1 = (f32[264,128]{1,0:T(8,128)}, f32[264,128]{1,0:T(8,128)S(1)}, u32[]{:S(2)}) copy-start(f32[264,128]{1,0:T(8,128)S(1)} %collective-permute-done.5.hx_hi) | copy-start | bytes 405508
  29.0 3.7 %collective-permute-start.8 = (f32[24,128]{1,0:T(8,128)}, f32[24,128]{1,0:T(8,128)S(1)}, u32[]{:S(2)}, u32[]{:S(2)}) collective-permute-start(f32[24,128]{1,0:T(8,128)} %get-tuple-element.40), channel_id=1, source_target_pairs={{0,8},{8,16},{16,24},{24,0},{1,9},{9,17},{17,25},{25,1},{2,10},{10... | collective-permute-start | bytes 36872 | tf_op jit(solution)/shard_map/ppermute | solution.py:44
  31.7 3.3 %collective-permute-start.9 = (f32[24,128]{1,0:T(8,128)}, f32[24,128]{1,0:T(8,128)S(1)}, u32[]{:S(2)}, u32[]{:S(2)}) collective-permute-start(f32[24,128]{1,0:T(8,128)} %get-tuple-element.41), channel_id=1, source_target_pairs={{0,24},{8,0},{16,8},{24,16},{1,25},{9,1},{17,9},{25,17},{2,26},{10... | collective-permute-start | bytes 36872 | tf_op jit(solution)/shard_map/ppermute | solution.py:44
  32.7 13.9 %copy-start.6 = (f32[24,128]{1,0:T(8,128)}, f32[24,128]{1,0:T(8,128)S(1)}, u32[]{:S(2)}) copy-start(f32[24,128]{1,0:T(8,128)S(1)} %collective-permute-done.8.hx_lo) | copy-start | bytes 36868
  35.0 11.7 %copy-start.7 = (f32[24,128]{1,0:T(8,128)}, f32[24,128]{1,0:T(8,128)S(1)}, u32[]{:S(2)}) copy-start(f32[24,128]{1,0:T(8,128)S(1)} %collective-permute-done.9.hx_hi) | copy-start | bytes 36868
  37.2 9.5 %collective-permute-start.10 = (f32[16,128]{1,0:T(8,128)S(1)}, f32[16,128]{1,0:T(8,128)S(1)}, u32[]{:S(2)}, u32[]{:S(2)}) collective-permute-start(f32[16,128]{1,0:T(8,128)S(1)} %pad.15), channel_id=1, source_target_pairs={{0,1},{1,2},{2,3},{3,4},{4,5},{5,6},{6,7},{7,0},{8,9},{9,10},{10,1... | collective-permute-start | bytes 24584 | tf_op jit(solution)/shard_map/ppermute | solution.py:44
  37.3 9.4 %collective-permute-start.11 = (f32[16,128]{1,0:T(8,128)S(1)}, f32[16,128]{1,0:T(8,128)S(1)}, u32[]{:S(2)}, u32[]{:S(2)}) collective-permute-start(f32[16,128]{1,0:T(8,128)S(1)} %pad.17), channel_id=1, source_target_pairs={{0,7},{1,0},{2,1},{3,2},{4,3},{5,4},{6,5},{7,6},{8,15},{9,8},{10,9... | collective-permute-start | bytes 24584 | tf_op jit(solution)/shard_map/ppermute | solution.py:44
  46.7 0.6 %copy-start.10 = (f32[16,128]{1,0:T(8,128)}, f32[16,128]{1,0:T(8,128)S(1)}, u32[]{:S(2)}) copy-start(f32[16,128]{1,0:T(8,128)S(1)} %collective-permute-done.10.hy_lo) | copy-start | bytes 24580
  46.7 0.6 %copy-start.11 = (f32[16,128]{1,0:T(8,128)}, f32[16,128]{1,0:T(8,128)S(1)}, u32[]{:S(2)}) copy-start(f32[16,128]{1,0:T(8,128)S(1)} %collective-permute-done.11.hy_hi) | copy-start | bytes 24580

commit v9 on v8

--- a/solution.py
+++ b/solution.py
@@ -325,10 +325,15 @@
     return keep(ok, buf[pl.ds(row, b.size), pl.ds(2 * c, 1)]), keep(ok, buf[pl.ds(row, b.size), pl.ds(2 * c + 1, 1)])
 
 
-def fill_x2(b, scratch, slot, src, field, lo_buf, hi_buf, valid):
+def fill_x2(b, scratch, slot, src, field, lo_buf, hi_buf, valid, layers=None):
     size = b.size
-    scratch[slot, :, 2 : 2 + size, :] = src[field]
-    for z in range(b.layers):
+    if layers is None:
+        scratch[slot, :, 2 : 2 + size, :] = src[field]
+        layers = range(b.layers)
+    else:
+        for z in layers:
+            scratch[slot, z, 2 : 2 + size, :] = src[field, z]
+    for z in layers:
         scratch[slot, z, 0:2, :] = keep(valid[0], read_x_halo(b, lo_buf, slot, z))
         scratch[slot, z, 2 + size :, :] = keep(valid[1], read_x_halo(b, hi_buf, slot, z))
 
@@ -411,7 +416,7 @@
 def stress_block(b, depth, face_only, w, mem, vel, mat, mech, metric, mtab, atab, outputs, sx,
                  hx_lo, hx_hi, hy_lo, hy_hi, valid):
     for slot in range(3):
-        fill_x2(b, sx, slot, vel, slot, hx_lo, hx_hi, valid)
+        fill_x2(b, sx, slot, vel, slot, hx_lo, hx_hi, valid, [depth] if face_only else None)
     for z in ([depth] if face_only else range(b.layers)):
         dx = [slope_x(sx, slot, z, b.size, b.spacing) for slot in range(3)]
         dy = [

time: 49.8 us -> 49.8 us (level)
  no operation moved by 1% of the time
where the time goes in v9:
time: 49.8 us; the launch traced here: 49.5 us
  starting transfers between devices  21.2 us (43%)
  Pallas kernels  16 us (32%)
  waiting for transfers between devices  5.78 us (12%)
  local copies, waits for them, and re-layouts  3.18 us (6%)
  other arithmetic  2.52 us (5%)
  between operations  0.79 us (2%)
    ppermute x12, starting transfers between devices, shift_from(): return lax.ppermute(block, axis, pairs)  21.2 us
    ppermute x12, waiting for transfers between devices, shift_from(): return lax.ppermute(block, axis, pairs)  5.78 us
    pallas_call x1, Pallas kernels, local(): pl.pallas_call(functools.partial(stress_kernel, blocks, False), out_shape...  4.92 us
    pallas_call x1, Pallas kernels, local(): pl.pallas_call(functools.partial(velocity_kernel, blocks), out_shape=(f32...  3.84 us
    pallas_call x1, Pallas kernels, local(): pl.pallas_call(functools.partial(stress_kernel, blocks, True), out_shape=...  2.82 us
    unnamed x24, local copies, waits for them, and re-layouts  2.61 us
    pallas_call x1, Pallas kernels, local(): pl.pallas_call(functools.partial(pack_kernel, blocks), out_shape=halo_sha...  2.25 us
    pallas_call x1, Pallas kernels, face_call(): pl.pallas_call(functools.partial(face_kernel, blocks, fine.layers - 1), o...  2.19 us
  transfers between devices with their start and end apart: 12, of which 4 were waited for; matrix products, arithmetic and copies ran while one was open for 2% of the time, Pallas kernels for 10%

profile of v9, /device:TPU:1, one launch (start us, length us, event | category | flops | bytes accessed | tf_op | source)
XLA Modules:
  0.0 49.5 jit_solution(9737708460794438256)
XLA Ops:
  0.6 2.2 %shard_map.156 = (f32[264,128]{1,0:T(8,128)}, f32[264,128]{1,0:T(8,128)}, f32[88,128]{1,0:T(8,128)}, f32[88,128]{1,0:T(8,128)}) custom-call(f32[9,12,6,384]{3,2,1,0:T(8,128)} %fw.7, f32[9,8,2,128]{3,2,1,0:T(2,128)} %cw.7), custom_call_target="tpu_custom_call" | custom-call | tf_op jit(solution)/shard_map/pallas_call | solution.py:720
  2.9 2.6 %collective-permute-start = (f32[264,128]{1,0:T(8,128)}, f32[264,128]{1,0:T(8,128)S(1)}, u32[]{:S(2)}, u32[]{:S(2)}) collective-permute-start(f32[264,128]{1,0:T(8,128)} %get-tuple-element.26), channel_id=1, source_target_pairs={{0,8},{8,16},{16,24},{24,0},{1,9},{9,17},{17,25},{25,1},{2,10},{10... | collective-permute-start | bytes 405512 | tf_op jit(solution)/shard_map/ppermute | solution.py:44
  5.5 1.2 %collective-permute-start.2 = (f32[88,128]{1,0:T(8,128)}, f32[88,128]{1,0:T(8,128)S(1)}, u32[]{:S(2)}, u32[]{:S(2)}) collective-permute-start(f32[88,128]{1,0:T(8,128)} %get-tuple-element.28), channel_id=1, source_target_pairs={{0,1},{1,2},{2,3},{3,4},{4,5},{5,6},{6,7},{7,0},{8,9},{9,10},{10,1... | collective-permute-start | bytes 135176 | tf_op jit(solution)/shard_map/ppermute | solution.py:44
  6.7 3.0 %collective-permute-start.3 = (f32[88,128]{1,0:T(8,128)}, f32[88,128]{1,0:T(8,128)S(1)}, u32[]{:S(2)}, u32[]{:S(2)}) collective-permute-start(f32[88,128]{1,0:T(8,128)} %get-tuple-element.29), channel_id=1, source_target_pairs={{0,7},{1,0},{2,1},{3,2},{4,3},{5,4},{6,5},{7,6},{8,15},{9,8},{10,9... | collective-permute-start | bytes 135176 | tf_op jit(solution)/shard_map/ppermute | solution.py:44
  9.8 0.6 %add_convert_fusion.flags = s32[4]{0:T(128)} fusion(pred[1]{0:T(512)(128)(4,1)} %bitcast.3, pred[1]{0:T(512)(128)(4,1)} %bitcast.2, pred[1]{0:T(512)(128)(4,1)} %bitcast.1, pred[1]{0:T(512)(128)(4,1)} %bitcast), kind=kLoop, calls=%fused_computation.9 | loop fusion | flops 16 | bytes 20 | tf_op jit(solution)/shard_map/convert_element_type | solution.py:50
  10.4 1.1 %collective-permute-done.2.hy_lo = f32[88,128]{1,0:T(8,128)S(1)} collective-permute-done((f32[88,128]{1,0:T(8,128)}, f32[88,128]{1,0:T(8,128)S(1)}, u32[]{:S(2)}, u32[]{:S(2)}) %collective-permute-start.2) | collective-permute-done | bytes 45088 | tf_op jit(solution)/shard_map/ppermute | solution.py:44
  11.5 0.6 %copy-done.8 = f32[88,128]{1,0:T(8,128)} copy-done((f32[88,128]{1,0:T(8,128)}, f32[88,128]{1,0:T(8,128)S(1)}, u32[]{:S(2)}) %copy-start.8) | copy-done | bytes 45080
  12.2 0.7 %copy-done.5 = f32[264,128]{1,0:T(8,128)} copy-done((f32[264,128]{1,0:T(8,128)}, f32[264,128]{1,0:T(8,128)S(1)}, u32[]{:S(2)}) %copy-start.5) | copy-done | bytes 135192
  12.8 3.8 %shard_map.157 = (f32[3,12,6,384]{3,2,1,0:T(8,128)}, f32[3,8,2,128]{3,2,1,0:T(2,128)}, f32[264,128]{1,0:T(8,128)}, f32[264,128]{1,0:T(8,128)}, f32[88,128]{1,0:T(8,128)}, /*index=5*/f32[88,128]{1,0:T(8,128)}) custom-call(f32[9,12,6,384]{3,2,1,0:T(8,128)} %fw.7, f32[9,8,2,128]{3,2,1,0:T(2,128)} %cw.7, f32[264,128]{1,0:T(8,128)} %copy-done.4, ...), custom_call_target="tpu_custom_call" | custom-call | tf_op jit(solution)/shard_map/pallas_call | solution.py:728
  16.7 2.7 %collective-permute-start.4 = (f32[264,128]{1,0:T(8,128)}, f32[264,128]{1,0:T(8,128)S(1)}, u32[]{:S(2)}, u32[]{:S(2)}) collective-permute-start(f32[264,128]{1,0:T(8,128)} %get-tuple-element.32), channel_id=1, source_target_pairs={{0,8},{8,16},{16,24},{24,0},{1,9},{9,17},{17,25},{25,1},{2,10},{10... | collective-permute-start | bytes 405512 | tf_op jit(solution)/shard_map/ppermute | solution.py:44
  19.4 0.9 %collective-permute-start.6 = (f32[88,128]{1,0:T(8,128)}, f32[88,128]{1,0:T(8,128)S(1)}, u32[]{:S(2)}, u32[]{:S(2)}) collective-permute-start(f32[88,128]{1,0:T(8,128)} %get-tuple-element.34), channel_id=1, source_target_pairs={{0,1},{1,2},{2,3},{3,4},{4,5},{5,6},{6,7},{7,0},{8,9},{9,10},{10,1... | collective-permute-start | bytes 135176 | tf_op jit(solution)/shard_map/ppermute | solution.py:44
  20.3 3.5 %collective-permute-start.7 = (f32[88,128]{1,0:T(8,128)}, f32[88,128]{1,0:T(8,128)S(1)}, u32[]{:S(2)}, u32[]{:S(2)}) collective-permute-start(f32[88,128]{1,0:T(8,128)} %get-tuple-element.35), channel_id=1, source_target_pairs={{0,7},{1,0},{2,1},{3,2},{4,3},{5,4},{6,5},{7,6},{8,15},{9,8},{10,9... | collective-permute-start | bytes 135176 | tf_op jit(solution)/shard_map/ppermute | solution.py:44
  23.8 1.6 %collective-permute-done.6.hy_lo = f32[88,128]{1,0:T(8,128)S(1)} collective-permute-done((f32[88,128]{1,0:T(8,128)}, f32[88,128]{1,0:T(8,128)S(1)}, u32[]{:S(2)}, u32[]{:S(2)}) %collective-permute-start.6) | collective-permute-done | bytes 45088 | tf_op jit(solution)/shard_map/ppermute | solution.py:44
  25.5 0.6 %copy-done.2 = f32[88,128]{1,0:T(8,128)} copy-done((f32[88,128]{1,0:T(8,128)}, f32[88,128]{1,0:T(8,128)S(1)}, u32[]{:S(2)}) %copy-start.2) | copy-done | bytes 45080
  26.2 2.8 %shard_map.159 = (f32[6,6,384]{2,1,0:T(8,128)}, f32[6,2,128]{2,1,0:T(2,128)}, f32[24,128]{1,0:T(8,128)}, f32[24,128]{1,0:T(8,128)}, f32[8,128]{1,0:T(8,128)}, /*index=5*/f32[8,128]{1,0:T(8,128)}) custom-call(f32[9,12,6,384]{3,2,1,0:T(8,128)} %fw.7, f32[6,12,6,384]{3,2,1,0:T(8,128)} %fmem.3, f32[3,12,6,384]{3,2,1,0:T(8,128)} %get-tuple-element.30.fvel, ...), custom_call_target="tpu_custom_call" | custom-call | tf_op jit(solution)/shard_map/pallas_call | solution.py:743
  29.0 2.7 %collective-permute-start.8 = (f32[24,128]{1,0:T(8,128)}, f32[24,128]{1,0:T(8,128)S(1)}, u32[]{:S(2)}, u32[]{:S(2)}) collective-permute-start(f32[24,128]{1,0:T(8,128)} %get-tuple-element.40), channel_id=1, source_target_pairs={{0,8},{8,16},{16,24},{24,0},{1,9},{9,17},{17,25},{25,1},{2,10},{10... | collective-permute-start | bytes 36872 | tf_op jit(solution)/shard_map/ppermute | solution.py:44
  31.7 1.0 %collective-permute-done.8.hx_lo = f32[24,128]{1,0:T(8,128)S(1)} collective-permute-done((f32[24,128]{1,0:T(8,128)}, f32[24,128]{1,0:T(8,128)S(1)}, u32[]{:S(2)}, u32[]{:S(2)}) %collective-permute-start.8) | collective-permute-done | bytes 12320 | tf_op jit(solution)/shard_map/ppermute | solution.py:44
  33.1 1.9 %collective-permute-done.9.hx_hi = f32[24,128]{1,0:T(8,128)S(1)} collective-permute-done((f32[24,128]{1,0:T(8,128)}, f32[24,128]{1,0:T(8,128)S(1)}, u32[]{:S(2)}, u32[]{:S(2)}) %collective-permute-start.9) | collective-permute-done | bytes 12320 | tf_op jit(solution)/shard_map/ppermute | solution.py:44
  35.8 0.7 %select_maximum_fusion = f32[12,128]{1,0:T(8,128)S(1)} fusion(f32[4,6]{1,0:T(4,128)S(1)} %bitcast.22, f32[8,128]{1,0:T(8,128)} %get-tuple-element.43), kind=kLoop, calls=%fused_computation | loop fusion | flops 4608 | bytes 10336 | tf_op jit(solution)/shard_map/concatenate | solution.py:671
  36.5 0.7 %select_maximum_fusion.1 = f32[12,128]{1,0:T(8,128)S(1)} fusion(f32[4,6]{1,0:T(4,128)S(1)} %bitcast.23, f32[8,128]{1,0:T(8,128)} %get-tuple-element.42), kind=kLoop, calls=%fused_computation.1 | loop fusion | flops 4608 | bytes 10336 | tf_op jit(solution)/shard_map/concatenate | solution.py:671
  37.3 4.5 %collective-permute-start.11 = (f32[16,128]{1,0:T(8,128)S(1)}, f32[16,128]{1,0:T(8,128)S(1)}, u32[]{:S(2)}, u32[]{:S(2)}) collective-permute-start(f32[16,128]{1,0:T(8,128)S(1)} %pad.17), channel_id=1, source_target_pairs={{0,7},{1,0},{2,1},{3,2},{4,3},{5,4},{6,5},{7,6},{8,15},{9,8},{10,9... | collective-permute-start | bytes 24584 | tf_op jit(solution)/shard_map/ppermute | solution.py:44
  41.7 4.9 %shard_map.158 = (f32[9,12,6,384]{3,2,1,0:T(8,128)}, f32[6,12,6,384]{3,2,1,0:T(8,128)}, f32[9,8,2,128]{3,2,1,0:T(2,128)}, f32[6,8,2,128]{3,2,1,0:T(2,128)}) custom-call(f32[9,12,6,384]{3,2,1,0:T(8,128)} %fw.7, f32[6,12,6,384]{3,2,1,0:T(8,128)} %fmem.3, f32[3,12,6,384]{3,2,1,0:T(8,128)} %get-tuple-element.30.fvel, f32[9,8,2,128]{3,2,1,0:T(2,128)} %cw.7, ...), custom_call_target="tpu_custom_call" | custom-call | tf_op jit(solution)/shard_map/pallas_call | solution.py:753
  46.7 0.6 %copy-done.10 = f32[16,128]{1,0:T(8,128)} copy-done((f32[16,128]{1,0:T(8,128)}, f32[16,128]{1,0:T(8,128)S(1)}, u32[]{:S(2)}) %copy-start.10) | copy-done | bytes 8216
  47.3 2.2 %shard_map.160 = (f32[9,12,6,384]{3,2,1,0:T(8,128)}, f32[9,8,2,128]{3,2,1,0:T(2,128)}) custom-call(f32[9,12,6,384]{3,2,1,0:T(8,128)} %get-tuple-element.36.fout_in, f32[9,8,2,128]{3,2,1,0:T(2,128)} %get-tuple-element.37.cout_in, f32[6,6,384]{2,1,0:T(8,128)} %get-tuple-element.38.fface, ...), custom_call_target="tpu_custom_call", output_to_operand_aliasing={{0}: (0, {}), {1}: (1, {})} | custom-call | tf_op jit(solution)/shard_map/pallas_call | solution.py:686
  (50 shorter events, 1.4 us)
Async XLA Ops:
  2.9 8.6 %collective-permute-start = (f32[264,128]{1,0:T(8,128)}, f32[264,128]{1,0:T(8,128)S(1)}, u32[]{:S(2)}, u32[]{:S(2)}) collective-permute-start(f32[264,128]{1,0:T(8,128)} %get-tuple-element.26), channel_id=1, source_target_pairs={{0,8},{8,16},{16,24},{24,0},{1,9},{9,17},{17,25},{25,1},{2,10},{10... | collective-permute-start | bytes 405512 | tf_op jit(solution)/shard_map/ppermute | solution.py:44
  5.5 6.1 %collective-permute-start.1 = (f32[264,128]{1,0:T(8,128)}, f32[264,128]{1,0:T(8,128)S(1)}, u32[]{:S(2)}, u32[]{:S(2)}) collective-permute-start(f32[264,128]{1,0:T(8,128)} %get-tuple-element.27), channel_id=1, source_target_pairs={{0,24},{8,0},{16,8},{24,16},{1,25},{9,1},{17,9},{25,17},{2,26},{10... | collective-permute-start | bytes 405512 | tf_op jit(solution)/shard_map/ppermute | solution.py:44
  5.5 6.0 %collective-permute-start.2 = (f32[88,128]{1,0:T(8,128)}, f32[88,128]{1,0:T(8,128)S(1)}, u32[]{:S(2)}, u32[]{:S(2)}) collective-permute-start(f32[88,128]{1,0:T(8,128)} %get-tuple-element.28), channel_id=1, source_target_pairs={{0,1},{1,2},{2,3},{3,4},{4,5},{5,6},{6,7},{7,0},{8,9},{9,10},{10,1... | collective-permute-start | bytes 135176 | tf_op jit(solution)/shard_map/ppermute | solution.py:44
  6.7 4.8 %collective-permute-start.3 = (f32[88,128]{1,0:T(8,128)}, f32[88,128]{1,0:T(8,128)S(1)}, u32[]{:S(2)}, u32[]{:S(2)}) collective-permute-start(f32[88,128]{1,0:T(8,128)} %get-tuple-element.29), channel_id=1, source_target_pairs={{0,7},{1,0},{2,1},{3,2},{4,3},{5,4},{6,5},{7,6},{8,15},{9,8},{10,9... | collective-permute-start | bytes 135176 | tf_op jit(solution)/shard_map/ppermute | solution.py:44
  11.5 0.6 %copy-start.8 = (f32[88,128]{1,0:T(8,128)}, f32[88,128]{1,0:T(8,128)S(1)}, u32[]{:S(2)}) copy-start(f32[88,128]{1,0:T(8,128)S(1)} %collective-permute-done.2.hy_lo) | copy-start | bytes 135172
  11.5 0.6 %copy-start.9 = (f32[88,128]{1,0:T(8,128)}, f32[88,128]{1,0:T(8,128)S(1)}, u32[]{:S(2)}) copy-start(f32[88,128]{1,0:T(8,128)S(1)} %collective-permute-done.3.hy_hi) | copy-start | bytes 135172
  11.5 0.7 %copy-start.4 = (f32[264,128]{1,0:T(8,128)}, f32[264,128]{1,0:T(8,128)S(1)}, u32[]{:S(2)}) copy-start(f32[264,128]{1,0:T(8,128)S(1)} %collective-permute-done.hx_lo) | copy-start | bytes 405508
  12.2 0.7 %copy-start.5 = (f32[264,128]{1,0:T(8,128)}, f32[264,128]{1,0:T(8,128)S(1)}, u32[]{:S(2)}) copy-start(f32[264,128]{1,0:T(8,128)S(1)} %collective-permute-done.1.hx_hi) | copy-start | bytes 405508
  16.7 8.8 %collective-permute-start.4 = (f32[264,128]{1,0:T(8,128)}, f32[264,128]{1,0:T(8,128)S(1)}, u32[]{:S(2)}, u32[]{:S(2)}) collective-permute-start(f32[264,128]{1,0:T(8,128)} %get-tuple-element.32), channel_id=1, source_target_pairs={{0,8},{8,16},{16,24},{24,0},{1,9},{9,17},{17,25},{25,1},{2,10},{10... | collective-permute-start | bytes 405512 | tf_op jit(solution)/shard_map/ppermute | solution.py:44
  19.4 6.1 %collective-permute-start.5 = (f32[264,128]{1,0:T(8,128)}, f32[264,128]{1,0:T(8,128)S(1)}, u32[]{:S(2)}, u32[]{:S(2)}) collective-permute-start(f32[264,128]{1,0:T(8,128)} %get-tuple-element.33), channel_id=1, source_target_pairs={{0,24},{8,0},{16,8},{24,16},{1,25},{9,1},{17,9},{25,17},{2,26},{10... | collective-permute-start | bytes 405512 | tf_op jit(solution)/shard_map/ppermute | solution.py:44
  19.4 6.1 %collective-permute-start.6 = (f32[88,128]{1,0:T(8,128)}, f32[88,128]{1,0:T(8,128)S(1)}, u32[]{:S(2)}, u32[]{:S(2)}) collective-permute-start(f32[88,128]{1,0:T(8,128)} %get-tuple-element.34), channel_id=1, source_target_pairs={{0,1},{1,2},{2,3},{3,4},{4,5},{5,6},{6,7},{7,0},{8,9},{9,10},{10,1... | collective-permute-start | bytes 135176 | tf_op jit(solution)/shard_map/ppermute | solution.py:44
  20.3 5.1 %collective-permute-start.7 = (f32[88,128]{1,0:T(8,128)}, f32[88,128]{1,0:T(8,128)S(1)}, u32[]{:S(2)}, u32[]{:S(2)}) collective-permute-start(f32[88,128]{1,0:T(8,128)} %get-tuple-element.35), channel_id=1, source_target_pairs={{0,7},{1,0},{2,1},{3,2},{4,3},{5,4},{6,5},{7,6},{8,15},{9,8},{10,9... | collective-permute-start | bytes 135176 | tf_op jit(solution)/shard_map/ppermute | solution.py:44
  25.4 0.6 %copy-start.2 = (f32[88,128]{1,0:T(8,128)}, f32[88,128]{1,0:T(8,128)S(1)}, u32[]{:S(2)}) copy-start(f32[88,128]{1,0:T(8,128)S(1)} %collective-permute-done.6.hy_lo) | copy-start | bytes 135172
  25.4 0.6 %copy-start.3 = (f32[88,128]{1,0:T(8,128)}, f32[88,128]{1,0:T(8,128)S(1)}, u32[]{:S(2)}) copy-start(f32[88,128]{1,0:T(8,128)S(1)} %collective-permute-done.7.hy_hi) | copy-start | bytes 135172
  25.5 0.7 %copy-start = (f32[264,128]{1,0:T(8,128)}, f32[264,128]{1,0:T(8,128)S(1)}, u32[]{:S(2)}) copy-start(f32[264,128]{1,0:T(8,128)S(1)} %collective-permute-done.4.hx_lo) | copy-start | bytes 405508
  25.5 0.7 %copy-start.1 = (f32[264,128]{1,0:T(8,128)}, f32[264,128]{1,0:T(8,128)S(1)}, u32[]{:S(2)}) copy-start(f32[264,128]{1,0:T(8,128)S(1)} %collective-permute-done.5.hx_hi) | copy-start | bytes 405508
  29.0 3.7 %collective-permute-start.8 = (f32[24,128]{1,0:T(8,128)}, f32[24,128]{1,0:T(8,128)S(1)}, u32[]{:S(2)}, u32[]{:S(2)}) collective-permute-start(f32[24,128]{1,0:T(8,128)} %get-tuple-element.40), channel_id=1, source_target_pairs={{0,8},{8,16},{16,24},{24,0},{1,9},{9,17},{17,25},{25,1},{2,10},{10... | collective-permute-start | bytes 36872 | tf_op jit(solution)/shard_map/ppermute | solution.py:44
  31.7 3.3 %collective-permute-start.9 = (f32[24,128]{1,0:T(8,128)}, f32[24,128]{1,0:T(8,128)S(1)}, u32[]{:S(2)}, u32[]{:S(2)}) collective-permute-start(f32[24,128]{1,0:T(8,128)} %get-tuple-element.41), channel_id=1, source_target_pairs={{0,24},{8,0},{16,8},{24,16},{1,25},{9,1},{17,9},{25,17},{2,26},{10... | collective-permute-start | bytes 36872 | tf_op jit(solution)/shard_map/ppermute | solution.py:44
  32.7 13.9 %copy-start.6 = (f32[24,128]{1,0:T(8,128)}, f32[24,128]{1,0:T(8,128)S(1)}, u32[]{:S(2)}) copy-start(f32[24,128]{1,0:T(8,128)S(1)} %collective-permute-done.8.hx_lo) | copy-start | bytes 36868
  35.0 11.7 %copy-start.7 = (f32[24,128]{1,0:T(8,128)}, f32[24,128]{1,0:T(8,128)S(1)}, u32[]{:S(2)}) copy-start(f32[24,128]{1,0:T(8,128)S(1)} %collective-permute-done.9.hx_hi) | copy-start | bytes 36868
  37.2 9.5 %collective-permute-start.10 = (f32[16,128]{1,0:T(8,128)S(1)}, f32[16,128]{1,0:T(8,128)S(1)}, u32[]{:S(2)}, u32[]{:S(2)}) collective-permute-start(f32[16,128]{1,0:T(8,128)S(1)} %pad.15), channel_id=1, source_target_pairs={{0,1},{1,2},{2,3},{3,4},{4,5},{5,6},{6,7},{7,0},{8,9},{9,10},{10,1... | collective-permute-start | bytes 24584 | tf_op jit(solution)/shard_map/ppermute | solution.py:44
  37.3 9.4 %collective-permute-start.11 = (f32[16,128]{1,0:T(8,128)S(1)}, f32[16,128]{1,0:T(8,128)S(1)}, u32[]{:S(2)}, u32[]{:S(2)}) collective-permute-start(f32[16,128]{1,0:T(8,128)S(1)} %pad.17), channel_id=1, source_target_pairs={{0,7},{1,0},{2,1},{3,2},{4,3},{5,4},{6,5},{7,6},{8,15},{9,8},{10,9... | collective-permute-start | bytes 24584 | tf_op jit(solution)/shard_map/ppermute | solution.py:44
  46.7 0.6 %copy-start.10 = (f32[16,128]{1,0:T(8,128)}, f32[16,128]{1,0:T(8,128)S(1)}, u32[]{:S(2)}) copy-start(f32[16,128]{1,0:T(8,128)S(1)} %collective-permute-done.10.hy_lo) | copy-start | bytes 24580
  46.7 0.6 %copy-start.11 = (f32[16,128]{1,0:T(8,128)}, f32[16,128]{1,0:T(8,128)S(1)}, u32[]{:S(2)}) copy-start(f32[16,128]{1,0:T(8,128)S(1)} %collective-permute-done.11.hy_hi) | copy-start | bytes 24580

commit v10 on v7

--- a/solution.py
+++ b/solution.py
@@ -348,35 +348,63 @@
 VELOCITY = (0, 1, 2)
 
 
-def pack_kernel(blocks, fw, cw, x_prev, x_next, y_prev, y_next):
-    for b, w in zip(blocks, (fw, cw)):
-        write_rims_split(b, w, x_prev, x_next, y_prev, y_next)
-
-
-def write_rims_split(b, w, x_prev, x_next, y_prev, y_next):
-    size, lanes = b.size, b.lanes
-    for c, field in enumerate(STRESS_X):
+def pack_kernel(blocks, fw, cw, x_prev, x_next, y_prev, y_next, *scratch):
+    sems = scratch[-1]
+    copies, views = [], []
+    for n, (b, w) in enumerate(zip(blocks, (fw, cw))):
+        xs_lo, xs_hi, ys_lo, ys_hi = scratch[4 * n : 4 * n + 4]
+        size, lanes = b.size, b.lanes
+        jobs = []
+        for c, field in enumerate(STRESS_X):
+            jobs.append((w.at[field, :, pl.ds(0, 2), :], xs_lo.at[c]))
+            jobs.append((w.at[field, :, pl.ds(size - 2, 2), :], xs_hi.at[c]))
+        for c, field in enumerate(STRESS_Y):
+            jobs.append((w.at[field, :, :, pl.ds(0, 128)], ys_lo.at[c]))
+            jobs.append((w.at[field, :, :, pl.ds(lanes - 128, 128)], ys_hi.at[c]))
+        for src, dst in jobs:
+            copy = pltpu.make_async_copy(src, dst, sems.at[len(copies)])
+            copy.start()
+            copies.append(copy)
+        views.append((b, xs_lo, xs_hi, ys_lo, ys_hi))
+    for copy in copies:
+        copy.wait()
+    for b, xs_lo, xs_hi, ys_lo, ys_hi in views:
+        size = b.size
+        for c in range(3):
+            for z in range(b.layers):
+                lo = xs_lo[c, z]
+                hi = xs_hi[c, z]
+                for j in range(b.chunks):
+                    row = b.x_base + ((c * b.layers + z) * b.chunks + j) * 2
+                    x_prev[row : row + 2, :] = lo[:, j * 128 : (j + 1) * 128]
+                    x_next[row : row + 2, :] = hi[:, j * 128 : (j + 1) * 128]
+        lane = lax.broadcasted_iota(jnp.int32, (size, 128), 1)
         for z in range(b.layers):
-            lo = w[field, z, 0:2, :]
-            hi = w[field, z, size - 2 : size, :]
-            for j in range(b.chunks):
-                row = b.x_base + ((c * b.layers + z) * b.chunks + j) * 2
-                x_prev[row : row + 2, :] = lo[:, j * 128 : (j + 1) * 128]
-                x_next[row : row + 2, :] = hi[:, j * 128 : (j + 1) * 128]
-    lane = lax.broadcasted_iota(jnp.int32, (size, 128), 1)
-    for z in range(b.layers):
-        acc_lo = jnp.zeros((size, 128), jnp.float32)
-        acc_hi = jnp.zeros((size, 128), jnp.float32)
-        for c, field in enumerate(STRESS_Y):
-            v = w[field, z]
-            rl = v if c == 0 else pltpu.roll(v, 2 * c, 1)
-            rh = pltpu.roll(v, (2 * c + 2) % lanes, 1)
-            keep = (lane >= 2 * c) & (lane < 2 * c + 2)
-            acc_lo = jnp.where(keep, rl[:, 0:128], acc_lo)
-            acc_hi = jnp.where(keep, rh[:, 0:128], acc_hi)
-        row = b.y_base + z * size
-        y_prev[row : row + size, :] = acc_lo
-        y_next[row : row + size, :] = acc_hi
+            acc_lo = jnp.zeros((size, 128), jnp.float32)
+            acc_hi = jnp.zeros((size, 128), jnp.float32)
+            for c in range(3):
+                vl = ys_lo[c, z]
+                vh = ys_hi[c, z]
+                rl = vl if c == 0 else pltpu.roll(vl, 2 * c, 1)
+                rh = pltpu.roll(vh, (2 * c + 2) % 128, 1)
+                keep_lanes = (lane >= 2 * c) & (lane < 2 * c + 2)
+                acc_lo = jnp.where(keep_lanes, rl, acc_lo)
+                acc_hi = jnp.where(keep_lanes, rh, acc_hi)
+            row = b.y_base + z * size
+            y_prev[row : row + size, :] = acc_lo
+            y_next[row : row + size, :] = acc_hi
+
+
+def pack_scratch(blocks):
+    shapes = []
+    for b in blocks:
+        shapes += [
+            pltpu.VMEM((3, b.layers, 2, b.lanes), jnp.float32),
+            pltpu.VMEM((3, b.layers, 2, b.lanes), jnp.float32),
+            pltpu.VMEM((3, b.layers, b.size, 128), jnp.float32),
+            pltpu.VMEM((3, b.layers, b.size, 128), jnp.float32),
+        ]
+    return shapes + [pltpu.SemaphoreType.DMA((12 * len(blocks),))]
 
 
 def velocity_block(b, w, mat, metric, table, out, sx, hx_lo, hx_hi, hy_lo, hy_hi, valid):
@@ -710,8 +738,9 @@
     rims = pl.pallas_call(
         functools.partial(pack_kernel, blocks),
         out_shape=halo_shapes(x_rows, y_rows),
-        in_specs=vmem_specs(2),
+        in_specs=[pl.BlockSpec(memory_space=pl.ANY)] * 2,
         out_specs=tuple(vmem_specs(4)),
+        scratch_shapes=pack_scratch(blocks),
     )(fine_wave, coarse_wave)
     halos = receive(rims)
 

time: 48.1 us -> 48 us (level)
  no operation moved by 1% of the time
where the time goes in v10:
time: 48 us; the launch traced here: 47.7 us
  starting transfers between devices  21.3 us (44%)
  Pallas kernels  13.2 us (28%)
  waiting for transfers between devices  6.71 us (14%)
  local copies, waits for them, and re-layouts  3.17 us (7%)
  other arithmetic  2.54 us (5%)
  between operations  0.77 us (2%)
    ppermute x12, starting transfers between devices, shift_from(): return lax.ppermute(block, axis, pairs)  21.3 us
    ppermute x12, waiting for transfers between devices, shift_from(): return lax.ppermute(block, axis, pairs)  6.71 us
    pallas_call x1, Pallas kernels, local(): pl.pallas_call(functools.partial(stress_kernel, blocks), out_shape=(f32(f...  5.1 us
    pallas_call x1, Pallas kernels, local(): pl.pallas_call(functools.partial(velocity_kernel, blocks), out_shape=(f32...  3.84 us
    unnamed x24, local copies, waits for them, and re-layouts  2.61 us
    pallas_call x1, Pallas kernels, face_call(): pl.pallas_call(functools.partial(face_kernel, blocks, fine.layers - 1), o...  2.19 us
    pallas_call x1, Pallas kernels, local(): pl.pallas_call(functools.partial(pack_kernel, blocks), out_shape=halo_sha...  2.1 us
    concatenate x2, other arithmetic, with_corners(): joined = jnp.concatenate([y_rim, extra])  1.37 us
  transfers between devices with their start and end apart: 12, of which 5 were waited for; matrix products, arithmetic and copies ran while one was open for 2% of the time, Pallas kernels for 0%

profile of v10, /device:TPU:1, one launch (start us, length us, event | category | flops | bytes accessed | tf_op | source)
XLA Modules:
  0.0 47.7 jit_solution(16601495121228108963)
XLA Ops:
  0.6 2.1 %shard_map.156 = (f32[264,128]{1,0:T(8,128)}, f32[264,128]{1,0:T(8,128)}, f32[88,128]{1,0:T(8,128)}, f32[88,128]{1,0:T(8,128)}) custom-call(f32[9,12,6,384]{3,2,1,0:T(8,128)} %fw.5, f32[9,8,2,128]{3,2,1,0:T(2,128)} %cw.5), custom_call_target="tpu_custom_call" | custom-call | tf_op jit(solution)/shard_map/pallas_call | solution.py:738
  2.7 2.6 %collective-permute-start = (f32[264,128]{1,0:T(8,128)}, f32[264,128]{1,0:T(8,128)S(1)}, u32[]{:S(2)}, u32[]{:S(2)}) collective-permute-start(f32[264,128]{1,0:T(8,128)} %get-tuple-element.26), channel_id=1, source_target_pairs={{0,8},{8,16},{16,24},{24,0},{1,9},{9,17},{17,25},{25,1},{2,10},{10... | collective-permute-start | bytes 405512 | tf_op jit(solution)/shard_map/ppermute | solution.py:44
  5.4 1.2 %collective-permute-start.2 = (f32[88,128]{1,0:T(8,128)}, f32[88,128]{1,0:T(8,128)S(1)}, u32[]{:S(2)}, u32[]{:S(2)}) collective-permute-start(f32[88,128]{1,0:T(8,128)} %get-tuple-element.28), channel_id=1, source_target_pairs={{0,1},{1,2},{2,3},{3,4},{4,5},{5,6},{6,7},{7,0},{8,9},{9,10},{10,1... | collective-permute-start | bytes 135176 | tf_op jit(solution)/shard_map/ppermute | solution.py:44
  6.6 3.0 %collective-permute-start.3 = (f32[88,128]{1,0:T(8,128)}, f32[88,128]{1,0:T(8,128)S(1)}, u32[]{:S(2)}, u32[]{:S(2)}) collective-permute-start(f32[88,128]{1,0:T(8,128)} %get-tuple-element.29), channel_id=1, source_target_pairs={{0,7},{1,0},{2,1},{3,2},{4,3},{5,4},{6,5},{7,6},{8,15},{9,8},{10,9... | collective-permute-start | bytes 135176 | tf_op jit(solution)/shard_map/ppermute | solution.py:44
  9.7 0.6 %add_convert_fusion.flags = s32[4]{0:T(128)} fusion(pred[1]{0:T(512)(128)(4,1)} %bitcast.3, pred[1]{0:T(512)(128)(4,1)} %bitcast.2, pred[1]{0:T(512)(128)(4,1)} %bitcast.1, pred[1]{0:T(512)(128)(4,1)} %bitcast), kind=kLoop, calls=%fused_computation.9 | loop fusion | flops 16 | bytes 20 | tf_op jit(solution)/shard_map/convert_element_type | solution.py:50
  10.3 1.1 %collective-permute-done.2.hy_lo = f32[88,128]{1,0:T(8,128)S(1)} collective-permute-done((f32[88,128]{1,0:T(8,128)}, f32[88,128]{1,0:T(8,128)S(1)}, u32[]{:S(2)}, u32[]{:S(2)}) %collective-permute-start.2) | collective-permute-done | bytes 45088 | tf_op jit(solution)/shard_map/ppermute | solution.py:44
  11.4 0.6 %copy-done.6 = f32[88,128]{1,0:T(8,128)} copy-done((f32[88,128]{1,0:T(8,128)}, f32[88,128]{1,0:T(8,128)S(1)}, u32[]{:S(2)}) %copy-start.6) | copy-done | bytes 45080
  12.1 0.7 %copy-done.1 = f32[264,128]{1,0:T(8,128)} copy-done((f32[264,128]{1,0:T(8,128)}, f32[264,128]{1,0:T(8,128)S(1)}, u32[]{:S(2)}) %copy-start.1) | copy-done | bytes 135192
  12.7 3.8 %shard_map.157 = (f32[3,12,6,384]{3,2,1,0:T(8,128)}, f32[3,8,2,128]{3,2,1,0:T(2,128)}, f32[264,128]{1,0:T(8,128)}, f32[264,128]{1,0:T(8,128)}, f32[88,128]{1,0:T(8,128)}, /*index=5*/f32[88,128]{1,0:T(8,128)}) custom-call(f32[9,12,6,384]{3,2,1,0:T(8,128)} %fw.5, f32[9,8,2,128]{3,2,1,0:T(2,128)} %cw.5, f32[264,128]{1,0:T(8,128)} %copy-done, ...), custom_call_target="tpu_custom_call" | custom-call | tf_op jit(solution)/shard_map/pallas_call | solution.py:747
  16.6 2.7 %collective-permute-start.4 = (f32[264,128]{1,0:T(8,128)}, f32[264,128]{1,0:T(8,128)S(1)}, u32[]{:S(2)}, u32[]{:S(2)}) collective-permute-start(f32[264,128]{1,0:T(8,128)} %get-tuple-element.32), channel_id=1, source_target_pairs={{0,8},{8,16},{16,24},{24,0},{1,9},{9,17},{17,25},{25,1},{2,10},{10... | collective-permute-start | bytes 405512 | tf_op jit(solution)/shard_map/ppermute | solution.py:44
  19.3 0.9 %collective-permute-start.6 = (f32[88,128]{1,0:T(8,128)}, f32[88,128]{1,0:T(8,128)S(1)}, u32[]{:S(2)}, u32[]{:S(2)}) collective-permute-start(f32[88,128]{1,0:T(8,128)} %get-tuple-element.34), channel_id=1, source_target_pairs={{0,1},{1,2},{2,3},{3,4},{4,5},{5,6},{6,7},{7,0},{8,9},{9,10},{10,1... | collective-permute-start | bytes 135176 | tf_op jit(solution)/shard_map/ppermute | solution.py:44
  20.2 3.5 %collective-permute-start.7 = (f32[88,128]{1,0:T(8,128)}, f32[88,128]{1,0:T(8,128)S(1)}, u32[]{:S(2)}, u32[]{:S(2)}) collective-permute-start(f32[88,128]{1,0:T(8,128)} %get-tuple-element.35), channel_id=1, source_target_pairs={{0,7},{1,0},{2,1},{3,2},{4,3},{5,4},{6,5},{7,6},{8,15},{9,8},{10,9... | collective-permute-start | bytes 135176 | tf_op jit(solution)/shard_map/ppermute | solution.py:44
  23.7 1.6 %collective-permute-done.6.hy_lo = f32[88,128]{1,0:T(8,128)S(1)} collective-permute-done((f32[88,128]{1,0:T(8,128)}, f32[88,128]{1,0:T(8,128)S(1)}, u32[]{:S(2)}, u32[]{:S(2)}) %collective-permute-start.6) | collective-permute-done | bytes 45088 | tf_op jit(solution)/shard_map/ppermute | solution.py:44
  25.4 0.6 %copy-done.8 = f32[88,128]{1,0:T(8,128)} copy-done((f32[88,128]{1,0:T(8,128)}, f32[88,128]{1,0:T(8,128)S(1)}, u32[]{:S(2)}) %copy-start.8) | copy-done | bytes 45080
  26.1 5.1 %shard_map.158 = (f32[9,12,6,384]{3,2,1,0:T(8,128)}, f32[6,12,6,384]{3,2,1,0:T(8,128)}, f32[6,6,384]{2,1,0:T(8,128)}, f32[9,8,2,128]{3,2,1,0:T(2,128)}, f32[6,8,...) custom-call(f32[9,12,6,384]{3,2,1,0:T(8,128)} %fw.5, ...), custom_call_target="tpu_custom_call" | custom-call | tf_op jit(solution)/shard_map/pallas_call | solution.py:758
  31.2 2.7 %collective-permute-start.8 = (f32[24,128]{1,0:T(8,128)}, f32[24,128]{1,0:T(8,128)S(1)}, u32[]{:S(2)}, u32[]{:S(2)}) collective-permute-start(f32[24,128]{1,0:T(8,128)} %get-tuple-element.40), channel_id=1, source_target_pairs={{0,8},{8,16},{16,24},{24,0},{1,9},{9,17},{17,25},{25,1},{2,10},{10... | collective-permute-start | bytes 36872 | tf_op jit(solution)/shard_map/ppermute | solution.py:44
  33.9 1.0 %collective-permute-done.8.hx_lo = f32[24,128]{1,0:T(8,128)S(1)} collective-permute-done((f32[24,128]{1,0:T(8,128)}, f32[24,128]{1,0:T(8,128)S(1)}, u32[]{:S(2)}, u32[]{:S(2)}) %collective-permute-start.8) | collective-permute-done | bytes 12320 | tf_op jit(solution)/shard_map/ppermute | solution.py:44
  35.3 1.9 %collective-permute-done.9.hx_hi = f32[24,128]{1,0:T(8,128)S(1)} collective-permute-done((f32[24,128]{1,0:T(8,128)}, f32[24,128]{1,0:T(8,128)S(1)}, u32[]{:S(2)}, u32[]{:S(2)}) %collective-permute-start.9) | collective-permute-done | bytes 12320 | tf_op jit(solution)/shard_map/ppermute | solution.py:44
  38.0 0.7 %select_maximum_fusion = f32[12,128]{1,0:T(8,128)S(1)} fusion(f32[4,6]{1,0:T(4,128)S(1)} %bitcast.22, f32[8,128]{1,0:T(8,128)} %get-tuple-element.43), kind=kLoop, calls=%fused_computation | loop fusion | flops 4608 | bytes 10336 | tf_op jit(solution)/shard_map/concatenate | solution.py:689
  38.7 0.7 %select_maximum_fusion.1 = f32[12,128]{1,0:T(8,128)S(1)} fusion(f32[4,6]{1,0:T(4,128)S(1)} %bitcast.23, f32[8,128]{1,0:T(8,128)} %get-tuple-element.42), kind=kLoop, calls=%fused_computation.1 | loop fusion | flops 4608 | bytes 10336 | tf_op jit(solution)/shard_map/concatenate | solution.py:689
  39.4 4.5 %collective-permute-start.11 = (f32[16,128]{1,0:T(8,128)S(1)}, f32[16,128]{1,0:T(8,128)S(1)}, u32[]{:S(2)}, u32[]{:S(2)}) collective-permute-start(f32[16,128]{1,0:T(8,128)S(1)} %pad.17), channel_id=1, source_target_pairs={{0,7},{1,0},{2,1},{3,2},{4,3},{5,4},{6,5},{7,6},{8,15},{9,8},{10,9... | collective-permute-start | bytes 24584 | tf_op jit(solution)/shard_map/ppermute | solution.py:44
  43.9 1.0 %collective-permute-done.10.hy_lo = f32[16,128]{1,0:T(8,128)S(1)} collective-permute-done((f32[16,128]{1,0:T(8,128)S(1)}, f32[16,128]{1,0:T(8,128)S(1)}, u32[]{:S(2)}, u32[]{:S(2)}) %collective-permute-start.10) | collective-permute-done | bytes 8224 | tf_op jit(solution)/shard_map/ppermute | solution.py:44
  44.9 0.6 %copy-done.10 = f32[16,128]{1,0:T(8,128)} copy-done((f32[16,128]{1,0:T(8,128)}, f32[16,128]{1,0:T(8,128)S(1)}, u32[]{:S(2)}) %copy-start.10) | copy-done | bytes 8216
  45.5 2.2 %shard_map.159 = (f32[9,12,6,384]{3,2,1,0:T(8,128)}, f32[9,8,2,128]{3,2,1,0:T(2,128)}) custom-call(f32[9,12,6,384]{3,2,1,0:T(8,128)} %get-tuple-element.36.fout_in, f32[9,8,2,128]{3,2,1,0:T(2,128)} %get-tuple-element.37.cout_in, f32[6,6,384]{2,1,0:T(8,128)} %get-tuple-element.38.fface, ...), custom_call_target="tpu_custom_call", output_to_operand_aliasing={{0}: (0, {}), {1}: (1, {})} | custom-call | tf_op jit(solution)/shard_map/pallas_call | solution.py:704
  (49 shorter events, 1.4 us)
Async XLA Ops:
  2.7 8.7 %collective-permute-start = (f32[264,128]{1,0:T(8,128)}, f32[264,128]{1,0:T(8,128)S(1)}, u32[]{:S(2)}, u32[]{:S(2)}) collective-permute-start(f32[264,128]{1,0:T(8,128)} %get-tuple-element.26), channel_id=1, source_target_pairs={{0,8},{8,16},{16,24},{24,0},{1,9},{9,17},{17,25},{25,1},{2,10},{10... | collective-permute-start | bytes 405512 | tf_op jit(solution)/shard_map/ppermute | solution.py:44
  5.4 6.1 %collective-permute-start.1 = (f32[264,128]{1,0:T(8,128)}, f32[264,128]{1,0:T(8,128)S(1)}, u32[]{:S(2)}, u32[]{:S(2)}) collective-permute-start(f32[264,128]{1,0:T(8,128)} %get-tuple-element.27), channel_id=1, source_target_pairs={{0,24},{8,0},{16,8},{24,16},{1,25},{9,1},{17,9},{25,17},{2,26},{10... | collective-permute-start | bytes 405512 | tf_op jit(solution)/shard_map/ppermute | solution.py:44
  5.4 6.0 %collective-permute-start.2 = (f32[88,128]{1,0:T(8,128)}, f32[88,128]{1,0:T(8,128)S(1)}, u32[]{:S(2)}, u32[]{:S(2)}) collective-permute-start(f32[88,128]{1,0:T(8,128)} %get-tuple-element.28), channel_id=1, source_target_pairs={{0,1},{1,2},{2,3},{3,4},{4,5},{5,6},{6,7},{7,0},{8,9},{9,10},{10,1... | collective-permute-start | bytes 135176 | tf_op jit(solution)/shard_map/ppermute | solution.py:44
  6.6 4.8 %collective-permute-start.3 = (f32[88,128]{1,0:T(8,128)}, f32[88,128]{1,0:T(8,128)S(1)}, u32[]{:S(2)}, u32[]{:S(2)}) collective-permute-start(f32[88,128]{1,0:T(8,128)} %get-tuple-element.29), channel_id=1, source_target_pairs={{0,7},{1,0},{2,1},{3,2},{4,3},{5,4},{6,5},{7,6},{8,15},{9,8},{10,9... | collective-permute-start | bytes 135176 | tf_op jit(solution)/shard_map/ppermute | solution.py:44
  11.4 0.6 %copy-start.6 = (f32[88,128]{1,0:T(8,128)}, f32[88,128]{1,0:T(8,128)S(1)}, u32[]{:S(2)}) copy-start(f32[88,128]{1,0:T(8,128)S(1)} %collective-permute-done.2.hy_lo) | copy-start | bytes 135172
  11.4 0.6 %copy-start.7 = (f32[88,128]{1,0:T(8,128)}, f32[88,128]{1,0:T(8,128)S(1)}, u32[]{:S(2)}) copy-start(f32[88,128]{1,0:T(8,128)S(1)} %collective-permute-done.3.hy_hi) | copy-start | bytes 135172
  11.4 0.7 %copy-start = (f32[264,128]{1,0:T(8,128)}, f32[264,128]{1,0:T(8,128)S(1)}, u32[]{:S(2)}) copy-start(f32[264,128]{1,0:T(8,128)S(1)} %collective-permute-done.hx_lo) | copy-start | bytes 405508
  12.1 0.7 %copy-start.1 = (f32[264,128]{1,0:T(8,128)}, f32[264,128]{1,0:T(8,128)S(1)}, u32[]{:S(2)}) copy-start(f32[264,128]{1,0:T(8,128)S(1)} %collective-permute-done.1.hx_hi) | copy-start | bytes 405508
  16.6 8.8 %collective-permute-start.4 = (f32[264,128]{1,0:T(8,128)}, f32[264,128]{1,0:T(8,128)S(1)}, u32[]{:S(2)}, u32[]{:S(2)}) collective-permute-start(f32[264,128]{1,0:T(8,128)} %get-tuple-element.32), channel_id=1, source_target_pairs={{0,8},{8,16},{16,24},{24,0},{1,9},{9,17},{17,25},{25,1},{2,10},{10... | collective-permute-start | bytes 405512 | tf_op jit(solution)/shard_map/ppermute | solution.py:44
  19.3 6.1 %collective-permute-start.5 = (f32[264,128]{1,0:T(8,128)}, f32[264,128]{1,0:T(8,128)S(1)}, u32[]{:S(2)}, u32[]{:S(2)}) collective-permute-start(f32[264,128]{1,0:T(8,128)} %get-tuple-element.33), channel_id=1, source_target_pairs={{0,24},{8,0},{16,8},{24,16},{1,25},{9,1},{17,9},{25,17},{2,26},{10... | collective-permute-start | bytes 405512 | tf_op jit(solution)/shard_map/ppermute | solution.py:44
  19.3 6.1 %collective-permute-start.6 = (f32[88,128]{1,0:T(8,128)}, f32[88,128]{1,0:T(8,128)S(1)}, u32[]{:S(2)}, u32[]{:S(2)}) collective-permute-start(f32[88,128]{1,0:T(8,128)} %get-tuple-element.34), channel_id=1, source_target_pairs={{0,1},{1,2},{2,3},{3,4},{4,5},{5,6},{6,7},{7,0},{8,9},{9,10},{10,1... | collective-permute-start | bytes 135176 | tf_op jit(solution)/shard_map/ppermute | solution.py:44
  20.2 5.1 %collective-permute-start.7 = (f32[88,128]{1,0:T(8,128)}, f32[88,128]{1,0:T(8,128)S(1)}, u32[]{:S(2)}, u32[]{:S(2)}) collective-permute-start(f32[88,128]{1,0:T(8,128)} %get-tuple-element.35), channel_id=1, source_target_pairs={{0,7},{1,0},{2,1},{3,2},{4,3},{5,4},{6,5},{7,6},{8,15},{9,8},{10,9... | collective-permute-start | bytes 135176 | tf_op jit(solution)/shard_map/ppermute | solution.py:44
  25.4 0.6 %copy-start.8 = (f32[88,128]{1,0:T(8,128)}, f32[88,128]{1,0:T(8,128)S(1)}, u32[]{:S(2)}) copy-start(f32[88,128]{1,0:T(8,128)S(1)} %collective-permute-done.6.hy_lo) | copy-start | bytes 135172
  25.4 0.6 %copy-start.9 = (f32[88,128]{1,0:T(8,128)}, f32[88,128]{1,0:T(8,128)S(1)}, u32[]{:S(2)}) copy-start(f32[88,128]{1,0:T(8,128)S(1)} %collective-permute-done.7.hy_hi) | copy-start | bytes 135172
  25.4 0.7 %copy-start.2 = (f32[264,128]{1,0:T(8,128)}, f32[264,128]{1,0:T(8,128)S(1)}, u32[]{:S(2)}) copy-start(f32[264,128]{1,0:T(8,128)S(1)} %collective-permute-done.4.hx_lo) | copy-start | bytes 405508
  25.4 0.7 %copy-start.3 = (f32[264,128]{1,0:T(8,128)}, f32[264,128]{1,0:T(8,128)S(1)}, u32[]{:S(2)}) copy-start(f32[264,128]{1,0:T(8,128)S(1)} %collective-permute-done.5.hx_hi) | copy-start | bytes 405508
  31.2 3.7 %collective-permute-start.8 = (f32[24,128]{1,0:T(8,128)}, f32[24,128]{1,0:T(8,128)S(1)}, u32[]{:S(2)}, u32[]{:S(2)}) collective-permute-start(f32[24,128]{1,0:T(8,128)} %get-tuple-element.40), channel_id=1, source_target_pairs={{0,8},{8,16},{16,24},{24,0},{1,9},{9,17},{17,25},{25,1},{2,10},{10... | collective-permute-start | bytes 36872 | tf_op jit(solution)/shard_map/ppermute | solution.py:44
  33.9 3.3 %collective-permute-start.9 = (f32[24,128]{1,0:T(8,128)}, f32[24,128]{1,0:T(8,128)S(1)}, u32[]{:S(2)}, u32[]{:S(2)}) collective-permute-start(f32[24,128]{1,0:T(8,128)} %get-tuple-element.41), channel_id=1, source_target_pairs={{0,24},{8,0},{16,8},{24,16},{1,25},{9,1},{17,9},{25,17},{2,26},{10... | collective-permute-start | bytes 36872 | tf_op jit(solution)/shard_map/ppermute | solution.py:44
  34.9 10.0 %copy-start.4 = (f32[24,128]{1,0:T(8,128)}, f32[24,128]{1,0:T(8,128)S(1)}, u32[]{:S(2)}) copy-start(f32[24,128]{1,0:T(8,128)S(1)} %collective-permute-done.8.hx_lo) | copy-start | bytes 36868
  37.2 7.7 %copy-start.5 = (f32[24,128]{1,0:T(8,128)}, f32[24,128]{1,0:T(8,128)S(1)}, u32[]{:S(2)}) copy-start(f32[24,128]{1,0:T(8,128)S(1)} %collective-permute-done.9.hx_hi) | copy-start | bytes 36868
  39.4 5.5 %collective-permute-start.10 = (f32[16,128]{1,0:T(8,128)S(1)}, f32[16,128]{1,0:T(8,128)S(1)}, u32[]{:S(2)}, u32[]{:S(2)}) collective-permute-start(f32[16,128]{1,0:T(8,128)S(1)} %pad.15), channel_id=1, source_target_pairs={{0,1},{1,2},{2,3},{3,4},{4,5},{5,6},{6,7},{7,0},{8,9},{9,10},{10,1... | collective-permute-start | bytes 24584 | tf_op jit(solution)/shard_map/ppermute | solution.py:44
  39.4 5.5 %collective-permute-start.11 = (f32[16,128]{1,0:T(8,128)S(1)}, f32[16,128]{1,0:T(8,128)S(1)}, u32[]{:S(2)}, u32[]{:S(2)}) collective-permute-start(f32[16,128]{1,0:T(8,128)S(1)} %pad.17), channel_id=1, source_target_pairs={{0,7},{1,0},{2,1},{3,2},{4,3},{5,4},{6,5},{7,6},{8,15},{9,8},{10,9... | collective-permute-start | bytes 24584 | tf_op jit(solution)/shard_map/ppermute | solution.py:44
  44.9 0.6 %copy-start.10 = (f32[16,128]{1,0:T(8,128)}, f32[16,128]{1,0:T(8,128)S(1)}, u32[]{:S(2)}) copy-start(f32[16,128]{1,0:T(8,128)S(1)} %collective-permute-done.10.hy_lo) | copy-start | bytes 24580
  44.9 0.6 %copy-start.11 = (f32[16,128]{1,0:T(8,128)}, f32[16,128]{1,0:T(8,128)S(1)}, u32[]{:S(2)}) copy-start(f32[16,128]{1,0:T(8,128)S(1)} %collective-permute-done.11.hy_hi) | copy-start | bytes 24580

commit v11 on v7

--- a/solution.py
+++ b/solution.py
@@ -1,11 +1,11 @@
 import functools
-import math
 
 import jax
 import jax.numpy as jnp
 import numpy as np
 from jax import lax
 from jax.sharding import PartitionSpec as P
+
 
 step_size = 0.1
 penalty = 0.1 * 48.0 / 17.0
@@ -15,10 +15,6 @@
     [4.0 / 43.0, -59.0 / 86.0, 0.0, 59.0 / 86.0, -4.0 / 43.0, 0.0],
     [3.0 / 98.0, 0.0, -59.0 / 98.0, 0.0, 32.0 / 49.0, -4.0 / 49.0],
 ]
-
-
-def sbp_table(layers, spacing):
-    return jnp.asarray(sbp_numpy(layers, spacing))
 
 
 def sbp_numpy(layers, spacing):
@@ -58,157 +54,6 @@
     return jnp.where(ok, value, 0.0)
 
 
-def packed_shift(blocks, axis, offset):
-    sizes = [math.prod(b.shape) for b in blocks]
-    joined = jnp.concatenate([b.reshape(-1) for b in blocks])
-    moved = shift_from(joined, axis, offset)
-    out, start = [], 0
-    for b, size in zip(blocks, sizes):
-        out.append(moved[start : start + size].reshape(b.shape))
-        start += size
-    return out
-
-
-def exchange(blocks, width):
-    x_lo = packed_shift([b[..., -width:, :] for b in blocks], "gx", 1)
-    x_hi = packed_shift([b[..., :width, :] for b in blocks], "gx", -1)
-    y_lo = packed_shift([b[..., -width:] for b in blocks], "gy", 1)
-    y_hi = packed_shift([b[..., :width] for b in blocks], "gy", -1)
-    return [(x_lo[i], x_hi[i], y_lo[i], y_hi[i]) for i in range(len(blocks))]
-
-
-def central_diff(padded, along, spacing):
-    length = padded.shape[along] - 4
-    s = lambda o: lax.slice_in_dim(padded, o, o + length, axis=along)
-    return (s(0) - 8.0 * s(1) + 8.0 * s(3) - s(4)) / (12.0 * spacing)
-
-
-def diff_x(block, halo, spacing):
-    x_lo, x_hi, _, _ = halo
-    return central_diff(jnp.concatenate([x_lo, block, x_hi], axis=-2), block.ndim - 2, spacing)
-
-
-def diff_y(block, halo, spacing):
-    _, _, y_lo, y_hi = halo
-    return central_diff(jnp.concatenate([y_lo, block, y_hi], axis=-1), block.ndim - 1, spacing)
-
-
-def vertical_diff(fields, matrix):
-    return jnp.einsum("kz,czxy->ckxy", matrix, fields, precision=lax.Precision.HIGHEST)
-
-
-def lookup_table(grid_cell_index, values):
-    result = jnp.zeros(grid_cell_index.shape, jnp.float32)
-    for kind_at in range(values.shape[0]):
-        result = jnp.where(grid_cell_index == kind_at, values[kind_at], result)
-    return result
-
-
-def velocity_step(wave, halo_x3, halo_y3, buoyancy, metric, matrix, spacing):
-    sx = jnp.stack([wave[3], wave[6], wave[7]])
-    sy = jnp.stack([wave[6], wave[4], wave[8]])
-    slope_x = diff_x(sx, halo_x3, spacing)
-    slope_y = diff_y(sy, halo_y3, spacing)
-    slope_z = metric * vertical_diff(jnp.stack([wave[7], wave[8], wave[5]]), matrix)
-    rate_x = slope_x[0] + slope_y[0] + slope_z[0]
-    rate_y = slope_x[1] + slope_y[1] + slope_z[1]
-    rate_z = slope_x[2] + slope_y[2] + slope_z[2]
-    return wave[:3] + step_size * (buoyancy * jnp.stack([rate_x, rate_y, rate_z]))
-
-
-def stress_step(wave, memory, velocity, halo, lame, shear, decay, strength, metric, matrix, spacing):
-    slope_x = diff_x(velocity, halo, spacing)
-    slope_y = diff_y(velocity, halo, spacing)
-    slope_z = metric * vertical_diff(velocity, matrix)
-    cell_volume = lame * (slope_x[0] + slope_y[1] + slope_z[2])
-    rate = jnp.stack(
-        [
-            cell_volume + 2.0 * shear * slope_x[0],
-            cell_volume + 2.0 * shear * slope_y[1],
-            cell_volume + 2.0 * shear * slope_z[2],
-            shear * (slope_y[0] + slope_x[1]),
-            shear * (slope_z[0] + slope_x[2]),
-            shear * (slope_z[1] + slope_y[2]),
-        ]
-    )
-    memory_new = decay * memory + (1.0 - decay) * strength * rate
-    stress = wave[3:] + step_size * (rate - memory_new)
-    return stress, memory_new
-
-
-def face_of(velocity, stress, depth):
-    return jnp.stack(
-        [
-            velocity[0, depth],
-            velocity[1, depth],
-            velocity[2, depth],
-            stress[4, depth],
-            stress[5, depth],
-            stress[2, depth],
-        ]
-    )
-
-
-def pad_faces(faces):
-    x_lo = packed_shift([f[:, -1:, :] for f in faces], "gx", 1)
-    x_hi = packed_shift([f[:, :1, :] for f in faces], "gx", -1)
-    faces = [jnp.concatenate([lo, f, hi], axis=1) for lo, f, hi in zip(x_lo, faces, x_hi)]
-    y_lo = packed_shift([f[:, :, -1:] for f in faces], "gy", 1)
-    y_hi = packed_shift([f[:, :, :1] for f in faces], "gy", -1)
-    return [jnp.concatenate([lo, f, hi], axis=2) for lo, f, hi in zip(y_lo, faces, y_hi)]
-
-
-def shifted(padded, offset, length, along):
-    return lax.slice_in_dim(padded, offset, offset + length, axis=along)
-
-
-def prolong_axis(padded, along):
-    length = padded.shape[along] - 2
-    left = shifted(padded, 0, length, along)
-    middle = shifted(padded, 1, length, along)
-    right = shifted(padded, 2, length, along)
-    parts = jnp.stack(
-        [(left + 2.0 * middle) / 3.0, middle, (2.0 * middle + right) / 3.0], axis=along + 1
-    )
-    shape = list(middle.shape)
-    shape[along] = shape[along] * 3
-    return parts.reshape(tuple(shape))
-
-
-def split_three(padded, offset, length, along):
-    part = shifted(padded, offset, 3 * length, along)
-    return part.reshape(part.shape[:along] + (length, 3) + part.shape[along + 1 :])
-
-
-def pick_part(parts, number, along):
-    return lax.index_in_dim(parts, number, along + 1, keepdims=False)
-
-
-def restrict_axis(padded, along):
-    length = (padded.shape[along] - 2) // 3
-    first = split_three(padded, 0, length, along)
-    middle = split_three(padded, 1, length, along)
-    last = split_three(padded, 2, length, along)
-    return (
-        pick_part(first, 0, along)
-        + 2.0 * pick_part(middle, 0, along)
-        + 3.0 * pick_part(middle, 1, along)
-        + 2.0 * pick_part(middle, 2, along)
-        + pick_part(last, 2, along)
-    ) / 9.0
-
-
-def assemble(velocity, stress, face, depth):
-    replace = {0: face[0], 1: face[1], 2: face[2], 7: face[3], 8: face[4], 5: face[5]}
-    fields = [velocity[0], velocity[1], velocity[2]] + [stress[k] for k in range(6)]
-    rows = []
-    for k, field in enumerate(fields):
-        if k in replace:
-            field = lax.dynamic_update_slice_in_dim(field, replace[k][None], depth, axis=0)
-        rows.append(field)
-    return jnp.stack(rows)
-
-
 from jax.experimental import pallas as pl
 from jax.experimental.pallas import tpu as pltpu
 
@@ -225,27 +70,9 @@
     return result
 
 
-def fill_x(scratch, slot, lo, block, hi):
-    width = lo.shape[-2]
-    size = block.shape[-2]
-    scratch[slot, :, 0:width, :] = lo
-    scratch[slot, :, width : width + size, :] = block
-    scratch[slot, :, width + size :, :] = hi
-
-
 def slope_x(scratch, slot, z, size, spacing):
     s = lambda o: scratch[slot, z, o : o + size, :]
     return (s(0) - 8.0 * s(1) + 8.0 * s(3) - s(4)) / (12.0 * spacing)
-
-
-def slope_y(f, lo, hi, spacing):
-    n = f.shape[-1]
-    lane = lax.broadcasted_iota(jnp.int32, f.shape, f.ndim - 1)
-    m1 = jnp.where(lane == 0, lo[:, 1:2], pltpu.roll(f, 1, f.ndim - 1))
-    m2 = jnp.where(lane == 0, lo[:, 0:1], jnp.where(lane == 1, lo[:, 1:2], pltpu.roll(f, 2, f.ndim - 1)))
-    p1 = jnp.where(lane == n - 1, hi[:, 0:1], pltpu.roll(f, n - 1, f.ndim - 1))
-    p2 = jnp.where(lane == n - 2, hi[:, 0:1], jnp.where(lane == n - 1, hi[:, 1:2], pltpu.roll(f, n - 2, f.ndim - 1)))
-    return (m2 - 8.0 * m1 + 8.0 * p1 - p2) / (12.0 * spacing)
 
 
 def slope_z(field_ref, index, row):
@@ -257,11 +84,10 @@
 
 
 class Block:
-    def __init__(self, shape, spacing, has_metric, x_base, y_base):
+    def __init__(self, shape, spacing, x_base, y_base):
         self.layers, self.size, self.lanes = shape
         self.chunks = self.lanes // 128
         self.spacing = spacing
-        self.has_metric = has_metric
         self.rows = sbp_rows(self.layers, spacing)
         self.x_base, self.y_base = x_base, y_base
 
@@ -275,8 +101,8 @@
 
 
 def plan_blocks(fine_shape, coarse_shape):
-    fine = Block(fine_shape, 1.0, True, 0, 0)
-    coarse = Block(coarse_shape, 3.0, False, fine.x_rows, fine.y_rows)
+    fine = Block(fine_shape, 1.0, 0, 0)
+    coarse = Block(coarse_shape, 3.0, fine.x_rows, fine.y_rows)
     fine.fx_base, fine.fy_base = 0, 0
     coarse.fx_base, coarse.fy_base = 6 * fine.chunks, fine.size
     corner_base = fine.size + coarse.size
@@ -506,13 +332,6 @@
     x_lo = shift_from(x_next, "gx", 1)
     x_hi = shift_from(x_prev, "gx", -1)
     return x_lo, x_hi, y_lo, y_hi
-
-
-def put_face(out, face, depth):
-    out = lax.dynamic_update_slice(out, face[0:3][:, None], (0, depth, 0, 0))
-    out = lax.dynamic_update_slice(out, face[5:6][:, None], (5, depth, 0, 0))
-    out = lax.dynamic_update_slice(out, face[3:5][:, None], (7, depth, 0, 0))
-    return out
 
 
 def prolong_y_matrix(coarse_lanes):
@@ -634,16 +453,6 @@
         copy.wait()
 
 
-def diag_from(block, dx, dy):
-    nx, ny = lax.axis_size("gx"), lax.axis_size("gy")
-    pairs = []
-    for i in range(nx):
-        for j in range(ny):
-            if 0 <= i + dx < nx and 0 <= j + dy < ny:
-                pairs.append((i * ny + j, (i + dx) * ny + (j + dy)))
-    return lax.ppermute(block, ("gx", "gy"), pairs)
-
-
 def row_ends(buf, blocks, at_end):
     out = []
     for b in blocks:
@@ -764,4 +573,5 @@
         P(None, None, "gx", "gy"),
         P(None, None, "gx", "gy"),
     )
+
     return jax.shard_map(local, mesh=mesh, in_specs=in_specs, out_specs=out_specs, check_vma=False)

time: 48.1 us -> 48.1 us (level)
  no operation moved by 1% of the time
where the time goes in v11:
time: 48.1 us; the launch traced here: 47.8 us
  starting transfers between devices  21.2 us (44%)
  Pallas kernels  13.4 us (28%)
  waiting for transfers between devices  6.71 us (14%)
  local copies, waits for them, and re-layouts  3.17 us (7%)
  other arithmetic  2.54 us (5%)
  between operations  0.77 us (2%)
    ppermute x12, starting transfers between devices, shift_from(): return lax.ppermute(block, axis, pairs)  21.2 us
    ppermute x12, waiting for transfers between devices, shift_from(): return lax.ppermute(block, axis, pairs)  6.71 us
    pallas_call x1, Pallas kernels, local(): pl.pallas_call(functools.partial(stress_kernel, blocks), out_shape=(f32(f...  5.1 us
    pallas_call x1, Pallas kernels, local(): pl.pallas_call(functools.partial(velocity_kernel, blocks), out_shape=(f32...  3.84 us
    unnamed x24, local copies, waits for them, and re-layouts  2.61 us
    pallas_call x1, Pallas kernels, local(): pl.pallas_call(functools.partial(pack_kernel, blocks), out_shape=halo_sha...  2.25 us
    pallas_call x1, Pallas kernels, face_call(): pl.pallas_call(functools.partial(face_kernel, blocks, fine.layers - 1), o...  2.19 us
    concatenate x2, other arithmetic, with_corners(): joined = jnp.concatenate([y_rim, extra])  1.37 us
  transfers between devices with their start and end apart: 12, of which 5 were waited for; matrix products, arithmetic and copies ran while one was open for 2% of the time, Pallas kernels for 0%

profile of v11, /device:TPU:1, one launch (start us, length us, event | category | flops | bytes accessed | tf_op | source)
XLA Modules:
  0.0 47.8 jit_solution(7435459537857785375)
XLA Ops:
  0.6 2.2 %shard_map.156 = (f32[264,128]{1,0:T(8,128)}, f32[264,128]{1,0:T(8,128)}, f32[88,128]{1,0:T(8,128)}, f32[88,128]{1,0:T(8,128)}) custom-call(f32[9,12,6,384]{3,2,1,0:T(8,128)} %fw.5, f32[9,8,2,128]{3,2,1,0:T(2,128)} %cw.5), custom_call_target="tpu_custom_call" | custom-call | tf_op jit(solution)/shard_map/pallas_call | solution.py:519
  2.9 2.6 %collective-permute-start = (f32[264,128]{1,0:T(8,128)}, f32[264,128]{1,0:T(8,128)S(1)}, u32[]{:S(2)}, u32[]{:S(2)}) collective-permute-start(f32[264,128]{1,0:T(8,128)} %get-tuple-element.26), channel_id=1, source_target_pairs={{0,8},{8,16},{16,24},{24,0},{1,9},{9,17},{17,25},{25,1},{2,10},{10... | collective-permute-start | bytes 405512 | tf_op jit(solution)/shard_map/ppermute | solution.py:40
  5.5 1.2 %collective-permute-start.2 = (f32[88,128]{1,0:T(8,128)}, f32[88,128]{1,0:T(8,128)S(1)}, u32[]{:S(2)}, u32[]{:S(2)}) collective-permute-start(f32[88,128]{1,0:T(8,128)} %get-tuple-element.28), channel_id=1, source_target_pairs={{0,1},{1,2},{2,3},{3,4},{4,5},{5,6},{6,7},{7,0},{8,9},{9,10},{10,1... | collective-permute-start | bytes 135176 | tf_op jit(solution)/shard_map/ppermute | solution.py:40
  6.7 3.0 %collective-permute-start.3 = (f32[88,128]{1,0:T(8,128)}, f32[88,128]{1,0:T(8,128)S(1)}, u32[]{:S(2)}, u32[]{:S(2)}) collective-permute-start(f32[88,128]{1,0:T(8,128)} %get-tuple-element.29), channel_id=1, source_target_pairs={{0,7},{1,0},{2,1},{3,2},{4,3},{5,4},{6,5},{7,6},{8,15},{9,8},{10,9... | collective-permute-start | bytes 135176 | tf_op jit(solution)/shard_map/ppermute | solution.py:40
  9.8 0.6 %add_convert_fusion.flags = s32[4]{0:T(128)} fusion(pred[1]{0:T(512)(128)(4,1)} %bitcast.3, pred[1]{0:T(512)(128)(4,1)} %bitcast.2, pred[1]{0:T(512)(128)(4,1)} %bitcast.1, pred[1]{0:T(512)(128)(4,1)} %bitcast), kind=kLoop, calls=%fused_computation.9 | loop fusion | flops 16 | bytes 20 | tf_op jit(solution)/shard_map/convert_element_type | solution.py:46
  10.4 1.1 %collective-permute-done.2.hy_lo = f32[88,128]{1,0:T(8,128)S(1)} collective-permute-done((f32[88,128]{1,0:T(8,128)}, f32[88,128]{1,0:T(8,128)S(1)}, u32[]{:S(2)}, u32[]{:S(2)}) %collective-permute-start.2) | collective-permute-done | bytes 45088 | tf_op jit(solution)/shard_map/ppermute | solution.py:40
  11.5 0.6 %copy-done.6 = f32[88,128]{1,0:T(8,128)} copy-done((f32[88,128]{1,0:T(8,128)}, f32[88,128]{1,0:T(8,128)S(1)}, u32[]{:S(2)}) %copy-start.6) | copy-done | bytes 45080
  12.2 0.7 %copy-done.1 = f32[264,128]{1,0:T(8,128)} copy-done((f32[264,128]{1,0:T(8,128)}, f32[264,128]{1,0:T(8,128)S(1)}, u32[]{:S(2)}) %copy-start.1) | copy-done | bytes 135192
  12.8 3.8 %shard_map.157 = (f32[3,12,6,384]{3,2,1,0:T(8,128)}, f32[3,8,2,128]{3,2,1,0:T(2,128)}, f32[264,128]{1,0:T(8,128)}, f32[264,128]{1,0:T(8,128)}, f32[88,128]{1,0:T(8,128)}, /*index=5*/f32[88,128]{1,0:T(8,128)}) custom-call(f32[9,12,6,384]{3,2,1,0:T(8,128)} %fw.5, f32[9,8,2,128]{3,2,1,0:T(2,128)} %cw.5, f32[264,128]{1,0:T(8,128)} %copy-done, ...), custom_call_target="tpu_custom_call" | custom-call | tf_op jit(solution)/shard_map/pallas_call | solution.py:527
  16.7 2.7 %collective-permute-start.4 = (f32[264,128]{1,0:T(8,128)}, f32[264,128]{1,0:T(8,128)S(1)}, u32[]{:S(2)}, u32[]{:S(2)}) collective-permute-start(f32[264,128]{1,0:T(8,128)} %get-tuple-element.32), channel_id=1, source_target_pairs={{0,8},{8,16},{16,24},{24,0},{1,9},{9,17},{17,25},{25,1},{2,10},{10... | collective-permute-start | bytes 405512 | tf_op jit(solution)/shard_map/ppermute | solution.py:40
  19.4 0.9 %collective-permute-start.6 = (f32[88,128]{1,0:T(8,128)}, f32[88,128]{1,0:T(8,128)S(1)}, u32[]{:S(2)}, u32[]{:S(2)}) collective-permute-start(f32[88,128]{1,0:T(8,128)} %get-tuple-element.34), channel_id=1, source_target_pairs={{0,1},{1,2},{2,3},{3,4},{4,5},{5,6},{6,7},{7,0},{8,9},{9,10},{10,1... | collective-permute-start | bytes 135176 | tf_op jit(solution)/shard_map/ppermute | solution.py:40
  20.3 3.5 %collective-permute-start.7 = (f32[88,128]{1,0:T(8,128)}, f32[88,128]{1,0:T(8,128)S(1)}, u32[]{:S(2)}, u32[]{:S(2)}) collective-permute-start(f32[88,128]{1,0:T(8,128)} %get-tuple-element.35), channel_id=1, source_target_pairs={{0,7},{1,0},{2,1},{3,2},{4,3},{5,4},{6,5},{7,6},{8,15},{9,8},{10,9... | collective-permute-start | bytes 135176 | tf_op jit(solution)/shard_map/ppermute | solution.py:40
  23.8 1.6 %collective-permute-done.6.hy_lo = f32[88,128]{1,0:T(8,128)S(1)} collective-permute-done((f32[88,128]{1,0:T(8,128)}, f32[88,128]{1,0:T(8,128)S(1)}, u32[]{:S(2)}, u32[]{:S(2)}) %collective-permute-start.6) | collective-permute-done | bytes 45088 | tf_op jit(solution)/shard_map/ppermute | solution.py:40
  25.5 0.6 %copy-done.8 = f32[88,128]{1,0:T(8,128)} copy-done((f32[88,128]{1,0:T(8,128)}, f32[88,128]{1,0:T(8,128)S(1)}, u32[]{:S(2)}) %copy-start.8) | copy-done | bytes 45080
  26.2 5.1 %shard_map.158 = (f32[9,12,6,384]{3,2,1,0:T(8,128)}, f32[6,12,6,384]{3,2,1,0:T(8,128)}, f32[6,6,384]{2,1,0:T(8,128)}, f32[9,8,2,128]{3,2,1,0:T(2,128)}, f32[6,8,...) custom-call(f32[9,12,6,384]{3,2,1,0:T(8,128)} %fw.5, ...), custom_call_target="tpu_custom_call" | custom-call | tf_op jit(solution)/shard_map/pallas_call | solution.py:538
  31.3 2.7 %collective-permute-start.8 = (f32[24,128]{1,0:T(8,128)}, f32[24,128]{1,0:T(8,128)S(1)}, u32[]{:S(2)}, u32[]{:S(2)}) collective-permute-start(f32[24,128]{1,0:T(8,128)} %get-tuple-element.40), channel_id=1, source_target_pairs={{0,8},{8,16},{16,24},{24,0},{1,9},{9,17},{17,25},{25,1},{2,10},{10... | collective-permute-start | bytes 36872 | tf_op jit(solution)/shard_map/ppermute | solution.py:40
  34.0 1.0 %collective-permute-done.8.hx_lo = f32[24,128]{1,0:T(8,128)S(1)} collective-permute-done((f32[24,128]{1,0:T(8,128)}, f32[24,128]{1,0:T(8,128)S(1)}, u32[]{:S(2)}, u32[]{:S(2)}) %collective-permute-start.8) | collective-permute-done | bytes 12320 | tf_op jit(solution)/shard_map/ppermute | solution.py:40
  35.4 1.9 %collective-permute-done.9.hx_hi = f32[24,128]{1,0:T(8,128)S(1)} collective-permute-done((f32[24,128]{1,0:T(8,128)}, f32[24,128]{1,0:T(8,128)S(1)}, u32[]{:S(2)}, u32[]{:S(2)}) %collective-permute-start.9) | collective-permute-done | bytes 12320 | tf_op jit(solution)/shard_map/ppermute | solution.py:40
  38.1 0.7 %select_maximum_fusion = f32[12,128]{1,0:T(8,128)S(1)} fusion(f32[4,6]{1,0:T(4,128)S(1)} %bitcast.22, f32[8,128]{1,0:T(8,128)} %get-tuple-element.43), kind=kLoop, calls=%fused_computation | loop fusion | flops 4608 | bytes 10336 | tf_op jit(solution)/shard_map/concatenate | solution.py:470
  38.8 0.7 %select_maximum_fusion.1 = f32[12,128]{1,0:T(8,128)S(1)} fusion(f32[4,6]{1,0:T(4,128)S(1)} %bitcast.23, f32[8,128]{1,0:T(8,128)} %get-tuple-element.42), kind=kLoop, calls=%fused_computation.1 | loop fusion | flops 4608 | bytes 10336 | tf_op jit(solution)/shard_map/concatenate | solution.py:470
  39.5 4.5 %collective-permute-start.11 = (f32[16,128]{1,0:T(8,128)S(1)}, f32[16,128]{1,0:T(8,128)S(1)}, u32[]{:S(2)}, u32[]{:S(2)}) collective-permute-start(f32[16,128]{1,0:T(8,128)S(1)} %pad.17), channel_id=1, source_target_pairs={{0,7},{1,0},{2,1},{3,2},{4,3},{5,4},{6,5},{7,6},{8,15},{9,8},{10,9... | collective-permute-start | bytes 24584 | tf_op jit(solution)/shard_map/ppermute | solution.py:40
  44.0 1.0 %collective-permute-done.10.hy_lo = f32[16,128]{1,0:T(8,128)S(1)} collective-permute-done((f32[16,128]{1,0:T(8,128)S(1)}, f32[16,128]{1,0:T(8,128)S(1)}, u32[]{:S(2)}, u32[]{:S(2)}) %collective-permute-start.10) | collective-permute-done | bytes 8224 | tf_op jit(solution)/shard_map/ppermute | solution.py:40
  45.0 0.6 %copy-done.10 = f32[16,128]{1,0:T(8,128)} copy-done((f32[16,128]{1,0:T(8,128)}, f32[16,128]{1,0:T(8,128)S(1)}, u32[]{:S(2)}) %copy-start.10) | copy-done | bytes 8216
  45.6 2.2 %shard_map.159 = (f32[9,12,6,384]{3,2,1,0:T(8,128)}, f32[9,8,2,128]{3,2,1,0:T(2,128)}) custom-call(f32[9,12,6,384]{3,2,1,0:T(8,128)} %get-tuple-element.36.fout_in, f32[9,8,2,128]{3,2,1,0:T(2,128)} %get-tuple-element.37.cout_in, f32[6,6,384]{2,1,0:T(8,128)} %get-tuple-element.38.fface, ...), custom_call_target="tpu_custom_call", output_to_operand_aliasing={{0}: (0, {}), {1}: (1, {})} | custom-call | tf_op jit(solution)/shard_map/pallas_call | solution.py:485
  (49 shorter events, 1.4 us)
Async XLA Ops:
  2.9 8.6 %collective-permute-start = (f32[264,128]{1,0:T(8,128)}, f32[264,128]{1,0:T(8,128)S(1)}, u32[]{:S(2)}, u32[]{:S(2)}) collective-permute-start(f32[264,128]{1,0:T(8,128)} %get-tuple-element.26), channel_id=1, source_target_pairs={{0,8},{8,16},{16,24},{24,0},{1,9},{9,17},{17,25},{25,1},{2,10},{10... | collective-permute-start | bytes 405512 | tf_op jit(solution)/shard_map/ppermute | solution.py:40
  5.5 6.1 %collective-permute-start.1 = (f32[264,128]{1,0:T(8,128)}, f32[264,128]{1,0:T(8,128)S(1)}, u32[]{:S(2)}, u32[]{:S(2)}) collective-permute-start(f32[264,128]{1,0:T(8,128)} %get-tuple-element.27), channel_id=1, source_target_pairs={{0,24},{8,0},{16,8},{24,16},{1,25},{9,1},{17,9},{25,17},{2,26},{10... | collective-permute-start | bytes 405512 | tf_op jit(solution)/shard_map/ppermute | solution.py:40
  5.5 6.0 %collective-permute-start.2 = (f32[88,128]{1,0:T(8,128)}, f32[88,128]{1,0:T(8,128)S(1)}, u32[]{:S(2)}, u32[]{:S(2)}) collective-permute-start(f32[88,128]{1,0:T(8,128)} %get-tuple-element.28), channel_id=1, source_target_pairs={{0,1},{1,2},{2,3},{3,4},{4,5},{5,6},{6,7},{7,0},{8,9},{9,10},{10,1... | collective-permute-start | bytes 135176 | tf_op jit(solution)/shard_map/ppermute | solution.py:40
  6.7 4.8 %collective-permute-start.3 = (f32[88,128]{1,0:T(8,128)}, f32[88,128]{1,0:T(8,128)S(1)}, u32[]{:S(2)}, u32[]{:S(2)}) collective-permute-start(f32[88,128]{1,0:T(8,128)} %get-tuple-element.29), channel_id=1, source_target_pairs={{0,7},{1,0},{2,1},{3,2},{4,3},{5,4},{6,5},{7,6},{8,15},{9,8},{10,9... | collective-permute-start | bytes 135176 | tf_op jit(solution)/shard_map/ppermute | solution.py:40
  11.5 0.6 %copy-start.6 = (f32[88,128]{1,0:T(8,128)}, f32[88,128]{1,0:T(8,128)S(1)}, u32[]{:S(2)}) copy-start(f32[88,128]{1,0:T(8,128)S(1)} %collective-permute-done.2.hy_lo) | copy-start | bytes 135172
  11.5 0.6 %copy-start.7 = (f32[88,128]{1,0:T(8,128)}, f32[88,128]{1,0:T(8,128)S(1)}, u32[]{:S(2)}) copy-start(f32[88,128]{1,0:T(8,128)S(1)} %collective-permute-done.3.hy_hi) | copy-start | bytes 135172
  11.5 0.7 %copy-start = (f32[264,128]{1,0:T(8,128)}, f32[264,128]{1,0:T(8,128)S(1)}, u32[]{:S(2)}) copy-start(f32[264,128]{1,0:T(8,128)S(1)} %collective-permute-done.hx_lo) | copy-start | bytes 405508
  12.2 0.7 %copy-start.1 = (f32[264,128]{1,0:T(8,128)}, f32[264,128]{1,0:T(8,128)S(1)}, u32[]{:S(2)}) copy-start(f32[264,128]{1,0:T(8,128)S(1)} %collective-permute-done.1.hx_hi) | copy-start | bytes 405508
  16.7 8.8 %collective-permute-start.4 = (f32[264,128]{1,0:T(8,128)}, f32[264,128]{1,0:T(8,128)S(1)}, u32[]{:S(2)}, u32[]{:S(2)}) collective-permute-start(f32[264,128]{1,0:T(8,128)} %get-tuple-element.32), channel_id=1, source_target_pairs={{0,8},{8,16},{16,24},{24,0},{1,9},{9,17},{17,25},{25,1},{2,10},{10... | collective-permute-start | bytes 405512 | tf_op jit(solution)/shard_map/ppermute | solution.py:40
  19.4 6.1 %collective-permute-start.5 = (f32[264,128]{1,0:T(8,128)}, f32[264,128]{1,0:T(8,128)S(1)}, u32[]{:S(2)}, u32[]{:S(2)}) collective-permute-start(f32[264,128]{1,0:T(8,128)} %get-tuple-element.33), channel_id=1, source_target_pairs={{0,24},{8,0},{16,8},{24,16},{1,25},{9,1},{17,9},{25,17},{2,26},{10... | collective-permute-start | bytes 405512 | tf_op jit(solution)/shard_map/ppermute | solution.py:40
  19.4 6.1 %collective-permute-start.6 = (f32[88,128]{1,0:T(8,128)}, f32[88,128]{1,0:T(8,128)S(1)}, u32[]{:S(2)}, u32[]{:S(2)}) collective-permute-start(f32[88,128]{1,0:T(8,128)} %get-tuple-element.34), channel_id=1, source_target_pairs={{0,1},{1,2},{2,3},{3,4},{4,5},{5,6},{6,7},{7,0},{8,9},{9,10},{10,1... | collective-permute-start | bytes 135176 | tf_op jit(solution)/shard_map/ppermute | solution.py:40
  20.3 5.1 %collective-permute-start.7 = (f32[88,128]{1,0:T(8,128)}, f32[88,128]{1,0:T(8,128)S(1)}, u32[]{:S(2)}, u32[]{:S(2)}) collective-permute-start(f32[88,128]{1,0:T(8,128)} %get-tuple-element.35), channel_id=1, source_target_pairs={{0,7},{1,0},{2,1},{3,2},{4,3},{5,4},{6,5},{7,6},{8,15},{9,8},{10,9... | collective-permute-start | bytes 135176 | tf_op jit(solution)/shard_map/ppermute | solution.py:40
  25.4 0.6 %copy-start.8 = (f32[88,128]{1,0:T(8,128)}, f32[88,128]{1,0:T(8,128)S(1)}, u32[]{:S(2)}) copy-start(f32[88,128]{1,0:T(8,128)S(1)} %collective-permute-done.6.hy_lo) | copy-start | bytes 135172
  25.4 0.6 %copy-start.9 = (f32[88,128]{1,0:T(8,128)}, f32[88,128]{1,0:T(8,128)S(1)}, u32[]{:S(2)}) copy-start(f32[88,128]{1,0:T(8,128)S(1)} %collective-permute-done.7.hy_hi) | copy-start | bytes 135172
  25.5 0.7 %copy-start.2 = (f32[264,128]{1,0:T(8,128)}, f32[264,128]{1,0:T(8,128)S(1)}, u32[]{:S(2)}) copy-start(f32[264,128]{1,0:T(8,128)S(1)} %collective-permute-done.4.hx_lo) | copy-start | bytes 405508
  25.5 0.7 %copy-start.3 = (f32[264,128]{1,0:T(8,128)}, f32[264,128]{1,0:T(8,128)S(1)}, u32[]{:S(2)}) copy-start(f32[264,128]{1,0:T(8,128)S(1)} %collective-permute-done.5.hx_hi) | copy-start | bytes 405508
  31.3 3.7 %collective-permute-start.8 = (f32[24,128]{1,0:T(8,128)}, f32[24,128]{1,0:T(8,128)S(1)}, u32[]{:S(2)}, u32[]{:S(2)}) collective-permute-start(f32[24,128]{1,0:T(8,128)} %get-tuple-element.40), channel_id=1, source_target_pairs={{0,8},{8,16},{16,24},{24,0},{1,9},{9,17},{17,25},{25,1},{2,10},{10... | collective-permute-start | bytes 36872 | tf_op jit(solution)/shard_map/ppermute | solution.py:40
  34.0 3.3 %collective-permute-start.9 = (f32[24,128]{1,0:T(8,128)}, f32[24,128]{1,0:T(8,128)S(1)}, u32[]{:S(2)}, u32[]{:S(2)}) collective-permute-start(f32[24,128]{1,0:T(8,128)} %get-tuple-element.41), channel_id=1, source_target_pairs={{0,24},{8,0},{16,8},{24,16},{1,25},{9,1},{17,9},{25,17},{2,26},{10... | collective-permute-start | bytes 36872 | tf_op jit(solution)/shard_map/ppermute | solution.py:40
  35.0 10.0 %copy-start.4 = (f32[24,128]{1,0:T(8,128)}, f32[24,128]{1,0:T(8,128)S(1)}, u32[]{:S(2)}) copy-start(f32[24,128]{1,0:T(8,128)S(1)} %collective-permute-done.8.hx_lo) | copy-start | bytes 36868
  37.3 7.7 %copy-start.5 = (f32[24,128]{1,0:T(8,128)}, f32[24,128]{1,0:T(8,128)S(1)}, u32[]{:S(2)}) copy-start(f32[24,128]{1,0:T(8,128)S(1)} %collective-permute-done.9.hx_hi) | copy-start | bytes 36868
  39.5 5.5 %collective-permute-start.10 = (f32[16,128]{1,0:T(8,128)S(1)}, f32[16,128]{1,0:T(8,128)S(1)}, u32[]{:S(2)}, u32[]{:S(2)}) collective-permute-start(f32[16,128]{1,0:T(8,128)S(1)} %pad.15), channel_id=1, source_target_pairs={{0,1},{1,2},{2,3},{3,4},{4,5},{5,6},{6,7},{7,0},{8,9},{9,10},{10,1... | collective-permute-start | bytes 24584 | tf_op jit(solution)/shard_map/ppermute | solution.py:40
  39.5 5.5 %collective-permute-start.11 = (f32[16,128]{1,0:T(8,128)S(1)}, f32[16,128]{1,0:T(8,128)S(1)}, u32[]{:S(2)}, u32[]{:S(2)}) collective-permute-start(f32[16,128]{1,0:T(8,128)S(1)} %pad.17), channel_id=1, source_target_pairs={{0,7},{1,0},{2,1},{3,2},{4,3},{5,4},{6,5},{7,6},{8,15},{9,8},{10,9... | collective-permute-start | bytes 24584 | tf_op jit(solution)/shard_map/ppermute | solution.py:40
  45.0 0.6 %copy-start.10 = (f32[16,128]{1,0:T(8,128)}, f32[16,128]{1,0:T(8,128)S(1)}, u32[]{:S(2)}) copy-start(f32[16,128]{1,0:T(8,128)S(1)} %collective-permute-done.10.hy_lo) | copy-start | bytes 24580
  45.0 0.6 %copy-start.11 = (f32[16,128]{1,0:T(8,128)}, f32[16,128]{1,0:T(8,128)S(1)}, u32[]{:S(2)}) copy-start(f32[16,128]{1,0:T(8,128)S(1)} %collective-permute-done.11.hy_hi) | copy-start | bytes 24580

commit v12 on v7

--- a/solution.py
+++ b/solution.py
@@ -658,8 +658,7 @@
     lo, hi = row_ends(x_lo, blocks, at_end), row_ends(x_hi, blocks, at_end)
     extra = jnp.stack([lo, hi], axis=1).reshape(2 * len(blocks), 6)
     extra = jnp.pad(extra, ((0, 0), (0, 128 - 6)))
-    joined = jnp.concatenate([y_rim, extra])
-    return jnp.pad(joined, ((0, round8(joined.shape[0]) - joined.shape[0]), (0, 0)))
+    return lax.dynamic_update_slice(y_rim, extra, (blocks[0].corner_rows[0], 0))
 
 
 def face_call(blocks, fine_out, coarse_out, fine_face, coarse_face, rims):
@@ -725,7 +724,7 @@
 
     vhalos = receive(vrims)
     fx_rows = 6 * (fine.chunks + coarse.chunks)
-    fy_rows = round8(fine.size + coarse.size)
+    fy_rows = round8(fine.size + coarse.size + 4)
     fine_out, fine_mem, fine_face, coarse_out, coarse_mem, coarse_face, *face_rims = pl.pallas_call(
         functools.partial(stress_kernel, blocks),
         out_shape=(

time: 48.1 us -> 47.7 us (level)
  other arithmetic: 2.54 us -> 1.17 us
  local copies, waits for them, and re-layouts: 3.17 us -> 4.33 us
    concatenate x2 -> x0, other arithmetic: 1.37 us -> none  [with_corners(): joined = jnp.concatenate([y_rim, extra])]
    dynamic_update_slice x0 -> x2, local copies, waits for them, and re-layouts: none -> 1.16 us  [with_corners(): return lax.dynamic_update_slice(y_rim, extra, (blocks[0].corner_rows[0], 0))]
  transfers between devices with their start and end apart: 12 -> 12, of which waited for: 5 -> 6; matrix products, arithmetic and copies ran while one was open for 2% -> 3% of each run, Pallas kernels for 0% -> 0%
where the time goes in v12:
time: 47.7 us; the launch traced here: 47.5 us
  starting transfers between devices  21.1 us (44%)
  Pallas kernels  13.4 us (28%)
  waiting for transfers between devices  6.74 us (14%)
  local copies, waits for them, and re-layouts  4.33 us (9%)
  other arithmetic  1.17 us (2%)
  between operations  0.75 us (2%)
    ppermute x12, starting transfers between devices, shift_from(): return lax.ppermute(block, axis, pairs)  21.1 us
    ppermute x12, waiting for transfers between devices, shift_from(): return lax.ppermute(block, axis, pairs)  6.74 us
    pallas_call x1, Pallas kernels, local(): pl.pallas_call(functools.partial(stress_kernel, blocks), out_shape=(f32(f...  5.1 us
    pallas_call x1, Pallas kernels, local(): pl.pallas_call(functools.partial(velocity_kernel, blocks), out_shape=(f32...  3.84 us
    unnamed x24, local copies, waits for them, and re-layouts  2.62 us
    pallas_call x1, Pallas kernels, local(): pl.pallas_call(functools.partial(pack_kernel, blocks), out_shape=halo_sha...  2.25 us
    pallas_call x1, Pallas kernels, face_call(): pl.pallas_call(functools.partial(face_kernel, blocks, fine.layers - 1), o...  2.19 us
    dynamic_update_slice x2, local copies, waits for them, and re-layouts, with_corners(): return lax.dynamic_update_slice(y_rim, extra, (blocks[0].corner_rows[0], 0))  1.16 us
  transfers between devices with their start and end apart: 12, of which 6 were waited for; matrix products, arithmetic and copies ran while one was open for 3% of the time, Pallas kernels for 0%

profile of v12, /device:TPU:1, one launch (start us, length us, event | category | flops | bytes accessed | tf_op | source)
XLA Modules:
  0.0 47.5 jit_solution(12484789586474930457)
XLA Ops:
  0.6 2.2 %shard_map.156 = (f32[264,128]{1,0:T(8,128)}, f32[264,128]{1,0:T(8,128)}, f32[88,128]{1,0:T(8,128)}, f32[88,128]{1,0:T(8,128)}) custom-call(f32[9,12,6,384]{3,2,1,0:T(8,128)} %fw.5, f32[9,8,2,128]{3,2,1,0:T(2,128)} %cw.5), custom_call_target="tpu_custom_call" | custom-call | tf_op jit(solution)/shard_map/pallas_call | solution.py:709
  2.9 2.6 %collective-permute-start = (f32[264,128]{1,0:T(8,128)}, f32[264,128]{1,0:T(8,128)S(1)}, u32[]{:S(2)}, u32[]{:S(2)}) collective-permute-start(f32[264,128]{1,0:T(8,128)} %get-tuple-element.26), channel_id=1, source_target_pairs={{0,8},{8,16},{16,24},{24,0},{1,9},{9,17},{17,25},{25,1},{2,10},{10... | collective-permute-start | bytes 405512 | tf_op jit(solution)/shard_map/ppermute | solution.py:44
  5.5 1.2 %collective-permute-start.2 = (f32[88,128]{1,0:T(8,128)}, f32[88,128]{1,0:T(8,128)S(1)}, u32[]{:S(2)}, u32[]{:S(2)}) collective-permute-start(f32[88,128]{1,0:T(8,128)} %get-tuple-element.28), channel_id=1, source_target_pairs={{0,1},{1,2},{2,3},{3,4},{4,5},{5,6},{6,7},{7,0},{8,9},{9,10},{10,1... | collective-permute-start | bytes 135176 | tf_op jit(solution)/shard_map/ppermute | solution.py:44
  6.7 3.0 %collective-permute-start.3 = (f32[88,128]{1,0:T(8,128)}, f32[88,128]{1,0:T(8,128)S(1)}, u32[]{:S(2)}, u32[]{:S(2)}) collective-permute-start(f32[88,128]{1,0:T(8,128)} %get-tuple-element.29), channel_id=1, source_target_pairs={{0,7},{1,0},{2,1},{3,2},{4,3},{5,4},{6,5},{7,6},{8,15},{9,8},{10,9... | collective-permute-start | bytes 135176 | tf_op jit(solution)/shard_map/ppermute | solution.py:44
  9.8 0.6 %add_convert_fusion.flags = s32[4]{0:T(128)} fusion(pred[1]{0:T(512)(128)(4,1)} %bitcast.3, pred[1]{0:T(512)(128)(4,1)} %bitcast.2, pred[1]{0:T(512)(128)(4,1)} %bitcast.1, pred[1]{0:T(512)(128)(4,1)} %bitcast), kind=kLoop, calls=%fused_computation.8 | loop fusion | flops 16 | bytes 20 | tf_op jit(solution)/shard_map/convert_element_type | solution.py:50
  10.4 1.1 %collective-permute-done.2.hy_lo = f32[88,128]{1,0:T(8,128)S(1)} collective-permute-done((f32[88,128]{1,0:T(8,128)}, f32[88,128]{1,0:T(8,128)S(1)}, u32[]{:S(2)}, u32[]{:S(2)}) %collective-permute-start.2) | collective-permute-done | bytes 45088 | tf_op jit(solution)/shard_map/ppermute | solution.py:44
  11.5 0.6 %copy-done.6 = f32[88,128]{1,0:T(8,128)} copy-done((f32[88,128]{1,0:T(8,128)}, f32[88,128]{1,0:T(8,128)S(1)}, u32[]{:S(2)}) %copy-start.6) | copy-done | bytes 45080
  12.2 0.7 %copy-done.1 = f32[264,128]{1,0:T(8,128)} copy-done((f32[264,128]{1,0:T(8,128)}, f32[264,128]{1,0:T(8,128)S(1)}, u32[]{:S(2)}) %copy-start.1) | copy-done | bytes 135192
  12.8 3.8 %shard_map.157 = (f32[3,12,6,384]{3,2,1,0:T(8,128)}, f32[3,8,2,128]{3,2,1,0:T(2,128)}, f32[264,128]{1,0:T(8,128)}, f32[264,128]{1,0:T(8,128)}, f32[88,128]{1,0:T(8,128)}, /*index=5*/f32[88,128]{1,0:T(8,128)}) custom-call(f32[9,12,6,384]{3,2,1,0:T(8,128)} %fw.5, f32[9,8,2,128]{3,2,1,0:T(2,128)} %cw.5, f32[264,128]{1,0:T(8,128)} %copy-done, ...), custom_call_target="tpu_custom_call" | custom-call | tf_op jit(solution)/shard_map/pallas_call | solution.py:717
  16.7 2.7 %collective-permute-start.4 = (f32[264,128]{1,0:T(8,128)}, f32[264,128]{1,0:T(8,128)S(1)}, u32[]{:S(2)}, u32[]{:S(2)}) collective-permute-start(f32[264,128]{1,0:T(8,128)} %get-tuple-element.32), channel_id=1, source_target_pairs={{0,8},{8,16},{16,24},{24,0},{1,9},{9,17},{17,25},{25,1},{2,10},{10... | collective-permute-start | bytes 405512 | tf_op jit(solution)/shard_map/ppermute | solution.py:44
  19.4 0.9 %collective-permute-start.6 = (f32[88,128]{1,0:T(8,128)}, f32[88,128]{1,0:T(8,128)S(1)}, u32[]{:S(2)}, u32[]{:S(2)}) collective-permute-start(f32[88,128]{1,0:T(8,128)} %get-tuple-element.34), channel_id=1, source_target_pairs={{0,1},{1,2},{2,3},{3,4},{4,5},{5,6},{6,7},{7,0},{8,9},{9,10},{10,1... | collective-permute-start | bytes 135176 | tf_op jit(solution)/shard_map/ppermute | solution.py:44
  20.3 3.5 %collective-permute-start.7 = (f32[88,128]{1,0:T(8,128)}, f32[88,128]{1,0:T(8,128)S(1)}, u32[]{:S(2)}, u32[]{:S(2)}) collective-permute-start(f32[88,128]{1,0:T(8,128)} %get-tuple-element.35), channel_id=1, source_target_pairs={{0,7},{1,0},{2,1},{3,2},{4,3},{5,4},{6,5},{7,6},{8,15},{9,8},{10,9... | collective-permute-start | bytes 135176 | tf_op jit(solution)/shard_map/ppermute | solution.py:44
  23.8 1.6 %collective-permute-done.6.hy_lo = f32[88,128]{1,0:T(8,128)S(1)} collective-permute-done((f32[88,128]{1,0:T(8,128)}, f32[88,128]{1,0:T(8,128)S(1)}, u32[]{:S(2)}, u32[]{:S(2)}) %collective-permute-start.6) | collective-permute-done | bytes 45088 | tf_op jit(solution)/shard_map/ppermute | solution.py:44
  25.5 0.6 %copy-done.8 = f32[88,128]{1,0:T(8,128)} copy-done((f32[88,128]{1,0:T(8,128)}, f32[88,128]{1,0:T(8,128)S(1)}, u32[]{:S(2)}) %copy-start.8) | copy-done | bytes 45080
  26.2 5.1 %shard_map.158 = (f32[9,12,6,384]{3,2,1,0:T(8,128)}, f32[6,12,6,384]{3,2,1,0:T(8,128)}, f32[6,6,384]{2,1,0:T(8,128)}, f32[9,8,2,128]{3,2,1,0:T(2,128)}, f32[6,8,...) custom-call(f32[9,12,6,384]{3,2,1,0:T(8,128)} %fw.5, ...), custom_call_target="tpu_custom_call" | custom-call | tf_op jit(solution)/shard_map/pallas_call | solution.py:728
  31.3 2.7 %collective-permute-start.8 = (f32[24,128]{1,0:T(8,128)}, f32[24,128]{1,0:T(8,128)S(1)}, u32[]{:S(2)}, u32[]{:S(2)}) collective-permute-start(f32[24,128]{1,0:T(8,128)} %get-tuple-element.40), channel_id=1, source_target_pairs={{0,8},{8,16},{16,24},{24,0},{1,9},{9,17},{17,25},{25,1},{2,10},{10... | collective-permute-start | bytes 36872 | tf_op jit(solution)/shard_map/ppermute | solution.py:44
  34.0 1.0 %collective-permute-done.8.hx_lo = f32[24,128]{1,0:T(8,128)S(1)} collective-permute-done((f32[24,128]{1,0:T(8,128)}, f32[24,128]{1,0:T(8,128)S(1)}, u32[]{:S(2)}, u32[]{:S(2)}) %collective-permute-start.8) | collective-permute-done | bytes 12320 | tf_op jit(solution)/shard_map/ppermute | solution.py:44
  35.4 1.9 %collective-permute-done.9.hx_hi = f32[24,128]{1,0:T(8,128)S(1)} collective-permute-done((f32[24,128]{1,0:T(8,128)}, f32[24,128]{1,0:T(8,128)S(1)}, u32[]{:S(2)}, u32[]{:S(2)}) %collective-permute-start.9) | collective-permute-done | bytes 12320 | tf_op jit(solution)/shard_map/ppermute | solution.py:44
  38.1 0.6 %pad_dynamic-update-slice_fusion.1 = f32[16,128]{1,0:T(8,128)} fusion(f32[16,128]{1,0:T(8,128)} %get-tuple-element.42, f32[4,6]{1,0:T(4,128)S(1)} %bitcast.23), kind=kLoop, calls=%fused_computation.7 | loop fusion | bytes 2144 | tf_op jit(solution)/shard_map/dynamic_update_slice | solution.py:661
  38.6 0.6 %pad_dynamic-update-slice_fusion = f32[16,128]{1,0:T(8,128)} fusion(f32[16,128]{1,0:T(8,128)} %get-tuple-element.43, f32[4,6]{1,0:T(4,128)S(1)} %bitcast.22), kind=kLoop, calls=%fused_computation.6 | loop fusion | bytes 2144 | tf_op jit(solution)/shard_map/dynamic_update_slice | solution.py:661
  39.2 4.4 %collective-permute-start.11 = (f32[16,128]{1,0:T(8,128)}, f32[16,128]{1,0:T(8,128)S(1)}, u32[]{:S(2)}, u32[]{:S(2)}) collective-permute-start(f32[16,128]{1,0:T(8,128)} %pad_dynamic-update-slice_fusion), channel_id=1, source_target_pairs={{0,7},{1,0},{2,1},{3,2},{4,3},{5,4},{6,5},{7,6},{8,15},{9,8},{10,9... | collective-permute-start | bytes 24584 | tf_op jit(solution)/shard_map/ppermute | solution.py:44
  43.7 0.7 %collective-permute-done.10.hy_lo = f32[16,128]{1,0:T(8,128)S(1)} collective-permute-done((f32[16,128]{1,0:T(8,128)}, f32[16,128]{1,0:T(8,128)S(1)}, u32[]{:S(2)}, u32[]{:S(2)}) %collective-permute-start.10) | collective-permute-done | bytes 8224 | tf_op jit(solution)/shard_map/ppermute | solution.py:44
  44.3 0.3 collective-permute-done.11.hy_hi
  45.3 2.2 %shard_map.159 = (f32[9,12,6,384]{3,2,1,0:T(8,128)}, f32[9,8,2,128]{3,2,1,0:T(2,128)}) custom-call(f32[9,12,6,384]{3,2,1,0:T(8,128)} %get-tuple-element.36.fout_in, f32[9,8,2,128]{3,2,1,0:T(2,128)} %get-tuple-element.37.cout_in, f32[6,6,384]{2,1,0:T(8,128)} %get-tuple-element.38.fface, ...), custom_call_target="tpu_custom_call", output_to_operand_aliasing={{0}: (0, {}), {1}: (1, {})} | custom-call | tf_op jit(solution)/shard_map/pallas_call | solution.py:675
  (47 shorter events, 1.9 us)
Async XLA Ops:
  2.9 8.6 %collective-permute-start = (f32[264,128]{1,0:T(8,128)}, f32[264,128]{1,0:T(8,128)S(1)}, u32[]{:S(2)}, u32[]{:S(2)}) collective-permute-start(f32[264,128]{1,0:T(8,128)} %get-tuple-element.26), channel_id=1, source_target_pairs={{0,8},{8,16},{16,24},{24,0},{1,9},{9,17},{17,25},{25,1},{2,10},{10... | collective-permute-start | bytes 405512 | tf_op jit(solution)/shard_map/ppermute | solution.py:44
  5.5 6.1 %collective-permute-start.1 = (f32[264,128]{1,0:T(8,128)}, f32[264,128]{1,0:T(8,128)S(1)}, u32[]{:S(2)}, u32[]{:S(2)}) collective-permute-start(f32[264,128]{1,0:T(8,128)} %get-tuple-element.27), channel_id=1, source_target_pairs={{0,24},{8,0},{16,8},{24,16},{1,25},{9,1},{17,9},{25,17},{2,26},{10... | collective-permute-start | bytes 405512 | tf_op jit(solution)/shard_map/ppermute | solution.py:44
  5.5 6.0 %collective-permute-start.2 = (f32[88,128]{1,0:T(8,128)}, f32[88,128]{1,0:T(8,128)S(1)}, u32[]{:S(2)}, u32[]{:S(2)}) collective-permute-start(f32[88,128]{1,0:T(8,128)} %get-tuple-element.28), channel_id=1, source_target_pairs={{0,1},{1,2},{2,3},{3,4},{4,5},{5,6},{6,7},{7,0},{8,9},{9,10},{10,1... | collective-permute-start | bytes 135176 | tf_op jit(solution)/shard_map/ppermute | solution.py:44
  6.7 4.8 %collective-permute-start.3 = (f32[88,128]{1,0:T(8,128)}, f32[88,128]{1,0:T(8,128)S(1)}, u32[]{:S(2)}, u32[]{:S(2)}) collective-permute-start(f32[88,128]{1,0:T(8,128)} %get-tuple-element.29), channel_id=1, source_target_pairs={{0,7},{1,0},{2,1},{3,2},{4,3},{5,4},{6,5},{7,6},{8,15},{9,8},{10,9... | collective-permute-start | bytes 135176 | tf_op jit(solution)/shard_map/ppermute | solution.py:44
  11.5 0.6 %copy-start.6 = (f32[88,128]{1,0:T(8,128)}, f32[88,128]{1,0:T(8,128)S(1)}, u32[]{:S(2)}) copy-start(f32[88,128]{1,0:T(8,128)S(1)} %collective-permute-done.2.hy_lo) | copy-start | bytes 135172
  11.5 0.6 %copy-start.7 = (f32[88,128]{1,0:T(8,128)}, f32[88,128]{1,0:T(8,128)S(1)}, u32[]{:S(2)}) copy-start(f32[88,128]{1,0:T(8,128)S(1)} %collective-permute-done.3.hy_hi) | copy-start | bytes 135172
  11.5 0.7 %copy-start = (f32[264,128]{1,0:T(8,128)}, f32[264,128]{1,0:T(8,128)S(1)}, u32[]{:S(2)}) copy-start(f32[264,128]{1,0:T(8,128)S(1)} %collective-permute-done.hx_lo) | copy-start | bytes 405508
  12.2 0.7 %copy-start.1 = (f32[264,128]{1,0:T(8,128)}, f32[264,128]{1,0:T(8,128)S(1)}, u32[]{:S(2)}) copy-start(f32[264,128]{1,0:T(8,128)S(1)} %collective-permute-done.1.hx_hi) | copy-start | bytes 405508
  16.7 8.8 %collective-permute-start.4 = (f32[264,128]{1,0:T(8,128)}, f32[264,128]{1,0:T(8,128)S(1)}, u32[]{:S(2)}, u32[]{:S(2)}) collective-permute-start(f32[264,128]{1,0:T(8,128)} %get-tuple-element.32), channel_id=1, source_target_pairs={{0,8},{8,16},{16,24},{24,0},{1,9},{9,17},{17,25},{25,1},{2,10},{10... | collective-permute-start | bytes 405512 | tf_op jit(solution)/shard_map/ppermute | solution.py:44
  19.4 6.1 %collective-permute-start.5 = (f32[264,128]{1,0:T(8,128)}, f32[264,128]{1,0:T(8,128)S(1)}, u32[]{:S(2)}, u32[]{:S(2)}) collective-permute-start(f32[264,128]{1,0:T(8,128)} %get-tuple-element.33), channel_id=1, source_target_pairs={{0,24},{8,0},{16,8},{24,16},{1,25},{9,1},{17,9},{25,17},{2,26},{10... | collective-permute-start | bytes 405512 | tf_op jit(solution)/shard_map/ppermute | solution.py:44
  19.4 6.1 %collective-permute-start.6 = (f32[88,128]{1,0:T(8,128)}, f32[88,128]{1,0:T(8,128)S(1)}, u32[]{:S(2)}, u32[]{:S(2)}) collective-permute-start(f32[88,128]{1,0:T(8,128)} %get-tuple-element.34), channel_id=1, source_target_pairs={{0,1},{1,2},{2,3},{3,4},{4,5},{5,6},{6,7},{7,0},{8,9},{9,10},{10,1... | collective-permute-start | bytes 135176 | tf_op jit(solution)/shard_map/ppermute | solution.py:44
  20.3 5.1 %collective-permute-start.7 = (f32[88,128]{1,0:T(8,128)}, f32[88,128]{1,0:T(8,128)S(1)}, u32[]{:S(2)}, u32[]{:S(2)}) collective-permute-start(f32[88,128]{1,0:T(8,128)} %get-tuple-element.35), channel_id=1, source_target_pairs={{0,7},{1,0},{2,1},{3,2},{4,3},{5,4},{6,5},{7,6},{8,15},{9,8},{10,9... | collective-permute-start | bytes 135176 | tf_op jit(solution)/shard_map/ppermute | solution.py:44
  25.4 0.6 %copy-start.8 = (f32[88,128]{1,0:T(8,128)}, f32[88,128]{1,0:T(8,128)S(1)}, u32[]{:S(2)}) copy-start(f32[88,128]{1,0:T(8,128)S(1)} %collective-permute-done.6.hy_lo) | copy-start | bytes 135172
  25.4 0.6 %copy-start.9 = (f32[88,128]{1,0:T(8,128)}, f32[88,128]{1,0:T(8,128)S(1)}, u32[]{:S(2)}) copy-start(f32[88,128]{1,0:T(8,128)S(1)} %collective-permute-done.7.hy_hi) | copy-start | bytes 135172
  25.5 0.7 %copy-start.2 = (f32[264,128]{1,0:T(8,128)}, f32[264,128]{1,0:T(8,128)S(1)}, u32[]{:S(2)}) copy-start(f32[264,128]{1,0:T(8,128)S(1)} %collective-permute-done.4.hx_lo) | copy-start | bytes 405508
  25.5 0.7 %copy-start.3 = (f32[264,128]{1,0:T(8,128)}, f32[264,128]{1,0:T(8,128)S(1)}, u32[]{:S(2)}) copy-start(f32[264,128]{1,0:T(8,128)S(1)} %collective-permute-done.5.hx_hi) | copy-start | bytes 405508
  31.3 3.7 %collective-permute-start.8 = (f32[24,128]{1,0:T(8,128)}, f32[24,128]{1,0:T(8,128)S(1)}, u32[]{:S(2)}, u32[]{:S(2)}) collective-permute-start(f32[24,128]{1,0:T(8,128)} %get-tuple-element.40), channel_id=1, source_target_pairs={{0,8},{8,16},{16,24},{24,0},{1,9},{9,17},{17,25},{25,1},{2,10},{10... | collective-permute-start | bytes 36872 | tf_op jit(solution)/shard_map/ppermute | solution.py:44
  34.0 3.3 %collective-permute-start.9 = (f32[24,128]{1,0:T(8,128)}, f32[24,128]{1,0:T(8,128)S(1)}, u32[]{:S(2)}, u32[]{:S(2)}) collective-permute-start(f32[24,128]{1,0:T(8,128)} %get-tuple-element.41), channel_id=1, source_target_pairs={{0,24},{8,0},{16,8},{24,16},{1,25},{9,1},{17,9},{25,17},{2,26},{10... | collective-permute-start | bytes 36872 | tf_op jit(solution)/shard_map/ppermute | solution.py:44
  35.0 9.7 %copy-start.4 = (f32[24,128]{1,0:T(8,128)}, f32[24,128]{1,0:T(8,128)S(1)}, u32[]{:S(2)}) copy-start(f32[24,128]{1,0:T(8,128)S(1)} %collective-permute-done.8.hx_lo) | copy-start | bytes 36868
  37.3 7.4 %copy-start.5 = (f32[24,128]{1,0:T(8,128)}, f32[24,128]{1,0:T(8,128)S(1)}, u32[]{:S(2)}) copy-start(f32[24,128]{1,0:T(8,128)S(1)} %collective-permute-done.9.hx_hi) | copy-start | bytes 36868
  38.6 5.7 %collective-permute-start.10 = (f32[16,128]{1,0:T(8,128)}, f32[16,128]{1,0:T(8,128)S(1)}, u32[]{:S(2)}, u32[]{:S(2)}) collective-permute-start(f32[16,128]{1,0:T(8,128)} %pad_dynamic-update-slice_fusion.1), channel_id=1, source_target_pairs={{0,1},{1,2},{2,3},{3,4},{4,5},{5,6},{6,7},{7,0},{8,9},{9,10},{10,1... | collective-permute-start | bytes 24584 | tf_op jit(solution)/shard_map/ppermute | solution.py:44
  39.2 5.4 %collective-permute-start.11 = (f32[16,128]{1,0:T(8,128)}, f32[16,128]{1,0:T(8,128)S(1)}, u32[]{:S(2)}, u32[]{:S(2)}) collective-permute-start(f32[16,128]{1,0:T(8,128)} %pad_dynamic-update-slice_fusion), channel_id=1, source_target_pairs={{0,7},{1,0},{2,1},{3,2},{4,3},{5,4},{6,5},{7,6},{8,15},{9,8},{10,9... | collective-permute-start | bytes 24584 | tf_op jit(solution)/shard_map/ppermute | solution.py:44
  44.3 0.6 %copy-start.10 = (f32[16,128]{1,0:T(8,128)}, f32[16,128]{1,0:T(8,128)S(1)}, u32[]{:S(2)}) copy-start(f32[16,128]{1,0:T(8,128)S(1)} %collective-permute-done.10.hy_lo) | copy-start | bytes 24580
  44.7 0.6 %copy-start.11 = (f32[16,128]{1,0:T(8,128)}, f32[16,128]{1,0:T(8,128)S(1)}, u32[]{:S(2)}) copy-start(f32[16,128]{1,0:T(8,128)S(1)} %collective-permute-done.11.hy_hi) | copy-start | bytes 24580

commit v13 on v12

--- a/solution.py
+++ b/solution.py
@@ -219,10 +219,13 @@
 
 
 def pick(values_ref, row, index):
-    result = jnp.zeros(index.shape, jnp.float32)
-    for kind_at in range(values_ref.shape[1]):
-        result = jnp.where(index == kind_at, values_ref[row, kind_at], result)
-    return result
+    level = [values_ref[row, kind_at] for kind_at in range(values_ref.shape[1])]
+    bit = 0
+    while len(level) > 1:
+        on = (index & (1 << bit)) != 0
+        level = [jnp.where(on, level[k + 1], level[k]) for k in range(0, len(level), 2)]
+        bit += 1
+    return level[0]
 
 
 def fill_x(scratch, slot, lo, block, hi):

time: 47.7 us -> 47.6 us (level)
  no operation moved by 1% of the time
where the time goes in v13:
time: 47.6 us; the launch traced here: 47.4 us
  starting transfers between devices  21.1 us (44%)
  Pallas kernels  13.3 us (28%)
  waiting for transfers between devices  6.74 us (14%)
  local copies, waits for them, and re-layouts  4.33 us (9%)
  other arithmetic  1.17 us (2%)
  between operations  0.75 us (2%)
    ppermute x12, starting transfers between devices, shift_from(): return lax.ppermute(block, axis, pairs)  21.1 us
    ppermute x12, waiting for transfers between devices, shift_from(): return lax.ppermute(block, axis, pairs)  6.74 us
    pallas_call x1, Pallas kernels, local(): pl.pallas_call(functools.partial(stress_kernel, blocks), out_shape=(f32(f...  5.08 us
    pallas_call x1, Pallas kernels, local(): pl.pallas_call(functools.partial(velocity_kernel, blocks), out_shape=(f32...  3.81 us
    unnamed x24, local copies, waits for them, and re-layouts  2.62 us
    pallas_call x1, Pallas kernels, local(): pl.pallas_call(functools.partial(pack_kernel, blocks), out_shape=halo_sha...  2.25 us
    pallas_call x1, Pallas kernels, face_call(): pl.pallas_call(functools.partial(face_kernel, blocks, fine.layers - 1), o...  2.19 us
    dynamic_update_slice x2, local copies, waits for them, and re-layouts, with_corners(): return lax.dynamic_update_slice(y_rim, extra, (blocks[0].corner_rows[0], 0))  1.16 us
  transfers between devices with their start and end apart: 12, of which 6 were waited for; matrix products, arithmetic and copies ran while one was open for 3% of the time, Pallas kernels for 0%

profile of v13, /device:TPU:1, one launch (start us, length us, event | category | flops | bytes accessed | tf_op | source)
XLA Modules:
  0.0 47.4 jit_solution(68551676898059480)
XLA Ops:
  0.6 2.2 %shard_map.156 = (f32[264,128]{1,0:T(8,128)}, f32[264,128]{1,0:T(8,128)}, f32[88,128]{1,0:T(8,128)}, f32[88,128]{1,0:T(8,128)}) custom-call(f32[9,12,6,384]{3,2,1,0:T(8,128)} %fw.5, f32[9,8,2,128]{3,2,1,0:T(2,128)} %cw.5), custom_call_target="tpu_custom_call" | custom-call | tf_op jit(solution)/shard_map/pallas_call | solution.py:712
  2.9 2.6 %collective-permute-start = (f32[264,128]{1,0:T(8,128)}, f32[264,128]{1,0:T(8,128)S(1)}, u32[]{:S(2)}, u32[]{:S(2)}) collective-permute-start(f32[264,128]{1,0:T(8,128)} %get-tuple-element.26), channel_id=1, source_target_pairs={{0,8},{8,16},{16,24},{24,0},{1,9},{9,17},{17,25},{25,1},{2,10},{10... | collective-permute-start | bytes 405512 | tf_op jit(solution)/shard_map/ppermute | solution.py:44
  5.5 1.2 %collective-permute-start.2 = (f32[88,128]{1,0:T(8,128)}, f32[88,128]{1,0:T(8,128)S(1)}, u32[]{:S(2)}, u32[]{:S(2)}) collective-permute-start(f32[88,128]{1,0:T(8,128)} %get-tuple-element.28), channel_id=1, source_target_pairs={{0,1},{1,2},{2,3},{3,4},{4,5},{5,6},{6,7},{7,0},{8,9},{9,10},{10,1... | collective-permute-start | bytes 135176 | tf_op jit(solution)/shard_map/ppermute | solution.py:44
  6.7 3.0 %collective-permute-start.3 = (f32[88,128]{1,0:T(8,128)}, f32[88,128]{1,0:T(8,128)S(1)}, u32[]{:S(2)}, u32[]{:S(2)}) collective-permute-start(f32[88,128]{1,0:T(8,128)} %get-tuple-element.29), channel_id=1, source_target_pairs={{0,7},{1,0},{2,1},{3,2},{4,3},{5,4},{6,5},{7,6},{8,15},{9,8},{10,9... | collective-permute-start | bytes 135176 | tf_op jit(solution)/shard_map/ppermute | solution.py:44
  9.8 0.6 %add_convert_fusion.flags = s32[4]{0:T(128)} fusion(pred[1]{0:T(512)(128)(4,1)} %bitcast.3, pred[1]{0:T(512)(128)(4,1)} %bitcast.2, pred[1]{0:T(512)(128)(4,1)} %bitcast.1, pred[1]{0:T(512)(128)(4,1)} %bitcast), kind=kLoop, calls=%fused_computation.8 | loop fusion | flops 16 | bytes 20 | tf_op jit(solution)/shard_map/convert_element_type | solution.py:50
  10.4 1.1 %collective-permute-done.2.hy_lo = f32[88,128]{1,0:T(8,128)S(1)} collective-permute-done((f32[88,128]{1,0:T(8,128)}, f32[88,128]{1,0:T(8,128)S(1)}, u32[]{:S(2)}, u32[]{:S(2)}) %collective-permute-start.2) | collective-permute-done | bytes 45088 | tf_op jit(solution)/shard_map/ppermute | solution.py:44
  11.5 0.6 %copy-done.6 = f32[88,128]{1,0:T(8,128)} copy-done((f32[88,128]{1,0:T(8,128)}, f32[88,128]{1,0:T(8,128)S(1)}, u32[]{:S(2)}) %copy-start.6) | copy-done | bytes 45080
  12.2 0.7 %copy-done.1 = f32[264,128]{1,0:T(8,128)} copy-done((f32[264,128]{1,0:T(8,128)}, f32[264,128]{1,0:T(8,128)S(1)}, u32[]{:S(2)}) %copy-start.1) | copy-done | bytes 135192
  12.8 3.8 %shard_map.157 = (f32[3,12,6,384]{3,2,1,0:T(8,128)}, f32[3,8,2,128]{3,2,1,0:T(2,128)}, f32[264,128]{1,0:T(8,128)}, f32[264,128]{1,0:T(8,128)}, f32[88,128]{1,0:T(8,128)}, /*index=5*/f32[88,128]{1,0:T(8,128)}) custom-call(f32[9,12,6,384]{3,2,1,0:T(8,128)} %fw.5, f32[9,8,2,128]{3,2,1,0:T(2,128)} %cw.5, f32[264,128]{1,0:T(8,128)} %copy-done, ...), custom_call_target="tpu_custom_call" | custom-call | tf_op jit(solution)/shard_map/pallas_call | solution.py:720
  16.7 2.7 %collective-permute-start.4 = (f32[264,128]{1,0:T(8,128)}, f32[264,128]{1,0:T(8,128)S(1)}, u32[]{:S(2)}, u32[]{:S(2)}) collective-permute-start(f32[264,128]{1,0:T(8,128)} %get-tuple-element.32), channel_id=1, source_target_pairs={{0,8},{8,16},{16,24},{24,0},{1,9},{9,17},{17,25},{25,1},{2,10},{10... | collective-permute-start | bytes 405512 | tf_op jit(solution)/shard_map/ppermute | solution.py:44
  19.3 0.9 %collective-permute-start.6 = (f32[88,128]{1,0:T(8,128)}, f32[88,128]{1,0:T(8,128)S(1)}, u32[]{:S(2)}, u32[]{:S(2)}) collective-permute-start(f32[88,128]{1,0:T(8,128)} %get-tuple-element.34), channel_id=1, source_target_pairs={{0,1},{1,2},{2,3},{3,4},{4,5},{5,6},{6,7},{7,0},{8,9},{9,10},{10,1... | collective-permute-start | bytes 135176 | tf_op jit(solution)/shard_map/ppermute | solution.py:44
  20.3 3.5 %collective-permute-start.7 = (f32[88,128]{1,0:T(8,128)}, f32[88,128]{1,0:T(8,128)S(1)}, u32[]{:S(2)}, u32[]{:S(2)}) collective-permute-start(f32[88,128]{1,0:T(8,128)} %get-tuple-element.35), channel_id=1, source_target_pairs={{0,7},{1,0},{2,1},{3,2},{4,3},{5,4},{6,5},{7,6},{8,15},{9,8},{10,9... | collective-permute-start | bytes 135176 | tf_op jit(solution)/shard_map/ppermute | solution.py:44
  23.8 1.6 %collective-permute-done.6.hy_lo = f32[88,128]{1,0:T(8,128)S(1)} collective-permute-done((f32[88,128]{1,0:T(8,128)}, f32[88,128]{1,0:T(8,128)S(1)}, u32[]{:S(2)}, u32[]{:S(2)}) %collective-permute-start.6) | collective-permute-done | bytes 45088 | tf_op jit(solution)/shard_map/ppermute | solution.py:44
  25.5 0.6 %copy-done.8 = f32[88,128]{1,0:T(8,128)} copy-done((f32[88,128]{1,0:T(8,128)}, f32[88,128]{1,0:T(8,128)S(1)}, u32[]{:S(2)}) %copy-start.8) | copy-done | bytes 45080
  26.2 5.1 %shard_map.158 = (f32[9,12,6,384]{3,2,1,0:T(8,128)}, f32[6,12,6,384]{3,2,1,0:T(8,128)}, f32[6,6,384]{2,1,0:T(8,128)}, f32[9,8,2,128]{3,2,1,0:T(2,128)}, f32[6,8,...) custom-call(f32[9,12,6,384]{3,2,1,0:T(8,128)} %fw.5, ...), custom_call_target="tpu_custom_call" | custom-call | tf_op jit(solution)/shard_map/pallas_call | solution.py:731
  31.2 2.7 %collective-permute-start.8 = (f32[24,128]{1,0:T(8,128)}, f32[24,128]{1,0:T(8,128)S(1)}, u32[]{:S(2)}, u32[]{:S(2)}) collective-permute-start(f32[24,128]{1,0:T(8,128)} %get-tuple-element.40), channel_id=1, source_target_pairs={{0,8},{8,16},{16,24},{24,0},{1,9},{9,17},{17,25},{25,1},{2,10},{10... | collective-permute-start | bytes 36872 | tf_op jit(solution)/shard_map/ppermute | solution.py:44
  33.9 1.0 %collective-permute-done.8.hx_lo = f32[24,128]{1,0:T(8,128)S(1)} collective-permute-done((f32[24,128]{1,0:T(8,128)}, f32[24,128]{1,0:T(8,128)S(1)}, u32[]{:S(2)}, u32[]{:S(2)}) %collective-permute-start.8) | collective-permute-done | bytes 12320 | tf_op jit(solution)/shard_map/ppermute | solution.py:44
  35.3 1.9 %collective-permute-done.9.hx_hi = f32[24,128]{1,0:T(8,128)S(1)} collective-permute-done((f32[24,128]{1,0:T(8,128)}, f32[24,128]{1,0:T(8,128)S(1)}, u32[]{:S(2)}, u32[]{:S(2)}) %collective-permute-start.9) | collective-permute-done | bytes 12320 | tf_op jit(solution)/shard_map/ppermute | solution.py:44
  38.0 0.6 %pad_dynamic-update-slice_fusion.1 = f32[16,128]{1,0:T(8,128)} fusion(f32[16,128]{1,0:T(8,128)} %get-tuple-element.42, f32[4,6]{1,0:T(4,128)S(1)} %bitcast.23), kind=kLoop, calls=%fused_computation.7 | loop fusion | bytes 2144 | tf_op jit(solution)/shard_map/dynamic_update_slice | solution.py:664
  38.6 0.6 %pad_dynamic-update-slice_fusion = f32[16,128]{1,0:T(8,128)} fusion(f32[16,128]{1,0:T(8,128)} %get-tuple-element.43, f32[4,6]{1,0:T(4,128)S(1)} %bitcast.22), kind=kLoop, calls=%fused_computation.6 | loop fusion | bytes 2144 | tf_op jit(solution)/shard_map/dynamic_update_slice | solution.py:664
  39.2 4.4 %collective-permute-start.11 = (f32[16,128]{1,0:T(8,128)}, f32[16,128]{1,0:T(8,128)S(1)}, u32[]{:S(2)}, u32[]{:S(2)}) collective-permute-start(f32[16,128]{1,0:T(8,128)} %pad_dynamic-update-slice_fusion), channel_id=1, source_target_pairs={{0,7},{1,0},{2,1},{3,2},{4,3},{5,4},{6,5},{7,6},{8,15},{9,8},{10,9... | collective-permute-start | bytes 24584 | tf_op jit(solution)/shard_map/ppermute | solution.py:44
  43.6 0.7 %collective-permute-done.10.hy_lo = f32[16,128]{1,0:T(8,128)S(1)} collective-permute-done((f32[16,128]{1,0:T(8,128)}, f32[16,128]{1,0:T(8,128)S(1)}, u32[]{:S(2)}, u32[]{:S(2)}) %collective-permute-start.10) | collective-permute-done | bytes 8224 | tf_op jit(solution)/shard_map/ppermute | solution.py:44
  44.3 0.3 collective-permute-done.11.hy_hi
  45.2 2.2 %shard_map.159 = (f32[9,12,6,384]{3,2,1,0:T(8,128)}, f32[9,8,2,128]{3,2,1,0:T(2,128)}) custom-call(f32[9,12,6,384]{3,2,1,0:T(8,128)} %get-tuple-element.36.fout_in, f32[9,8,2,128]{3,2,1,0:T(2,128)} %get-tuple-element.37.cout_in, f32[6,6,384]{2,1,0:T(8,128)} %get-tuple-element.38.fface, ...), custom_call_target="tpu_custom_call", output_to_operand_aliasing={{0}: (0, {}), {1}: (1, {})} | custom-call | tf_op jit(solution)/shard_map/pallas_call | solution.py:678
  (47 shorter events, 1.9 us)
Async XLA Ops:
  2.9 8.6 %collective-permute-start = (f32[264,128]{1,0:T(8,128)}, f32[264,128]{1,0:T(8,128)S(1)}, u32[]{:S(2)}, u32[]{:S(2)}) collective-permute-start(f32[264,128]{1,0:T(8,128)} %get-tuple-element.26), channel_id=1, source_target_pairs={{0,8},{8,16},{16,24},{24,0},{1,9},{9,17},{17,25},{25,1},{2,10},{10... | collective-permute-start | bytes 405512 | tf_op jit(solution)/shard_map/ppermute | solution.py:44
  5.5 6.1 %collective-permute-start.1 = (f32[264,128]{1,0:T(8,128)}, f32[264,128]{1,0:T(8,128)S(1)}, u32[]{:S(2)}, u32[]{:S(2)}) collective-permute-start(f32[264,128]{1,0:T(8,128)} %get-tuple-element.27), channel_id=1, source_target_pairs={{0,24},{8,0},{16,8},{24,16},{1,25},{9,1},{17,9},{25,17},{2,26},{10... | collective-permute-start | bytes 405512 | tf_op jit(solution)/shard_map/ppermute | solution.py:44
  5.5 6.0 %collective-permute-start.2 = (f32[88,128]{1,0:T(8,128)}, f32[88,128]{1,0:T(8,128)S(1)}, u32[]{:S(2)}, u32[]{:S(2)}) collective-permute-start(f32[88,128]{1,0:T(8,128)} %get-tuple-element.28), channel_id=1, source_target_pairs={{0,1},{1,2},{2,3},{3,4},{4,5},{5,6},{6,7},{7,0},{8,9},{9,10},{10,1... | collective-permute-start | bytes 135176 | tf_op jit(solution)/shard_map/ppermute | solution.py:44
  6.7 4.8 %collective-permute-start.3 = (f32[88,128]{1,0:T(8,128)}, f32[88,128]{1,0:T(8,128)S(1)}, u32[]{:S(2)}, u32[]{:S(2)}) collective-permute-start(f32[88,128]{1,0:T(8,128)} %get-tuple-element.29), channel_id=1, source_target_pairs={{0,7},{1,0},{2,1},{3,2},{4,3},{5,4},{6,5},{7,6},{8,15},{9,8},{10,9... | collective-permute-start | bytes 135176 | tf_op jit(solution)/shard_map/ppermute | solution.py:44
  11.5 0.6 %copy-start.6 = (f32[88,128]{1,0:T(8,128)}, f32[88,128]{1,0:T(8,128)S(1)}, u32[]{:S(2)}) copy-start(f32[88,128]{1,0:T(8,128)S(1)} %collective-permute-done.2.hy_lo) | copy-start | bytes 135172
  11.5 0.6 %copy-start.7 = (f32[88,128]{1,0:T(8,128)}, f32[88,128]{1,0:T(8,128)S(1)}, u32[]{:S(2)}) copy-start(f32[88,128]{1,0:T(8,128)S(1)} %collective-permute-done.3.hy_hi) | copy-start | bytes 135172
  11.5 0.7 %copy-start = (f32[264,128]{1,0:T(8,128)}, f32[264,128]{1,0:T(8,128)S(1)}, u32[]{:S(2)}) copy-start(f32[264,128]{1,0:T(8,128)S(1)} %collective-permute-done.hx_lo) | copy-start | bytes 405508
  12.2 0.7 %copy-start.1 = (f32[264,128]{1,0:T(8,128)}, f32[264,128]{1,0:T(8,128)S(1)}, u32[]{:S(2)}) copy-start(f32[264,128]{1,0:T(8,128)S(1)} %collective-permute-done.1.hx_hi) | copy-start | bytes 405508
  16.7 8.8 %collective-permute-start.4 = (f32[264,128]{1,0:T(8,128)}, f32[264,128]{1,0:T(8,128)S(1)}, u32[]{:S(2)}, u32[]{:S(2)}) collective-permute-start(f32[264,128]{1,0:T(8,128)} %get-tuple-element.32), channel_id=1, source_target_pairs={{0,8},{8,16},{16,24},{24,0},{1,9},{9,17},{17,25},{25,1},{2,10},{10... | collective-permute-start | bytes 405512 | tf_op jit(solution)/shard_map/ppermute | solution.py:44
  19.3 6.1 %collective-permute-start.5 = (f32[264,128]{1,0:T(8,128)}, f32[264,128]{1,0:T(8,128)S(1)}, u32[]{:S(2)}, u32[]{:S(2)}) collective-permute-start(f32[264,128]{1,0:T(8,128)} %get-tuple-element.33), channel_id=1, source_target_pairs={{0,24},{8,0},{16,8},{24,16},{1,25},{9,1},{17,9},{25,17},{2,26},{10... | collective-permute-start | bytes 405512 | tf_op jit(solution)/shard_map/ppermute | solution.py:44
  19.3 6.1 %collective-permute-start.6 = (f32[88,128]{1,0:T(8,128)}, f32[88,128]{1,0:T(8,128)S(1)}, u32[]{:S(2)}, u32[]{:S(2)}) collective-permute-start(f32[88,128]{1,0:T(8,128)} %get-tuple-element.34), channel_id=1, source_target_pairs={{0,1},{1,2},{2,3},{3,4},{4,5},{5,6},{6,7},{7,0},{8,9},{9,10},{10,1... | collective-permute-start | bytes 135176 | tf_op jit(solution)/shard_map/ppermute | solution.py:44
  20.3 5.1 %collective-permute-start.7 = (f32[88,128]{1,0:T(8,128)}, f32[88,128]{1,0:T(8,128)S(1)}, u32[]{:S(2)}, u32[]{:S(2)}) collective-permute-start(f32[88,128]{1,0:T(8,128)} %get-tuple-element.35), channel_id=1, source_target_pairs={{0,7},{1,0},{2,1},{3,2},{4,3},{5,4},{6,5},{7,6},{8,15},{9,8},{10,9... | collective-permute-start | bytes 135176 | tf_op jit(solution)/shard_map/ppermute | solution.py:44
  25.4 0.6 %copy-start.8 = (f32[88,128]{1,0:T(8,128)}, f32[88,128]{1,0:T(8,128)S(1)}, u32[]{:S(2)}) copy-start(f32[88,128]{1,0:T(8,128)S(1)} %collective-permute-done.6.hy_lo) | copy-start | bytes 135172
  25.4 0.6 %copy-start.9 = (f32[88,128]{1,0:T(8,128)}, f32[88,128]{1,0:T(8,128)S(1)}, u32[]{:S(2)}) copy-start(f32[88,128]{1,0:T(8,128)S(1)} %collective-permute-done.7.hy_hi) | copy-start | bytes 135172
  25.4 0.7 %copy-start.2 = (f32[264,128]{1,0:T(8,128)}, f32[264,128]{1,0:T(8,128)S(1)}, u32[]{:S(2)}) copy-start(f32[264,128]{1,0:T(8,128)S(1)} %collective-permute-done.4.hx_lo) | copy-start | bytes 405508
  25.4 0.7 %copy-start.3 = (f32[264,128]{1,0:T(8,128)}, f32[264,128]{1,0:T(8,128)S(1)}, u32[]{:S(2)}) copy-start(f32[264,128]{1,0:T(8,128)S(1)} %collective-permute-done.5.hx_hi) | copy-start | bytes 405508
  31.2 3.7 %collective-permute-start.8 = (f32[24,128]{1,0:T(8,128)}, f32[24,128]{1,0:T(8,128)S(1)}, u32[]{:S(2)}, u32[]{:S(2)}) collective-permute-start(f32[24,128]{1,0:T(8,128)} %get-tuple-element.40), channel_id=1, source_target_pairs={{0,8},{8,16},{16,24},{24,0},{1,9},{9,17},{17,25},{25,1},{2,10},{10... | collective-permute-start | bytes 36872 | tf_op jit(solution)/shard_map/ppermute | solution.py:44
  33.9 3.3 %collective-permute-start.9 = (f32[24,128]{1,0:T(8,128)}, f32[24,128]{1,0:T(8,128)S(1)}, u32[]{:S(2)}, u32[]{:S(2)}) collective-permute-start(f32[24,128]{1,0:T(8,128)} %get-tuple-element.41), channel_id=1, source_target_pairs={{0,24},{8,0},{16,8},{24,16},{1,25},{9,1},{17,9},{25,17},{2,26},{10... | collective-permute-start | bytes 36872 | tf_op jit(solution)/shard_map/ppermute | solution.py:44
  35.0 9.7 %copy-start.4 = (f32[24,128]{1,0:T(8,128)}, f32[24,128]{1,0:T(8,128)S(1)}, u32[]{:S(2)}) copy-start(f32[24,128]{1,0:T(8,128)S(1)} %collective-permute-done.8.hx_lo) | copy-start | bytes 36868
  37.2 7.4 %copy-start.5 = (f32[24,128]{1,0:T(8,128)}, f32[24,128]{1,0:T(8,128)S(1)}, u32[]{:S(2)}) copy-start(f32[24,128]{1,0:T(8,128)S(1)} %collective-permute-done.9.hx_hi) | copy-start | bytes 36868
  38.6 5.7 %collective-permute-start.10 = (f32[16,128]{1,0:T(8,128)}, f32[16,128]{1,0:T(8,128)S(1)}, u32[]{:S(2)}, u32[]{:S(2)}) collective-permute-start(f32[16,128]{1,0:T(8,128)} %pad_dynamic-update-slice_fusion.1), channel_id=1, source_target_pairs={{0,1},{1,2},{2,3},{3,4},{4,5},{5,6},{6,7},{7,0},{8,9},{9,10},{10,1... | collective-permute-start | bytes 24584 | tf_op jit(solution)/shard_map/ppermute | solution.py:44
  39.2 5.4 %collective-permute-start.11 = (f32[16,128]{1,0:T(8,128)}, f32[16,128]{1,0:T(8,128)S(1)}, u32[]{:S(2)}, u32[]{:S(2)}) collective-permute-start(f32[16,128]{1,0:T(8,128)} %pad_dynamic-update-slice_fusion), channel_id=1, source_target_pairs={{0,7},{1,0},{2,1},{3,2},{4,3},{5,4},{6,5},{7,6},{8,15},{9,8},{10,9... | collective-permute-start | bytes 24584 | tf_op jit(solution)/shard_map/ppermute | solution.py:44
  44.3 0.6 %copy-start.10 = (f32[16,128]{1,0:T(8,128)}, f32[16,128]{1,0:T(8,128)S(1)}, u32[]{:S(2)}) copy-start(f32[16,128]{1,0:T(8,128)S(1)} %collective-permute-done.10.hy_lo) | copy-start | bytes 24580
  44.6 0.6 %copy-start.11 = (f32[16,128]{1,0:T(8,128)}, f32[16,128]{1,0:T(8,128)S(1)}, u32[]{:S(2)}) copy-start(f32[16,128]{1,0:T(8,128)S(1)} %collective-permute-done.11.hy_hi) | copy-start | bytes 24580
